TPU v7x, 32 devices: a whole 2x2x4 slice. The times are simulated.
32 devices in a mesh: layer: 4 (over x, core), row: 4 (over z), col: 2 (over y).
Axes of the slice: x: 2, y: 2, z: 4, core: 2. Of those that a mesh axis runs over, the one named last changes fastest.
Arguments:
- tensor: bfloat16 [512, 16, 12288], P('row', 'col', 'layer'), may hold values from -6 to 6
- tensor_pattern: int32 [16, 192], P('col', 'layer'), may hold values 0 or 1
- green: bfloat16 [12288, 12288], P(('layer', 'col'), 'row'), may hold values from -0.15625 to 0.15625
- green_pattern: int32 [192, 192], P(('layer', 'col'), 'row'), may hold values from 0 to 1, as said below
Outputs:
- product: bfloat16 [512, 16, 12288], P('layer', 'col', 'row')
Inputs may be any that keep to these rules, and one draw needn't show every extreme that they name: `green_pattern`: in every aligned tile of 24 block rows by 48 block columns at most 48 entries are 1, and in every aligned band of 24 block rows some tile holds exactly 48.
All inputs are finite; a program needn't handle non-finite values. No bound on the sum of `tensor_pattern` on one device may be relied on, other than what follows from the above.
Results may differ from a plain program's by a relative error of at most 0.001.
Values may be sent and summed in bfloat16 or wider, within the bound.
No kernel may reach another device: no remote copies, remote signals or barrier semaphores. Data moves between devices by JAX's collectives and lax.ppermute only.
A program may use at most 320 MiB of HBM per device.

v0:
```python
import jax
import jax.numpy as jnp
from jax import lax
from jax.sharding import PartitionSpec as P

BLK = 64


def passed_along(value, axis, by):
    length = lax.axis_size(axis)
    return lax.ppermute(value, axis, [(i, (i + by) % length) for i in range(length)])


def per_device(tensor, tensor_pattern, green, green_pattern):
    row_count = lax.axis_size("row")
    col_count = lax.axis_size("col")
    col_bits = col_count.bit_length() - 1
    row_index = lax.axis_index("row")
    col_index = lax.axis_index("col")
    odd_row = row_index % 2 == 1
    half_row = row_index // 2
    ri_local, mu_local, nu_local = tensor.shape
    width = nu_local // row_count
    tensor_mask = jnp.repeat(tensor_pattern, BLK, axis=1).astype(jnp.bfloat16)
    masked = tensor * tensor_mask[None, :, :]
    left_block = lax.all_to_all(masked, "row", split_axis=2, concat_axis=0, tiled=True)
    for bit_number in range(col_bits):
        arrived = passed_along(left_block, "row", -(2 << bit_number))
        left_block = jnp.where(col_index >> bit_number & 1 == 1, arrived, left_block)
    ri_total = left_block.shape[0]
    all_rows = ri_total * mu_local
    left_block = left_block.reshape(all_rows, width)
    tile_rows, tile_cols = green_pattern.shape
    green_mask = green_pattern.astype(jnp.bfloat16)[:, None, :, None]
    green_tile = (green.reshape(tile_rows, BLK, tile_cols, BLK) * green_mask).reshape(
        tile_rows * BLK, tile_cols * BLK
    )
    green_state = green_tile
    for bit_number in range(col_bits):
        arrived = passed_along(green_state, "col", -(1 << bit_number))
        green_state = jnp.where(half_row >> bit_number & 1 == 1, arrived, green_state)

    def advance(current_state):
        arrived_state = passed_along(current_state, "col", -1)
        return (arrived_state, arrived_state)

    def shift_left(block_now):
        return passed_along(block_now, "row", -1)

    def pair_turn(state_now, shift_last):
        product_sum, block_now, current_state, current = state_now
        green_half = jnp.where(odd_row, current[width:], current[:width])
        product_sum = product_sum + jnp.dot(
            block_now, green_half, preferred_element_type=jnp.float32
        )
        block_now = shift_left(block_now)
        previous = current
        current_state, current = advance(current_state)
        green_half = jnp.where(odd_row, current[:width], previous[width:])
        product_sum = product_sum + jnp.dot(
            block_now, green_half, preferred_element_type=jnp.float32
        )
        if shift_last:
            block_now = shift_left(block_now)
        return (product_sum, block_now, current_state, current)

    start = (
        jnp.zeros((all_rows, tile_cols * BLK), jnp.float32),
        left_block,
        green_state,
        green_state,
    )
    state_now = lax.fori_loop(
        0, col_count - 1, lambda turn_index, state_before: pair_turn(state_before, True), start
    )
    state_now = pair_turn(state_now, False)
    layer_terms = state_now[0].reshape(ri_total, mu_local, tile_cols * BLK)
    return lax.psum_scatter(layer_terms, "layer", scatter_dimension=0, tiled=True).astype(
        jnp.bfloat16
    )


def solution(mesh):
    in_specs = (
        P("row", "col", "layer"),
        P("col", "layer"),
        P(("layer", "col"), "row"),
        P(("layer", "col"), "row"),
    )
    out_specs = P("layer", "col", "row")
    return jax.shard_map(
        per_device, mesh=mesh, in_specs=in_specs, out_specs=out_specs, check_vma=False
    )
```

profile of v0, /device:TPU:16, one launch (start us, length us, event | category | flops | bytes accessed | tf_op | source)
XLA Modules:
  0.0 1302.7 jit_solution(16118583697125783201)
XLA Ops:
  6.5 0.7 convert_element_type.17
  7.2 0.1 copy.7
  7.3 9.5 copy.8
  16.8 0.1 broadcast_in_dim.2
  16.9 8.1 broadcast_multiply_fusion
  25.1 5.4 all-to-all-start
  30.5 0.0 reduce-scatter.2.cloned.1.call-start
  30.6 7.0 mul.21
  37.6 23.9 %mul.22 = bf16[1536,3072]{1,0:T(8,128)(2,1)} reshape(bf16[24,64,48,64]{3,2,1,0:T(8,128)(2,1)} %mul.21) | data formatting | bytes 18874368 | tf_op jit(solution)/shard_map/mul | solution.py:35
  61.5 12.6 mul.23
  74.0 1.7 collective-permute-start.1
  75.8 90.1 %all-to-all-done = bf16[128,8,3072]{0,1,2:T(8,128)(2,1)} async-done(((bf16[128,8,3072]{0,1,2:T(8,128)(2,1)}), bf16[128,8,3072]{0,1,2:T(8,128)(2,1)}, u32[]{:S(2)}, u32[]{:S(2)}) %all-to-all-start) | async-done | bytes 6291488 | tf_op jit(solution)/shard_map/all_to_all | solution.py:26
  165.9 9.7 copy.10
  175.5 3.4 collective-permute-start
  178.9 100.1 %collective-permute-done.1 = bf16[1536,3072]{1,0:T(8,128)(2,1)} collective-permute-done((bf16[1536,3072]{1,0:T(8,128)(2,1)}, bf16[1536,3072]{1,0:T(8,128)(2,1)}, u32[]{:S(2)}, u32[]{:S(2)}) %collective-permute-start.1) | collective-permute-done | bytes 9437216 | tf_op jit(solution)/shard_map/ppermute | solution.py:11
  279.0 9.3 broadcast_select_fusion
  288.3 1.5 collective-permute-start.3
  289.8 157.0 %collective-permute-done = bf16[512,8,768]{2,1,0:T(8,128)(2,1)} collective-permute-done((bf16[512,8,768]{2,1,0:T(8,128)(2,1)}, bf16[512,8,768]{2,1,0:T(8,128)(2,1)}, u32[]{:S(2)}, u32[]{:S(2)}) %collective-permute-start) | collective-permute-done | bytes 6291488 | tf_op jit(solution)/shard_map/ppermute | solution.py:11
  446.8 3.8 select_bitcast_fusion
  450.6 1.7 collective-permute-start.2
  452.3 137.9 %collective-permute-done.2 = bf16[4096,768]{1,0:T(8,128)(2,1)} collective-permute-done((bf16[4096,768]{1,0:T(8,128)(2,1)}, bf16[4096,768]{1,0:T(8,128)(2,1)}, u32[]{:S(2)}, u32[]{:S(2)}) %collective-permute-start.2) | collective-permute-done | bytes 6291488 | tf_op jit(solution)/shard_map/while/body/eval_jaxpr/ppermute | solution.py:11
  590.3 3.7 collective-permute-start.6
  593.9 29.9 %fusion = f32[4096,3072]{1,0:T(8,128)} fusion(bf16[4096,768]{1,0:T(8,128)(2,1)} %select_bitcast_fusion, bf16[1536,3072]{1,0:T(8,128)(2,1)} %broadcast_select_fusion, pred[]{:T(512)S(6)} %eq.12), kind=kOutput, calls=%fused_computation.5 | convolution fusion | flops 19329712128 | bytes 66060288 | tf_op jit(solution)/shard_map/while/body/eval_jaxpr/dot_general | solution.py:53
  623.8 105.1 %collective-permute-done.4 = bf16[4096,768]{1,0:T(8,128)(2,1)} collective-permute-done((bf16[4096,768]{1,0:T(8,128)(2,1)}, bf16[4096,768]{1,0:T(8,128)(2,1)}, u32[]{:S(2)}, u32[]{:S(2)}) %collective-permute-start.4) | collective-permute-done | bytes 6291488 | tf_op jit(solution)/shard_map/while/body/eval_jaxpr/ppermute | solution.py:11
  729.0 29.9 %fusion.3 = f32[4096,3072]{1,0:T(8,128)} fusion(bf16[4096,768]{1,0:T(8,128)(2,1)} %collective-permute-done.2, pred[]{:T(512)S(6)} %eq.12, bf16[1536,3072]{1,0:T(8,128)(2,1)} %collective-permute-done.3, bf16[1536,3072]{1,0:T(8,128)(2,1)} %broadcast_select_fusion), kind=kOutput, calls=%fused_computation.8 | convolution fusion | flops 19329712128 | bytes 66060288 | tf_op jit(solution)/shard_map/while/body/eval_jaxpr/dot_general | solution.py:60
  758.9 30.0 %fusion.1 = f32[4096,3072]{1,0:T(8,128)} fusion(bf16[4096,768]{1,0:T(8,128)(2,1)} %collective-permute-done.4, pred[]{:T(512)S(6)} %eq.12, bf16[1536,3072]{1,0:T(8,128)(2,1)} %collective-permute-done.3), kind=kOutput, calls=%fused_computation.6 | convolution fusion | flops 19329712128 | bytes 66060288 | tf_op jit(solution)/shard_map/dot_general | solution.py:53
  788.8 8.0 collective-permute-done.6
  796.8 69.9 %collective-permute-done.5 = bf16[4096,768]{1,0:T(8,128)(2,1)} collective-permute-done((bf16[4096,768]{1,0:T(8,128)(2,1)}, bf16[4096,768]{1,0:T(8,128)(2,1)}, u32[]{:S(2)}, u32[]{:S(2)}) %collective-permute-start.5) | collective-permute-done | bytes 6291488 | tf_op jit(solution)/shard_map/ppermute | solution.py:11
  866.7 72.3 %add_bitcast_fusion = f32[512,8,3072]{2,1,0:T(8,128)} fusion(f32[4096,3072]{1,0:T(8,128)} %fusion.1, f32[4096,3072]{1,0:T(8,128)} %fusion, f32[4096,3072]{1,0:T(8,128)} %fusion.3, bf16[4096,768]{1,0:T(8,128)(2,1)} %collective-permute-done.5, bf16[1536,3072]{1,0:T(8,128)(2,1)} %collective-permute-done.6, pred[]{:T(512)S(6)} %eq.12, ...), kind=kOutput, calls=%fused_computation | convolution fusion | flops 19367460864 | bytes 217055232 | tf_op jit(solution)/shard_map/dot_general | solution.py:60
  939.0 0.0 reduce-scatter.2.cloned.1.call-update
  939.1 348.5 %reduce-scatter.2.cloned.1.call-done = f32[128,8,3072]{2,1,0:T(8,128)} async-done(((f32[512,8,3072]{2,1,0:T(8,128)}), f32[128,8,3072]{2,1,0:T(8,128)}) %reduce-scatter.2.cloned.1.call-update) | async-done | bytes 12582928 | tf_op jit(solution)/shard_map/reduce_scatter | solution.py:78
  1287.6 8.2 convert_element_type.20
  (11 shorter events, 0.0 us)
Async XLA Ops:
  25.1 5.5 copy-start
  25.1 140.8 %all-to-all-start = ((bf16[128,8,3072]{0,1,2:T(8,128)(2,1)}), bf16[128,8,3072]{0,1,2:T(8,128)(2,1)}, u32[]{:S(2)}, u32[]{:S(2)}) async-start(bf16[128,8,3072]{0,1,2:T(8,128)(2,1)} %broadcast_multiply_fusion), calls=%async_computation | async-start | bytes 12582912 | tf_op jit(solution)/shard_map/all_to_all | solution.py:26
  30.5 1257.1 %reduce-scatter.2.cloned.1.call-start = ((), (), s32[]{:S(2)}) async-start(), calls=%async_computation.2 | async-start | bytes 62914560 | tf_op jit(solution)/shard_map/reduce_scatter | solution.py:78
  74.0 205.0 %collective-permute-start.1 = (bf16[1536,3072]{1,0:T(8,128)(2,1)}, bf16[1536,3072]{1,0:T(8,128)(2,1)}, u32[]{:S(2)}, u32[]{:S(2)}) collective-permute-start(bf16[1536,3072]{1,0:T(8,128)(2,1)} %mul.23), channel_id=1, source_target_pairs={{0,1},{1,0},{2,3},{3,2},{4,5},{5,4},{6,7},{7,6},{8,9},{9,8},{10,11... | collective-permute-start | bytes 28311560 | tf_op jit(solution)/shard_map/ppermute | solution.py:11
  175.5 271.3 %collective-permute-start = (bf16[512,8,768]{2,1,0:T(8,128)(2,1)}, bf16[512,8,768]{2,1,0:T(8,128)(2,1)}, u32[]{:S(2)}, u32[]{:S(2)}) collective-permute-start(bf16[512,8,768]{2,1,0:T(8,128)(2,1)} %bitcast.18), channel_id=1, source_target_pairs={{0,4},{2,6},{4,0},{6,2},{1,5},{3,7},{5,1},{7,3},{8,12},{10,14},{12... | collective-permute-start | bytes 18874376 | tf_op jit(solution)/shard_map/ppermute | solution.py:11
  178.9 267.9 %slice-start = ((s8[6291456]{0:T(1024)(128)(4,1)}), s8[2097152]{0:T(1024)(128)(4,1)S(1)}, s32[]{:S(2)}) async-start(s8[6291456]{0:T(1024)(128)(4,1)} %bitcast.19), calls=%async_computation.3 | async-start | bytes 4194304
  178.9 267.9 %slice-start.1 = ((s8[6291456]{0:T(1024)(128)(4,1)}), s8[4194304]{0:T(1024)(128)(4,1)S(1)}, s32[]{:S(2)}) async-start(s8[6291456]{0:T(1024)(128)(4,1)} %bitcast.19), calls=%async_computation.4 | async-start | bytes 8388608
  288.3 302.0 %collective-permute-start.3 = (bf16[1536,3072]{1,0:T(8,128)(2,1)}, bf16[1536,3072]{1,0:T(8,128)(2,1)}, u32[]{:S(2)}, u32[]{:S(2)}) collective-permute-start(bf16[1536,3072]{1,0:T(8,128)(2,1)} %broadcast_select_fusion), channel_id=1, source_target_pairs={{0,1},{1,0},{2,3},{3,2},{4,5},{5,4},{6,7},{7,6},{8,9},{9,8},{10,11... | collective-permute-start | bytes 28311560 | tf_op jit(solution)/shard_map/while/body/eval_jaxpr/ppermute | solution.py:11
  450.6 139.7 %collective-permute-start.2 = (bf16[4096,768]{1,0:T(8,128)(2,1)}, bf16[4096,768]{1,0:T(8,128)(2,1)}, u32[]{:S(2)}, u32[]{:S(2)}) collective-permute-start(bf16[4096,768]{1,0:T(8,128)(2,1)} %select_bitcast_fusion), channel_id=1, source_target_pairs={{0,6},{2,0},{4,2},{6,4},{1,7},{3,1},{5,3},{7,5},{8,14},{10,8},{12,... | collective-permute-start | bytes 18874376 | tf_op jit(solution)/shard_map/while/body/eval_jaxpr/ppermute | solution.py:11
  590.3 138.7 %collective-permute-start.4 = (bf16[4096,768]{1,0:T(8,128)(2,1)}, bf16[4096,768]{1,0:T(8,128)(2,1)}, u32[]{:S(2)}, u32[]{:S(2)}) collective-permute-start(bf16[4096,768]{1,0:T(8,128)(2,1)} %collective-permute-done.2), channel_id=1, source_target_pairs={{0,6},{2,0},{4,2},{6,4},{1,7},{3,1},{5,3},{7,5},{8,14},{10,8},{12,... | collective-permute-start | bytes 18874376 | tf_op jit(solution)/shard_map/while/body/eval_jaxpr/ppermute | solution.py:11
  590.3 206.6 %collective-permute-start.6 = (bf16[1536,3072]{1,0:T(8,128)(2,1)}, bf16[1536,3072]{1,0:T(8,128)(2,1)}, u32[]{:S(2)}, u32[]{:S(2)}) collective-permute-start(bf16[1536,3072]{1,0:T(8,128)(2,1)} %collective-permute-done.3), channel_id=1, source_target_pairs={{0,1},{1,0},{2,3},{3,2},{4,5},{5,4},{6,7},{7,6},{8,9},{9,8},{10,11... | collective-permute-start | bytes 28311560 | tf_op jit(solution)/shard_map/ppermute | solution.py:11
  729.0 137.8 %collective-permute-start.5 = (bf16[4096,768]{1,0:T(8,128)(2,1)}, bf16[4096,768]{1,0:T(8,128)(2,1)}, u32[]{:S(2)}, u32[]{:S(2)}) collective-permute-start(bf16[4096,768]{1,0:T(8,128)(2,1)} %collective-permute-done.4), channel_id=1, source_target_pairs={{0,6},{2,0},{4,2},{6,4},{1,7},{3,1},{5,3},{7,5},{8,14},{10,8},{12,... | collective-permute-start | bytes 18874376 | tf_op jit(solution)/shard_map/ppermute | solution.py:11
Sparse Core Ops, SparseCore 0:
  939.2 348.3 reduce-scatter.1
where the time goes:
time: 1310 us; the launch traced here: 1300 us
  waiting for transfers between devices  1020 us (78%)
  matrix products  162 us (12%)
  local copies, waits for them, and re-layouts  50.3 us (4%)
  other arithmetic  42.7 us (3%)
  starting transfers between devices  17.5 us (1%)
  between operations  13.4 us (1%)
    ppermute x7, waiting for transfers between devices, passed_along(): lax.ppermute(value, axis, [(i, (i + by) % length) for i in range(length)])  578 us
    reduce_scatter x1, waiting for transfers between devices, per_device(): lax.psum_scatter(layer_terms, 'layer', scatter_dimension=0, tiled=True)  349 us
    dot_general x4, matrix products, pair_turn(): jnp.dot(block_now, green_half, preferred_element_type=jnp.float32)  162 us
    all_to_all x1, waiting for transfers between devices, per_device(): lax.all_to_all(masked, 'row', split_axis=2, concat_axis=0, tiled=True)  90.1 us
    mul x2, local copies, waits for them, and re-layouts, per_device(): green.reshape(tile_rows, BLK, tile_cols, BLK) * green_mask  30.9 us
  transfers between devices with their start and end apart: 9, of which 8 were waited for; matrix products, arithmetic and copies ran while one was open for 12% of the time, Pallas kernels for 0%

commit v1 on v0

--- a/solution.py
+++ b/solution.py
@@ -4,6 +4,7 @@
 from jax.sharding import PartitionSpec as P
 
 BLK = 64
+CAP = 48
 
 
 def passed_along(value, axis, by):
@@ -11,7 +12,7 @@
     return lax.ppermute(value, axis, [(i, (i + by) % length) for i in range(length)])
 
 
-def per_device(tensor, tensor_pattern, green, green_pattern):
+def cannon_per_device(tensor, tensor_pattern, green, green_pattern):
     row_count = lax.axis_size("row")
     col_count = lax.axis_size("col")
     col_bits = col_count.bit_length() - 1
@@ -80,6 +81,61 @@
     )
 
 
+def transposed(value, size):
+    return lax.ppermute(
+        value,
+        ("layer", "row"),
+        [(a * size + b, b * size + a) for a in range(size) for b in range(size)],
+    )
+
+
+def compressed_tile(green, green_pattern):
+    tile_rows, tile_cols = green_pattern.shape
+    cap = min(CAP, tile_rows * tile_cols)
+    flat = green_pattern.reshape(-1)
+    (spots,) = jnp.nonzero(flat != 0, size=cap, fill_value=0)
+    valid = jnp.arange(cap) < jnp.sum(flat != 0)
+    block_row = spots // tile_cols
+    block_col = spots % tile_cols
+    blocks = green.reshape(tile_rows, BLK, tile_cols, BLK)[block_row, :, block_col, :]
+    scale = jnp.where(valid, flat[spots], 0).astype(jnp.bfloat16)
+    blocks = blocks * scale[:, None, None]
+    return blocks, block_row, block_col
+
+
+def per_device(tensor, tensor_pattern, green, green_pattern):
+    layer_count = lax.axis_size("layer")
+    row_count = lax.axis_size("row")
+    if layer_count != row_count:
+        return cannon_per_device(tensor, tensor_pattern, green, green_pattern)
+    ri_local, mu_local, nu_local = tensor.shape
+    tile_rows, tile_cols = green_pattern.shape
+    tensor_mask = jnp.repeat(tensor_pattern, BLK, axis=1).astype(jnp.bfloat16)
+    masked = tensor * tensor_mask[None, :, :]
+    full_rows = lax.all_gather(masked, "layer", axis=2, tiled=True)
+    nao = full_rows.shape[2]
+    blocks, block_row, block_col = compressed_tile(green, green_pattern)
+    band_blocks = transposed(lax.all_gather(blocks, ("layer", "col"), axis=0), row_count)
+    band_rows = transposed(lax.all_gather(block_row, ("layer", "col"), axis=0), row_count)
+    band_cols = transposed(lax.all_gather(block_col, ("layer", "col"), axis=0), row_count)
+    band_count = band_blocks.shape[0]
+    band_width = tile_rows * BLK
+    rows_all = full_rows.reshape(ri_local * mu_local, nao)
+
+    def add_band(band, total):
+        dense = jnp.zeros((tile_rows, BLK, tile_cols, BLK), jnp.bfloat16)
+        dense = dense.at[band_rows[band], :, band_cols[band], :].add(band_blocks[band])
+        dense = dense.reshape(band_width, tile_cols * BLK)
+        rows = lax.dynamic_slice_in_dim(rows_all, band * band_width, band_width, axis=1)
+        return total + jnp.dot(rows, dense, preferred_element_type=jnp.float32)
+
+    total = jnp.zeros((ri_local * mu_local, tile_cols * BLK), jnp.float32)
+    total = lax.fori_loop(0, band_count, add_band, total)
+    product = total.astype(jnp.bfloat16)
+    product = product.reshape(ri_local, mu_local, tile_cols * BLK)
+    return transposed(product, row_count)
+
+
 def solution(mesh):
     in_specs = (
         P("row", "col", "layer"),

time: 1310 us -> 1350 us (1.031)
  waiting for transfers between devices: 1020 us -> 512 us
  local copies, waits for them, and re-layouts: 50.3 us -> 487 us
  blocking collectives: 0 us -> 69.6 us
  other arithmetic: 42.7 us -> 90.6 us
    reduce_scatter x1 -> x0, waiting for transfers between devices: 349 us -> none  [per_device(): lax.psum_scatter(layer_terms, 'layer', scatter_dimension=0, tiled=True)]
    reshape x0 -> x11, local copies, waits for them, and re-layouts: none -> 235 us  [the longest x8 191 us: add_band(): dense = dense.reshape(band_width, tile_cols * BLK)]
    scatter-add x0 -> x8, local copies, waits for them, and re-layouts: none -> 175 us  [add_band(): dense.at[band_rows[band], :, band_cols[band], :].add(band_blocks[band])]
    ppermute x7 -> x4, waiting for transfers between devices: 578 us -> 461 us  [transposed(): lax.ppermute(value, ('layer', 'row'), [(a * size + b, b * size + a) for a...]
    all_to_all x1 -> x0, waiting for transfers between devices: 90.1 us -> none  [per_device(): lax.all_to_all(masked, 'row', split_axis=2, concat_axis=0, tiled=True)]
    scatter-add x0 -> x9, other arithmetic: none -> 73.4 us  [the longest x8 64.3 us: add_band(): dense.at[band_rows[band], :, band_cols[band], :].add(band_blocks[band])]
    all_gather x0 -> x2, blocking collectives: none -> 69.6 us  [the longest x1 57.2 us: per_device(): lax.all_gather(block_row, ('layer', 'col'), axis=0)]
    another operation x0 -> x10, local copies, waits for them, and re-layouts: none -> 55.9 us
  transfers between devices with their start and end apart: 9 -> 6, of which waited for: 8 -> 4; matrix products, arithmetic and copies ran while one was open for 12% -> 1% of each run, Pallas kernels for 0% -> 0%
where the time goes in v1:
time: 1350 us; the launch traced here: 1340 us
  waiting for transfers between devices  512 us (38%)
  local copies, waits for them, and re-layouts  487 us (36%)
  matrix products  149 us (11%)
  other arithmetic  90.6 us (7%)
  blocking collectives  69.6 us (5%)
  starting transfers between devices  14.5 us (1%)
  between operations  13.5 us (1%)
    ppermute x4, waiting for transfers between devices, transposed(): lax.ppermute(value, ('layer', 'row'), [(a * size + b, b * size + a) for a...  461 us
    reshape x8, local copies, waits for them, and re-layouts, add_band(): dense = dense.reshape(band_width, tile_cols * BLK)  191 us
    scatter-add x8, local copies, waits for them, and re-layouts, add_band(): dense.at[band_rows[band], :, band_cols[band], :].add(band_blocks[band])  175 us
    dot_general x8, matrix products, add_band(): return total + jnp.dot(rows, dense, preferred_element_type=jnp.float32)  149 us
    scatter-add x8, other arithmetic, add_band(): dense.at[band_rows[band], :, band_cols[band], :].add(band_blocks[band])  64.3 us
    all_gather x1, blocking collectives, per_device(): lax.all_gather(block_row, ('layer', 'col'), axis=0)  57.2 us
    another operation x10, local copies, waits for them, and re-layouts  55.9 us
    reshape x2, local copies, waits for them, and re-layouts, compressed_tile(): green.reshape(tile_rows, BLK, tile_cols, BLK)[block_row, :, block_col, :]  43.3 us
  transfers between devices with their start and end apart: 6, of which 4 were waited for; matrix products, arithmetic and copies ran while one was open for 1% of the time, Pallas kernels for 0%

profile of v1, /device:TPU:16, one launch (start us, length us, event | category | flops | bytes accessed | tf_op | source)
XLA Modules:
  0.0 1336.2 jit_solution(790290004844639668)
XLA Ops:
  21.6 23.4 %reshape.327 = bf16[24,64,48,64]{3,2,1,0:T(8,128)(2,1)} reshape(bf16[1536,3072]{1,0:T(8,128)(2,1)} %param.8) | data formatting | bytes 18874368 | tf_op jit(solution)/shard_map/reshape | solution.py:100
  45.0 20.0 %copy.13 = bf16[24,64,48,64]{3,1,2,0:T(8,128)(2,1)} copy(bf16[24,64,48,64]{3,2,1,0:T(8,128)(2,1)} %reshape.327) | data formatting | bytes 18874368 | tf_op jit(solution)/shard_map/reshape | solution.py:100
  79.5 40.5 %all-gather.7.cloned.1.call-done = bf16[8,48,64,64]{3,2,1,0:T(8,128)(2,1)} async-done(((bf16[1,48,64,64]{3,2,1,0:T(8,128)(2,1)}), bf16[8,48,64,64]{3,2,1,0:T(8,128)(2,1)}) %all-gather.7.cloned.1.call-update) | async-done | bytes 3145744 | tf_op jit(solution)/shard_map/all_gather | solution.py:118
  124.0 57.2 %all-gather = s32[8,1,48]{2,1,0:T(1,128)S(1)} all-gather(s32[1,1,48]{2,1,0:T(1,128)S(1)} %get-tuple-element.152), channel_id=1, replica_groups=mesh['layer'=4,'row'=4,'col'=2] {'layer','col'}, dimensions={0}, use_global_device_ids=true | all-gather | bytes 1728 | tf_op jit(solution)/shard_map/all_gather | solution.py:119
  184.0 12.5 all-gather.1
  201.9 192.2 %collective-permute-done = s32[8,48]{1,0:T(8,128)S(1)} collective-permute-done((s32[8,48]{1,0:T(8,128)S(1)}, s32[8,48]{1,0:T(8,128)S(1)}, u32[]{:S(2)}, u32[]{:S(2)}) %collective-permute-start) | collective-permute-done | bytes 1568 | tf_op jit(solution)/shard_map/ppermute | solution.py:85
  404.9 644.4 %while.14 = (s32[]{:T(128)}, f32[1024,3072]{1,0:T(8,128)}, bf16[1024,12288]{1,0:T(8,128)(2,1)}, s32[8,48]{1,0:T(8,128)S(1)}, s32[8,48]{1,0:T(8,128)S(1)}, /*inde...) while((s32[]{:T(128)}, f32[1024,3072]{1,0:T(8,128)}, ...), condition=%wide.region_7.8_spmd.clone, body=%wide.region_5.7_spmd.clone.sunk | while | flops 9670165504 | bytes 86901872 | solution.py:133
  420.5 21.9 %copy.17 = bf16[24,64,48,64]{3,2,1,0:T(8,128)(2,1)} copy(bf16[24,64,48,64]{3,1,2,0:T(8,128)(2,1)} %scatter_fusion) | data formatting | bytes 18874368 | tf_op jit(solution)/shard_map/while/body/eval_jaxpr/scatter-add | solution.py:127
  442.4 23.9 %reshape.380 = bf16[1536,3072]{1,0:T(8,128)(2,1)} reshape(bf16[24,64,48,64]{3,2,1,0:T(8,128)(2,1)} %copy.17) | data formatting | bytes 18874368 | tf_op jit(solution)/shard_map/while/body/eval_jaxpr/reshape | solution.py:128
  466.2 16.9 %select_add_fusion.2 = f32[1024,3072]{1,0:T(8,128)} fusion(f32[1024,3072]{1,0:T(8,128)} %get-tuple-element.202, pred[]{:T(512)S(6)} %compare.28, bf16[1536,3072]{1,0:T(8,128)(2,1)} %reshape.380, bf16[1024,12288]{1,0:T(8,128)(2,1)} %get-tuple-element.214, s32[]{:T(128)S(6)} %select_n.315), kind=kOutput, calls=%fused_computation.4.clone.1 | convolution fusion | flops 9669967872 | bytes 37748740 | tf_op jit(solution)/shard_map/while/body/eval_jaxpr/dot_general | solution.py:130
  498.6 21.9 %copy.17 = bf16[24,64,48,64]{3,2,1,0:T(8,128)(2,1)} copy(bf16[24,64,48,64]{3,1,2,0:T(8,128)(2,1)} %scatter_fusion) | data formatting | bytes 18874368 | tf_op jit(solution)/shard_map/while/body/eval_jaxpr/scatter-add | solution.py:127
  520.6 23.9 %reshape.380 = bf16[1536,3072]{1,0:T(8,128)(2,1)} reshape(bf16[24,64,48,64]{3,2,1,0:T(8,128)(2,1)} %copy.17) | data formatting | bytes 18874368 | tf_op jit(solution)/shard_map/while/body/eval_jaxpr/reshape | solution.py:128
  544.4 18.8 %select_add_fusion.2 = f32[1024,3072]{1,0:T(8,128)} fusion(f32[1024,3072]{1,0:T(8,128)} %get-tuple-element.202, pred[]{:T(512)S(6)} %compare.28, bf16[1536,3072]{1,0:T(8,128)(2,1)} %reshape.380, bf16[1024,12288]{1,0:T(8,128)(2,1)} %get-tuple-element.214, s32[]{:T(128)S(6)} %select_n.315), kind=kOutput, calls=%fused_computation.4.clone.1 | convolution fusion | flops 9669967872 | bytes 37748740 | tf_op jit(solution)/shard_map/while/body/eval_jaxpr/dot_general | solution.py:130
  579.6 21.9 %copy.17 = bf16[24,64,48,64]{3,2,1,0:T(8,128)(2,1)} copy(bf16[24,64,48,64]{3,1,2,0:T(8,128)(2,1)} %scatter_fusion) | data formatting | bytes 18874368 | tf_op jit(solution)/shard_map/while/body/eval_jaxpr/scatter-add | solution.py:127
  601.5 23.9 %reshape.380 = bf16[1536,3072]{1,0:T(8,128)(2,1)} reshape(bf16[24,64,48,64]{3,2,1,0:T(8,128)(2,1)} %copy.17) | data formatting | bytes 18874368 | tf_op jit(solution)/shard_map/while/body/eval_jaxpr/reshape | solution.py:128
  625.4 18.8 %select_add_fusion.2 = f32[1024,3072]{1,0:T(8,128)} fusion(f32[1024,3072]{1,0:T(8,128)} %get-tuple-element.202, pred[]{:T(512)S(6)} %compare.28, bf16[1536,3072]{1,0:T(8,128)(2,1)} %reshape.380, bf16[1024,12288]{1,0:T(8,128)(2,1)} %get-tuple-element.214, s32[]{:T(128)S(6)} %select_n.315), kind=kOutput, calls=%fused_computation.4.clone.1 | convolution fusion | flops 9669967872 | bytes 37748740 | tf_op jit(solution)/shard_map/while/body/eval_jaxpr/dot_general | solution.py:130
  660.5 21.9 %copy.17 = bf16[24,64,48,64]{3,2,1,0:T(8,128)(2,1)} copy(bf16[24,64,48,64]{3,1,2,0:T(8,128)(2,1)} %scatter_fusion) | data formatting | bytes 18874368 | tf_op jit(solution)/shard_map/while/body/eval_jaxpr/scatter-add | solution.py:127
  682.5 23.9 %reshape.380 = bf16[1536,3072]{1,0:T(8,128)(2,1)} reshape(bf16[24,64,48,64]{3,2,1,0:T(8,128)(2,1)} %copy.17) | data formatting | bytes 18874368 | tf_op jit(solution)/shard_map/while/body/eval_jaxpr/reshape | solution.py:128
  706.3 18.9 %select_add_fusion.2 = f32[1024,3072]{1,0:T(8,128)} fusion(f32[1024,3072]{1,0:T(8,128)} %get-tuple-element.202, pred[]{:T(512)S(6)} %compare.28, bf16[1536,3072]{1,0:T(8,128)(2,1)} %reshape.380, bf16[1024,12288]{1,0:T(8,128)(2,1)} %get-tuple-element.214, s32[]{:T(128)S(6)} %select_n.315), kind=kOutput, calls=%fused_computation.4.clone.1 | convolution fusion | flops 9669967872 | bytes 37748740 | tf_op jit(solution)/shard_map/while/body/eval_jaxpr/dot_general | solution.py:130
  741.7 21.9 %copy.17 = bf16[24,64,48,64]{3,2,1,0:T(8,128)(2,1)} copy(bf16[24,64,48,64]{3,1,2,0:T(8,128)(2,1)} %scatter_fusion) | data formatting | bytes 18874368 | tf_op jit(solution)/shard_map/while/body/eval_jaxpr/scatter-add | solution.py:127
  763.6 23.9 %reshape.380 = bf16[1536,3072]{1,0:T(8,128)(2,1)} reshape(bf16[24,64,48,64]{3,2,1,0:T(8,128)(2,1)} %copy.17) | data formatting | bytes 18874368 | tf_op jit(solution)/shard_map/while/body/eval_jaxpr/reshape | solution.py:128
  787.5 18.8 %select_add_fusion.2 = f32[1024,3072]{1,0:T(8,128)} fusion(f32[1024,3072]{1,0:T(8,128)} %get-tuple-element.202, pred[]{:T(512)S(6)} %compare.28, bf16[1536,3072]{1,0:T(8,128)(2,1)} %reshape.380, bf16[1024,12288]{1,0:T(8,128)(2,1)} %get-tuple-element.214, s32[]{:T(128)S(6)} %select_n.315), kind=kOutput, calls=%fused_computation.4.clone.1 | convolution fusion | flops 9669967872 | bytes 37748740 | tf_op jit(solution)/shard_map/while/body/eval_jaxpr/dot_general | solution.py:130
  822.8 21.9 %copy.17 = bf16[24,64,48,64]{3,2,1,0:T(8,128)(2,1)} copy(bf16[24,64,48,64]{3,1,2,0:T(8,128)(2,1)} %scatter_fusion) | data formatting | bytes 18874368 | tf_op jit(solution)/shard_map/while/body/eval_jaxpr/scatter-add | solution.py:127
  844.7 23.9 %reshape.380 = bf16[1536,3072]{1,0:T(8,128)(2,1)} reshape(bf16[24,64,48,64]{3,2,1,0:T(8,128)(2,1)} %copy.17) | data formatting | bytes 18874368 | tf_op jit(solution)/shard_map/while/body/eval_jaxpr/reshape | solution.py:128
  868.5 18.7 %select_add_fusion.2 = f32[1024,3072]{1,0:T(8,128)} fusion(f32[1024,3072]{1,0:T(8,128)} %get-tuple-element.202, pred[]{:T(512)S(6)} %compare.28, bf16[1536,3072]{1,0:T(8,128)(2,1)} %reshape.380, bf16[1024,12288]{1,0:T(8,128)(2,1)} %get-tuple-element.214, s32[]{:T(128)S(6)} %select_n.315), kind=kOutput, calls=%fused_computation.4.clone.1 | convolution fusion | flops 9669967872 | bytes 37748740 | tf_op jit(solution)/shard_map/while/body/eval_jaxpr/dot_general | solution.py:130
  903.8 21.9 %copy.17 = bf16[24,64,48,64]{3,2,1,0:T(8,128)(2,1)} copy(bf16[24,64,48,64]{3,1,2,0:T(8,128)(2,1)} %scatter_fusion) | data formatting | bytes 18874368 | tf_op jit(solution)/shard_map/while/body/eval_jaxpr/scatter-add | solution.py:127
  925.8 23.9 %reshape.380 = bf16[1536,3072]{1,0:T(8,128)(2,1)} reshape(bf16[24,64,48,64]{3,2,1,0:T(8,128)(2,1)} %copy.17) | data formatting | bytes 18874368 | tf_op jit(solution)/shard_map/while/body/eval_jaxpr/reshape | solution.py:128
  949.6 18.8 %select_add_fusion.2 = f32[1024,3072]{1,0:T(8,128)} fusion(f32[1024,3072]{1,0:T(8,128)} %get-tuple-element.202, pred[]{:T(512)S(6)} %compare.28, bf16[1536,3072]{1,0:T(8,128)(2,1)} %reshape.380, bf16[1024,12288]{1,0:T(8,128)(2,1)} %get-tuple-element.214, s32[]{:T(128)S(6)} %select_n.315), kind=kOutput, calls=%fused_computation.4.clone.1 | convolution fusion | flops 9669967872 | bytes 37748740 | tf_op jit(solution)/shard_map/while/body/eval_jaxpr/dot_general | solution.py:130
  984.6 21.9 %copy.17 = bf16[24,64,48,64]{3,2,1,0:T(8,128)(2,1)} copy(bf16[24,64,48,64]{3,1,2,0:T(8,128)(2,1)} %scatter_fusion) | data formatting | bytes 18874368 | tf_op jit(solution)/shard_map/while/body/eval_jaxpr/scatter-add | solution.py:127
  1006.5 23.9 %reshape.380 = bf16[1536,3072]{1,0:T(8,128)(2,1)} reshape(bf16[24,64,48,64]{3,2,1,0:T(8,128)(2,1)} %copy.17) | data formatting | bytes 18874368 | tf_op jit(solution)/shard_map/while/body/eval_jaxpr/reshape | solution.py:128
  1030.4 18.9 %select_add_fusion.2 = f32[1024,3072]{1,0:T(8,128)} fusion(f32[1024,3072]{1,0:T(8,128)} %get-tuple-element.202, pred[]{:T(512)S(6)} %compare.28, bf16[1536,3072]{1,0:T(8,128)(2,1)} %reshape.380, bf16[1024,12288]{1,0:T(8,128)(2,1)} %get-tuple-element.214, s32[]{:T(128)S(6)} %select_n.315), kind=kOutput, calls=%fused_computation.4.clone.1 | convolution fusion | flops 9669967872 | bytes 37748740 | tf_op jit(solution)/shard_map/while/body/eval_jaxpr/dot_general | solution.py:130
  1057.8 268.8 %collective-permute-done.3 = bf16[128,8,3072]{2,1,0:T(8,128)(2,1)S(1)} collective-permute-done((bf16[128,8,3072]{2,1,0:T(8,128)(2,1)S(1)}, bf16[128,8,3072]{2,1,0:T(8,128)(2,1)S(1)}, u32[]{:S(2)}, u32[]{:S(2)}) %collective-permute-start.3) | collective-permute-done | bytes 6291488 | tf_op jit(solution)/shard_map/ppermute | solution.py:85
  (73 shorter events, 193.3 us)
Async XLA Ops:
  6.5 113.5 %all-gather.7.cloned.1.call-start = ((), (), s32[]{:S(2)}) async-start(), calls=%async_computation.1 | async-start | bytes 7077888 | tf_op jit(solution)/shard_map/all_gather | solution.py:118
  45.0 28.3 %copy-start = (s32[8,48]{1,0:T(8,128)S(1)}, s32[8,48]{1,0:T(8,128)}, u32[]{:S(2)}) copy-start(s32[8,48]{1,0:T(8,128)} %param.7) | copy-start | bytes 4612
  73.3 331.6 %all-gather.5.cloned.1.call-start = ((), (), s32[]{:S(2)}) async-start(), calls=%async_computation | async-start | bytes 31457280 | tf_op jit(solution)/shard_map/all_gather | solution.py:115
  120.0 274.1 %collective-permute-start.2 = (bf16[8,48,64,64]{3,2,1,0:T(8,128)(2,1)}, bf16[8,48,64,64]{3,2,1,0:T(8,128)(2,1)}, u32[]{:S(2)}, u32[]{:S(2)}) collective-permute-start(bf16[8,48,64,64]{3,2,1,0:T(8,128)(2,1)} %all-gather.7.cloned.1.call-done), channel_id=1, source_target_pairs={{0,0},{2,8},{4,16},{6,24},{8,2},{10,10},{12,18},{14,26},{16,4},{18... | collective-permute-start | bytes 9437192 | tf_op jit(solution)/shard_map/ppermute | solution.py:85
  181.1 212.9 %collective-permute-start = (s32[8,48]{1,0:T(8,128)S(1)}, s32[8,48]{1,0:T(8,128)S(1)}, u32[]{:S(2)}, u32[]{:S(2)}) collective-permute-start(s32[8,48]{1,0:T(8,128)S(1)} %bitcast.53), channel_id=1, source_target_pairs={{0,0},{2,8},{4,16},{6,24},{8,2},{10,10},{12,18},{14,26},{16,4},{18... | collective-permute-start | bytes 4616 | tf_op jit(solution)/shard_map/ppermute | solution.py:85
  196.5 197.6 %collective-permute-start.1 = (s32[8,48]{1,0:T(8,128)S(1)}, s32[8,48]{1,0:T(8,128)S(1)}, u32[]{:S(2)}, u32[]{:S(2)}) collective-permute-start(s32[8,48]{1,0:T(8,128)S(1)} %bitcast.54), channel_id=1, source_target_pairs={{0,0},{2,8},{4,16},{6,24},{8,2},{10,10},{12,18},{14,26},{16,4},{18... | collective-permute-start | bytes 4616 | tf_op jit(solution)/shard_map/ppermute | solution.py:85
  1054.8 271.8 %collective-permute-start.3 = (bf16[128,8,3072]{2,1,0:T(8,128)(2,1)S(1)}, bf16[128,8,3072]{2,1,0:T(8,128)(2,1)S(1)}, u32[]{:S(2)}, u32[]{:S(2)}) collective-permute-start(bf16[128,8,3072]{2,1,0:T(8,128)(2,1)S(1)} %convert_bitcast_fusion), channel_id=1, source_target_pairs={{0,0},{2,8},{4,16},{6,24},{8,2},{10,10},{12,18},{14,26},{16,4},{18... | collective-permute-start | bytes 18874376 | tf_op jit(solution)/shard_map/ppermute | solution.py:85
Sparse Core Ops, SparseCore 0:
  73.4 46.5 all-gather.6
  121.6 283.2 all-gather.4

commit v2 on v1

--- a/solution.py
+++ b/solution.py
@@ -1,10 +1,14 @@
 import jax
 import jax.numpy as jnp
 from jax import lax
+from jax.experimental import pallas as pl
+from jax.experimental.pallas import tpu as pltpu
 from jax.sharding import PartitionSpec as P
 
 BLK = 64
 CAP = 48
+LANE = 128
+ROW_CHUNK = 256
 
 
 def passed_along(value, axis, by):
@@ -103,6 +107,60 @@
     return blocks, block_row, block_col
 
 
+def padded_blocks(blocks, block_rows, block_cols):
+    empty = jnp.zeros_like(blocks)
+    left = (block_cols % 2 == 0)[:, None, None]
+    top = (block_rows % 2 == 0)[:, None, None]
+    half = jnp.concatenate([jnp.where(left, blocks, empty), jnp.where(left, empty, blocks)], axis=2)
+    empty = jnp.zeros_like(half)
+    return jnp.concatenate([jnp.where(top, half, empty), jnp.where(top, empty, half)], axis=1)
+
+
+def block_sparse_product(rows_all, blocks, block_rows, block_cols, width):
+    row_total, nao = rows_all.shape
+    entries = blocks.shape[0]
+    chunks = width // LANE
+    chunk_of = block_cols // 2
+    order = jnp.argsort(chunk_of)
+    chunk_sorted = chunk_of[order]
+    starts = jnp.searchsorted(chunk_sorted, jnp.arange(chunks + 1), side="left").astype(jnp.int32)
+    k_sorted = (block_rows[order] // 2).astype(jnp.int32)
+    padded = padded_blocks(blocks, block_rows, block_cols)[order]
+    row_chunk = min(ROW_CHUNK, row_total)
+
+    def kernel(starts_ref, k_ref, t_ref, g_ref, o_ref):
+        for chunk in range(chunks):
+            def body(entry, acc):
+                k = pl.multiple_of(k_ref[entry] * LANE, LANE)
+                return acc + jnp.dot(
+                    t_ref[:, pl.ds(k, LANE)], g_ref[entry], preferred_element_type=jnp.float32
+                )
+
+            acc = lax.fori_loop(
+                starts_ref[chunk],
+                starts_ref[chunk + 1],
+                body,
+                jnp.zeros((row_chunk, LANE), jnp.float32),
+            )
+            o_ref[:, chunk * LANE : (chunk + 1) * LANE] = acc.astype(o_ref.dtype)
+
+    grid_spec = pltpu.PrefetchScalarGridSpec(
+        num_scalar_prefetch=2,
+        grid=(row_total // row_chunk,),
+        in_specs=[
+            pl.BlockSpec((row_chunk, nao), lambda i, s, k: (i, 0)),
+            pl.BlockSpec((entries, LANE, LANE), lambda i, s, k: (0, 0, 0)),
+        ],
+        out_specs=pl.BlockSpec((row_chunk, width), lambda i, s, k: (i, 0)),
+    )
+    return pl.pallas_call(
+        kernel,
+        grid_spec=grid_spec,
+        out_shape=jax.ShapeDtypeStruct((row_total, width), jnp.bfloat16),
+        compiler_params=pltpu.CompilerParams(vmem_limit_bytes=56 * 1024 * 1024),
+    )(starts, k_sorted, rows_all, padded)
+
+
 def per_device(tensor, tensor_pattern, green, green_pattern):
     layer_count = lax.axis_size("layer")
     row_count = lax.axis_size("row")
@@ -118,20 +176,12 @@
     band_blocks = transposed(lax.all_gather(blocks, ("layer", "col"), axis=0), row_count)
     band_rows = transposed(lax.all_gather(block_row, ("layer", "col"), axis=0), row_count)
     band_cols = transposed(lax.all_gather(block_col, ("layer", "col"), axis=0), row_count)
+    rows_all = full_rows.reshape(ri_local * mu_local, nao)
     band_count = band_blocks.shape[0]
-    band_width = tile_rows * BLK
-    rows_all = full_rows.reshape(ri_local * mu_local, nao)
-
-    def add_band(band, total):
-        dense = jnp.zeros((tile_rows, BLK, tile_cols, BLK), jnp.bfloat16)
-        dense = dense.at[band_rows[band], :, band_cols[band], :].add(band_blocks[band])
-        dense = dense.reshape(band_width, tile_cols * BLK)
-        rows = lax.dynamic_slice_in_dim(rows_all, band * band_width, band_width, axis=1)
-        return total + jnp.dot(rows, dense, preferred_element_type=jnp.float32)
-
-    total = jnp.zeros((ri_local * mu_local, tile_cols * BLK), jnp.float32)
-    total = lax.fori_loop(0, band_count, add_band, total)
-    product = total.astype(jnp.bfloat16)
+    entry_rows = (band_rows + jnp.arange(band_count)[:, None] * tile_rows).reshape(-1)
+    entry_cols = band_cols.reshape(-1)
+    entry_blocks = band_blocks.reshape(-1, BLK, BLK)
+    product = block_sparse_product(rows_all, entry_blocks, entry_rows, entry_cols, tile_cols * BLK)
     product = product.reshape(ri_local, mu_local, tile_cols * BLK)
     return transposed(product, row_count)
 

time: 1350 us -> 950 us (0.70)
  local copies, waits for them, and re-layouts: 487 us -> 83.5 us
  Pallas kernels: 0 us -> 252 us
  matrix products: 149 us -> 0 us
  other arithmetic: 90.6 us -> 41.9 us
  blocking collectives: 69.6 us -> 25.1 us
    pallas_call x0 -> x1, Pallas kernels: none -> 252 us  [block_sparse_product(): pl.pallas_call(kernel, grid_spec=grid_spec, out_shape=jax.ShapeDtypeStruc...]
    reshape x8 -> x2, local copies, waits for them, and re-layouts: 191 us -> 0.16 us  [the longest x1 0.08 us: per_device(): (band_rows + jnp.arange(band_count)[:, None] * tile_rows).reshape(-1)]
    scatter-add x8 -> x0, local copies, waits for them, and re-layouts: 175 us -> none  [add_band(): dense.at[band_rows[band], :, band_cols[band], :].add(band_blocks[band])]
    dot_general x8 -> x0, matrix products: 149 us -> none  [add_band(): return total + jnp.dot(rows, dense, preferred_element_type=jnp.float32)]
    scatter-add x8 -> x0, other arithmetic: 64.3 us -> none  [add_band(): dense.at[band_rows[band], :, band_cols[band], :].add(band_blocks[band])]
    another operation x10 -> x2, local copies, waits for them, and re-layouts: 55.9 us -> 0.21 us
    ppermute x4, waiting for transfers between devices: 461 us -> 508 us  [transposed(): lax.ppermute(value, ('layer', 'row'), [(a * size + b, b * size + a) for a...]
    all_gather x1, blocking collectives: 57.2 us -> 12.6 us  [per_device(): lax.all_gather(block_row, ('layer', 'col'), axis=0)]
  transfers between devices with their start and end apart: 6 -> 6, of which waited for: 4 -> 3; matrix products, arithmetic and copies ran while one was open for 1% -> 6% of each run, Pallas kernels for 0% -> 0%
where the time goes in v2:
time: 950 us; the launch traced here: 942 us
  waiting for transfers between devices  508 us (53%)
  Pallas kernels  252 us (27%)
  local copies, waits for them, and re-layouts  83.5 us (9%)
  other arithmetic  41.9 us (4%)
  blocking collectives  25.1 us (3%)
  starting transfers between devices  17.2 us (2%)
  between operations  13.6 us (1%)
    ppermute x4, waiting for transfers between devices, transposed(): lax.ppermute(value, ('layer', 'row'), [(a * size + b, b * size + a) for a...  508 us
    pallas_call x1, Pallas kernels, block_sparse_product(): pl.pallas_call(kernel, grid_spec=grid_spec, out_shape=jax.ShapeDtypeStruc...  252 us
    reshape x2, local copies, waits for them, and re-layouts, compressed_tile(): green.reshape(tile_rows, BLK, tile_cols, BLK)[block_row, :, block_col, :]  43.3 us
  transfers between devices with their start and end apart: 6, of which 3 were waited for; matrix products, arithmetic and copies ran while one was open for 6% of the time, Pallas kernels for 0%

profile of v2, /device:TPU:16, one launch (start us, length us, event | category | flops | bytes accessed | tf_op | source)
XLA Modules:
  0.0 942.0 jit_solution(3947273013171648858)
XLA Ops:
  7.2 1.4 fusion.25
  8.6 0.8 reshape.321
  10.1 9.2 scatter_custom_fusion
  19.4 0.8 fusion.11
  20.2 0.8 gather_fusion.4
  21.6 23.4 %reshape.320 = bf16[24,64,48,64]{3,2,1,0:T(8,128)(2,1)} reshape(bf16[1536,3072]{1,0:T(8,128)(2,1)} %param.8) | data formatting | bytes 18874368 | tf_op jit(solution)/shard_map/reshape | solution.py:104
  45.0 20.0 %copy.14 = bf16[24,64,48,64]{3,1,2,0:T(8,128)(2,1)} copy(bf16[24,64,48,64]{3,2,1,0:T(8,128)(2,1)} %reshape.320) | data formatting | bytes 18874368 | tf_op jit(solution)/shard_map/reshape | solution.py:104
  65.0 7.2 gather_fusion.3
  72.2 1.0 bitcast_multiply_fusion
  73.6 5.9 broadcast_multiply_fusion
  80.2 12.6 %all-gather = s32[8,1,48]{2,1,0:T(1,128)S(1)} all-gather(s32[1,1,48]{2,1,0:T(1,128)S(1)} %get-tuple-element.108), channel_id=1, replica_groups=mesh['layer'=4,'row'=4,'col'=2] {'layer','col'}, dimensions={0}, use_global_device_ids=true | all-gather | bytes 1728 | tf_op jit(solution)/shard_map/all_gather | solution.py:178
  92.8 2.7 collective-permute-start
  95.5 12.6 %all-gather.1 = s32[8,1,48]{2,1,0:T(1,128)S(1)} all-gather(s32[1,1,48]{2,1,0:T(1,128)S(1)} %get-tuple-element.107), channel_id=1, replica_groups=mesh['layer'=4,'row'=4,'col'=2] {'layer','col'}, dimensions={0}, use_global_device_ids=true | all-gather | bytes 1728 | tf_op jit(solution)/shard_map/all_gather | solution.py:177
  108.0 4.7 collective-permute-start.1
  112.9 3.7 sort.17
  116.6 2.8 gather_fusion.1
  120.0 3.5 collective-permute-start.2
  123.5 6.9 while.24
  123.6 0.7 gather_fusion
  124.3 0.7 gather_fusion
  125.1 0.7 gather_fusion
  125.9 0.7 gather_fusion
  131.2 2.8 gather_fusion.2
  134.6 259.2 %collective-permute-done.2 = bf16[8,48,64,64]{3,2,1,0:T(8,128)(2,1)} collective-permute-done((bf16[8,48,64,64]{3,2,1,0:T(8,128)(2,1)}, bf16[8,48,64,64]{3,2,1,0:T(8,128)(2,1)}, u32[]{:S(2)}, u32[]{:S(2)}) %collective-permute-start.2) | collective-permute-done | bytes 3145760 | tf_op jit(solution)/shard_map/ppermute | solution.py:89
  393.8 4.3 bitcast_select_fusion
  398.1 6.4 broadcast_select_fusion.3
  404.5 5.2 pad_maximum_fusion
  409.7 16.0 %gather_fusion.5 = bf16[384,128,128]{2,1,0:T(8,128)(2,1)} fusion(bf16[384,128,128]{2,1,0:T(8,128)(2,1)} %pad_maximum_fusion, s32[1024]{0:T(1024)S(1)} %pad_clamp_fusion.2), kind=kCustom, calls=%fused_computation.5 | custom fusion | bytes 25167360 | tf_op jit(solution)/shard_map/gather | solution.py:128
  425.6 252.2 %shard_map.46 = bf16[1024,3072]{1,0:T(8,128)(2,1)} custom-call(s32[25]{0:T(128)} %convert_element_type.44.starts_ref, s32[384]{0:T(512)} %add_select_fusion.5.k_ref, bf16[1024,12288]{1,0:T(8,128)(2,1)} %bitcast.26, bf16[384,128,128]{2,1,0:T(8,128)(2,1)} %gather_fusion.5), custom_call_target="tpu_custom_call" | custom-call | tf_op jit(solution)/shard_map/pallas_call | solution.py:156
  677.8 6.2 collective-permute-start.3
  684.0 248.4 %collective-permute-done.3 = bf16[128,8,3072]{2,1,0:T(8,128)(2,1)S(1)} collective-permute-done((bf16[128,8,3072]{2,1,0:T(8,128)(2,1)}, bf16[128,8,3072]{2,1,0:T(8,128)(2,1)S(1)}, u32[]{:S(2)}, u32[]{:S(2)}) %collective-permute-start.3) | collective-permute-done | bytes 6291488 | tf_op jit(solution)/shard_map/ppermute | solution.py:89
  932.4 2.7 copy.31
  (73 shorter events, 9.0 us)
Async XLA Ops:
  6.5 113.5 %all-gather.7.cloned.1.call-start = ((), (), s32[]{:S(2)}) async-start(), calls=%async_computation.1 | async-start | bytes 7077888 | tf_op jit(solution)/shard_map/all_gather | solution.py:176
  45.0 28.3 %copy-start = (s32[8,48]{1,0:T(8,128)S(1)}, s32[8,48]{1,0:T(8,128)}, u32[]{:S(2)}) copy-start(s32[8,48]{1,0:T(8,128)} %param.7) | copy-start | bytes 4612
  73.3 352.4 %all-gather.5.cloned.1.call-start = ((), (), s32[]{:S(2)}) async-start(), calls=%async_computation | async-start | bytes 31457280 | tf_op jit(solution)/shard_map/all_gather | solution.py:173
  92.8 20.0 %collective-permute-start = (s32[8,48]{1,0:T(8,128)S(1)}, s32[8,48]{1,0:T(8,128)S(1)}, u32[]{:S(2)}, u32[]{:S(2)}) collective-permute-start(s32[8,48]{1,0:T(8,128)S(1)} %bitcast.29), channel_id=1, source_target_pairs={{0,0},{2,8},{4,16},{6,24},{8,2},{10,10},{12,18},{14,26},{16,4},{18... | collective-permute-start | bytes 4616 | tf_op jit(solution)/shard_map/ppermute | solution.py:89
  108.0 22.4 %collective-permute-start.1 = (s32[8,48]{1,0:T(8,128)S(1)}, s32[8,48]{1,0:T(8,128)S(1)}, u32[]{:S(2)}, u32[]{:S(2)}) collective-permute-start(s32[8,48]{1,0:T(8,128)S(1)} %bitcast.28), channel_id=1, source_target_pairs={{0,0},{2,8},{4,16},{6,24},{8,2},{10,10},{12,18},{14,26},{16,4},{18... | collective-permute-start | bytes 4616 | tf_op jit(solution)/shard_map/ppermute | solution.py:89
  120.0 273.8 %collective-permute-start.2 = (bf16[8,48,64,64]{3,2,1,0:T(8,128)(2,1)}, bf16[8,48,64,64]{3,2,1,0:T(8,128)(2,1)}, u32[]{:S(2)}, u32[]{:S(2)}) collective-permute-start(bf16[8,48,64,64]{3,2,1,0:T(8,128)(2,1)} %all-gather.7.cloned.1.call-done), channel_id=1, source_target_pairs={{0,0},{2,8},{4,16},{6,24},{8,2},{10,10},{12,18},{14,26},{16,4},{18... | collective-permute-start | bytes 9437192 | tf_op jit(solution)/shard_map/ppermute | solution.py:89
  677.8 254.6 %collective-permute-start.3 = (bf16[128,8,3072]{2,1,0:T(8,128)(2,1)}, bf16[128,8,3072]{2,1,0:T(8,128)(2,1)S(1)}, u32[]{:S(2)}, u32[]{:S(2)}) collective-permute-start(bf16[128,8,3072]{2,1,0:T(8,128)(2,1)} %bitcast.27), channel_id=1, source_target_pairs={{0,0},{2,8},{4,16},{6,24},{8,2},{10,10},{12,18},{14,26},{16,4},{18... | collective-permute-start | bytes 18874376 | tf_op jit(solution)/shard_map/ppermute | solution.py:89
Sparse Core Ops, SparseCore 0:
  73.4 46.5 all-gather.6
  121.6 283.0 all-gather.4

commit v3 on v2

--- a/solution.py
+++ b/solution.py
@@ -8,7 +8,7 @@
 BLK = 64
 CAP = 48
 LANE = 128
-ROW_CHUNK = 256
+ROW_CHUNK = 512
 
 
 def passed_along(value, axis, by):
@@ -149,7 +149,9 @@
         grid=(row_total // row_chunk,),
         in_specs=[
             pl.BlockSpec((row_chunk, nao), lambda i, s, k: (i, 0)),
-            pl.BlockSpec((entries, LANE, LANE), lambda i, s, k: (0, 0, 0)),
+            pl.BlockSpec(
+                (entries, LANE, LANE), lambda i, s, k: (0, 0, 0), pipeline_mode=pl.Buffered(1)
+            ),
         ],
         out_specs=pl.BlockSpec((row_chunk, width), lambda i, s, k: (i, 0)),
     )
@@ -181,9 +183,14 @@
     entry_rows = (band_rows + jnp.arange(band_count)[:, None] * tile_rows).reshape(-1)
     entry_cols = band_cols.reshape(-1)
     entry_blocks = band_blocks.reshape(-1, BLK, BLK)
-    product = block_sparse_product(rows_all, entry_blocks, entry_rows, entry_cols, tile_cols * BLK)
-    product = product.reshape(ri_local, mu_local, tile_cols * BLK)
-    return transposed(product, row_count)
+    pieces = []
+    for start in range(0, ri_local * mu_local, ROW_CHUNK):
+        piece = block_sparse_product(
+            rows_all[start : start + ROW_CHUNK], entry_blocks, entry_rows, entry_cols, tile_cols * BLK
+        )
+        pieces.append(transposed(piece, row_count))
+    product = jnp.concatenate(pieces, axis=0)
+    return product.reshape(ri_local, mu_local, tile_cols * BLK)
 
 
 def solution(mesh):

time: 950 us -> 799 us (0.84)
  waiting for transfers between devices: 508 us -> 422 us
  Pallas kernels: 252 us -> 168 us
  local copies, waits for them, and re-layouts: 83.5 us -> 98.3 us
    ppermute x4 -> x5, waiting for transfers between devices: 508 us -> 422 us  [transposed(): lax.ppermute(value, ('layer', 'row'), [(a * size + b, b * size + a) for a...]
    pallas_call x1 -> x2, Pallas kernels: 252 us -> 168 us  [block_sparse_product(): pl.pallas_call(kernel, grid_spec=grid_spec, out_shape=jax.ShapeDtypeStruc...]
    slice x1 -> x2, local copies, waits for them, and re-layouts: 0.08 us -> 17.5 us  [the longest x1 17.4 us: per_device(): rows_all[start:start + ROW_CHUNK]]
    ppermute x4 -> x5, starting transfers between devices: 17.2 us -> 19.1 us  [transposed(): lax.ppermute(value, ('layer', 'row'), [(a * size + b, b * size + a) for a...]
  transfers between devices with their start and end apart: 6 -> 7, of which waited for: 3 -> 4; matrix products, arithmetic and copies ran while one was open for 6% -> 7% of each run, Pallas kernels for 0% -> 11%
where the time goes in v3:
time: 799 us; the launch traced here: 792 us
  waiting for transfers between devices  422 us (53%)
  Pallas kernels  168 us (21%)
  local copies, waits for them, and re-layouts  98.3 us (12%)
  other arithmetic  45 us (6%)
  blocking collectives  25.1 us (3%)
  starting transfers between devices  19.1 us (2%)
  between operations  13.6 us (2%)
    ppermute x5, waiting for transfers between devices, transposed(): lax.ppermute(value, ('layer', 'row'), [(a * size + b, b * size + a) for a...  422 us
    pallas_call x2, Pallas kernels, block_sparse_product(): pl.pallas_call(kernel, grid_spec=grid_spec, out_shape=jax.ShapeDtypeStruc...  168 us
    reshape x2, local copies, waits for them, and re-layouts, compressed_tile(): green.reshape(tile_rows, BLK, tile_cols, BLK)[block_row, :, block_col, :]  43.3 us
    ppermute x5, starting transfers between devices, transposed(): lax.ppermute(value, ('layer', 'row'), [(a * size + b, b * size + a) for a...  19.1 us
    slice x1, local copies, waits for them, and re-layouts, per_device(): rows_all[start:start + ROW_CHUNK]  17.4 us
  transfers between devices with their start and end apart: 7, of which 4 were waited for; matrix products, arithmetic and copies ran while one was open for 7% of the time, Pallas kernels for 11%

profile of v3, /device:TPU:16, one launch (start us, length us, event | category | flops | bytes accessed | tf_op | source)
XLA Modules:
  0.0 791.7 jit_solution(2982926271524262808)
XLA Ops:
  7.2 1.4 fusion.25
  8.6 0.8 reshape.320
  10.1 9.2 %scatter_custom_fusion = s32[48]{0:T(128)S(1)} fusion(s32[1152]{0:T(1024)S(1)} %fusion.13, s32[1152]{0:T(1024)S(1)} %broadcast.532, s32[]{:T(128)} %constant.133.clone.1), kind=kCustom, calls=%fused_computation.84 | custom fusion | flops 1152 | bytes 196 | tf_op jit(solution)/shard_map/scatter-add | solution.py:100
  19.4 0.8 fusion.11
  20.2 0.8 gather_fusion.4
  21.6 23.4 %reshape.319 = bf16[24,64,48,64]{3,2,1,0:T(8,128)(2,1)} reshape(bf16[1536,3072]{1,0:T(8,128)(2,1)} %param.8) | data formatting | bytes 18874368 | tf_op jit(solution)/shard_map/reshape | solution.py:104
  45.0 20.0 %copy.14 = bf16[24,64,48,64]{3,1,2,0:T(8,128)(2,1)} copy(bf16[24,64,48,64]{3,2,1,0:T(8,128)(2,1)} %reshape.319) | data formatting | bytes 18874368 | tf_op jit(solution)/shard_map/reshape | solution.py:104
  65.0 7.2 gather_fusion.3
  72.2 1.0 bitcast_multiply_fusion
  73.6 5.9 broadcast_multiply_fusion
  80.2 12.6 %all-gather = s32[8,1,48]{2,1,0:T(1,128)S(1)} all-gather(s32[1,1,48]{2,1,0:T(1,128)S(1)} %get-tuple-element.110), channel_id=1, replica_groups=mesh['layer'=4,'row'=4,'col'=2] {'layer','col'}, dimensions={0}, use_global_device_ids=true | all-gather | bytes 1728 | tf_op jit(solution)/shard_map/all_gather | solution.py:180
  92.8 2.7 collective-permute-start
  95.5 12.6 %all-gather.1 = s32[8,1,48]{2,1,0:T(1,128)S(1)} all-gather(s32[1,1,48]{2,1,0:T(1,128)S(1)} %get-tuple-element.109), channel_id=1, replica_groups=mesh['layer'=4,'row'=4,'col'=2] {'layer','col'}, dimensions={0}, use_global_device_ids=true | all-gather | bytes 1728 | tf_op jit(solution)/shard_map/all_gather | solution.py:179
  108.0 4.7 collective-permute-start.1
  112.9 3.7 sort.19
  116.6 2.8 gather_fusion.1
  120.0 3.5 collective-permute-start.2
  123.5 6.9 while.27
  131.2 2.8 gather_fusion.2
  134.6 259.2 %collective-permute-done.2 = bf16[8,48,64,64]{3,2,1,0:T(8,128)(2,1)} collective-permute-done((bf16[8,48,64,64]{3,2,1,0:T(8,128)(2,1)}, bf16[8,48,64,64]{3,2,1,0:T(8,128)(2,1)}, u32[]{:S(2)}, u32[]{:S(2)}) %collective-permute-start.2) | collective-permute-done | bytes 3145760 | tf_op jit(solution)/shard_map/ppermute | solution.py:89
  393.8 4.3 bitcast_select_fusion
  398.1 6.4 broadcast_select_fusion.3
  404.5 5.2 pad_maximum_fusion
  409.7 16.0 %gather_fusion.5 = bf16[384,128,128]{2,1,0:T(8,128)(2,1)} fusion(bf16[384,128,128]{2,1,0:T(8,128)(2,1)} %pad_maximum_fusion, s32[1024]{0:T(1024)S(1)} %pad_clamp_fusion.2), kind=kCustom, calls=%fused_computation.5 | custom fusion | bytes 25167360 | tf_op jit(solution)/shard_map/gather | solution.py:128
  425.6 17.4 %slice_bitcast_fusion.1 = (bf16[512,12288]{1,0:T(8,128)(2,1)}, bf16[512,12288]{1,0:T(8,128)(2,1)}) fusion(bf16[128,8,12288]{2,1,0:T(8,128)(2,1)} %all-gather.5.cloned.1.call-done), kind=kLoop, calls=%fused_computation.16 | loop fusion | bytes 50331648 | tf_op jit(solution)/shard_map/slice | solution.py:189
  443.0 84.1 %shard_map.46 = bf16[512,3072]{1,0:T(8,128)(2,1)} custom-call(s32[25]{0:T(128)} %convert_element_type.45.starts_ref, s32[384]{0:T(512)} %add_select_fusion.5.k_ref, bf16[512,12288]{1,0:T(8,128)(2,1)} %get-tuple-element.103.t_ref, bf16[384,128,128]{2,1,0:T(8,128)(2,1)} %gather_fusion.5), custom_call_target="tpu_custom_call" | custom-call | tf_op jit(solution)/shard_map/pallas_call | solution.py:158
  527.1 6.2 collective-permute-start.3
  533.4 84.1 %shard_map.47 = bf16[512,3072]{1,0:T(8,128)(2,1)} custom-call(s32[25]{0:T(128)} %convert_element_type.45.starts_ref, s32[384]{0:T(512)} %add_select_fusion.5.k_ref, bf16[512,12288]{1,0:T(8,128)(2,1)} %get-tuple-element.104.t_ref, bf16[384,128,128]{2,1,0:T(8,128)(2,1)} %gather_fusion.5), custom_call_target="tpu_custom_call" | custom-call | tf_op jit(solution)/shard_map/pallas_call | solution.py:158
  617.4 1.9 collective-permute-start.4
  619.4 95.1 %collective-permute-done.3 = bf16[512,3072]{1,0:T(8,128)(2,1)S(1)} collective-permute-done((bf16[512,3072]{1,0:T(8,128)(2,1)}, bf16[512,3072]{1,0:T(8,128)(2,1)S(1)}, u32[]{:S(2)}, u32[]{:S(2)}) %collective-permute-start.3) | collective-permute-done | bytes 3145760 | tf_op jit(solution)/shard_map/ppermute | solution.py:89
  714.4 67.3 %collective-permute-done.4 = bf16[512,3072]{1,0:T(8,128)(2,1)S(1)} collective-permute-done((bf16[512,3072]{1,0:T(8,128)(2,1)}, bf16[512,3072]{1,0:T(8,128)(2,1)S(1)}, u32[]{:S(2)}, u32[]{:S(2)}) %collective-permute-start.4) | collective-permute-done | bytes 3145760 | tf_op jit(solution)/shard_map/ppermute | solution.py:89
  781.7 3.1 maximum_bitcast_fusion
  (77 shorter events, 11.9 us)
Async XLA Ops:
  6.5 113.5 %all-gather.7.cloned.1.call-start = ((), (), s32[]{:S(2)}) async-start(), calls=%async_computation.1 | async-start | bytes 7077888 | tf_op jit(solution)/shard_map/all_gather | solution.py:178
  45.0 28.3 %copy-start = (s32[8,48]{1,0:T(8,128)S(1)}, s32[8,48]{1,0:T(8,128)}, u32[]{:S(2)}) copy-start(s32[8,48]{1,0:T(8,128)} %param.7) | copy-start | bytes 4612
  73.3 352.4 %all-gather.5.cloned.1.call-start = ((), (), s32[]{:S(2)}) async-start(), calls=%async_computation | async-start | bytes 31457280 | tf_op jit(solution)/shard_map/all_gather | solution.py:175
  92.8 20.0 %collective-permute-start = (s32[8,48]{1,0:T(8,128)S(1)}, s32[8,48]{1,0:T(8,128)S(1)}, u32[]{:S(2)}, u32[]{:S(2)}) collective-permute-start(s32[8,48]{1,0:T(8,128)S(1)} %bitcast.31), channel_id=1, source_target_pairs={{0,0},{2,8},{4,16},{6,24},{8,2},{10,10},{12,18},{14,26},{16,4},{18... | collective-permute-start | bytes 4616 | tf_op jit(solution)/shard_map/ppermute | solution.py:89
  108.0 22.4 %collective-permute-start.1 = (s32[8,48]{1,0:T(8,128)S(1)}, s32[8,48]{1,0:T(8,128)S(1)}, u32[]{:S(2)}, u32[]{:S(2)}) collective-permute-start(s32[8,48]{1,0:T(8,128)S(1)} %bitcast.30), channel_id=1, source_target_pairs={{0,0},{2,8},{4,16},{6,24},{8,2},{10,10},{12,18},{14,26},{16,4},{18... | collective-permute-start | bytes 4616 | tf_op jit(solution)/shard_map/ppermute | solution.py:89
  120.0 273.8 %collective-permute-start.2 = (bf16[8,48,64,64]{3,2,1,0:T(8,128)(2,1)}, bf16[8,48,64,64]{3,2,1,0:T(8,128)(2,1)}, u32[]{:S(2)}, u32[]{:S(2)}) collective-permute-start(bf16[8,48,64,64]{3,2,1,0:T(8,128)(2,1)} %all-gather.7.cloned.1.call-done), channel_id=1, source_target_pairs={{0,0},{2,8},{4,16},{6,24},{8,2},{10,10},{12,18},{14,26},{16,4},{18... | collective-permute-start | bytes 9437192 | tf_op jit(solution)/shard_map/ppermute | solution.py:89
  527.1 187.3 %collective-permute-start.3 = (bf16[512,3072]{1,0:T(8,128)(2,1)}, bf16[512,3072]{1,0:T(8,128)(2,1)S(1)}, u32[]{:S(2)}, u32[]{:S(2)}) collective-permute-start(bf16[512,3072]{1,0:T(8,128)(2,1)} %shard_map.46), channel_id=1, source_target_pairs={{0,0},{2,8},{4,16},{6,24},{8,2},{10,10},{12,18},{14,26},{16,4},{18... | collective-permute-start | bytes 9437192 | tf_op jit(solution)/shard_map/ppermute | solution.py:89
  617.4 164.3 %collective-permute-start.4 = (bf16[512,3072]{1,0:T(8,128)(2,1)}, bf16[512,3072]{1,0:T(8,128)(2,1)S(1)}, u32[]{:S(2)}, u32[]{:S(2)}) collective-permute-start(bf16[512,3072]{1,0:T(8,128)(2,1)} %shard_map.47), channel_id=1, source_target_pairs={{0,0},{2,8},{4,16},{6,24},{8,2},{10,10},{12,18},{14,26},{16,4},{18... | collective-permute-start | bytes 9437192 | tf_op jit(solution)/shard_map/ppermute | solution.py:89
Sparse Core Ops, SparseCore 0:
  73.4 46.5 all-gather.6
  121.6 283.0 all-gather.4

commit v4 on v3

--- a/solution.py
+++ b/solution.py
@@ -101,7 +101,11 @@
     valid = jnp.arange(cap) < jnp.sum(flat != 0)
     block_row = spots // tile_cols
     block_col = spots % tile_cols
-    blocks = green.reshape(tile_rows, BLK, tile_cols, BLK)[block_row, :, block_col, :]
+    windows = jax.vmap(
+        lambda r, c: lax.dynamic_slice(green, (r * BLK, c * LANE), (BLK, LANE))
+    )(block_row, block_col // 2)
+    left = (block_col % 2 == 0)[:, None, None]
+    blocks = jnp.where(left, windows[:, :, :BLK], windows[:, :, BLK:])
     scale = jnp.where(valid, flat[spots], 0).astype(jnp.bfloat16)
     blocks = blocks * scale[:, None, None]
     return blocks, block_row, block_col
@@ -172,17 +176,30 @@
     tile_rows, tile_cols = green_pattern.shape
     tensor_mask = jnp.repeat(tensor_pattern, BLK, axis=1).astype(jnp.bfloat16)
     masked = tensor * tensor_mask[None, :, :]
-    full_rows = lax.all_gather(masked, "layer", axis=2, tiled=True)
-    nao = full_rows.shape[2]
+    own = masked.reshape(ri_local * mu_local, nu_local)
+    layer_index = lax.axis_index("layer")
+    col_count = lax.axis_size("col")
     blocks, block_row, block_col = compressed_tile(green, green_pattern)
-    band_blocks = transposed(lax.all_gather(blocks, ("layer", "col"), axis=0), row_count)
-    band_rows = transposed(lax.all_gather(block_row, ("layer", "col"), axis=0), row_count)
-    band_cols = transposed(lax.all_gather(block_col, ("layer", "col"), axis=0), row_count)
-    rows_all = full_rows.reshape(ri_local * mu_local, nao)
-    band_count = band_blocks.shape[0]
-    entry_rows = (band_rows + jnp.arange(band_count)[:, None] * tile_rows).reshape(-1)
-    entry_cols = band_cols.reshape(-1)
-    entry_blocks = band_blocks.reshape(-1, BLK, BLK)
+    blocks, block_row, block_col = (
+        lax.all_gather(transposed(part, row_count), ("row", "col"), axis=0)
+        for part in (blocks, block_row, block_col)
+    )
+    band_count = blocks.shape[0]
+    band = jnp.arange(band_count)[:, None]
+    if layer_count == 4:
+        across = lax.ppermute(own, "layer", [(i, i ^ 2) for i in range(4)])
+        pair = jnp.concatenate([own, across], axis=1)
+        partner = lax.ppermute(pair, "layer", [(i, i ^ 1) for i in range(4)])
+        rows_all = jnp.concatenate([pair, partner], axis=1)
+        source = (band // col_count) ^ layer_index
+        position = jnp.array([0, 2, 1, 3], jnp.int32)[source]
+    else:
+        rows_all = lax.all_gather(own, "layer", axis=1, tiled=True)
+        position = band // col_count
+    entry_rows = (position * col_count + band % col_count) * tile_rows + block_row
+    entry_rows = entry_rows.reshape(-1)
+    entry_cols = block_col.reshape(-1)
+    entry_blocks = blocks.reshape(-1, BLK, BLK)
     pieces = []
     for start in range(0, ri_local * mu_local, ROW_CHUNK):
         piece = block_sparse_product(

time: 799 us -> 880 us (1.10)
  local copies, waits for them, and re-layouts: 98.3 us -> 178 us
  waiting for transfers between devices: 422 us -> 387 us
  other arithmetic: 45 us -> 72.1 us
    ppermute x5, waiting for transfers between devices: 422 us -> 181 us  [transposed(): lax.ppermute(value, ('layer', 'row'), [(a * size + b, b * size + a) for a...]
    gather x1 -> x145, local copies, waits for them, and re-layouts: 7.24 us -> 129 us  [compressed_tile(): green.reshape(tile_rows, BLK, tile_cols, BLK)[block_row, :, block_col, :]]
    ppermute x0 -> x2, waiting for transfers between devices: none -> 116 us  [the longest x1 116 us: per_device(): across = lax.ppermute(own, 'layer', [(i, i ^ 2) for i in range(4)])]
    all_gather x2 -> x1, waiting for transfers between devices: 0.57 us -> 89.5 us  [per_device(): lax.all_gather(transposed(part, row_count), ('row', 'col'), axis=0)]
    reshape x4 -> x1, local copies, waits for them, and re-layouts: 43.5 us -> 0.08 us  [per_device(): entry_rows = entry_rows.reshape(-1)]
    unnamed x0 -> x1, blocking collectives: none -> 32 us
    concatenate x0 -> x3, other arithmetic: none -> 28.2 us  [the longest x1 17.5 us: per_device(): rows_all = jnp.concatenate([pair, partner], axis=1)]
    all_gather x2 -> x0, blocking collectives: 25.1 us -> none  [the longest x1 12.6 us: per_device(): lax.all_gather(block_col, ('layer', 'col'), axis=0)]
  transfers between devices with their start and end apart: 7 -> 8, of which waited for: 4 -> 4; matrix products, arithmetic and copies ran while one was open for 7% -> 23% of each run, Pallas kernels for 11% -> 10%
where the time goes in v4:
time: 880 us; the launch traced here: 872 us
  waiting for transfers between devices  387 us (44%)
  local copies, waits for them, and re-layouts  178 us (20%)
  Pallas kernels  168 us (19%)
  other arithmetic  72.1 us (8%)
  blocking collectives  32 us (4%)
  starting transfers between devices  19.9 us (2%)
  between operations  14.3 us (2%)
    ppermute x5, waiting for transfers between devices, transposed(): lax.ppermute(value, ('layer', 'row'), [(a * size + b, b * size + a) for a...  181 us
    pallas_call x2, Pallas kernels, block_sparse_product(): pl.pallas_call(kernel, grid_spec=grid_spec, out_shape=jax.ShapeDtypeStruc...  168 us
    gather x144, local copies, waits for them, and re-layouts  129 us
    ppermute x1, waiting for transfers between devices, per_device(): across = lax.ppermute(own, 'layer', [(i, i ^ 2) for i in range(4)])  116 us
    all_gather x1, waiting for transfers between devices, per_device(): lax.all_gather(transposed(part, row_count), ('row', 'col'), axis=0)  89.5 us
    unnamed x1, blocking collectives  32 us
    ppermute x5, starting transfers between devices, transposed(): lax.ppermute(value, ('layer', 'row'), [(a * size + b, b * size + a) for a...  18.4 us
  transfers between devices with their start and end apart: 8, of which 4 were waited for; matrix products, arithmetic and copies ran while one was open for 23% of the time, Pallas kernels for 10%

profile of v4, /device:TPU:16, one launch (start us, length us, event | category | flops | bytes accessed | tf_op | source)
XLA Modules:
  0.0 872.2 jit_solution(7200272164366223105)
XLA Ops:
  7.5 5.9 multiply_bitcast_fusion
  15.6 9.2 %scatter_custom_fusion = s32[48]{0:T(128)S(1)} fusion(s32[1152]{0:T(1024)S(1)} %fusion.11, s32[1152]{0:T(1024)S(1)} %broadcast.653, s32[]{:T(128)} %copy.38), kind=kCustom, calls=%fused_computation.103 | custom fusion | flops 1152 | bytes 196 | tf_op jit(solution)/shard_map/scatter-add | solution.py:100
  29.1 5.7 collective-permute-start.1
  35.1 116.0 %collective-permute-done.2 = bf16[1024,3072]{1,0:T(8,128)(2,1)} collective-permute-done((bf16[1024,3072]{1,0:T(8,128)(2,1)}, bf16[1024,3072]{1,0:T(8,128)(2,1)}, u32[]{:S(2)}, u32[]{:S(2)}) %collective-permute-start.2) | collective-permute-done | bytes 6291488 | tf_op jit(solution)/shard_map/ppermute | solution.py:190
  151.0 10.7 %pad_maximum_fusion.1 = bf16[1024,6144]{1,0:T(8,128)(2,1)} fusion(bf16[1024,3072]{1,0:T(8,128)(2,1)} %collective-permute-done.2, bf16[1024,3072]{1,0:T(8,128)(2,1)} %multiply_bitcast_fusion), kind=kLoop, calls=%fused_computation.18 | loop fusion | flops 25165824 | bytes 25165824 | tf_op jit(solution)/shard_map/concatenate | solution.py:191
  161.7 129.3 %while.28 = (s32[]{:T(128)}, bf16[1536,3072]{1,0:T(8,128)(2,1)}, s32[48,2]{0,1:T(2,128)S(1)}, bf16[48,64,128]{2,1,0:T(8,128)(2,1)S(1)}, s32[]{:T(128)}) while((s32[]{:T(128)}, bf16[1536,3072]{1,0:T(8,128)(2,1)}, s32[48,2]{0,1:T(2,128)S(1)}, bf16[48,64,128]{2,1,0:T(8,128)(2,1)S(1)}, s32[]{:T(128)}) %tuple.60), condition=%wide.while_cond, body=%wide.while_body.sunk | while | flops 2 | bytes 32885 | solution.py:105
  162.3 2.0 bitcast_dynamic-update-slice_fusion.2
  165.0 2.0 bitcast_dynamic-update-slice_fusion.2
  167.7 2.0 bitcast_dynamic-update-slice_fusion.2
  173.1 2.0 bitcast_dynamic-update-slice_fusion.2
  175.8 2.0 bitcast_dynamic-update-slice_fusion.2
  178.5 2.0 bitcast_dynamic-update-slice_fusion.2
  292.9 3.2 collective-permute-start.4
  298.6 32.0 %all-reduce.2 = (s32[384]{0:T(512)S(1)}, s32[384]{0:T(512)S(1)}) all-reduce(s32[384]{0:T(512)S(1)} %dynamic-update-slice.2, s32[384]{0:T(512)S(1)} %dynamic-update-slice.3), channel_id=2, replica_groups=mesh['layer'=4,'row'=4,'col'=2] {'row','col'}, use_global_device_ids=true, to_apply=%add | all-reduce | flops 768 | bytes 6144
  330.5 3.8 sort.19
  334.3 2.8 gather_fusion.1
  338.1 6.9 while.29
  345.8 2.8 gather_fusion.3
  349.2 89.5 %all-gather.5.cloned.1.call-done = bf16[384,64,64]{2,1,0:T(8,128)(2,1)} async-done(((bf16[48,64,64]{2,1,0:T(8,128)(2,1)}), bf16[384,64,64]{2,1,0:T(8,128)(2,1)}) %all-gather.5.cloned.1.call-update) | async-done | bytes 3145744 | tf_op jit(solution)/shard_map/all_gather | solution.py:184
  438.7 4.2 broadcast_select_fusion.3
  443.0 6.4 broadcast_select_fusion.5
  449.4 5.3 pad_maximum_fusion.2
  454.7 15.8 %gather_fusion.5 = bf16[384,128,128]{2,1,0:T(8,128)(2,1)} fusion(bf16[384,128,128]{2,1,0:T(8,128)(2,1)} %pad_maximum_fusion.2, s32[1024]{0:T(1024)S(1)} %pad_clamp_fusion.3), kind=kCustom, calls=%fused_computation.5 | custom fusion | bytes 25167360 | tf_op jit(solution)/shard_map/gather | solution.py:132
  470.5 17.5 %pad_maximum_fusion = bf16[1024,12288]{1,0:T(8,128)(2,1)} fusion(bf16[1024,6144]{1,0:T(8,128)(2,1)} %collective-permute-done.3, bf16[1024,3072]{1,0:T(8,128)(2,1)} %collective-permute-done.2, bf16[1024,3072]{1,0:T(8,128)(2,1)} %multiply_bitcast_fusion), kind=kLoop, calls=%fused_computation.17 | loop fusion | flops 75497472 | bytes 50331648 | tf_op jit(solution)/shard_map/concatenate | solution.py:193
  488.0 17.4 %fusion.29 = (bf16[512,12288]{1,0:T(8,128)(2,1)}, bf16[512,12288]{1,0:T(8,128)(2,1)}) fusion(bf16[1024,12288]{1,0:T(8,128)(2,1)} %pad_maximum_fusion), kind=kLoop, calls=%fused_computation.107 | loop fusion | bytes 50331648 | tf_op jit(solution)/shard_map/slice | solution.py:206
  505.3 84.1 %shard_map.56 = bf16[512,3072]{1,0:T(8,128)(2,1)} custom-call(s32[25]{0:T(128)} %convert_element_type.45.starts_ref, s32[384]{0:T(512)} %add_select_fusion.6.k_ref, bf16[512,12288]{1,0:T(8,128)(2,1)} %get-tuple-element.134.t_ref, bf16[384,128,128]{2,1,0:T(8,128)(2,1)} %gather_fusion.5), custom_call_target="tpu_custom_call" | custom-call | tf_op jit(solution)/shard_map/pallas_call | solution.py:162
  589.5 4.2 collective-permute-start.6
  593.7 84.1 %shard_map.55 = bf16[512,3072]{1,0:T(8,128)(2,1)} custom-call(s32[25]{0:T(128)} %convert_element_type.45.starts_ref, s32[384]{0:T(512)} %add_select_fusion.6.k_ref, bf16[512,12288]{1,0:T(8,128)(2,1)} %get-tuple-element.133.t_ref, bf16[384,128,128]{2,1,0:T(8,128)(2,1)} %gather_fusion.5), custom_call_target="tpu_custom_call" | custom-call | tf_op jit(solution)/shard_map/pallas_call | solution.py:162
  677.8 3.4 collective-permute-start.5
  681.2 113.7 %collective-permute-done.6 = bf16[512,3072]{1,0:T(8,128)(2,1)S(1)} collective-permute-done((bf16[512,3072]{1,0:T(8,128)(2,1)}, bf16[512,3072]{1,0:T(8,128)(2,1)S(1)}, u32[]{:S(2)}, u32[]{:S(2)}) %collective-permute-start.6) | collective-permute-done | bytes 3145760 | tf_op jit(solution)/shard_map/ppermute | solution.py:89
  794.9 67.3 %collective-permute-done.5 = bf16[512,3072]{1,0:T(8,128)(2,1)S(1)} collective-permute-done((bf16[512,3072]{1,0:T(8,128)(2,1)}, bf16[512,3072]{1,0:T(8,128)(2,1)S(1)}, u32[]{:S(2)}, u32[]{:S(2)}) %collective-permute-start.5) | collective-permute-done | bytes 3145760 | tf_op jit(solution)/shard_map/ppermute | solution.py:89
  862.2 3.1 maximum_bitcast_fusion
  (240 shorter events, 136.7 us)
Async XLA Ops:
  6.5 8.4 copy-start.2
  6.5 432.2 %all-gather.5.cloned.1.call-start = ((), (), s32[]{:S(2)}) async-start(), calls=%async_computation | async-start | bytes 7077888 | tf_op jit(solution)/shard_map/all_gather | solution.py:184
  13.4 137.6 %collective-permute-start.2 = (bf16[1024,3072]{1,0:T(8,128)(2,1)}, bf16[1024,3072]{1,0:T(8,128)(2,1)}, u32[]{:S(2)}, u32[]{:S(2)}) collective-permute-start(bf16[1024,3072]{1,0:T(8,128)(2,1)} %multiply_bitcast_fusion), channel_id=1, source_target_pairs={{0,16},{8,24},{16,0},{24,8},{1,17},{9,25},{17,1},{25,9},{2,18},{10... | collective-permute-start | bytes 18874376 | tf_op jit(solution)/shard_map/ppermute | solution.py:190
  27.2 270.9 %collective-permute-start = (s32[48]{0:T(128)S(1)}, s32[48]{0:T(128)S(1)}, u32[]{:S(2)}, u32[]{:S(2)}) collective-permute-start(s32[48]{0:T(128)S(1)} %get-tuple-element.127), channel_id=1, source_target_pairs={{0,0},{2,8},{4,16},{6,24},{8,2},{10,10},{12,18},{14,26},{16,4},{18... | collective-permute-start | bytes 584 | tf_op jit(solution)/shard_map/ppermute | solution.py:89
  29.1 269.2 %collective-permute-start.1 = (s32[48]{0:T(128)S(1)}, s32[48]{0:T(128)S(1)}, u32[]{:S(2)}, u32[]{:S(2)}) collective-permute-start(s32[48]{0:T(128)S(1)} %and_select_fusion.1), channel_id=1, source_target_pairs={{0,0},{2,8},{4,16},{6,24},{8,2},{10,10},{12,18},{14,26},{16,4},{18... | collective-permute-start | bytes 584 | tf_op jit(solution)/shard_map/ppermute | solution.py:89
  35.0 261.1 %copy-start = (s32[4]{0:T(128)S(1)}, s32[4]{0:T(128)}, u32[]{:S(2)}) copy-start(s32[4]{0:T(128)} %constant.194.clone) | copy-start | bytes 52
  35.0 261.8 %copy-start.3 = (u32[32]{0:T(128)S(1)}, u32[32]{0:T(128)}, u32[]{:S(2)}) copy-start(u32[32]{0:T(128)} %constant.211) | copy-start | bytes 388
  161.7 308.8 %collective-permute-start.3 = (bf16[1024,6144]{1,0:T(8,128)(2,1)}, bf16[1024,6144]{1,0:T(8,128)(2,1)}, u32[]{:S(2)}, u32[]{:S(2)}) collective-permute-start(bf16[1024,6144]{1,0:T(8,128)(2,1)} %pad_maximum_fusion.1), channel_id=1, source_target_pairs={{0,8},{8,0},{16,24},{24,16},{1,9},{9,1},{17,25},{25,17},{2,10},{10... | collective-permute-start | bytes 37748744 | tf_op jit(solution)/shard_map/ppermute | solution.py:192
  292.9 44.2 %collective-permute-start.4 = (bf16[48,64,64]{2,1,0:T(8,128)(2,1)S(1)}, bf16[48,64,64]{2,1,0:T(8,128)(2,1)S(1)}, u32[]{:S(2)}, u32[]{:S(2)}) collective-permute-start(bf16[48,64,64]{2,1,0:T(8,128)(2,1)S(1)} %select_multiply_fusion), channel_id=1, source_target_pairs={{0,0},{2,8},{4,16},{6,24},{8,2},{10,10},{12,18},{14,26},{16,4},{18... | collective-permute-start | bytes 1179656 | tf_op jit(solution)/shard_map/ppermute | solution.py:89
  337.1 0.9 copy-start.1
  589.5 205.4 %collective-permute-start.6 = (bf16[512,3072]{1,0:T(8,128)(2,1)}, bf16[512,3072]{1,0:T(8,128)(2,1)S(1)}, u32[]{:S(2)}, u32[]{:S(2)}) collective-permute-start(bf16[512,3072]{1,0:T(8,128)(2,1)} %shard_map.56), channel_id=1, source_target_pairs={{0,0},{2,8},{4,16},{6,24},{8,2},{10,10},{12,18},{14,26},{16,4},{18... | collective-permute-start | bytes 9437192 | tf_op jit(solution)/shard_map/ppermute | solution.py:89
  677.8 184.4 %collective-permute-start.5 = (bf16[512,3072]{1,0:T(8,128)(2,1)}, bf16[512,3072]{1,0:T(8,128)(2,1)S(1)}, u32[]{:S(2)}, u32[]{:S(2)}) collective-permute-start(bf16[512,3072]{1,0:T(8,128)(2,1)} %shard_map.55), channel_id=1, source_target_pairs={{0,0},{2,8},{4,16},{6,24},{8,2},{10,10},{12,18},{14,26},{16,4},{18... | collective-permute-start | bytes 9437192 | tf_op jit(solution)/shard_map/ppermute | solution.py:89
Sparse Core Ops, SparseCore 0:
  338.2 100.4 all-gather.4

commit v5 on v4

--- a/solution.py
+++ b/solution.py
@@ -8,7 +8,7 @@
 BLK = 64
 CAP = 48
 LANE = 128
-ROW_CHUNK = 512
+COL_PIECES = 2
 
 
 def passed_along(value, axis, by):
@@ -101,11 +101,7 @@
     valid = jnp.arange(cap) < jnp.sum(flat != 0)
     block_row = spots // tile_cols
     block_col = spots % tile_cols
-    windows = jax.vmap(
-        lambda r, c: lax.dynamic_slice(green, (r * BLK, c * LANE), (BLK, LANE))
-    )(block_row, block_col // 2)
-    left = (block_col % 2 == 0)[:, None, None]
-    blocks = jnp.where(left, windows[:, :, :BLK], windows[:, :, BLK:])
+    blocks = green.reshape(tile_rows, BLK, tile_cols, BLK)[block_row, :, block_col, :]
     scale = jnp.where(valid, flat[spots], 0).astype(jnp.bfloat16)
     blocks = blocks * scale[:, None, None]
     return blocks, block_row, block_col
@@ -120,52 +116,59 @@
     return jnp.concatenate([jnp.where(top, half, empty), jnp.where(top, empty, half)], axis=1)
 
 
-def block_sparse_product(rows_all, blocks, block_rows, block_cols, width):
+def block_sparse_product(rows_all, blocks, block_rows, block_cols, width, pieces):
     row_total, nao = rows_all.shape
     entries = blocks.shape[0]
     chunks = width // LANE
+    piece_chunks = chunks // pieces
     chunk_of = block_cols // 2
     order = jnp.argsort(chunk_of)
     chunk_sorted = chunk_of[order]
     starts = jnp.searchsorted(chunk_sorted, jnp.arange(chunks + 1), side="left").astype(jnp.int32)
     k_sorted = (block_rows[order] // 2).astype(jnp.int32)
     padded = padded_blocks(blocks, block_rows, block_cols)[order]
-    row_chunk = min(ROW_CHUNK, row_total)
-
-    def kernel(starts_ref, k_ref, t_ref, g_ref, o_ref):
-        for chunk in range(chunks):
-            def body(entry, acc):
-                k = pl.multiple_of(k_ref[entry] * LANE, LANE)
-                return acc + jnp.dot(
-                    t_ref[:, pl.ds(k, LANE)], g_ref[entry], preferred_element_type=jnp.float32
+    results = []
+    for piece in range(pieces):
+        first = piece * piece_chunks
+
+        def kernel(starts_ref, k_ref, t_ref, g_ref, o_ref, first=first):
+            for chunk in range(piece_chunks):
+                def body(entry, acc):
+                    k = pl.multiple_of(k_ref[entry] * LANE, LANE)
+                    return acc + jnp.dot(
+                        t_ref[:, pl.ds(k, LANE)], g_ref[entry], preferred_element_type=jnp.float32
+                    )
+
+                acc = lax.fori_loop(
+                    starts_ref[first + chunk],
+                    starts_ref[first + chunk + 1],
+                    body,
+                    jnp.zeros((row_total, LANE), jnp.float32),
                 )
-
-            acc = lax.fori_loop(
-                starts_ref[chunk],
-                starts_ref[chunk + 1],
-                body,
-                jnp.zeros((row_chunk, LANE), jnp.float32),
-            )
-            o_ref[:, chunk * LANE : (chunk + 1) * LANE] = acc.astype(o_ref.dtype)
-
-    grid_spec = pltpu.PrefetchScalarGridSpec(
-        num_scalar_prefetch=2,
-        grid=(row_total // row_chunk,),
-        in_specs=[
-            pl.BlockSpec((row_chunk, nao), lambda i, s, k: (i, 0)),
-            pl.BlockSpec(
-                (entries, LANE, LANE), lambda i, s, k: (0, 0, 0), pipeline_mode=pl.Buffered(1)
-            ),
-        ],
-        out_specs=pl.BlockSpec((row_chunk, width), lambda i, s, k: (i, 0)),
-    )
-    return pl.pallas_call(
-        kernel,
-        grid_spec=grid_spec,
-        out_shape=jax.ShapeDtypeStruct((row_total, width), jnp.bfloat16),
-        compiler_params=pltpu.CompilerParams(vmem_limit_bytes=56 * 1024 * 1024),
-    )(starts, k_sorted, rows_all, padded)
-
+                o_ref[:, chunk * LANE : (chunk + 1) * LANE] = acc.astype(o_ref.dtype)
+
+        grid_spec = pltpu.PrefetchScalarGridSpec(
+            num_scalar_prefetch=2,
+            grid=(1,),
+            in_specs=[
+                pl.BlockSpec(
+                    (row_total, nao), lambda i, s, k: (0, 0), pipeline_mode=pl.Buffered(1)
+                ),
+                pl.BlockSpec(
+                    (entries, LANE, LANE), lambda i, s, k: (0, 0, 0), pipeline_mode=pl.Buffered(1)
+                ),
+            ],
+            out_specs=pl.BlockSpec((row_total, piece_chunks * LANE), lambda i, s, k: (0, 0)),
+        )
+        results.append(
+            pl.pallas_call(
+                kernel,
+                grid_spec=grid_spec,
+                out_shape=jax.ShapeDtypeStruct((row_total, piece_chunks * LANE), jnp.bfloat16),
+                compiler_params=pltpu.CompilerParams(vmem_limit_bytes=60 * 1024 * 1024),
+            )(starts, k_sorted, rows_all, padded)
+        )
+    return results
 
 def per_device(tensor, tensor_pattern, green, green_pattern):
     layer_count = lax.axis_size("layer")
@@ -200,15 +203,11 @@
     entry_rows = entry_rows.reshape(-1)
     entry_cols = block_col.reshape(-1)
     entry_blocks = blocks.reshape(-1, BLK, BLK)
-    pieces = []
-    for start in range(0, ri_local * mu_local, ROW_CHUNK):
-        piece = block_sparse_product(
-            rows_all[start : start + ROW_CHUNK], entry_blocks, entry_rows, entry_cols, tile_cols * BLK
-        )
-        pieces.append(transposed(piece, row_count))
-    product = jnp.concatenate(pieces, axis=0)
+    pieces = block_sparse_product(
+        rows_all, entry_blocks, entry_rows, entry_cols, tile_cols * BLK, COL_PIECES
+    )
+    product = jnp.concatenate([transposed(piece, row_count) for piece in pieces], axis=1)
     return product.reshape(ri_local, mu_local, tile_cols * BLK)
-
 
 def solution(mesh):
     in_specs = (

time: 880 us -> 844 us (0.959)
  waiting for transfers between devices: 387 us -> 493 us
  local copies, waits for them, and re-layouts: 178 us -> 82.9 us
  Pallas kernels: 168 us -> 131 us
    gather x144 -> x1, local copies, waits for them, and re-layouts: 129 us -> 7.24 us  [compressed_tile(): green.reshape(tile_rows, BLK, tile_cols, BLK)[block_row, :, block_col, :]]
    ppermute x5, waiting for transfers between devices: 181 us -> 265 us  [transposed(): lax.ppermute(value, ('layer', 'row'), [(a * size + b, b * size + a) for a...]
    reshape x0 -> x2, local copies, waits for them, and re-layouts: none -> 43.3 us  [compressed_tile(): green.reshape(tile_rows, BLK, tile_cols, BLK)[block_row, :, block_col, :]]
    pallas_call x2, Pallas kernels: 168 us -> 131 us  [block_sparse_product(): pl.pallas_call(kernel, grid_spec=grid_spec, out_shape=jax.ShapeDtypeStruc...]
    ppermute x1, waiting for transfers between devices: 116 us -> 136 us  [per_device(): across = lax.ppermute(own, 'layer', [(i, i ^ 2) for i in range(4)])]
    slice x2 -> x1, local copies, waits for them, and re-layouts: 17.5 us -> 0.08 us  [the longest x1 17.4 us: per_device(): rows_all[start:start + ROW_CHUNK]]
  transfers between devices with their start and end apart: 8 -> 8, of which waited for: 4 -> 4; matrix products, arithmetic and copies ran while one was open for 23% -> 14% of each run, Pallas kernels for 10% -> 0%
where the time goes in v5:
time: 844 us; the launch traced here: 840 us
  waiting for transfers between devices  493 us (58%)
  Pallas kernels  131 us (16%)
  local copies, waits for them, and re-layouts  82.9 us (10%)
  other arithmetic  68 us (8%)
  blocking collectives  30.7 us (4%)
  starting transfers between devices  20 us (2%)
  between operations  14.4 us (2%)
    ppermute x5, waiting for transfers between devices, transposed(): lax.ppermute(value, ('layer', 'row'), [(a * size + b, b * size + a) for a...  265 us
    ppermute x1, waiting for transfers between devices, per_device(): across = lax.ppermute(own, 'layer', [(i, i ^ 2) for i in range(4)])  136 us
    pallas_call x2, Pallas kernels, block_sparse_product(): pl.pallas_call(kernel, grid_spec=grid_spec, out_shape=jax.ShapeDtypeStruc...  131 us
    all_gather x1, waiting for transfers between devices, per_device(): lax.all_gather(transposed(part, row_count), ('row', 'col'), axis=0)  92.4 us
    reshape x2, local copies, waits for them, and re-layouts, compressed_tile(): green.reshape(tile_rows, BLK, tile_cols, BLK)[block_row, :, block_col, :]  43.3 us
    unnamed x1, blocking collectives  30.7 us
    ppermute x5, starting transfers between devices, transposed(): lax.ppermute(value, ('layer', 'row'), [(a * size + b, b * size + a) for a...  18.4 us
    concatenate x1, other arithmetic, per_device(): rows_all = jnp.concatenate([pair, partner], axis=1)  17.5 us
  transfers between devices with their start and end apart: 8, of which 4 were waited for; matrix products, arithmetic and copies ran while one was open for 14% of the time, Pallas kernels for 0%

profile of v5, /device:TPU:16, one launch (start us, length us, event | category | flops | bytes accessed | tf_op | source)
XLA Modules:
  0.0 840.3 jit_solution(508736214029663090)
XLA Ops:
  7.5 3.2 multiply_bitcast_fusion
  10.7 1.6 collective-permute-start.2
  12.3 135.8 %collective-permute-done.2 = bf16[1024,3072]{1,0:T(8,128)(2,1)S(1)} collective-permute-done((bf16[1024,3072]{1,0:T(8,128)(2,1)S(1)}, bf16[1024,3072]{1,0:T(8,128)(2,1)S(1)}, u32[]{:S(2)}, u32[]{:S(2)}) %collective-permute-start.2) | collective-permute-done | bytes 6291488 | tf_op jit(solution)/shard_map/ppermute | solution.py:193
  148.0 9.2 %pad_maximum_fusion.1 = bf16[1024,6144]{1,0:T(8,128)(2,1)} fusion(bf16[1024,3072]{1,0:T(8,128)(2,1)S(1)} %collective-permute-done.2, bf16[1024,3072]{1,0:T(8,128)(2,1)S(1)} %multiply_bitcast_fusion), kind=kLoop, calls=%fused_computation.17 | loop fusion | flops 25165824 | bytes 25165824 | tf_op jit(solution)/shard_map/concatenate | solution.py:194
  158.0 9.2 %scatter_custom_fusion = s32[48]{0:T(128)S(1)} fusion(s32[1152]{0:T(1024)S(1)} %fusion.13, s32[1152]{0:T(1024)S(1)} %broadcast.505, s32[]{:T(128)} %copy.30), kind=kCustom, calls=%fused_computation.93 | custom fusion | flops 1152 | bytes 196 | tf_op jit(solution)/shard_map/scatter-add | solution.py:100
  168.0 0.8 fusion.11
  169.4 3.2 collective-permute-start.1
  172.6 4.5 collective-permute-start
  177.2 23.4 %reshape.333 = bf16[24,64,48,64]{3,2,1,0:T(8,128)(2,1)} reshape(bf16[1536,3072]{1,0:T(8,128)(2,1)} %param.9) | data formatting | bytes 18874368 | tf_op jit(solution)/shard_map/reshape | solution.py:104
  200.6 20.0 %copy.11 = bf16[24,64,48,64]{3,1,2,0:T(8,128)(2,1)} copy(bf16[24,64,48,64]{3,2,1,0:T(8,128)(2,1)} %reshape.333) | data formatting | bytes 18874368 | tf_op jit(solution)/shard_map/reshape | solution.py:104
  220.5 0.8 gather_fusion.5
  221.3 7.2 gather_fusion.4
  229.3 3.2 collective-permute-start.4
  235.1 30.7 %all-reduce.2 = (s32[384]{0:T(512)S(1)}, s32[384]{0:T(512)S(1)}) all-reduce(s32[384]{0:T(512)S(1)} %dynamic-update-slice, s32[384]{0:T(512)S(1)} %dynamic-update-slice.1), channel_id=2, replica_groups=mesh['layer'=4,'row'=4,'col'=2] {'row','col'}, use_global_device_ids=true, to_apply=%add | all-reduce | flops 768 | bytes 6144
  266.0 3.8 sort.17
  269.9 2.8 gather_fusion.1
  272.7 2.8 gather_fusion.3
  275.5 0.9 copy-done.4
  276.4 6.9 while.24
  284.4 92.4 %all-gather.5.cloned.1.call-done = bf16[384,64,64]{2,1,0:T(8,128)(2,1)} async-done(((bf16[48,64,64]{2,1,0:T(8,128)(2,1)}), bf16[384,64,64]{2,1,0:T(8,128)(2,1)}) %all-gather.5.cloned.1.call-update) | async-done | bytes 3145744 | tf_op jit(solution)/shard_map/all_gather | solution.py:187
  376.8 4.2 broadcast_select_fusion.3
  381.1 6.4 broadcast_select_fusion.5
  387.5 5.2 pad_maximum_fusion.2
  392.8 16.0 %gather_fusion.6 = bf16[384,128,128]{2,1,0:T(8,128)(2,1)} fusion(bf16[384,128,128]{2,1,0:T(8,128)(2,1)} %pad_maximum_fusion.2, s32[1024]{0:T(1024)S(1)} %pad_clamp_fusion.3), kind=kCustom, calls=%fused_computation.6 | custom fusion | bytes 25167360 | tf_op jit(solution)/shard_map/gather | solution.py:129
  408.7 17.5 %pad_maximum_fusion.t_ref = bf16[1024,12288]{1,0:T(8,128)(2,1)} fusion(bf16[1024,6144]{1,0:T(8,128)(2,1)} %collective-permute-done.3, bf16[1024,3072]{1,0:T(8,128)(2,1)} %copy-done.2, bf16[1024,3072]{1,0:T(8,128)(2,1)} %copy-done.1), kind=kLoop, calls=%fused_computation.16 | loop fusion | flops 75497472 | bytes 50331648 | tf_op jit(solution)/shard_map/concatenate | solution.py:196
  426.2 89.1 %shard_map.55 = bf16[1024,1536]{1,0:T(8,128)(2,1)} custom-call(s32[25]{0:T(128)} %convert_element_type.44.starts_ref, s32[384]{0:T(512)} %add_select_fusion.5.k_ref, bf16[1024,12288]{1,0:T(8,128)(2,1)} %pad_maximum_fusion.t_ref, bf16[384,128,128]{2,1,0:T(8,128)(2,1)} %gather_fusion.6), custom_call_target="tpu_custom_call" | custom-call | tf_op jit(solution)/shard_map/pallas_call | solution.py:164
  515.3 42.0 %shard_map.56 = bf16[1024,1536]{1,0:T(8,128)(2,1)} custom-call(s32[25]{0:T(128)} %convert_element_type.44.starts_ref, s32[384]{0:T(512)} %add_select_fusion.5.k_ref, bf16[1024,12288]{1,0:T(8,128)(2,1)} %pad_maximum_fusion.t_ref, bf16[384,128,128]{2,1,0:T(8,128)(2,1)} %gather_fusion.6), custom_call_target="tpu_custom_call" | custom-call | tf_op jit(solution)/shard_map/pallas_call | solution.py:164
  557.3 4.2 collective-permute-start.5
  561.5 3.4 collective-permute-start.6
  564.9 197.5 %collective-permute-done.5 = bf16[1024,1536]{1,0:T(8,128)(2,1)S(1)} collective-permute-done((bf16[1024,1536]{1,0:T(8,128)(2,1)S(1)}, bf16[1024,1536]{1,0:T(8,128)(2,1)S(1)}, u32[]{:S(2)}, u32[]{:S(2)}) %collective-permute-start.5) | collective-permute-done | bytes 3145760 | tf_op jit(solution)/shard_map/ppermute | solution.py:89
  762.4 67.4 %collective-permute-done.6 = bf16[1024,1536]{1,0:T(8,128)(2,1)S(1)} collective-permute-done((bf16[1024,1536]{1,0:T(8,128)(2,1)}, bf16[1024,1536]{1,0:T(8,128)(2,1)S(1)}, u32[]{:S(2)}, u32[]{:S(2)}) %collective-permute-start.6) | collective-permute-done | bytes 3145760 | tf_op jit(solution)/shard_map/ppermute | solution.py:89
  829.8 3.7 maximum_bitcast_fusion
  (99 shorter events, 13.9 us)
Async XLA Ops:
  6.5 370.3 %all-gather.5.cloned.1.call-start = ((), (), s32[]{:S(2)}) async-start(), calls=%async_computation | async-start | bytes 7077888 | tf_op jit(solution)/shard_map/all_gather | solution.py:187
  10.7 146.6 %copy-start.1 = (bf16[1024,3072]{1,0:T(8,128)(2,1)}, bf16[1024,3072]{1,0:T(8,128)(2,1)S(1)}, u32[]{:S(2)}) copy-start(bf16[1024,3072]{1,0:T(8,128)(2,1)S(1)} %multiply_bitcast_fusion) | copy-start | bytes 18874372
  10.7 146.6 %copy-start.5 = (s32[24,48]{1,0:T(8,128)S(1)}, s32[24,48]{1,0:T(8,128)}, u32[]{:S(2)}) copy-start(s32[24,48]{1,0:T(8,128)} %param.10) | copy-start | bytes 13828
  10.7 137.3 %collective-permute-start.2 = (bf16[1024,3072]{1,0:T(8,128)(2,1)S(1)}, bf16[1024,3072]{1,0:T(8,128)(2,1)S(1)}, u32[]{:S(2)}, u32[]{:S(2)}) collective-permute-start(bf16[1024,3072]{1,0:T(8,128)(2,1)S(1)} %multiply_bitcast_fusion), channel_id=1, source_target_pairs={{0,16},{8,24},{16,0},{24,8},{1,17},{9,25},{17,1},{25,9},{2,18},{10... | collective-permute-start | bytes 18874376 | tf_op jit(solution)/shard_map/ppermute | solution.py:193
  148.0 9.2 %copy-start.2 = (bf16[1024,3072]{1,0:T(8,128)(2,1)}, bf16[1024,3072]{1,0:T(8,128)(2,1)S(1)}, u32[]{:S(2)}) copy-start(bf16[1024,3072]{1,0:T(8,128)(2,1)S(1)} %collective-permute-done.2) | copy-start | bytes 18874372
  157.3 251.4 %collective-permute-start.3 = (bf16[1024,6144]{1,0:T(8,128)(2,1)}, bf16[1024,6144]{1,0:T(8,128)(2,1)}, u32[]{:S(2)}, u32[]{:S(2)}) collective-permute-start(bf16[1024,6144]{1,0:T(8,128)(2,1)} %pad_maximum_fusion.1), channel_id=1, source_target_pairs={{0,8},{8,0},{16,24},{24,16},{1,9},{9,1},{17,25},{25,17},{2,10},{10... | collective-permute-start | bytes 37748744 | tf_op jit(solution)/shard_map/ppermute | solution.py:195
  169.4 65.2 %collective-permute-start.1 = (s32[48]{0:T(128)S(1)}, s32[48]{0:T(128)S(1)}, u32[]{:S(2)}, u32[]{:S(2)}) collective-permute-start(s32[48]{0:T(128)S(1)} %get-tuple-element.103), channel_id=1, source_target_pairs={{0,0},{2,8},{4,16},{6,24},{8,2},{10,10},{12,18},{14,26},{16,4},{18... | collective-permute-start | bytes 584 | tf_op jit(solution)/shard_map/ppermute | solution.py:89
  172.6 62.2 %collective-permute-start = (s32[48]{0:T(128)S(1)}, s32[48]{0:T(128)S(1)}, u32[]{:S(2)}, u32[]{:S(2)}) collective-permute-start(s32[48]{0:T(128)S(1)} %and_select_fusion.3), channel_id=1, source_target_pairs={{0,0},{2,8},{4,16},{6,24},{8,2},{10,10},{12,18},{14,26},{16,4},{18... | collective-permute-start | bytes 584 | tf_op jit(solution)/shard_map/ppermute | solution.py:89
  200.6 32.0 %copy-start = (s32[4]{0:T(128)S(1)}, s32[4]{0:T(128)}, u32[]{:S(2)}) copy-start(s32[4]{0:T(128)} %constant.161.clone) | copy-start | bytes 52
  200.6 32.7 %copy-start.6 = (u32[32]{0:T(128)S(1)}, u32[32]{0:T(128)}, u32[]{:S(2)}) copy-start(u32[32]{0:T(128)} %constant.177) | copy-start | bytes 388
  229.3 46.2 %collective-permute-start.4 = (bf16[48,64,64]{2,1,0:T(8,128)(2,1)S(1)}, bf16[48,64,64]{2,1,0:T(8,128)(2,1)S(1)}, u32[]{:S(2)}, u32[]{:S(2)}) collective-permute-start(bf16[48,64,64]{2,1,0:T(8,128)(2,1)S(1)} %broadcast_multiply_fusion), channel_id=1, source_target_pairs={{0,0},{2,8},{4,16},{6,24},{8,2},{10,10},{12,18},{14,26},{16,4},{18... | collective-permute-start | bytes 1179656 | tf_op jit(solution)/shard_map/ppermute | solution.py:89
  275.5 0.9 copy-start.4
  515.3 42.0 %copy-start.3 = (bf16[1024,1536]{1,0:T(8,128)(2,1)S(1)}, bf16[1024,1536]{1,0:T(8,128)(2,1)}, u32[]{:S(2)}) copy-start(bf16[1024,1536]{1,0:T(8,128)(2,1)} %shard_map.55) | copy-start | bytes 9437188
  557.3 205.1 %collective-permute-start.5 = (bf16[1024,1536]{1,0:T(8,128)(2,1)S(1)}, bf16[1024,1536]{1,0:T(8,128)(2,1)S(1)}, u32[]{:S(2)}, u32[]{:S(2)}) collective-permute-start(bf16[1024,1536]{1,0:T(8,128)(2,1)S(1)} %copy-done.3), channel_id=1, source_target_pairs={{0,0},{2,8},{4,16},{6,24},{8,2},{10,10},{12,18},{14,26},{16,4},{18... | collective-permute-start | bytes 9437192 | tf_op jit(solution)/shard_map/ppermute | solution.py:89
  561.5 268.3 %collective-permute-start.6 = (bf16[1024,1536]{1,0:T(8,128)(2,1)}, bf16[1024,1536]{1,0:T(8,128)(2,1)S(1)}, u32[]{:S(2)}, u32[]{:S(2)}) collective-permute-start(bf16[1024,1536]{1,0:T(8,128)(2,1)} %shard_map.56), channel_id=1, source_target_pairs={{0,0},{2,8},{4,16},{6,24},{8,2},{10,10},{12,18},{14,26},{16,4},{18... | collective-permute-start | bytes 9437192 | tf_op jit(solution)/shard_map/ppermute | solution.py:89
Sparse Core Ops, SparseCore 0:
  276.5 100.2 all-gather.4

commit v6 on v5

--- a/solution.py
+++ b/solution.py
@@ -8,7 +8,7 @@
 BLK = 64
 CAP = 48
 LANE = 128
-COL_PIECES = 2
+ROW_CHUNK = 512
 
 
 def passed_along(value, axis, by):
@@ -189,24 +189,19 @@
     )
     band_count = blocks.shape[0]
     band = jnp.arange(band_count)[:, None]
-    if layer_count == 4:
-        across = lax.ppermute(own, "layer", [(i, i ^ 2) for i in range(4)])
-        pair = jnp.concatenate([own, across], axis=1)
-        partner = lax.ppermute(pair, "layer", [(i, i ^ 1) for i in range(4)])
-        rows_all = jnp.concatenate([pair, partner], axis=1)
-        source = (band // col_count) ^ layer_index
-        position = jnp.array([0, 2, 1, 3], jnp.int32)[source]
-    else:
-        rows_all = lax.all_gather(own, "layer", axis=1, tiled=True)
-        position = band // col_count
+    rows_all = lax.all_gather(own, "layer", axis=1, tiled=True)
+    position = band // col_count
     entry_rows = (position * col_count + band % col_count) * tile_rows + block_row
     entry_rows = entry_rows.reshape(-1)
     entry_cols = block_col.reshape(-1)
     entry_blocks = blocks.reshape(-1, BLK, BLK)
-    pieces = block_sparse_product(
-        rows_all, entry_blocks, entry_rows, entry_cols, tile_cols * BLK, COL_PIECES
-    )
-    product = jnp.concatenate([transposed(piece, row_count) for piece in pieces], axis=1)
+    pieces = []
+    for start in range(0, ri_local * mu_local, ROW_CHUNK):
+        (piece,) = block_sparse_product(
+            rows_all[start : start + ROW_CHUNK], entry_blocks, entry_rows, entry_cols, tile_cols * BLK, 1
+        )
+        pieces.append(transposed(piece, row_count))
+    product = jnp.concatenate(pieces, axis=0)
     return product.reshape(ri_local, mu_local, tile_cols * BLK)
 
 def solution(mesh):

time: 844 us -> 755 us (0.89)
  waiting for transfers between devices: 493 us -> 394 us
  Pallas kernels: 131 us -> 168 us
  blocking collectives: 30.7 us -> 5.81 us
  other arithmetic: 68 us -> 45.5 us
  local copies, waits for them, and re-layouts: 82.9 us -> 104 us
    ppermute x2 -> x0, waiting for transfers between devices: 136 us -> none  [the longest x1 136 us: per_device(): across = lax.ppermute(own, 'layer', [(i, i ^ 2) for i in range(4)])]
    all_gather x0 -> x1, waiting for transfers between devices: none -> 119 us  [per_device(): rows_all = lax.all_gather(own, 'layer', axis=1, tiled=True)]
    ppermute x5, waiting for transfers between devices: 265 us -> 219 us  [transposed(): lax.ppermute(value, ('layer', 'row'), [(a * size + b, b * size + a) for a...]
    pallas_call x2, Pallas kernels: 131 us -> 168 us  [block_sparse_product(): pl.pallas_call(kernel, grid_spec=grid_spec, out_shape=jax.ShapeDtypeStruc...]
    all_gather x1, waiting for transfers between devices: 92.4 us -> 56.1 us  [per_device(): lax.all_gather(transposed(part, row_count), ('row', 'col'), axis=0)]
    concatenate x2 -> x0, other arithmetic: 26.7 us -> none  [the longest x1 17.5 us: per_device(): rows_all = jnp.concatenate([pair, partner], axis=1)]
    unnamed x1, blocking collectives: 30.7 us -> 5.81 us
    slice x1 -> x2, local copies, waits for them, and re-layouts: 0.08 us -> 17.5 us  [the longest x1 17.4 us: per_device(): rows_all[start:start + ROW_CHUNK]]
  transfers between devices with their start and end apart: 8 -> 7, of which waited for: 4 -> 6; matrix products, arithmetic and copies ran while one was open for 14% -> 8% of each run, Pallas kernels for 0% -> 11%
where the time goes in v6:
time: 755 us; the launch traced here: 751 us
  waiting for transfers between devices  394 us (52%)
  Pallas kernels  168 us (22%)
  local copies, waits for them, and re-layouts  104 us (14%)
  other arithmetic  45.5 us (6%)
  starting transfers between devices  18.9 us (3%)
  between operations  14.3 us (2%)
    ppermute x5, waiting for transfers between devices, transposed(): lax.ppermute(value, ('layer', 'row'), [(a * size + b, b * size + a) for a...  219 us
    pallas_call x2, Pallas kernels, block_sparse_product(): pl.pallas_call(kernel, grid_spec=grid_spec, out_shape=jax.ShapeDtypeStruc...  168 us
    all_gather x1, waiting for transfers between devices, per_device(): rows_all = lax.all_gather(own, 'layer', axis=1, tiled=True)  119 us
    all_gather x1, waiting for transfers between devices, per_device(): lax.all_gather(transposed(part, row_count), ('row', 'col'), axis=0)  56.1 us
    reshape x2, local copies, waits for them, and re-layouts, compressed_tile(): green.reshape(tile_rows, BLK, tile_cols, BLK)[block_row, :, block_col, :]  43.3 us
    gather x1, local copies, waits for them, and re-layouts, block_sparse_product(): padded = padded_blocks(blocks, block_rows, block_cols)[order]  19.4 us
    ppermute x5, starting transfers between devices, transposed(): lax.ppermute(value, ('layer', 'row'), [(a * size + b, b * size + a) for a...  18.9 us
    slice x1, local copies, waits for them, and re-layouts, per_device(): rows_all[start:start + ROW_CHUNK]  17.4 us
  transfers between devices with their start and end apart: 7, of which 6 were waited for; matrix products, arithmetic and copies ran while one was open for 8% of the time, Pallas kernels for 11%

profile of v6, /device:TPU:16, one launch (start us, length us, event | category | flops | bytes accessed | tf_op | source)
XLA Modules:
  0.0 750.7 jit_solution(10350535858871521733)
XLA Ops:
  7.2 1.3 fusion.26
  8.6 0.8 reshape.290
  10.1 9.2 %scatter_custom_fusion = s32[48]{0:T(128)S(1)} fusion(s32[1152]{0:T(1024)S(1)} %fusion.13, s32[1152]{0:T(1024)S(1)} %broadcast.461, s32[]{:T(128)} %copy.29), kind=kCustom, calls=%fused_computation.87 | custom fusion | flops 1152 | bytes 196 | tf_op jit(solution)/shard_map/scatter-add | solution.py:100
  21.5 23.4 %reshape.289 = bf16[24,64,48,64]{3,2,1,0:T(8,128)(2,1)} reshape(bf16[1536,3072]{1,0:T(8,128)(2,1)} %param.8) | data formatting | bytes 18874368 | tf_op jit(solution)/shard_map/reshape | solution.py:104
  44.9 20.0 %copy.10 = bf16[24,64,48,64]{3,1,2,0:T(8,128)(2,1)} copy(bf16[24,64,48,64]{3,2,1,0:T(8,128)(2,1)} %reshape.289) | data formatting | bytes 18874368 | tf_op jit(solution)/shard_map/reshape | solution.py:104
  64.8 7.2 gather_fusion.3
  72.2 3.2 collective-permute-start.2
  75.4 34.3 %collective-permute-done.2 = bf16[48,64,64]{2,1,0:T(8,128)(2,1)S(1)} collective-permute-done((bf16[48,64,64]{2,1,0:T(8,128)(2,1)S(1)}, bf16[48,64,64]{2,1,0:T(8,128)(2,1)S(1)}, u32[]{:S(2)}, u32[]{:S(2)}) %collective-permute-start.2) | collective-permute-done | bytes 393248 | tf_op jit(solution)/shard_map/ppermute | solution.py:89
  109.7 0.9 copy-done
  110.9 5.9 multiply_bitcast_fusion
  117.5 6.2 collective-permute-start.1
  123.7 1.9 collective-permute-start
  127.1 3.9 collective-permute-done
  131.2 5.8 all-reduce.2
  137.3 3.7 sort.19
  141.0 2.8 gather_fusion.1
  143.8 6.9 while.27
  151.3 2.8 gather_fusion.2
  154.7 56.1 %all-gather.8.cloned.1.call-done = bf16[384,64,64]{2,1,0:T(8,128)(2,1)} async-done(((bf16[48,64,64]{2,1,0:T(8,128)(2,1)}), bf16[384,64,64]{2,1,0:T(8,128)(2,1)}) %all-gather.8.cloned.1.call-update) | async-done | bytes 3145744 | tf_op jit(solution)/shard_map/all_gather | solution.py:187
  210.8 4.3 broadcast_select_fusion.3
  215.1 6.4 broadcast_select_fusion.5
  221.5 6.8 pad_maximum_fusion
  228.3 19.4 %gather_fusion.5 = bf16[384,128,128]{2,1,0:T(8,128)(2,1)} fusion(bf16[384,128,128]{2,1,0:T(8,128)(2,1)} %pad_maximum_fusion, s32[1024]{0:T(1024)S(1)} %pad_clamp_fusion.2), kind=kCustom, calls=%fused_computation.5 | custom fusion | bytes 25167360 | tf_op jit(solution)/shard_map/gather | solution.py:129
  247.7 118.6 %all-gather.6.cloned.1.call-done = bf16[1024,12288]{1,0:T(8,128)(2,1)} async-done(((bf16[1024,3072]{1,0:T(8,128)(2,1)}), bf16[1024,12288]{1,0:T(8,128)(2,1)}) %all-gather.6.cloned.1.call-update) | async-done | bytes 25165840 | tf_op jit(solution)/shard_map/all_gather | solution.py:192
  366.3 17.4 %fusion.27 = (bf16[512,12288]{1,0:T(8,128)(2,1)}, bf16[512,12288]{1,0:T(8,128)(2,1)}) fusion(bf16[1024,12288]{1,0:T(8,128)(2,1)} %all-gather.6.cloned.1.call-done), kind=kLoop, calls=%fused_computation.90 | loop fusion | bytes 50331648 | tf_op jit(solution)/shard_map/slice | solution.py:201
  383.7 84.1 %shard_map.46 = bf16[512,3072]{1,0:T(8,128)(2,1)} custom-call(s32[25]{0:T(128)} %convert_element_type.45.starts_ref, s32[384]{0:T(512)} %add_select_fusion.5.k_ref, bf16[512,12288]{1,0:T(8,128)(2,1)} %get-tuple-element.107.t_ref, bf16[384,128,128]{2,1,0:T(8,128)(2,1)} %gather_fusion.5), custom_call_target="tpu_custom_call" | custom-call | tf_op jit(solution)/shard_map/pallas_call | solution.py:164
  467.8 2.2 collective-permute-start.3
  470.0 84.1 %shard_map.47 = bf16[512,3072]{1,0:T(8,128)(2,1)} custom-call(s32[25]{0:T(128)} %convert_element_type.45.starts_ref, s32[384]{0:T(512)} %add_select_fusion.5.k_ref, bf16[512,12288]{1,0:T(8,128)(2,1)} %get-tuple-element.108.t_ref, bf16[384,128,128]{2,1,0:T(8,128)(2,1)} %gather_fusion.5), custom_call_target="tpu_custom_call" | custom-call | tf_op jit(solution)/shard_map/pallas_call | solution.py:164
  554.1 5.4 collective-permute-start.4
  559.5 114.1 %collective-permute-done.3 = bf16[512,3072]{1,0:T(8,128)(2,1)S(1)} collective-permute-done((bf16[512,3072]{1,0:T(8,128)(2,1)}, bf16[512,3072]{1,0:T(8,128)(2,1)S(1)}, u32[]{:S(2)}, u32[]{:S(2)}) %collective-permute-start.3) | collective-permute-done | bytes 3145760 | tf_op jit(solution)/shard_map/ppermute | solution.py:89
  673.6 67.1 %collective-permute-done.4 = bf16[512,3072]{1,0:T(8,128)(2,1)S(1)} collective-permute-done((bf16[512,3072]{1,0:T(8,128)(2,1)}, bf16[512,3072]{1,0:T(8,128)(2,1)S(1)}, u32[]{:S(2)}, u32[]{:S(2)}) %collective-permute-start.4) | collective-permute-done | bytes 3145760 | tf_op jit(solution)/shard_map/ppermute | solution.py:89
  740.7 3.1 maximum_bitcast_fusion
  (86 shorter events, 13.8 us)
Async XLA Ops:
  6.5 204.3 %all-gather.8.cloned.1.call-start = ((), (), s32[]{:S(2)}) async-start(), calls=%async_computation.1 | async-start | bytes 7077888 | tf_op jit(solution)/shard_map/all_gather | solution.py:187
  44.9 65.8 %copy-start.1 = (s32[8,48]{1,0:T(8,128)S(1)}, s32[8,48]{1,0:T(8,128)}, u32[]{:S(2)}) copy-start(s32[8,48]{1,0:T(8,128)} %param.7) | copy-start | bytes 4612
  72.2 37.5 %collective-permute-start.2 = (bf16[48,64,64]{2,1,0:T(8,128)(2,1)S(1)}, bf16[48,64,64]{2,1,0:T(8,128)(2,1)S(1)}, u32[]{:S(2)}, u32[]{:S(2)}) collective-permute-start(bf16[48,64,64]{2,1,0:T(8,128)(2,1)S(1)} %broadcast_multiply_fusion), channel_id=1, source_target_pairs={{0,0},{2,8},{4,16},{6,24},{8,2},{10,10},{12,18},{14,26},{16,4},{18... | collective-permute-start | bytes 1179656 | tf_op jit(solution)/shard_map/ppermute | solution.py:89
  109.7 0.9 copy-start
  110.6 255.7 %all-gather.6.cloned.1.call-start = ((), (), s32[]{:S(2)}) async-start(), calls=%async_computation | async-start | bytes 31457280 | tf_op jit(solution)/shard_map/all_gather | solution.py:192
  116.9 8.8 %copy-start.2 = (u32[32]{0:T(128)S(1)}, u32[32]{0:T(128)}, u32[]{:S(2)}) copy-start(u32[32]{0:T(128)} %constant.179) | copy-start | bytes 388
  117.5 9.4 %collective-permute-start.1 = (s32[48]{0:T(128)S(1)}, s32[48]{0:T(128)S(1)}, u32[]{:S(2)}, u32[]{:S(2)}) collective-permute-start(s32[48]{0:T(128)S(1)} %get-tuple-element.103), channel_id=1, source_target_pairs={{0,0},{2,8},{4,16},{6,24},{8,2},{10,10},{12,18},{14,26},{16,4},{18... | collective-permute-start | bytes 584 | tf_op jit(solution)/shard_map/ppermute | solution.py:89
  123.7 7.3 collective-permute-start
  467.8 205.8 %collective-permute-start.3 = (bf16[512,3072]{1,0:T(8,128)(2,1)}, bf16[512,3072]{1,0:T(8,128)(2,1)S(1)}, u32[]{:S(2)}, u32[]{:S(2)}) collective-permute-start(bf16[512,3072]{1,0:T(8,128)(2,1)} %shard_map.46), channel_id=1, source_target_pairs={{0,0},{2,8},{4,16},{6,24},{8,2},{10,10},{12,18},{14,26},{16,4},{18... | collective-permute-start | bytes 9437192 | tf_op jit(solution)/shard_map/ppermute | solution.py:89
  554.1 186.6 %collective-permute-start.4 = (bf16[512,3072]{1,0:T(8,128)(2,1)}, bf16[512,3072]{1,0:T(8,128)(2,1)S(1)}, u32[]{:S(2)}, u32[]{:S(2)}) collective-permute-start(bf16[512,3072]{1,0:T(8,128)(2,1)} %shard_map.47), channel_id=1, source_target_pairs={{0,0},{2,8},{4,16},{6,24},{8,2},{10,10},{12,18},{14,26},{16,4},{18... | collective-permute-start | bytes 9437192 | tf_op jit(solution)/shard_map/ppermute | solution.py:89
Sparse Core Ops, SparseCore 0:
  110.7 100.0 all-gather.7
  212.4 153.8 all-gather.5

commit v7 on v6

--- a/solution.py
+++ b/solution.py
@@ -85,12 +85,23 @@
     )
 
 
-def transposed(value, size):
+def transposed(value, size, flip=0):
     return lax.ppermute(
         value,
         ("layer", "row"),
-        [(a * size + b, b * size + a) for a in range(size) for b in range(size)],
-    )
+        [(a * size + b, (b ^ flip) * size + (a ^ flip)) for a in range(size) for b in range(size)],
+    )
+
+
+def split_transposed(value, size):
+    if size != 4:
+        return transposed(value, size)
+    half = value.shape[0] // 2
+    direct = transposed(value[:half], size)
+    across = [(i, i ^ 2) for i in range(4)]
+    detour = lax.ppermute(value[half:], "layer", across)
+    detour = lax.ppermute(transposed(detour, size, 2), "layer", across)
+    return jnp.concatenate([direct, detour], axis=0)
 
 
 def compressed_tile(green, green_pattern):
@@ -200,7 +211,7 @@
         (piece,) = block_sparse_product(
             rows_all[start : start + ROW_CHUNK], entry_blocks, entry_rows, entry_cols, tile_cols * BLK, 1
         )
-        pieces.append(transposed(piece, row_count))
+        pieces.append(split_transposed(piece, row_count))
     product = jnp.concatenate(pieces, axis=0)
     return product.reshape(ri_local, mu_local, tile_cols * BLK)
 

time: 755 us -> 788 us (1.044)
  starting transfers between devices: 18.9 us -> 91.2 us
  waiting for transfers between devices: 394 us -> 353 us
    ppermute x5 -> x11, starting transfers between devices: 18.9 us -> 91.1 us  [the longest x2 67.2 us: split_transposed(): detour = lax.ppermute(transposed(detour, size, 2), 'layer', across)]
    ppermute x5 -> x11, waiting for transfers between devices: 219 us -> 178 us  [the longest x7 97.9 us: transposed(): lax.ppermute(value, ('layer', 'row'), [(a * size + b, (b ^ flip) * size +...]
  transfers between devices with their start and end apart: 7 -> 13, of which waited for: 6 -> 8; matrix products, arithmetic and copies ran while one was open for 8% -> 8% of each run, Pallas kernels for 11% -> 11%
where the time goes in v7:
time: 788 us; the launch traced here: 786 us
  waiting for transfers between devices  353 us (45%)
  Pallas kernels  168 us (21%)
  local copies, waits for them, and re-layouts  108 us (14%)
  starting transfers between devices  91.2 us (12%)
  other arithmetic  45.3 us (6%)
  between operations  14.3 us (2%)
    pallas_call x2, Pallas kernels, block_sparse_product(): pl.pallas_call(kernel, grid_spec=grid_spec, out_shape=jax.ShapeDtypeStruc...  168 us
    all_gather x1, waiting for transfers between devices, per_device(): rows_all = lax.all_gather(own, 'layer', axis=1, tiled=True)  119 us
    ppermute x7, waiting for transfers between devices, transposed(): lax.ppermute(value, ('layer', 'row'), [(a * size + b, (b ^ flip) * size +...  97.9 us
    ppermute x2, starting transfers between devices, split_transposed(): detour = lax.ppermute(transposed(detour, size, 2), 'layer', across)  67.2 us
    ppermute x2, waiting for transfers between devices, split_transposed(): detour = lax.ppermute(value[half:], 'layer', across)  61.7 us
    all_gather x1, waiting for transfers between devices, per_device(): lax.all_gather(transposed(part, row_count), ('row', 'col'), axis=0)  56.1 us
    reshape x2, local copies, waits for them, and re-layouts, compressed_tile(): green.reshape(tile_rows, BLK, tile_cols, BLK)[block_row, :, block_col, :]  43.3 us
    ppermute x7, starting transfers between devices, transposed(): lax.ppermute(value, ('layer', 'row'), [(a * size + b, (b ^ flip) * size +...  21.7 us
  transfers between devices with their start and end apart: 13, of which 8 were waited for; matrix products, arithmetic and copies ran while one was open for 8% of the time, Pallas kernels for 11%

profile of v7, /device:TPU:16, one launch (start us, length us, event | category | flops | bytes accessed | tf_op | source)
XLA Modules:
  0.0 786.2 jit_solution(18165333148595757454)
XLA Ops:
  10.1 9.2 %scatter_custom_fusion = s32[48]{0:T(128)S(1)} fusion(s32[1152]{0:T(1024)S(1)} %fusion.13, s32[1152]{0:T(1024)S(1)} %broadcast.461, s32[]{:T(128)} %copy.29), kind=kCustom, calls=%fused_computation.87 | custom fusion | flops 1152 | bytes 196 | tf_op jit(solution)/shard_map/scatter-add | solution.py:111
  21.5 23.4 %reshape.289 = bf16[24,64,48,64]{3,2,1,0:T(8,128)(2,1)} reshape(bf16[1536,3072]{1,0:T(8,128)(2,1)} %param.8) | data formatting | bytes 18874368 | tf_op jit(solution)/shard_map/reshape | solution.py:115
  44.9 20.0 %copy.10 = bf16[24,64,48,64]{3,1,2,0:T(8,128)(2,1)} copy(bf16[24,64,48,64]{3,2,1,0:T(8,128)(2,1)} %reshape.289) | data formatting | bytes 18874368 | tf_op jit(solution)/shard_map/reshape | solution.py:115
  64.8 7.2 gather_fusion.3
  72.2 3.2 collective-permute-start.2
  75.4 34.3 %collective-permute-done.2 = bf16[48,64,64]{2,1,0:T(8,128)(2,1)S(1)} collective-permute-done((bf16[48,64,64]{2,1,0:T(8,128)(2,1)S(1)}, bf16[48,64,64]{2,1,0:T(8,128)(2,1)S(1)}, u32[]{:S(2)}, u32[]{:S(2)}) %collective-permute-start.2) | collective-permute-done | bytes 393248 | tf_op jit(solution)/shard_map/ppermute | solution.py:89
  110.9 5.9 multiply_bitcast_fusion
  117.5 6.2 collective-permute-start.1
  127.1 3.9 collective-permute-done
  131.2 5.8 all-reduce.2
  137.3 3.7 sort.19
  141.0 2.8 gather_fusion.1
  143.8 6.9 while.27
  151.3 2.8 gather_fusion.2
  154.7 56.1 %all-gather.8.cloned.1.call-done = bf16[384,64,64]{2,1,0:T(8,128)(2,1)} async-done(((bf16[48,64,64]{2,1,0:T(8,128)(2,1)}), bf16[384,64,64]{2,1,0:T(8,128)(2,1)}) %all-gather.8.cloned.1.call-update) | async-done | bytes 3145744 | tf_op jit(solution)/shard_map/all_gather | solution.py:198
  210.8 4.3 broadcast_select_fusion.3
  215.1 6.4 broadcast_select_fusion.5
  221.5 6.8 pad_maximum_fusion
  228.3 19.4 %gather_fusion.5 = bf16[384,128,128]{2,1,0:T(8,128)(2,1)} fusion(bf16[384,128,128]{2,1,0:T(8,128)(2,1)} %pad_maximum_fusion, s32[1024]{0:T(1024)S(1)} %pad_clamp_fusion.2), kind=kCustom, calls=%fused_computation.5 | custom fusion | bytes 25167360 | tf_op jit(solution)/shard_map/gather | solution.py:140
  247.7 118.6 %all-gather.6.cloned.1.call-done = bf16[1024,12288]{1,0:T(8,128)(2,1)} async-done(((bf16[1024,3072]{1,0:T(8,128)(2,1)}), bf16[1024,12288]{1,0:T(8,128)(2,1)}) %all-gather.6.cloned.1.call-update) | async-done | bytes 25165840 | tf_op jit(solution)/shard_map/all_gather | solution.py:203
  366.3 17.4 %fusion.27 = (bf16[512,12288]{1,0:T(8,128)(2,1)}, bf16[512,12288]{1,0:T(8,128)(2,1)}) fusion(bf16[1024,12288]{1,0:T(8,128)(2,1)} %all-gather.6.cloned.1.call-done), kind=kLoop, calls=%fused_computation.90 | loop fusion | bytes 50331648 | tf_op jit(solution)/shard_map/slice | solution.py:212
  383.7 84.1 %shard_map.46 = bf16[512,3072]{1,0:T(8,128)(2,1)} custom-call(s32[25]{0:T(128)} %convert_element_type.45.starts_ref, s32[384]{0:T(512)} %add_select_fusion.5.k_ref, bf16[512,12288]{1,0:T(8,128)(2,1)} %get-tuple-element.107.t_ref, bf16[384,128,128]{2,1,0:T(8,128)(2,1)} %gather_fusion.5), custom_call_target="tpu_custom_call" | custom-call | tf_op jit(solution)/shard_map/pallas_call | solution.py:175
  467.8 2.1 fusion.28
  470.5 84.3 %shard_map.47 = bf16[512,3072]{1,0:T(8,128)(2,1)} custom-call(s32[25]{0:T(128)} %convert_element_type.45.starts_ref, s32[384]{0:T(512)} %add_select_fusion.5.k_ref, bf16[512,12288]{1,0:T(8,128)(2,1)} %get-tuple-element.108.t_ref, bf16[384,128,128]{2,1,0:T(8,128)(2,1)} %gather_fusion.5), custom_call_target="tpu_custom_call" | custom-call | tf_op jit(solution)/shard_map/pallas_call | solution.py:175
  560.5 61.7 %collective-permute-done.8 = bf16[256,3072]{1,0:T(8,128)(2,1)S(1)} collective-permute-done((bf16[256,3072]{1,0:T(8,128)(2,1)S(1)}, bf16[256,3072]{1,0:T(8,128)(2,1)S(1)}, u32[]{:S(2)}, u32[]{:S(2)}) %collective-permute-start.8) | collective-permute-done | bytes 1572896 | tf_op jit(solution)/shard_map/ppermute | solution.py:102
  624.9 5.7 collective-permute-start.7
  630.6 33.9 %collective-permute-start.6 = (bf16[256,3072]{1,0:T(8,128)(2,1)S(1)}, bf16[256,3072]{1,0:T(8,128)(2,1)S(1)}, u32[]{:S(2)}, u32[]{:S(2)}) collective-permute-start(bf16[256,3072]{1,0:T(8,128)(2,1)S(1)} %collective-permute-done.5), channel_id=1, source_target_pairs={{0,16},{8,24},{16,0},{24,8},{1,17},{9,25},{17,1},{25,9},{2,18},{10... | collective-permute-start | bytes 4718600 | tf_op jit(solution)/shard_map/ppermute | solution.py:103
  664.6 33.3 %collective-permute-start.10 = (bf16[256,3072]{1,0:T(8,128)(2,1)S(1)}, bf16[256,3072]{1,0:T(8,128)(2,1)S(1)}, u32[]{:S(2)}, u32[]{:S(2)}) collective-permute-start(bf16[256,3072]{1,0:T(8,128)(2,1)S(1)} %collective-permute-done.9), channel_id=1, source_target_pairs={{0,16},{8,24},{16,0},{24,8},{1,17},{9,25},{17,1},{25,9},{2,18},{10... | collective-permute-start | bytes 4718600 | tf_op jit(solution)/shard_map/ppermute | solution.py:103
  697.9 26.0 %collective-permute-done.3 = bf16[256,3072]{1,0:T(8,128)(2,1)S(1)} collective-permute-done((bf16[256,3072]{1,0:T(8,128)(2,1)S(1)}, bf16[256,3072]{1,0:T(8,128)(2,1)S(1)}, u32[]{:S(2)}, u32[]{:S(2)}) %collective-permute-start.3) | collective-permute-done | bytes 1572896 | tf_op jit(solution)/shard_map/ppermute | solution.py:89
  723.9 33.7 %collective-permute-done.7 = bf16[256,3072]{1,0:T(8,128)(2,1)S(1)} collective-permute-done((bf16[256,3072]{1,0:T(8,128)(2,1)S(1)}, bf16[256,3072]{1,0:T(8,128)(2,1)S(1)}, u32[]{:S(2)}, u32[]{:S(2)}) %collective-permute-start.7) | collective-permute-done | bytes 1572896 | tf_op jit(solution)/shard_map/ppermute | solution.py:89
  757.6 18.8 %collective-permute-done.10 = bf16[256,3072]{1,0:T(8,128)(2,1)S(1)} collective-permute-done((bf16[256,3072]{1,0:T(8,128)(2,1)S(1)}, bf16[256,3072]{1,0:T(8,128)(2,1)S(1)}, u32[]{:S(2)}, u32[]{:S(2)}) %collective-permute-start.10) | collective-permute-done | bytes 1572896 | tf_op jit(solution)/shard_map/ppermute | solution.py:103
  776.4 3.0 maximum_bitcast_fusion
  (100 shorter events, 27.7 us)
Async XLA Ops:
  6.5 204.3 %all-gather.8.cloned.1.call-start = ((), (), s32[]{:S(2)}) async-start(), calls=%async_computation.1 | async-start | bytes 7077888 | tf_op jit(solution)/shard_map/all_gather | solution.py:198
  44.9 65.8 %copy-start.1 = (s32[8,48]{1,0:T(8,128)S(1)}, s32[8,48]{1,0:T(8,128)}, u32[]{:S(2)}) copy-start(s32[8,48]{1,0:T(8,128)} %param.7) | copy-start | bytes 4612
  72.2 37.5 %collective-permute-start.2 = (bf16[48,64,64]{2,1,0:T(8,128)(2,1)S(1)}, bf16[48,64,64]{2,1,0:T(8,128)(2,1)S(1)}, u32[]{:S(2)}, u32[]{:S(2)}) collective-permute-start(bf16[48,64,64]{2,1,0:T(8,128)(2,1)S(1)} %broadcast_multiply_fusion), channel_id=1, source_target_pairs={{0,0},{2,8},{4,16},{6,24},{8,2},{10,10},{12,18},{14,26},{16,4},{18... | collective-permute-start | bytes 1179656 | tf_op jit(solution)/shard_map/ppermute | solution.py:89
  109.7 0.9 copy-start
  110.6 255.7 %all-gather.6.cloned.1.call-start = ((), (), s32[]{:S(2)}) async-start(), calls=%async_computation | async-start | bytes 31457280 | tf_op jit(solution)/shard_map/all_gather | solution.py:203
  116.9 8.8 %copy-start.2 = (u32[32]{0:T(128)S(1)}, u32[32]{0:T(128)}, u32[]{:S(2)}) copy-start(u32[32]{0:T(128)} %constant.179) | copy-start | bytes 388
  117.5 9.4 %collective-permute-start.1 = (s32[48]{0:T(128)S(1)}, s32[48]{0:T(128)S(1)}, u32[]{:S(2)}, u32[]{:S(2)}) collective-permute-start(s32[48]{0:T(128)S(1)} %get-tuple-element.103), channel_id=1, source_target_pairs={{0,0},{2,8},{4,16},{6,24},{8,2},{10,10},{12,18},{14,26},{16,4},{18... | collective-permute-start | bytes 584 | tf_op jit(solution)/shard_map/ppermute | solution.py:89
  123.7 7.3 collective-permute-start
  469.9 88.5 %collective-permute-start.4 = (bf16[256,3072]{1,0:T(8,128)(2,1)S(1)}, bf16[256,3072]{1,0:T(8,128)(2,1)}, u32[]{:S(2)}, u32[]{:S(2)}) collective-permute-start(bf16[256,3072]{1,0:T(8,128)(2,1)S(1)} %get-tuple-element.114), channel_id=1, source_target_pairs={{0,16},{8,24},{16,0},{24,8},{1,17},{9,25},{17,1},{25,9},{2,18},{10... | collective-permute-start | bytes 4718600 | tf_op jit(solution)/shard_map/ppermute | solution.py:102
  556.9 65.3 %collective-permute-start.8 = (bf16[256,3072]{1,0:T(8,128)(2,1)S(1)}, bf16[256,3072]{1,0:T(8,128)(2,1)S(1)}, u32[]{:S(2)}, u32[]{:S(2)}) collective-permute-start(bf16[256,3072]{1,0:T(8,128)(2,1)S(1)} %get-tuple-element.116), channel_id=1, source_target_pairs={{0,16},{8,24},{16,0},{24,8},{1,17},{9,25},{17,1},{25,9},{2,18},{10... | collective-permute-start | bytes 4718600 | tf_op jit(solution)/shard_map/ppermute | solution.py:102
  558.4 72.2 %collective-permute-start.5 = (bf16[256,3072]{1,0:T(8,128)(2,1)}, bf16[256,3072]{1,0:T(8,128)(2,1)S(1)}, u32[]{:S(2)}, u32[]{:S(2)}) collective-permute-start(bf16[256,3072]{1,0:T(8,128)(2,1)} %collective-permute-done.4), channel_id=1, source_target_pairs={{0,20},{2,28},{4,4},{6,12},{8,22},{10,30},{12,6},{14,14},{16,16},{... | collective-permute-start | bytes 4718600 | tf_op jit(solution)/shard_map/ppermute | solution.py:89
  622.2 42.4 %collective-permute-start.9 = (bf16[256,3072]{1,0:T(8,128)(2,1)S(1)}, bf16[256,3072]{1,0:T(8,128)(2,1)S(1)}, u32[]{:S(2)}, u32[]{:S(2)}) collective-permute-start(bf16[256,3072]{1,0:T(8,128)(2,1)S(1)} %collective-permute-done.8), channel_id=1, source_target_pairs={{0,20},{2,28},{4,4},{6,12},{8,22},{10,30},{12,6},{14,14},{16,16},{... | collective-permute-start | bytes 4718600 | tf_op jit(solution)/shard_map/ppermute | solution.py:89
  622.9 100.9 %collective-permute-start.3 = (bf16[256,3072]{1,0:T(8,128)(2,1)S(1)}, bf16[256,3072]{1,0:T(8,128)(2,1)S(1)}, u32[]{:S(2)}, u32[]{:S(2)}) collective-permute-start(bf16[256,3072]{1,0:T(8,128)(2,1)S(1)} %get-tuple-element.113), channel_id=1, source_target_pairs={{0,0},{2,8},{4,16},{6,24},{8,2},{10,10},{12,18},{14,26},{16,4},{18... | collective-permute-start | bytes 4718600 | tf_op jit(solution)/shard_map/ppermute | solution.py:89
  624.9 132.7 %collective-permute-start.7 = (bf16[256,3072]{1,0:T(8,128)(2,1)S(1)}, bf16[256,3072]{1,0:T(8,128)(2,1)S(1)}, u32[]{:S(2)}, u32[]{:S(2)}) collective-permute-start(bf16[256,3072]{1,0:T(8,128)(2,1)S(1)} %get-tuple-element.115), channel_id=1, source_target_pairs={{0,0},{2,8},{4,16},{6,24},{8,2},{10,10},{12,18},{14,26},{16,4},{18... | collective-permute-start | bytes 4718600 | tf_op jit(solution)/shard_map/ppermute | solution.py:89
  630.6 127.0 %collective-permute-start.6 = (bf16[256,3072]{1,0:T(8,128)(2,1)S(1)}, bf16[256,3072]{1,0:T(8,128)(2,1)S(1)}, u32[]{:S(2)}, u32[]{:S(2)}) collective-permute-start(bf16[256,3072]{1,0:T(8,128)(2,1)S(1)} %collective-permute-done.5), channel_id=1, source_target_pairs={{0,16},{8,24},{16,0},{24,8},{1,17},{9,25},{17,1},{25,9},{2,18},{10... | collective-permute-start | bytes 4718600 | tf_op jit(solution)/shard_map/ppermute | solution.py:103
  664.6 111.8 %collective-permute-start.10 = (bf16[256,3072]{1,0:T(8,128)(2,1)S(1)}, bf16[256,3072]{1,0:T(8,128)(2,1)S(1)}, u32[]{:S(2)}, u32[]{:S(2)}) collective-permute-start(bf16[256,3072]{1,0:T(8,128)(2,1)S(1)} %collective-permute-done.9), channel_id=1, source_target_pairs={{0,16},{8,24},{16,0},{24,8},{1,17},{9,25},{17,1},{25,9},{2,18},{10... | collective-permute-start | bytes 4718600 | tf_op jit(solution)/shard_map/ppermute | solution.py:103
Sparse Core Ops, SparseCore 0:
  110.7 100.0 all-gather.7
  212.4 153.8 all-gather.5

commit v8 on v6

--- a/solution.py
+++ b/solution.py
@@ -93,6 +93,25 @@
     )
 
 
+def gathered_windows(green, window_rows, window_cols):
+    count = window_rows.shape[0]
+
+    def kernel(rows_ref, cols_ref, green_ref, out_ref):
+        out_ref[0] = green_ref[...]
+
+    grid_spec = pltpu.PrefetchScalarGridSpec(
+        num_scalar_prefetch=2,
+        grid=(count,),
+        in_specs=[pl.BlockSpec((BLK, LANE), lambda e, r, c: (r[e], c[e]))],
+        out_specs=pl.BlockSpec((1, BLK, LANE), lambda e, r, c: (e, 0, 0)),
+    )
+    return pl.pallas_call(
+        kernel,
+        grid_spec=grid_spec,
+        out_shape=jax.ShapeDtypeStruct((count, BLK, LANE), green.dtype),
+    )(window_rows.astype(jnp.int32), window_cols.astype(jnp.int32), green)
+
+
 def compressed_tile(green, green_pattern):
     tile_rows, tile_cols = green_pattern.shape
     cap = min(CAP, tile_rows * tile_cols)
@@ -101,7 +120,9 @@
     valid = jnp.arange(cap) < jnp.sum(flat != 0)
     block_row = spots // tile_cols
     block_col = spots % tile_cols
-    blocks = green.reshape(tile_rows, BLK, tile_cols, BLK)[block_row, :, block_col, :]
+    windows = gathered_windows(green, block_row, block_col // 2)
+    left = (block_col % 2 == 0)[:, None, None]
+    blocks = jnp.where(left, windows[:, :, :BLK], windows[:, :, BLK:])
     scale = jnp.where(valid, flat[spots], 0).astype(jnp.bfloat16)
     blocks = blocks * scale[:, None, None]
     return blocks, block_row, block_col

time: 755 us -> 726 us (0.962)
  local copies, waits for them, and re-layouts: 104 us -> 53 us
  Pallas kernels: 168 us -> 184 us
    reshape x2 -> x0, local copies, waits for them, and re-layouts: 43.3 us -> none  [compressed_tile(): green.reshape(tile_rows, BLK, tile_cols, BLK)[block_row, :, block_col, :]]
    pallas_call x0 -> x1, Pallas kernels: none -> 16.1 us  [gathered_windows(): pl.pallas_call(kernel, grid_spec=grid_spec, out_shape=jax.ShapeDtypeStruc...]
  transfers between devices with their start and end apart: 7 -> 7, of which waited for: 6 -> 6; matrix products, arithmetic and copies ran while one was open for 8% -> 9% of each run, Pallas kernels for 11% -> 12%
where the time goes in v8:
time: 726 us; the launch traced here: 721 us
  waiting for transfers between devices  393 us (54%)
  Pallas kernels  184 us (25%)
  local copies, waits for them, and re-layouts  53 us (7%)
  other arithmetic  48.5 us (7%)
  starting transfers between devices  21.3 us (3%)
  between operations  14.3 us (2%)
    ppermute x5, waiting for transfers between devices, transposed(): lax.ppermute(value, ('layer', 'row'), [(a * size + b, b * size + a) for a...  218 us
    pallas_call x2, Pallas kernels, block_sparse_product(): pl.pallas_call(kernel, grid_spec=grid_spec, out_shape=jax.ShapeDtypeStruc...  168 us
    all_gather x1, waiting for transfers between devices, per_device(): rows_all = lax.all_gather(own, 'layer', axis=1, tiled=True)  119 us
    all_gather x1, waiting for transfers between devices, per_device(): lax.all_gather(transposed(part, row_count), ('row', 'col'), axis=0)  56.2 us
    ppermute x5, starting transfers between devices, transposed(): lax.ppermute(value, ('layer', 'row'), [(a * size + b, b * size + a) for a...  21.2 us
    gather x1, local copies, waits for them, and re-layouts, block_sparse_product(): padded = padded_blocks(blocks, block_rows, block_cols)[order]  19.4 us
    slice x1, local copies, waits for them, and re-layouts, per_device(): rows_all[start:start + ROW_CHUNK]  17.4 us
    pallas_call x1, Pallas kernels, gathered_windows(): pl.pallas_call(kernel, grid_spec=grid_spec, out_shape=jax.ShapeDtypeStruc...  16.1 us
  transfers between devices with their start and end apart: 7, of which 6 were waited for; matrix products, arithmetic and copies ran while one was open for 9% of the time, Pallas kernels for 12%

profile of v8, /device:TPU:16, one launch (start us, length us, event | category | flops | bytes accessed | tf_op | source)
XLA Modules:
  0.0 720.9 jit_solution(8173736318327778424)
XLA Ops:
  7.2 1.3 fusion.21
  8.6 0.8 reshape.263
  10.1 9.2 %scatter_custom_fusion = s32[48]{0:T(128)S(1)} fusion(s32[1152]{0:T(1024)S(1)} %fusion.7, s32[1152]{0:T(1024)S(1)} %broadcast.377, s32[]{:T(128)} %copy.26), kind=kCustom, calls=%fused_computation.80 | custom fusion | flops 1152 | bytes 196 | tf_op jit(solution)/shard_map/scatter-add | solution.py:119
  22.0 0.8 gather_fusion.3
  23.4 16.1 %shard_map.46 = bf16[48,64,128]{2,1,0:T(8,128)(2,1)} custom-call(s32[48]{0:T(128)} %and_select_fusion.2.rows_ref, s32[48]{0:T(128)} %and_select_fusion.cols_ref, bf16[1536,3072]{1,0:T(8,128)(2,1)} %green_ref.1), custom_call_target="tpu_custom_call" | custom-call | tf_op jit(solution)/shard_map/pallas_call | solution.py:108
  39.6 1.8 fusion.4
  41.4 5.5 collective-permute-start.2
  46.9 33.0 %collective-permute-done.2 = bf16[48,64,64]{2,1,0:T(8,128)(2,1)S(1)} collective-permute-done((bf16[48,64,64]{2,1,0:T(8,128)(2,1)S(1)}, bf16[48,64,64]{2,1,0:T(8,128)(2,1)S(1)}, u32[]{:S(2)}, u32[]{:S(2)}) %collective-permute-start.2) | collective-permute-done | bytes 393248 | tf_op jit(solution)/shard_map/ppermute | solution.py:89
  79.9 0.9 copy-done
  81.2 5.9 multiply_bitcast_fusion
  87.1 6.2 collective-permute-start
  93.3 1.9 collective-permute-start.1
  96.7 3.9 collective-permute-done.1
  100.8 6.3 all-reduce.2
  107.1 3.7 sort.19
  110.9 2.8 gather_fusion.1
  113.7 6.9 while.27
  121.4 2.8 gather_fusion.2
  124.8 56.2 %all-gather.8.cloned.1.call-done = bf16[384,64,64]{2,1,0:T(8,128)(2,1)} async-done(((bf16[48,64,64]{2,1,0:T(8,128)(2,1)}), bf16[384,64,64]{2,1,0:T(8,128)(2,1)}) %all-gather.8.cloned.1.call-update) | async-done | bytes 3145744 | tf_op jit(solution)/shard_map/all_gather | solution.py:208
  180.9 4.2 broadcast_select_fusion.3
  185.2 6.4 broadcast_select_fusion.5
  191.6 6.8 pad_maximum_fusion
  198.4 19.4 %gather_fusion.4 = bf16[384,128,128]{2,1,0:T(8,128)(2,1)} fusion(bf16[384,128,128]{2,1,0:T(8,128)(2,1)} %pad_maximum_fusion, s32[1024]{0:T(1024)S(1)} %pad_clamp_fusion.2), kind=kCustom, calls=%fused_computation.4 | custom fusion | bytes 25167360 | tf_op jit(solution)/shard_map/gather | solution.py:150
  217.8 118.6 %all-gather.6.cloned.1.call-done = bf16[1024,12288]{1,0:T(8,128)(2,1)} async-done(((bf16[1024,3072]{1,0:T(8,128)(2,1)}), bf16[1024,12288]{1,0:T(8,128)(2,1)}) %all-gather.6.cloned.1.call-update) | async-done | bytes 25165840 | tf_op jit(solution)/shard_map/all_gather | solution.py:213
  336.4 17.4 %fusion.22 = (bf16[512,12288]{1,0:T(8,128)(2,1)}, bf16[512,12288]{1,0:T(8,128)(2,1)}) fusion(bf16[1024,12288]{1,0:T(8,128)(2,1)} %all-gather.6.cloned.1.call-done), kind=kLoop, calls=%fused_computation.83 | loop fusion | bytes 50331648 | tf_op jit(solution)/shard_map/slice | solution.py:222
  353.8 84.3 %shard_map.48 = bf16[512,3072]{1,0:T(8,128)(2,1)} custom-call(s32[25]{0:T(128)} %convert_element_type.45.starts_ref, s32[384]{0:T(512)} %add_select_fusion.3.k_ref, bf16[512,12288]{1,0:T(8,128)(2,1)} %get-tuple-element.108.t_ref, bf16[384,128,128]{2,1,0:T(8,128)(2,1)} %gather_fusion.4), custom_call_target="tpu_custom_call" | custom-call | tf_op jit(solution)/shard_map/pallas_call | solution.py:185
  438.0 2.2 collective-permute-start.4
  440.2 84.1 %shard_map.47 = bf16[512,3072]{1,0:T(8,128)(2,1)} custom-call(s32[25]{0:T(128)} %convert_element_type.45.starts_ref, s32[384]{0:T(512)} %add_select_fusion.3.k_ref, bf16[512,12288]{1,0:T(8,128)(2,1)} %get-tuple-element.107.t_ref, bf16[384,128,128]{2,1,0:T(8,128)(2,1)} %gather_fusion.4), custom_call_target="tpu_custom_call" | custom-call | tf_op jit(solution)/shard_map/pallas_call | solution.py:185
  524.3 5.4 collective-permute-start.3
  529.8 114.1 %collective-permute-done.4 = bf16[512,3072]{1,0:T(8,128)(2,1)S(1)} collective-permute-done((bf16[512,3072]{1,0:T(8,128)(2,1)}, bf16[512,3072]{1,0:T(8,128)(2,1)S(1)}, u32[]{:S(2)}, u32[]{:S(2)}) %collective-permute-start.4) | collective-permute-done | bytes 3145760 | tf_op jit(solution)/shard_map/ppermute | solution.py:89
  643.8 67.1 %collective-permute-done.3 = bf16[512,3072]{1,0:T(8,128)(2,1)S(1)} collective-permute-done((bf16[512,3072]{1,0:T(8,128)(2,1)}, bf16[512,3072]{1,0:T(8,128)(2,1)S(1)}, u32[]{:S(2)}, u32[]{:S(2)}) %collective-permute-start.3) | collective-permute-done | bytes 3145760 | tf_op jit(solution)/shard_map/ppermute | solution.py:89
  710.9 3.1 maximum_bitcast_fusion
  (87 shorter events, 14.3 us)
Async XLA Ops:
  6.5 174.4 %all-gather.8.cloned.1.call-start = ((), (), s32[]{:S(2)}) async-start(), calls=%async_computation.1 | async-start | bytes 7077888 | tf_op jit(solution)/shard_map/all_gather | solution.py:208
  23.4 57.4 %copy-start.1 = (s32[8,48]{1,0:T(8,128)S(1)}, s32[8,48]{1,0:T(8,128)}, u32[]{:S(2)}) copy-start(s32[8,48]{1,0:T(8,128)} %param.7) | copy-start | bytes 4612
  41.4 38.5 %collective-permute-start.2 = (bf16[48,64,64]{2,1,0:T(8,128)(2,1)S(1)}, bf16[48,64,64]{2,1,0:T(8,128)(2,1)S(1)}, u32[]{:S(2)}, u32[]{:S(2)}) collective-permute-start(bf16[48,64,64]{2,1,0:T(8,128)(2,1)S(1)} %fusion.4), channel_id=1, source_target_pairs={{0,0},{2,8},{4,16},{6,24},{8,2},{10,10},{12,18},{14,26},{16,4},{18... | collective-permute-start | bytes 1179656 | tf_op jit(solution)/shard_map/ppermute | solution.py:89
  79.9 0.9 copy-start
  80.8 255.6 %all-gather.6.cloned.1.call-start = ((), (), s32[]{:S(2)}) async-start(), calls=%async_computation | async-start | bytes 31457280 | tf_op jit(solution)/shard_map/all_gather | solution.py:213
  87.1 6.2 copy-start.2
  87.1 8.2 %copy-start.3 = (u32[32]{0:T(128)S(1)}, u32[32]{0:T(128)}, u32[]{:S(2)}) copy-start(u32[32]{0:T(128)} %constant.176) | copy-start | bytes 388
  87.1 9.4 %collective-permute-start = (s32[48]{0:T(128)S(1)}, s32[48]{0:T(128)S(1)}, u32[]{:S(2)}, u32[]{:S(2)}) collective-permute-start(s32[48]{0:T(128)S(1)} %get-tuple-element.103), channel_id=1, source_target_pairs={{0,0},{2,8},{4,16},{6,24},{8,2},{10,10},{12,18},{14,26},{16,4},{18... | collective-permute-start | bytes 584 | tf_op jit(solution)/shard_map/ppermute | solution.py:89
  93.3 7.3 %collective-permute-start.1 = (s32[48]{0:T(128)S(1)}, s32[48]{0:T(128)S(1)}, u32[]{:S(2)}, u32[]{:S(2)}) collective-permute-start(s32[48]{0:T(128)S(1)} %copy-done.2), channel_id=1, source_target_pairs={{0,0},{2,8},{4,16},{6,24},{8,2},{10,10},{12,18},{14,26},{16,4},{18... | collective-permute-start | bytes 584 | tf_op jit(solution)/shard_map/ppermute | solution.py:89
  438.0 205.8 %collective-permute-start.4 = (bf16[512,3072]{1,0:T(8,128)(2,1)}, bf16[512,3072]{1,0:T(8,128)(2,1)S(1)}, u32[]{:S(2)}, u32[]{:S(2)}) collective-permute-start(bf16[512,3072]{1,0:T(8,128)(2,1)} %shard_map.48), channel_id=1, source_target_pairs={{0,0},{2,8},{4,16},{6,24},{8,2},{10,10},{12,18},{14,26},{16,4},{18... | collective-permute-start | bytes 9437192 | tf_op jit(solution)/shard_map/ppermute | solution.py:89
  524.3 186.6 %collective-permute-start.3 = (bf16[512,3072]{1,0:T(8,128)(2,1)}, bf16[512,3072]{1,0:T(8,128)(2,1)S(1)}, u32[]{:S(2)}, u32[]{:S(2)}) collective-permute-start(bf16[512,3072]{1,0:T(8,128)(2,1)} %shard_map.47), channel_id=1, source_target_pairs={{0,0},{2,8},{4,16},{6,24},{8,2},{10,10},{12,18},{14,26},{16,4},{18... | collective-permute-start | bytes 9437192 | tf_op jit(solution)/shard_map/ppermute | solution.py:89
Sparse Core Ops, SparseCore 0:
  80.9 99.9 all-gather.7
  182.5 153.8 all-gather.5

commit v9 on v8

--- a/solution.py
+++ b/solution.py
@@ -153,19 +153,25 @@
         first = piece * piece_chunks
 
         def kernel(starts_ref, k_ref, t_ref, g_ref, o_ref, first=first):
+            def window(entry):
+                return t_ref[:, pl.ds(pl.multiple_of(k_ref[entry] * LANE, LANE), LANE)]
+
+            def one(entry, acc):
+                return acc + jnp.dot(window(entry), g_ref[entry], preferred_element_type=jnp.float32)
+
             for chunk in range(piece_chunks):
-                def body(entry, acc):
-                    k = pl.multiple_of(k_ref[entry] * LANE, LANE)
-                    return acc + jnp.dot(
-                        t_ref[:, pl.ds(k, LANE)], g_ref[entry], preferred_element_type=jnp.float32
-                    )
-
-                acc = lax.fori_loop(
-                    starts_ref[first + chunk],
-                    starts_ref[first + chunk + 1],
-                    body,
-                    jnp.zeros((row_total, LANE), jnp.float32),
-                )
+                begin = starts_ref[first + chunk]
+                end = starts_ref[first + chunk + 1]
+                pairs = (end - begin) // 2
+
+                def two(pair, acc, begin=begin):
+                    entry = begin + 2 * pair
+                    lhs = jnp.concatenate([window(entry), window(entry + 1)], axis=1)
+                    rhs = jnp.concatenate([g_ref[entry], g_ref[entry + 1]], axis=0)
+                    return acc + jnp.dot(lhs, rhs, preferred_element_type=jnp.float32)
+
+                acc = lax.fori_loop(0, pairs, two, jnp.zeros((row_total, LANE), jnp.float32))
+                acc = lax.fori_loop(begin + 2 * pairs, end, one, acc)
                 o_ref[:, chunk * LANE : (chunk + 1) * LANE] = acc.astype(o_ref.dtype)
 
         grid_spec = pltpu.PrefetchScalarGridSpec(

time: 726 us -> 703 us (0.968)
  Pallas kernels: 184 us -> 138 us
  waiting for transfers between devices: 393 us -> 416 us
    pallas_call x2, Pallas kernels: 168 us -> 121 us  [block_sparse_product(): pl.pallas_call(kernel, grid_spec=grid_spec, out_shape=jax.ShapeDtypeStruc...]
    ppermute x5, waiting for transfers between devices: 218 us -> 242 us  [transposed(): lax.ppermute(value, ('layer', 'row'), [(a * size + b, b * size + a) for a...]
  transfers between devices with their start and end apart: 7 -> 7, of which waited for: 6 -> 6; matrix products, arithmetic and copies ran while one was open for 9% -> 9% of each run, Pallas kernels for 12% -> 9%
where the time goes in v9:
time: 703 us; the launch traced here: 697 us
  waiting for transfers between devices  416 us (59%)
  Pallas kernels  138 us (20%)
  local copies, waits for them, and re-layouts  53 us (8%)
  other arithmetic  48.5 us (7%)
  starting transfers between devices  19.6 us (3%)
  between operations  14.3 us (2%)
  blocking collectives  7.23 us (1%)
    ppermute x5, waiting for transfers between devices, transposed(): lax.ppermute(value, ('layer', 'row'), [(a * size + b, b * size + a) for a...  242 us
    pallas_call x2, Pallas kernels, block_sparse_product(): pl.pallas_call(kernel, grid_spec=grid_spec, out_shape=jax.ShapeDtypeStruc...  121 us
    all_gather x1, waiting for transfers between devices, per_device(): rows_all = lax.all_gather(own, 'layer', axis=1, tiled=True)  119 us
    all_gather x1, waiting for transfers between devices, per_device(): lax.all_gather(transposed(part, row_count), ('row', 'col'), axis=0)  56.2 us
    ppermute x5, starting transfers between devices, transposed(): lax.ppermute(value, ('layer', 'row'), [(a * size + b, b * size + a) for a...  19.5 us
    gather x1, local copies, waits for them, and re-layouts, block_sparse_product(): padded = padded_blocks(blocks, block_rows, block_cols)[order]  19.4 us
    slice x1, local copies, waits for them, and re-layouts, per_device(): rows_all[start:start + ROW_CHUNK]  17.4 us
    pallas_call x1, Pallas kernels, gathered_windows(): pl.pallas_call(kernel, grid_spec=grid_spec, out_shape=jax.ShapeDtypeStruc...  17.1 us
  transfers between devices with their start and end apart: 7, of which 6 were waited for; matrix products, arithmetic and copies ran while one was open for 9% of the time, Pallas kernels for 9%

profile of v9, /device:TPU:16, one launch (start us, length us, event | category | flops | bytes accessed | tf_op | source)
XLA Modules:
  0.0 696.9 jit_solution(8277307545273465678)
XLA Ops:
  7.2 1.3 fusion.21
  8.6 0.8 reshape.263
  10.1 9.2 %scatter_custom_fusion = s32[48]{0:T(128)S(1)} fusion(s32[1152]{0:T(1024)S(1)} %fusion.7, s32[1152]{0:T(1024)S(1)} %broadcast.377, s32[]{:T(128)} %copy.26), kind=kCustom, calls=%fused_computation.80 | custom fusion | flops 1152 | bytes 196 | tf_op jit(solution)/shard_map/scatter-add | solution.py:119
  22.0 0.8 gather_fusion.3
  23.4 17.1 %shard_map.46 = bf16[48,64,128]{2,1,0:T(8,128)(2,1)} custom-call(s32[48]{0:T(128)} %and_select_fusion.2.rows_ref, s32[48]{0:T(128)} %and_select_fusion.cols_ref, bf16[1536,3072]{1,0:T(8,128)(2,1)} %green_ref.1), custom_call_target="tpu_custom_call" | custom-call | tf_op jit(solution)/shard_map/pallas_call | solution.py:108
  40.5 1.8 fusion.4
  42.3 3.8 collective-permute-start.2
  46.2 32.7 %collective-permute-done.2 = bf16[48,64,64]{2,1,0:T(8,128)(2,1)S(1)} collective-permute-done((bf16[48,64,64]{2,1,0:T(8,128)(2,1)S(1)}, bf16[48,64,64]{2,1,0:T(8,128)(2,1)S(1)}, u32[]{:S(2)}, u32[]{:S(2)}) %collective-permute-start.2) | collective-permute-done | bytes 393248 | tf_op jit(solution)/shard_map/ppermute | solution.py:89
  78.9 0.9 copy-done
  80.1 5.9 multiply_bitcast_fusion
  86.1 6.2 collective-permute-start
  92.3 1.9 collective-permute-start.1
  95.7 3.8 collective-permute-done.1
  99.7 7.2 %all-reduce.2 = (s32[384]{0:T(512)S(1)}, s32[384]{0:T(512)S(1)}) all-reduce(s32[384]{0:T(512)S(1)} %dynamic-update-slice, s32[384]{0:T(512)S(1)} %dynamic-update-slice.1), channel_id=2, replica_groups=mesh['layer'=4,'row'=4,'col'=2] {'row','col'}, use_global_device_ids=true, to_apply=%add | all-reduce | flops 768 | bytes 6144
  106.9 3.7 sort.19
  110.7 2.8 gather_fusion.1
  113.5 6.9 while.27
  121.2 2.8 gather_fusion.2
  124.6 56.2 %all-gather.8.cloned.1.call-done = bf16[384,64,64]{2,1,0:T(8,128)(2,1)} async-done(((bf16[48,64,64]{2,1,0:T(8,128)(2,1)}), bf16[384,64,64]{2,1,0:T(8,128)(2,1)}) %all-gather.8.cloned.1.call-update) | async-done | bytes 3145744 | tf_op jit(solution)/shard_map/all_gather | solution.py:214
  180.8 4.2 broadcast_select_fusion.3
  185.0 6.4 broadcast_select_fusion.5
  191.5 6.8 pad_maximum_fusion
  198.3 19.4 %gather_fusion.4 = bf16[384,128,128]{2,1,0:T(8,128)(2,1)} fusion(bf16[384,128,128]{2,1,0:T(8,128)(2,1)} %pad_maximum_fusion, s32[1024]{0:T(1024)S(1)} %pad_clamp_fusion.2), kind=kCustom, calls=%fused_computation.4 | custom fusion | bytes 25167360 | tf_op jit(solution)/shard_map/gather | solution.py:150
  217.7 118.6 %all-gather.6.cloned.1.call-done = bf16[1024,12288]{1,0:T(8,128)(2,1)} async-done(((bf16[1024,3072]{1,0:T(8,128)(2,1)}), bf16[1024,12288]{1,0:T(8,128)(2,1)}) %all-gather.6.cloned.1.call-update) | async-done | bytes 25165840 | tf_op jit(solution)/shard_map/all_gather | solution.py:219
  336.3 17.4 %fusion.22 = (bf16[512,12288]{1,0:T(8,128)(2,1)}, bf16[512,12288]{1,0:T(8,128)(2,1)}) fusion(bf16[1024,12288]{1,0:T(8,128)(2,1)} %all-gather.6.cloned.1.call-done), kind=kLoop, calls=%fused_computation.83 | loop fusion | bytes 50331648 | tf_op jit(solution)/shard_map/slice | solution.py:228
  353.6 60.2 %shard_map.48 = bf16[512,3072]{1,0:T(8,128)(2,1)} custom-call(s32[25]{0:T(128)} %convert_element_type.45.starts_ref, s32[384]{0:T(512)} %add_select_fusion.3.k_ref, bf16[512,12288]{1,0:T(8,128)(2,1)} %get-tuple-element.108.t_ref, bf16[384,128,128]{2,1,0:T(8,128)(2,1)} %gather_fusion.4), custom_call_target="tpu_custom_call" | custom-call | tf_op jit(solution)/shard_map/pallas_call | solution.py:191
  413.9 2.2 collective-permute-start.4
  416.1 60.3 %shard_map.47 = bf16[512,3072]{1,0:T(8,128)(2,1)} custom-call(s32[25]{0:T(128)} %convert_element_type.45.starts_ref, s32[384]{0:T(512)} %add_select_fusion.3.k_ref, bf16[512,12288]{1,0:T(8,128)(2,1)} %get-tuple-element.107.t_ref, bf16[384,128,128]{2,1,0:T(8,128)(2,1)} %gather_fusion.4), custom_call_target="tpu_custom_call" | custom-call | tf_op jit(solution)/shard_map/pallas_call | solution.py:191
  476.3 5.4 collective-permute-start.3
  481.8 137.9 %collective-permute-done.4 = bf16[512,3072]{1,0:T(8,128)(2,1)S(1)} collective-permute-done((bf16[512,3072]{1,0:T(8,128)(2,1)}, bf16[512,3072]{1,0:T(8,128)(2,1)S(1)}, u32[]{:S(2)}, u32[]{:S(2)}) %collective-permute-start.4) | collective-permute-done | bytes 3145760 | tf_op jit(solution)/shard_map/ppermute | solution.py:89
  619.7 67.3 %collective-permute-done.3 = bf16[512,3072]{1,0:T(8,128)(2,1)S(1)} collective-permute-done((bf16[512,3072]{1,0:T(8,128)(2,1)}, bf16[512,3072]{1,0:T(8,128)(2,1)S(1)}, u32[]{:S(2)}, u32[]{:S(2)}) %collective-permute-start.3) | collective-permute-done | bytes 3145760 | tf_op jit(solution)/shard_map/ppermute | solution.py:89
  686.9 3.1 maximum_bitcast_fusion
  (87 shorter events, 14.3 us)
Async XLA Ops:
  6.5 174.3 %all-gather.8.cloned.1.call-start = ((), (), s32[]{:S(2)}) async-start(), calls=%async_computation.1 | async-start | bytes 7077888 | tf_op jit(solution)/shard_map/all_gather | solution.py:214
  23.4 56.4 %copy-start.1 = (s32[8,48]{1,0:T(8,128)S(1)}, s32[8,48]{1,0:T(8,128)}, u32[]{:S(2)}) copy-start(s32[8,48]{1,0:T(8,128)} %param.7) | copy-start | bytes 4612
  42.3 36.5 %collective-permute-start.2 = (bf16[48,64,64]{2,1,0:T(8,128)(2,1)S(1)}, bf16[48,64,64]{2,1,0:T(8,128)(2,1)S(1)}, u32[]{:S(2)}, u32[]{:S(2)}) collective-permute-start(bf16[48,64,64]{2,1,0:T(8,128)(2,1)S(1)} %fusion.4), channel_id=1, source_target_pairs={{0,0},{2,8},{4,16},{6,24},{8,2},{10,10},{12,18},{14,26},{16,4},{18... | collective-permute-start | bytes 1179656 | tf_op jit(solution)/shard_map/ppermute | solution.py:89
  78.9 0.9 copy-start
  79.8 256.5 %all-gather.6.cloned.1.call-start = ((), (), s32[]{:S(2)}) async-start(), calls=%async_computation | async-start | bytes 31457280 | tf_op jit(solution)/shard_map/all_gather | solution.py:219
  86.0 6.2 copy-start.2
  86.0 8.2 %copy-start.3 = (u32[32]{0:T(128)S(1)}, u32[32]{0:T(128)}, u32[]{:S(2)}) copy-start(u32[32]{0:T(128)} %constant.176) | copy-start | bytes 388
  86.1 9.4 %collective-permute-start = (s32[48]{0:T(128)S(1)}, s32[48]{0:T(128)S(1)}, u32[]{:S(2)}, u32[]{:S(2)}) collective-permute-start(s32[48]{0:T(128)S(1)} %get-tuple-element.103), channel_id=1, source_target_pairs={{0,0},{2,8},{4,16},{6,24},{8,2},{10,10},{12,18},{14,26},{16,4},{18... | collective-permute-start | bytes 584 | tf_op jit(solution)/shard_map/ppermute | solution.py:89
  92.3 7.2 %collective-permute-start.1 = (s32[48]{0:T(128)S(1)}, s32[48]{0:T(128)S(1)}, u32[]{:S(2)}, u32[]{:S(2)}) collective-permute-start(s32[48]{0:T(128)S(1)} %copy-done.2), channel_id=1, source_target_pairs={{0,0},{2,8},{4,16},{6,24},{8,2},{10,10},{12,18},{14,26},{16,4},{18... | collective-permute-start | bytes 584 | tf_op jit(solution)/shard_map/ppermute | solution.py:89
  413.9 205.8 %collective-permute-start.4 = (bf16[512,3072]{1,0:T(8,128)(2,1)}, bf16[512,3072]{1,0:T(8,128)(2,1)S(1)}, u32[]{:S(2)}, u32[]{:S(2)}) collective-permute-start(bf16[512,3072]{1,0:T(8,128)(2,1)} %shard_map.48), channel_id=1, source_target_pairs={{0,0},{2,8},{4,16},{6,24},{8,2},{10,10},{12,18},{14,26},{16,4},{18... | collective-permute-start | bytes 9437192 | tf_op jit(solution)/shard_map/ppermute | solution.py:89
  476.3 210.6 %collective-permute-start.3 = (bf16[512,3072]{1,0:T(8,128)(2,1)}, bf16[512,3072]{1,0:T(8,128)(2,1)S(1)}, u32[]{:S(2)}, u32[]{:S(2)}) collective-permute-start(bf16[512,3072]{1,0:T(8,128)(2,1)} %shard_map.47), channel_id=1, source_target_pairs={{0,0},{2,8},{4,16},{6,24},{8,2},{10,10},{12,18},{14,26},{16,4},{18... | collective-permute-start | bytes 9437192 | tf_op jit(solution)/shard_map/ppermute | solution.py:89
Sparse Core Ops, SparseCore 0:
  79.9 100.8 all-gather.7
  182.4 153.8 all-gather.5

commit v10 on v9

--- a/solution.py
+++ b/solution.py
@@ -216,7 +216,6 @@
     )
     band_count = blocks.shape[0]
     band = jnp.arange(band_count)[:, None]
-    rows_all = lax.all_gather(own, "layer", axis=1, tiled=True)
     position = band // col_count
     entry_rows = (position * col_count + band % col_count) * tile_rows + block_row
     entry_rows = entry_rows.reshape(-1)
@@ -224,8 +223,9 @@
     entry_blocks = blocks.reshape(-1, BLK, BLK)
     pieces = []
     for start in range(0, ri_local * mu_local, ROW_CHUNK):
+        rows = lax.all_gather(own[start : start + ROW_CHUNK], "layer", axis=1, tiled=True)
         (piece,) = block_sparse_product(
-            rows_all[start : start + ROW_CHUNK], entry_blocks, entry_rows, entry_cols, tile_cols * BLK, 1
+            rows, entry_blocks, entry_rows, entry_cols, tile_cols * BLK, 1
         )
         pieces.append(transposed(piece, row_count))
     product = jnp.concatenate(pieces, axis=0)

time: 703 us -> 614 us (0.87)
  waiting for transfers between devices: 416 us -> 351 us
  local copies, waits for them, and re-layouts: 53 us -> 35.4 us
    all_gather x1 -> x2, waiting for transfers between devices: 119 us -> 85.4 us  [per_device(): lax.all_gather(own[start:start + ROW_CHUNK], 'layer', axis=1, tiled=True)]
    ppermute x5, waiting for transfers between devices: 242 us -> 209 us  [transposed(): lax.ppermute(value, ('layer', 'row'), [(a * size + b, b * size + a) for a...]
    slice x2, local copies, waits for them, and re-layouts: 17.5 us -> 3.17 us  [the longest x1 3.1 us: per_device(): own[start:start + ROW_CHUNK]]
  transfers between devices with their start and end apart: 7 -> 8, of which waited for: 6 -> 7; matrix products, arithmetic and copies ran while one was open for 9% -> 10% of each run, Pallas kernels for 9% -> 20%
where the time goes in v10:
time: 614 us; the launch traced here: 607 us
  waiting for transfers between devices  351 us (57%)
  Pallas kernels  138 us (22%)
  other arithmetic  45.6 us (7%)
  local copies, waits for them, and re-layouts  35.4 us (6%)
  starting transfers between devices  16.9 us (3%)
  between operations  14 us (2%)
    ppermute x5, waiting for transfers between devices, transposed(): lax.ppermute(value, ('layer', 'row'), [(a * size + b, b * size + a) for a...  209 us
    pallas_call x2, Pallas kernels, block_sparse_product(): pl.pallas_call(kernel, grid_spec=grid_spec, out_shape=jax.ShapeDtypeStruc...  121 us
    all_gather x2, waiting for transfers between devices, per_device(): lax.all_gather(own[start:start + ROW_CHUNK], 'layer', axis=1, tiled=True)  85.4 us
    all_gather x1, waiting for transfers between devices, per_device(): lax.all_gather(transposed(part, row_count), ('row', 'col'), axis=0)  55.8 us
    pallas_call x1, Pallas kernels, gathered_windows(): pl.pallas_call(kernel, grid_spec=grid_spec, out_shape=jax.ShapeDtypeStruc...  17.6 us
    ppermute x5, starting transfers between devices, transposed(): lax.ppermute(value, ('layer', 'row'), [(a * size + b, b * size + a) for a...  16.8 us
    gather x1, local copies, waits for them, and re-layouts, block_sparse_product(): padded = padded_blocks(blocks, block_rows, block_cols)[order]  16 us
  transfers between devices with their start and end apart: 8, of which 7 were waited for; matrix products, arithmetic and copies ran while one was open for 10% of the time, Pallas kernels for 20%

profile of v10, /device:TPU:16, one launch (start us, length us, event | category | flops | bytes accessed | tf_op | source)
XLA Modules:
  0.0 607.2 jit_solution(13770930723528596841)
XLA Ops:
  7.2 1.3 fusion.21
  8.6 0.8 reshape.262
  10.1 9.2 %scatter_custom_fusion = s32[48]{0:T(128)S(1)} fusion(s32[1152]{0:T(1024)S(1)} %fusion.7, s32[1152]{0:T(1024)S(1)} %broadcast.377, s32[]{:T(128)} %copy.26), kind=kCustom, calls=%fused_computation.82 | custom fusion | flops 1152 | bytes 196 | tf_op jit(solution)/shard_map/scatter-add | solution.py:119
  23.4 17.6 %shard_map.46 = bf16[48,64,128]{2,1,0:T(8,128)(2,1)} custom-call(s32[48]{0:T(128)} %and_select_fusion.2.rows_ref, s32[48]{0:T(128)} %and_select_fusion.cols_ref, bf16[1536,3072]{1,0:T(8,128)(2,1)} %green_ref.1), custom_call_target="tpu_custom_call" | custom-call | tf_op jit(solution)/shard_map/pallas_call | solution.py:108
  41.1 1.8 fusion.4
  42.9 4.9 collective-permute-start.2
  47.7 32.6 %collective-permute-done.2 = bf16[48,64,64]{2,1,0:T(8,128)(2,1)S(1)} collective-permute-done((bf16[48,64,64]{2,1,0:T(8,128)(2,1)S(1)}, bf16[48,64,64]{2,1,0:T(8,128)(2,1)S(1)}, u32[]{:S(2)}, u32[]{:S(2)}) %collective-permute-start.2) | collective-permute-done | bytes 393248 | tf_op jit(solution)/shard_map/ppermute | solution.py:89
  80.3 0.9 copy-done
  81.6 3.2 broadcast_multiply_fusion
  84.8 3.1 slice_bitcast_fusion.1
  88.7 6.2 %collective-permute-start.1 = (s32[48]{0:T(128)S(1)}, s32[48]{0:T(128)S(1)}, u32[]{:S(2)}, u32[]{:S(2)}) collective-permute-start(s32[48]{0:T(128)S(1)} %copy-done.2), channel_id=1, source_target_pairs={{0,0},{2,8},{4,16},{6,24},{8,2},{10,10},{12,18},{14,26},{16,4},{18... | collective-permute-start | bytes 584 | tf_op jit(solution)/shard_map/ppermute | solution.py:89
  94.9 1.9 collective-permute-start
  98.3 3.8 collective-permute-done
  102.3 5.7 all-reduce.2
  108.2 3.7 sort.19
  112.0 2.8 gather_fusion.1
  114.8 6.9 %while.27 = (s32[]{:T(128)}, u32[25]{0:T(128)S(1)}, u32[25]{0:T(128)S(1)}, s32[384]{0:T(512)S(1)}, s32[]{:T(128)}, /*index=5*/s32[]{:T(128)}, s32[]{}) while((s32[]{:T(128)}, u32[25]{0:T(128)S(1)}, u32[25]{0:T(128)S(1)}, s32[384]{0:T(512)S(1)}, s32[]{:T(128)}, /*index=5*/s32[]{:T(128)}, s32[]{}) %tuple.39), condition=%wide.region_7.8_spmd.clone, body=%wide.region_6.7_spmd.clone.sunk | while | flops 1353 | bytes 5396 | solution.py:148
  122.2 2.8 gather_fusion.2
  125.6 55.8 %all-gather.11.cloned.1.call-done = bf16[384,64,64]{2,1,0:T(8,128)(2,1)} async-done(((bf16[48,64,64]{2,1,0:T(8,128)(2,1)}), bf16[384,64,64]{2,1,0:T(8,128)(2,1)}) %all-gather.11.cloned.1.call-update) | async-done | bytes 3145744 | tf_op jit(solution)/shard_map/all_gather | solution.py:214
  181.3 4.3 broadcast_select_fusion.3
  185.6 6.4 %broadcast_select_fusion.5 = (bf16[384,64,128]{2,1,0:T(8,128)(2,1)S(1)}, bf16[384,64,128]{2,1,0:T(8,128)(2,1)S(1)}) fusion(pred[384]{0:T(512)(128)(4,1)S(1)} %fusion.10, bf16[384,64,64]{2,1,0:T(8,128)(2,1)S(1)} %get-tuple-element.110, bf16[384,64,64]{2,1,0:T(8,128)(2,1)S(1)} %get-tuple-element.109), kind=kLoop, calls=%fused_computation.20 | loop fusion | flops 18874368 | bytes 18874752 | tf_op jit(solution)/shard_map/jit(_where)/select_n | solution.py:137
  192.0 6.6 %pad_maximum_fusion = bf16[384,128,128]{2,1,0:T(8,128)(2,1)} fusion(bf16[384,64,128]{2,1,0:T(8,128)(2,1)S(1)} %get-tuple-element.108, bf16[384,64,128]{2,1,0:T(8,128)(2,1)S(1)} %get-tuple-element.107), kind=kLoop, calls=%fused_computation.14 | loop fusion | flops 25165824 | bytes 25165824 | tf_op jit(solution)/shard_map/concatenate | solution.py:137
  198.6 16.0 %gather_fusion.4 = bf16[384,128,128]{2,1,0:T(8,128)(2,1)} fusion(bf16[384,128,128]{2,1,0:T(8,128)(2,1)} %pad_maximum_fusion, s32[1024]{0:T(1024)S(1)} %pad_clamp_fusion.2), kind=kCustom, calls=%fused_computation.4 | custom fusion | bytes 25167360 | tf_op jit(solution)/shard_map/gather | solution.py:150
  214.7 49.5 %all-gather.7.cloned.1.call-done.t_ref = bf16[512,12288]{1,0:T(8,128)(2,1)} async-done(((bf16[512,3072]{1,0:T(8,128)(2,1)}), bf16[512,12288]{1,0:T(8,128)(2,1)}) %all-gather.7.cloned.1.call-update) | async-done | bytes 12582928 | tf_op jit(solution)/shard_map/all_gather | solution.py:226
  264.1 60.6 %shard_map.47 = bf16[512,3072]{1,0:T(8,128)(2,1)} custom-call(s32[25]{0:T(128)} %convert_element_type.45.starts_ref, s32[384]{0:T(512)} %add_select_fusion.3.k_ref, bf16[512,12288]{1,0:T(8,128)(2,1)} %all-gather.7.cloned.1.call-done.t_ref, bf16[384,128,128]{2,1,0:T(8,128)(2,1)} %gather_fusion.4), custom_call_target="tpu_custom_call" | custom-call | tf_op jit(solution)/shard_map/pallas_call | solution.py:191
  324.7 1.9 collective-permute-start.3
  326.6 35.9 %all-gather.9.cloned.1.call-done.t_ref = bf16[512,12288]{1,0:T(8,128)(2,1)} async-done(((bf16[512,3072]{1,0:T(8,128)(2,1)}), bf16[512,12288]{1,0:T(8,128)(2,1)}) %all-gather.9.cloned.1.call-update) | async-done | bytes 12582928 | tf_op jit(solution)/shard_map/all_gather | solution.py:226
  362.5 60.1 %shard_map.48 = bf16[512,3072]{1,0:T(8,128)(2,1)} custom-call(s32[25]{0:T(128)} %convert_element_type.45.starts_ref, s32[384]{0:T(512)} %add_select_fusion.3.k_ref, bf16[512,12288]{1,0:T(8,128)(2,1)} %all-gather.9.cloned.1.call-done.t_ref, bf16[384,128,128]{2,1,0:T(8,128)(2,1)} %gather_fusion.4), custom_call_target="tpu_custom_call" | custom-call | tf_op jit(solution)/shard_map/pallas_call | solution.py:191
  422.6 1.9 collective-permute-start.4
  424.6 105.5 %collective-permute-done.3 = bf16[512,3072]{1,0:T(8,128)(2,1)S(1)} collective-permute-done((bf16[512,3072]{1,0:T(8,128)(2,1)}, bf16[512,3072]{1,0:T(8,128)(2,1)S(1)}, u32[]{:S(2)}, u32[]{:S(2)}) %collective-permute-start.3) | collective-permute-done | bytes 3145760 | tf_op jit(solution)/shard_map/ppermute | solution.py:89
  530.1 67.4 %collective-permute-done.4 = bf16[512,3072]{1,0:T(8,128)(2,1)S(1)} collective-permute-done((bf16[512,3072]{1,0:T(8,128)(2,1)}, bf16[512,3072]{1,0:T(8,128)(2,1)S(1)}, u32[]{:S(2)}, u32[]{:S(2)}) %collective-permute-start.4) | collective-permute-done | bytes 3145760 | tf_op jit(solution)/shard_map/ppermute | solution.py:89
  597.5 3.1 maximum_bitcast_fusion
  (90 shorter events, 15.7 us)
Async XLA Ops:
  6.5 174.8 %all-gather.11.cloned.1.call-start = ((), (), s32[]{:S(2)}) async-start(), calls=%async_computation.2 | async-start | bytes 7077888 | tf_op jit(solution)/shard_map/all_gather | solution.py:214
  23.4 57.9 %copy-start.1 = (s32[8,48]{1,0:T(8,128)S(1)}, s32[8,48]{1,0:T(8,128)}, u32[]{:S(2)}) copy-start(s32[8,48]{1,0:T(8,128)} %param.7) | copy-start | bytes 4612
  42.9 37.5 %collective-permute-start.2 = (bf16[48,64,64]{2,1,0:T(8,128)(2,1)S(1)}, bf16[48,64,64]{2,1,0:T(8,128)(2,1)S(1)}, u32[]{:S(2)}, u32[]{:S(2)}) collective-permute-start(bf16[48,64,64]{2,1,0:T(8,128)(2,1)S(1)} %fusion.4), channel_id=1, source_target_pairs={{0,0},{2,8},{4,16},{6,24},{8,2},{10,10},{12,18},{14,26},{16,4},{18... | collective-permute-start | bytes 1179656 | tf_op jit(solution)/shard_map/ppermute | solution.py:89
  80.3 0.9 copy-start
  81.2 182.9 %all-gather.7.cloned.1.call-start = ((), (), s32[]{:S(2)}) async-start(), calls=%async_computation | async-start | bytes 15728640 | tf_op jit(solution)/shard_map/all_gather | solution.py:226
  87.9 0.8 copy-start.2
  87.9 8.9 %copy-start.3 = (u32[32]{0:T(128)S(1)}, u32[32]{0:T(128)}, u32[]{:S(2)}) copy-start(u32[32]{0:T(128)} %constant.176) | copy-start | bytes 388
  87.9 274.6 %all-gather.9.cloned.1.call-start = ((), (), s32[]{:S(2)}) async-start(), calls=%async_computation.1 | async-start | bytes 15728640 | tf_op jit(solution)/shard_map/all_gather | solution.py:226
  88.7 9.4 %collective-permute-start.1 = (s32[48]{0:T(128)S(1)}, s32[48]{0:T(128)S(1)}, u32[]{:S(2)}, u32[]{:S(2)}) collective-permute-start(s32[48]{0:T(128)S(1)} %copy-done.2), channel_id=1, source_target_pairs={{0,0},{2,8},{4,16},{6,24},{8,2},{10,10},{12,18},{14,26},{16,4},{18... | collective-permute-start | bytes 584 | tf_op jit(solution)/shard_map/ppermute | solution.py:89
  94.9 7.2 %collective-permute-start = (s32[48]{0:T(128)S(1)}, s32[48]{0:T(128)S(1)}, u32[]{:S(2)}, u32[]{:S(2)}) collective-permute-start(s32[48]{0:T(128)S(1)} %get-tuple-element.103), channel_id=1, source_target_pairs={{0,0},{2,8},{4,16},{6,24},{8,2},{10,10},{12,18},{14,26},{16,4},{18... | collective-permute-start | bytes 584 | tf_op jit(solution)/shard_map/ppermute | solution.py:89
  324.7 205.4 %collective-permute-start.3 = (bf16[512,3072]{1,0:T(8,128)(2,1)}, bf16[512,3072]{1,0:T(8,128)(2,1)S(1)}, u32[]{:S(2)}, u32[]{:S(2)}) collective-permute-start(bf16[512,3072]{1,0:T(8,128)(2,1)} %shard_map.47), channel_id=1, source_target_pairs={{0,0},{2,8},{4,16},{6,24},{8,2},{10,10},{12,18},{14,26},{16,4},{18... | collective-permute-start | bytes 9437192 | tf_op jit(solution)/shard_map/ppermute | solution.py:89
  422.6 174.8 %collective-permute-start.4 = (bf16[512,3072]{1,0:T(8,128)(2,1)}, bf16[512,3072]{1,0:T(8,128)(2,1)S(1)}, u32[]{:S(2)}, u32[]{:S(2)}) collective-permute-start(bf16[512,3072]{1,0:T(8,128)(2,1)} %shard_map.48), channel_id=1, source_target_pairs={{0,0},{2,8},{4,16},{6,24},{8,2},{10,10},{12,18},{14,26},{16,4},{18... | collective-permute-start | bytes 9437192 | tf_op jit(solution)/shard_map/ppermute | solution.py:89
Sparse Core Ops, SparseCore 0:
  81.4 99.9 all-gather.10
  182.9 81.1 all-gather.6
  265.7 96.7 all-gather.8

commit v11 on v10

--- a/solution.py
+++ b/solution.py
@@ -85,11 +85,25 @@
     )
 
 
-def transposed(value, size):
+def spread(size):
+    return [2, 0, 3, 1] if size == 4 else list(range(size))
+
+
+def green_to_layers(value, size):
+    inverse = {quarter: layer for layer, quarter in enumerate(spread(size))}
     return lax.ppermute(
         value,
         ("layer", "row"),
-        [(a * size + b, b * size + a) for a in range(size) for b in range(size)],
+        [(a * size + b, inverse[b] * size + a) for a in range(size) for b in range(size)],
+    )
+
+
+def product_to_owners(value, size):
+    quarter = spread(size)
+    return lax.ppermute(
+        value,
+        ("layer", "row"),
+        [(a * size + b, b * size + quarter[a]) for a in range(size) for b in range(size)],
     )
 
 
@@ -145,7 +159,7 @@
     chunk_of = block_cols // 2
     order = jnp.argsort(chunk_of)
     chunk_sorted = chunk_of[order]
-    starts = jnp.searchsorted(chunk_sorted, jnp.arange(chunks + 1), side="left").astype(jnp.int32)
+    starts = jnp.searchsorted(chunk_sorted, jnp.arange(chunks + 1), side="left", method="compare_all").astype(jnp.int32)
     k_sorted = (block_rows[order] // 2).astype(jnp.int32)
     padded = padded_blocks(blocks, block_rows, block_cols)[order]
     results = []
@@ -211,7 +225,7 @@
     col_count = lax.axis_size("col")
     blocks, block_row, block_col = compressed_tile(green, green_pattern)
     blocks, block_row, block_col = (
-        lax.all_gather(transposed(part, row_count), ("row", "col"), axis=0)
+        lax.all_gather(green_to_layers(part, row_count), ("row", "col"), axis=0)
         for part in (blocks, block_row, block_col)
     )
     band_count = blocks.shape[0]
@@ -227,7 +241,7 @@
         (piece,) = block_sparse_product(
             rows, entry_blocks, entry_rows, entry_cols, tile_cols * BLK, 1
         )
-        pieces.append(transposed(piece, row_count))
+        pieces.append(product_to_owners(piece, row_count))
     product = jnp.concatenate(pieces, axis=0)
     return product.reshape(ri_local, mu_local, tile_cols * BLK)
 

time: 614 us -> 587 us (0.956)
  the two profiles are of different devices: /device:TPU:16 before, /device:TPU:1 now
where the time goes in v11:
time: 587 us; the launch traced here: 584 us
  waiting for transfers between devices  316 us (54%)
  Pallas kernels  138 us (24%)
  other arithmetic  45.3 us (8%)
  starting transfers between devices  31.5 us (5%)
  local copies, waits for them, and re-layouts  28.9 us (5%)
  between operations  13.9 us (2%)
  blocking collectives  11.5 us (2%)
    all_gather x2, waiting for transfers between devices, per_device(): lax.all_gather(own[start:start + ROW_CHUNK], 'layer', axis=1, tiled=True)  135 us
    pallas_call x2, Pallas kernels, block_sparse_product(): pl.pallas_call(kernel, grid_spec=grid_spec, out_shape=jax.ShapeDtypeStruc...  121 us
    ppermute x2, waiting for transfers between devices, product_to_owners(): lax.ppermute(value, ('layer', 'row'), [(a * size + b, b * size + quarter[...  103 us
    all_gather x1, waiting for transfers between devices, per_device(): lax.all_gather(green_to_layers(part, row_count), ('row', 'col'), axis=0)  66.7 us
    ppermute x3, starting transfers between devices, green_to_layers(): lax.ppermute(value, ('layer', 'row'), [(a * size + b, inverse[b] * size +...  30.6 us
    pallas_call x1, Pallas kernels, gathered_windows(): pl.pallas_call(kernel, grid_spec=grid_spec, out_shape=jax.ShapeDtypeStruc...  16.1 us
    gather x1, local copies, waits for them, and re-layouts, block_sparse_product(): padded = padded_blocks(blocks, block_rows, block_cols)[order]  16 us
  transfers between devices with their start and end apart: 8, of which 6 were waited for; matrix products, arithmetic and copies ran while one was open for 9% of the time, Pallas kernels for 21%

profile of v11, /device:TPU:1, one launch (start us, length us, event | category | flops | bytes accessed | tf_op | source)
XLA Modules:
  0.0 584.4 jit_solution(15161432637907677904)
XLA Ops:
  6.5 0.7 compare_convert_fusion
  7.2 1.3 fusion.17
  8.6 0.8 reshape.263
  10.1 9.2 %scatter_custom_fusion = s32[48]{0:T(128)S(1)} fusion(s32[1152]{0:T(1024)S(1)} %fusion.3, s32[1152]{0:T(1024)S(1)} %broadcast.367, s32[]{:T(128)} %constant.136.clone.1), kind=kCustom, calls=%fused_computation.75 | custom fusion | flops 1152 | bytes 196 | tf_op jit(solution)/shard_map/scatter-add | solution.py:133
  19.4 0.8 fusion.2
  22.0 0.8 gather_fusion.2
  23.4 16.1 %shard_map.46 = bf16[48,64,128]{2,1,0:T(8,128)(2,1)} custom-call(s32[48]{0:T(128)} %and_select_fusion.2.rows_ref, s32[48]{0:T(128)} %and_select_fusion.cols_ref, bf16[1536,3072]{1,0:T(8,128)(2,1)} %green_ref.1), custom_call_target="tpu_custom_call" | custom-call | tf_op jit(solution)/shard_map/pallas_call | solution.py:122
  39.5 1.8 fusion
  41.3 8.8 %collective-permute-start.2 = (bf16[48,64,64]{2,1,0:T(8,128)(2,1)S(1)}, bf16[48,64,64]{2,1,0:T(8,128)(2,1)S(1)}, u32[]{:S(2)}, u32[]{:S(2)}) collective-permute-start(bf16[48,64,64]{2,1,0:T(8,128)(2,1)S(1)} %fusion), channel_id=1, source_target_pairs={{0,8},{2,24},{4,0},{6,16},{8,10},{10,26},{12,2},{14,18},{16,12},{1... | collective-permute-start | bytes 1179656 | tf_op jit(solution)/shard_map/ppermute | solution.py:94
  50.1 8.9 %collective-permute-done.2 = bf16[48,64,64]{2,1,0:T(8,128)(2,1)S(1)} collective-permute-done((bf16[48,64,64]{2,1,0:T(8,128)(2,1)S(1)}, bf16[48,64,64]{2,1,0:T(8,128)(2,1)S(1)}, u32[]{:S(2)}, u32[]{:S(2)}) %collective-permute-start.2) | collective-permute-done | bytes 393248 | tf_op jit(solution)/shard_map/ppermute | solution.py:94
  59.1 0.9 copy-done
  60.3 3.2 broadcast_multiply_fusion
  63.5 3.1 slice_bitcast_fusion.1
  66.7 0.7 all-gather.9.cloned.1.call-update
  67.4 7.3 %collective-permute-start.1 = (s32[48]{0:T(128)S(1)}, s32[48]{0:T(128)S(1)}, u32[]{:S(2)}, u32[]{:S(2)}) collective-permute-start(s32[48]{0:T(128)S(1)} %copy-done.2), channel_id=1, source_target_pairs={{0,8},{2,24},{4,0},{6,16},{8,10},{10,26},{12,2},{14,18},{16,12},{1... | collective-permute-start | bytes 584 | tf_op jit(solution)/shard_map/ppermute | solution.py:94
  74.7 14.5 %collective-permute-start = (s32[48]{0:T(128)S(1)}, s32[48]{0:T(128)S(1)}, u32[]{:S(2)}, u32[]{:S(2)}) collective-permute-start(s32[48]{0:T(128)S(1)} %get-tuple-element.12), channel_id=1, source_target_pairs={{0,8},{2,24},{4,0},{6,16},{8,10},{10,26},{12,2},{14,18},{16,12},{1... | collective-permute-start | bytes 584 | tf_op jit(solution)/shard_map/ppermute | solution.py:94
  90.4 1.0 collective-permute-done.1
  91.8 11.5 %all-reduce.2 = (s32[384]{0:T(512)S(1)}, s32[384]{0:T(512)S(1)}) all-reduce(s32[384]{0:T(512)S(1)} %dynamic-update-slice, s32[384]{0:T(512)S(1)} %dynamic-update-slice.1), channel_id=2, replica_groups=mesh['layer'=4,'row'=4,'col'=2] {'row','col'}, use_global_device_ids=true, to_apply=%add | all-reduce | flops 768 | bytes 6144
  103.5 3.7 sort.19
  107.3 2.8 gather_fusion
  110.1 2.8 gather_fusion.1
  114.1 66.7 %all-gather.11.cloned.1.call-done = bf16[384,64,64]{2,1,0:T(8,128)(2,1)} async-done(((bf16[48,64,64]{2,1,0:T(8,128)(2,1)}), bf16[384,64,64]{2,1,0:T(8,128)(2,1)}) %all-gather.11.cloned.1.call-update) | async-done | bytes 3145744 | tf_op jit(solution)/shard_map/all_gather | solution.py:228
  180.8 4.2 broadcast_select_fusion.1
  185.1 6.4 %broadcast_select_fusion.3 = (bf16[384,64,128]{2,1,0:T(8,128)(2,1)S(1)}, bf16[384,64,128]{2,1,0:T(8,128)(2,1)S(1)}) fusion(pred[384]{0:T(512)(128)(4,1)S(1)} %fusion.6, bf16[384,64,64]{2,1,0:T(8,128)(2,1)S(1)} %get-tuple-element.17, bf16[384,64,64]{2,1,0:T(8,128)(2,1)S(1)} %get-tuple-element.16), kind=kLoop, calls=%fused_computation.11 | loop fusion | flops 18874368 | bytes 18874752 | tf_op jit(solution)/shard_map/jit(_where)/select_n | solution.py:151
  191.5 6.5 %pad_maximum_fusion = bf16[384,128,128]{2,1,0:T(8,128)(2,1)} fusion(bf16[384,64,128]{2,1,0:T(8,128)(2,1)S(1)} %get-tuple-element.15, bf16[384,64,128]{2,1,0:T(8,128)(2,1)S(1)} %get-tuple-element.14), kind=kLoop, calls=%fused_computation.5 | loop fusion | flops 25165824 | bytes 25165824 | tf_op jit(solution)/shard_map/concatenate | solution.py:151
  198.0 16.0 %gather_fusion.3 = bf16[384,128,128]{2,1,0:T(8,128)(2,1)} fusion(bf16[384,128,128]{2,1,0:T(8,128)(2,1)} %pad_maximum_fusion, s32[1024]{0:T(1024)S(1)} %pad_clamp_fusion.1), kind=kCustom, calls=%fused_computation.3 | custom fusion | bytes 25167360 | tf_op jit(solution)/shard_map/gather | solution.py:164
  214.0 49.7 %all-gather.7.cloned.1.call-done.t_ref = bf16[512,12288]{1,0:T(8,128)(2,1)} async-done(((bf16[512,3072]{1,0:T(8,128)(2,1)}), bf16[512,12288]{1,0:T(8,128)(2,1)}) %all-gather.7.cloned.1.call-update) | async-done | bytes 12582928 | tf_op jit(solution)/shard_map/all_gather | solution.py:240
  263.6 61.0 %shard_map.47 = bf16[512,3072]{1,0:T(8,128)(2,1)} custom-call(s32[25]{0:T(128)} %convert_reduce_fusion.starts_ref, s32[384]{0:T(512)} %add_select_fusion.3.k_ref, bf16[512,12288]{1,0:T(8,128)(2,1)} %all-gather.7.cloned.1.call-done.t_ref, bf16[384,128,128]{2,1,0:T(8,128)(2,1)} %gather_fusion.3), custom_call_target="tpu_custom_call" | custom-call | tf_op jit(solution)/shard_map/pallas_call | solution.py:205
  325.0 85.5 %all-gather.9.cloned.1.call-done.t_ref = bf16[512,12288]{1,0:T(8,128)(2,1)} async-done(((bf16[512,3072]{1,0:T(8,128)(2,1)}), bf16[512,12288]{1,0:T(8,128)(2,1)}) %all-gather.9.cloned.1.call-update) | async-done | bytes 12582928 | tf_op jit(solution)/shard_map/all_gather | solution.py:240
  410.5 60.5 %shard_map.48 = bf16[512,3072]{1,0:T(8,128)(2,1)} custom-call(s32[25]{0:T(128)} %convert_reduce_fusion.starts_ref, s32[384]{0:T(512)} %add_select_fusion.3.k_ref, bf16[512,12288]{1,0:T(8,128)(2,1)} %all-gather.9.cloned.1.call-done.t_ref, bf16[384,128,128]{2,1,0:T(8,128)(2,1)} %gather_fusion.3), custom_call_target="tpu_custom_call" | custom-call | tf_op jit(solution)/shard_map/pallas_call | solution.py:205
  471.5 103.2 %collective-permute-done.4 = bf16[512,3072]{1,0:T(8,128)(2,1)S(1)} collective-permute-done((bf16[512,3072]{1,0:T(8,128)(2,1)}, bf16[512,3072]{1,0:T(8,128)(2,1)S(1)}, u32[]{:S(2)}, u32[]{:S(2)}) %collective-permute-start.4) | collective-permute-done | bytes 3145760 | tf_op jit(solution)/shard_map/ppermute | solution.py:103
  574.7 3.1 maximum_bitcast_fusion
  (51 shorter events, 7.0 us)
Async XLA Ops:
  6.5 174.3 %all-gather.11.cloned.1.call-start = ((), (), s32[]{:S(2)}) async-start(), calls=%async_computation.2 | async-start | bytes 7077888 | tf_op jit(solution)/shard_map/all_gather | solution.py:228
  23.4 36.6 %copy-start.1 = (s32[8,48]{1,0:T(8,128)S(1)}, s32[8,48]{1,0:T(8,128)}, u32[]{:S(2)}) copy-start(s32[8,48]{1,0:T(8,128)} %param.5) | copy-start | bytes 4612
  41.3 17.7 %collective-permute-start.2 = (bf16[48,64,64]{2,1,0:T(8,128)(2,1)S(1)}, bf16[48,64,64]{2,1,0:T(8,128)(2,1)S(1)}, u32[]{:S(2)}, u32[]{:S(2)}) collective-permute-start(bf16[48,64,64]{2,1,0:T(8,128)(2,1)S(1)} %fusion), channel_id=1, source_target_pairs={{0,8},{2,24},{4,0},{6,16},{8,10},{10,26},{12,2},{14,18},{16,12},{1... | collective-permute-start | bytes 1179656 | tf_op jit(solution)/shard_map/ppermute | solution.py:94
  59.1 0.9 copy-start
  60.0 203.7 %all-gather.7.cloned.1.call-start = ((), (), s32[]{:S(2)}) async-start(), calls=%async_computation | async-start | bytes 15728640 | tf_op jit(solution)/shard_map/all_gather | solution.py:240
  66.6 0.8 copy-start.2
  66.6 22.6 %copy-start.3 = (u32[32]{0:T(128)S(1)}, u32[32]{0:T(128)}, u32[]{:S(2)}) copy-start(u32[32]{0:T(128)} %constant.147) | copy-start | bytes 388
  66.7 343.8 %all-gather.9.cloned.1.call-start = ((), (), s32[]{:S(2)}) async-start(), calls=%async_computation.1 | async-start | bytes 15728640 | tf_op jit(solution)/shard_map/all_gather | solution.py:240
  67.4 24.0 %collective-permute-start.1 = (s32[48]{0:T(128)S(1)}, s32[48]{0:T(128)S(1)}, u32[]{:S(2)}, u32[]{:S(2)}) collective-permute-start(s32[48]{0:T(128)S(1)} %copy-done.2), channel_id=1, source_target_pairs={{0,8},{2,24},{4,0},{6,16},{8,10},{10,26},{12,2},{14,18},{16,12},{1... | collective-permute-start | bytes 584 | tf_op jit(solution)/shard_map/ppermute | solution.py:94
  74.7 16.9 %collective-permute-start = (s32[48]{0:T(128)S(1)}, s32[48]{0:T(128)S(1)}, u32[]{:S(2)}, u32[]{:S(2)}) collective-permute-start(s32[48]{0:T(128)S(1)} %get-tuple-element.12), channel_id=1, source_target_pairs={{0,8},{2,24},{4,0},{6,16},{8,10},{10,26},{12,2},{14,18},{16,12},{1... | collective-permute-start | bytes 584 | tf_op jit(solution)/shard_map/ppermute | solution.py:94
  324.7 146.8 %collective-permute-start.3 = (bf16[512,3072]{1,0:T(8,128)(2,1)}, bf16[512,3072]{1,0:T(8,128)(2,1)S(1)}, u32[]{:S(2)}, u32[]{:S(2)}) collective-permute-start(bf16[512,3072]{1,0:T(8,128)(2,1)} %shard_map.47), channel_id=1, source_target_pairs={{0,4},{2,12},{4,20},{6,28},{8,0},{10,8},{12,16},{14,24},{16,6},{18... | collective-permute-start | bytes 9437192 | tf_op jit(solution)/shard_map/ppermute | solution.py:103
  470.9 103.7 %collective-permute-start.4 = (bf16[512,3072]{1,0:T(8,128)(2,1)}, bf16[512,3072]{1,0:T(8,128)(2,1)S(1)}, u32[]{:S(2)}, u32[]{:S(2)}) collective-permute-start(bf16[512,3072]{1,0:T(8,128)(2,1)} %shard_map.48), channel_id=1, source_target_pairs={{0,4},{2,12},{4,20},{6,28},{8,0},{10,8},{12,16},{14,24},{16,6},{18... | collective-permute-start | bytes 9437192 | tf_op jit(solution)/shard_map/ppermute | solution.py:103
Sparse Core Ops, SparseCore 0:
  60.1 120.6 all-gather.10
  182.4 81.2 all-gather.6
  265.2 145.2 all-gather.8

commit v12 on v11

--- a/solution.py
+++ b/solution.py
@@ -224,14 +224,18 @@
     layer_index = lax.axis_index("layer")
     col_count = lax.axis_size("col")
     blocks, block_row, block_col = compressed_tile(green, green_pattern)
+    parts = tuple(green_to_layers(part, row_count) for part in (blocks, block_row, block_col))
+    group = row_count * col_count
+    me = lax.axis_index("row") * col_count + lax.axis_index("col")
+    received = [parts]
+    for shift in range(1, group):
+        pairs = [(i, (i + shift) % group) for i in range(group)]
+        received.append(tuple(lax.ppermute(part, ("row", "col"), pairs) for part in parts))
     blocks, block_row, block_col = (
-        lax.all_gather(green_to_layers(part, row_count), ("row", "col"), axis=0)
-        for part in (blocks, block_row, block_col)
-    )
-    band_count = blocks.shape[0]
-    band = jnp.arange(band_count)[:, None]
-    position = band // col_count
-    entry_rows = (position * col_count + band % col_count) * tile_rows + block_row
+        jnp.stack([got[k] for got in received]) for k in range(len(parts))
+    )
+    band = ((me - jnp.arange(group)) % group)[:, None]
+    entry_rows = band * tile_rows + block_row
     entry_rows = entry_rows.reshape(-1)
     entry_cols = block_col.reshape(-1)
     entry_blocks = blocks.reshape(-1, BLK, BLK)

time: 587 us -> 559 us (0.952)
  the two profiles are of different devices: /device:TPU:1 before, /device:TPU:30 now
where the time goes in v12:
time: 559 us; the launch traced here: 556 us
  waiting for transfers between devices  284 us (51%)
  Pallas kernels  139 us (25%)
  starting transfers between devices  52.6 us (9%)
  other arithmetic  39.7 us (7%)
  local copies, waits for them, and re-layouts  27.1 us (5%)
  between operations  13.6 us (2%)
    ppermute x2, waiting for transfers between devices, product_to_owners(): lax.ppermute(value, ('layer', 'row'), [(a * size + b, b * size + quarter[...  144 us
    ppermute x21, waiting for transfers between devices, per_device(): lax.ppermute(part, ('row', 'col'), pairs)  140 us
    pallas_call x2, Pallas kernels, block_sparse_product(): pl.pallas_call(kernel, grid_spec=grid_spec, out_shape=jax.ShapeDtypeStruc...  121 us
    ppermute x21, starting transfers between devices, per_device(): lax.ppermute(part, ('row', 'col'), pairs)  45.8 us
    pallas_call x1, Pallas kernels, gathered_windows(): pl.pallas_call(kernel, grid_spec=grid_spec, out_shape=jax.ShapeDtypeStruc...  18.4 us
    gather x1, local copies, waits for them, and re-layouts, block_sparse_product(): padded = padded_blocks(blocks, block_rows, block_cols)[order]  15.9 us
  transfers between devices with their start and end apart: 28, of which 11 were waited for; matrix products, arithmetic and copies ran while one was open for 10% of the time, Pallas kernels for 25%

profile of v12, /device:TPU:30, one launch (start us, length us, event | category | flops | bytes accessed | tf_op | source)
XLA Modules:
  0.0 556.4 jit_solution(5137715468905889067)
XLA Ops:
  7.5 3.2 broadcast_multiply_fusion
  10.7 3.1 slice_bitcast_fusion.1
  15.3 9.2 %scatter_custom_fusion = s32[48]{0:T(128)S(1)} fusion(s32[1152]{0:T(1024)S(1)} %fusion.3, s32[1152]{0:T(1024)S(1)} %broadcast.324, s32[]{:T(128)} %constant.133.clone.1), kind=kCustom, calls=%fused_computation.80 | custom fusion | flops 1152 | bytes 196 | tf_op jit(solution)/shard_map/scatter-add | solution.py:133
  28.3 18.4 %shard_map.46 = bf16[48,64,128]{2,1,0:T(8,128)(2,1)} custom-call(s32[48]{0:T(128)} %copy-done.1, s32[48]{0:T(128)} %and_select_fusion.cols_ref, bf16[1536,3072]{1,0:T(8,128)(2,1)} %green_ref.1), custom_call_target="tpu_custom_call" | custom-call | tf_op jit(solution)/shard_map/pallas_call | solution.py:122
  48.1 1.8 fusion
  49.9 4.4 collective-permute-start.16
  54.4 2.9 collective-permute-start.3
  58.8 5.1 collective-permute-done.1
  63.9 24.5 %collective-permute-start.5 = (s32[48]{0:T(128)S(1)}, s32[48]{0:T(128)S(1)}, u32[]{:S(2)}, u32[]{:S(2)}) collective-permute-start(s32[48]{0:T(128)S(1)} %collective-permute-done), channel_id=1, source_target_pairs={{0,5},{1,6},{2,7},{3,0},{4,1},{5,2},{6,3},{7,4},{8,13},{9,14},{10,... | collective-permute-start | bytes 584 | tf_op jit(solution)/shard_map/ppermute | solution.py:233
  88.9 4.2 collective-permute-start.9
  93.2 2.0 collective-permute-start.10
  100.3 1.8 collective-permute-done.13
  103.6 2.4 collective-permute-done.15
  106.2 3.8 sort.19
  110.0 2.8 gather_fusion.1
  113.9 2.8 gather_fusion
  117.4 2.6 collective-permute-start.19
  120.0 1.8 collective-permute-start.20
  121.9 10.1 %collective-permute-done.17 = bf16[48,64,64]{2,1,0:T(8,128)(2,1)S(1)} collective-permute-done((bf16[48,64,64]{2,1,0:T(8,128)(2,1)S(1)}, bf16[48,64,64]{2,1,0:T(8,128)(2,1)S(1)}, u32[]{:S(2)}, u32[]{:S(2)}) %collective-permute-start.17) | collective-permute-done | bytes 393248 | tf_op jit(solution)/shard_map/ppermute | solution.py:233
  132.1 16.7 %collective-permute-done.18 = bf16[48,64,64]{2,1,0:T(8,128)(2,1)S(1)} collective-permute-done((bf16[48,64,64]{2,1,0:T(8,128)(2,1)S(1)}, bf16[48,64,64]{2,1,0:T(8,128)(2,1)S(1)}, u32[]{:S(2)}, u32[]{:S(2)}) %collective-permute-start.18) | collective-permute-done | bytes 393248 | tf_op jit(solution)/shard_map/ppermute | solution.py:233
  149.0 16.8 %collective-permute-done.19 = bf16[48,64,64]{2,1,0:T(8,128)(2,1)S(1)} collective-permute-done((bf16[48,64,64]{2,1,0:T(8,128)(2,1)S(1)}, bf16[48,64,64]{2,1,0:T(8,128)(2,1)S(1)}, u32[]{:S(2)}, u32[]{:S(2)}) %collective-permute-start.19) | collective-permute-done | bytes 393248 | tf_op jit(solution)/shard_map/ppermute | solution.py:233
  165.9 80.3 %collective-permute-done.20 = bf16[48,64,64]{2,1,0:T(8,128)(2,1)S(1)} collective-permute-done((bf16[48,64,64]{2,1,0:T(8,128)(2,1)S(1)}, bf16[48,64,64]{2,1,0:T(8,128)(2,1)S(1)}, u32[]{:S(2)}, u32[]{:S(2)}) %collective-permute-start.20) | collective-permute-done | bytes 393248 | tf_op jit(solution)/shard_map/ppermute | solution.py:233
  246.3 5.0 collective-permute-done.21
  251.7 1.6 bitcast_select_fusion.1
  253.3 6.3 %broadcast_select_fusion.1 = (bf16[384,64,128]{2,1,0:T(8,128)(2,1)S(1)}, bf16[384,64,128]{2,1,0:T(8,128)(2,1)S(1)}) fusion(pred[384]{0:T(512)(128)(4,1)S(1)} %fusion.6, bf16[384,64,64]{2,1,0:T(8,128)(2,1)S(1)} %get-tuple-element.15, bf16[384,64,64]{2,1,0:T(8,128)(2,1)S(1)} %get-tuple-element.14), kind=kLoop, calls=%fused_computation.11 | loop fusion | flops 18874368 | bytes 18874752 | tf_op jit(solution)/shard_map/jit(_where)/select_n | solution.py:151
  259.6 5.2 pad_maximum_fusion
  264.8 15.9 %gather_fusion.3 = bf16[384,128,128]{2,1,0:T(8,128)(2,1)} fusion(bf16[384,128,128]{2,1,0:T(8,128)(2,1)} %pad_maximum_fusion, s32[1024]{0:T(1024)S(1)} %pad_clamp_fusion.1), kind=kCustom, calls=%fused_computation.3 | custom fusion | bytes 25167360 | tf_op jit(solution)/shard_map/gather | solution.py:164
  280.7 60.4 %shard_map.47 = bf16[512,3072]{1,0:T(8,128)(2,1)} custom-call(s32[25]{0:T(128)} %convert_reduce_fusion.starts_ref, s32[384]{0:T(512)} %add_select_fusion.3.k_ref, bf16[512,12288]{1,0:T(8,128)(2,1)} %all-gather.3.cloned.1.call-done.t_ref, bf16[384,128,128]{2,1,0:T(8,128)(2,1)} %gather_fusion.3), custom_call_target="tpu_custom_call" | custom-call | tf_op jit(solution)/shard_map/pallas_call | solution.py:205
  341.2 60.3 %shard_map.48 = bf16[512,3072]{1,0:T(8,128)(2,1)} custom-call(s32[25]{0:T(128)} %convert_reduce_fusion.starts_ref, s32[384]{0:T(512)} %add_select_fusion.3.k_ref, bf16[512,12288]{1,0:T(8,128)(2,1)} %all-gather.5.cloned.1.call-done.t_ref, bf16[384,128,128]{2,1,0:T(8,128)(2,1)} %gather_fusion.3), custom_call_target="tpu_custom_call" | custom-call | tf_op jit(solution)/shard_map/pallas_call | solution.py:205
  402.7 110.0 %collective-permute-done.24 = bf16[512,3072]{1,0:T(8,128)(2,1)S(1)} collective-permute-done((bf16[512,3072]{1,0:T(8,128)(2,1)}, bf16[512,3072]{1,0:T(8,128)(2,1)S(1)}, u32[]{:S(2)}, u32[]{:S(2)}) %collective-permute-start.24) | collective-permute-done | bytes 3145760 | tf_op jit(solution)/shard_map/ppermute | solution.py:103
  512.7 33.7 %collective-permute-done.25 = bf16[512,3072]{1,0:T(8,128)(2,1)S(1)} collective-permute-done((bf16[512,3072]{1,0:T(8,128)(2,1)}, bf16[512,3072]{1,0:T(8,128)(2,1)S(1)}, u32[]{:S(2)}, u32[]{:S(2)}) %collective-permute-start.25) | collective-permute-done | bytes 3145760 | tf_op jit(solution)/shard_map/ppermute | solution.py:103
  546.4 3.1 maximum_bitcast_fusion
  (90 shorter events, 20.4 us)
Async XLA Ops:
  6.5 274.2 %all-gather.3.cloned.1.call-start = ((), (), s32[]{:S(2)}) async-start(), calls=%async_computation | async-start | bytes 15728640 | tf_op jit(solution)/shard_map/all_gather | solution.py:244
  13.8 0.8 copy-start
  13.8 327.3 %all-gather.5.cloned.1.call-start = ((), (), s32[]{:S(2)}) async-start(), calls=%async_computation.1 | async-start | bytes 15728640 | tf_op jit(solution)/shard_map/all_gather | solution.py:244
  26.6 27.7 %collective-permute-start = (s32[48]{0:T(128)S(1)}, s32[48]{0:T(128)S(1)}, u32[]{:S(2)}, u32[]{:S(2)}) collective-permute-start(s32[48]{0:T(128)S(1)} %get-tuple-element.10), channel_id=1, source_target_pairs={{0,8},{2,24},{4,0},{6,16},{8,10},{10,26},{12,2},{14,18},{16,12},{1... | collective-permute-start | bytes 584 | tf_op jit(solution)/shard_map/ppermute | solution.py:94
  27.1 1.2 copy-start.1
  27.1 30.2 %collective-permute-start.8 = (s32[48]{0:T(128)S(1)}, s32[48]{0:T(128)S(1)}, u32[]{:S(2)}, u32[]{:S(2)}) collective-permute-start(s32[48]{0:T(128)S(1)} %and_select_fusion.2.rows_ref), channel_id=1, source_target_pairs={{0,8},{2,24},{4,0},{6,16},{8,10},{10,26},{12,2},{14,18},{16,12},{1... | collective-permute-start | bytes 584 | tf_op jit(solution)/shard_map/ppermute | solution.py:94
  49.9 63.5 %collective-permute-start.16 = (bf16[48,64,64]{2,1,0:T(8,128)(2,1)S(1)}, bf16[48,64,64]{2,1,0:T(8,128)(2,1)S(1)}, u32[]{:S(2)}, u32[]{:S(2)}) collective-permute-start(bf16[48,64,64]{2,1,0:T(8,128)(2,1)S(1)} %fusion), channel_id=1, source_target_pairs={{0,8},{2,24},{4,0},{6,16},{8,10},{10,26},{12,2},{14,18},{16,12},{1... | collective-permute-start | bytes 1179656 | tf_op jit(solution)/shard_map/ppermute | solution.py:94
  54.3 9.6 %collective-permute-start.1 = (s32[48]{0:T(128)S(1)}, s32[48]{0:T(128)S(1)}, u32[]{:S(2)}, u32[]{:S(2)}) collective-permute-start(s32[48]{0:T(128)S(1)} %collective-permute-done), channel_id=1, source_target_pairs={{0,1},{1,2},{2,3},{3,4},{4,5},{5,6},{6,7},{7,0},{8,9},{9,10},{10,1... | collective-permute-start | bytes 584 | tf_op jit(solution)/shard_map/ppermute | solution.py:233
  54.4 34.0 %collective-permute-start.2 = (s32[48]{0:T(128)S(1)}, s32[48]{0:T(128)S(1)}, u32[]{:S(2)}, u32[]{:S(2)}) collective-permute-start(s32[48]{0:T(128)S(1)} %collective-permute-done), channel_id=1, source_target_pairs={{0,2},{1,3},{2,4},{3,5},{4,6},{5,7},{6,0},{7,1},{8,10},{9,11},{10,... | collective-permute-start | bytes 584 | tf_op jit(solution)/shard_map/ppermute | solution.py:233
  54.4 33.9 %collective-permute-start.3 = (s32[48]{0:T(128)S(1)}, s32[48]{0:T(128)S(1)}, u32[]{:S(2)}, u32[]{:S(2)}) collective-permute-start(s32[48]{0:T(128)S(1)} %collective-permute-done), channel_id=1, source_target_pairs={{0,3},{1,4},{2,5},{3,6},{4,7},{5,0},{6,1},{7,2},{8,11},{9,12},{10,... | collective-permute-start | bytes 584 | tf_op jit(solution)/shard_map/ppermute | solution.py:233
  57.3 31.6 %collective-permute-start.4 = (s32[48]{0:T(128)S(1)}, s32[48]{0:T(128)S(1)}, u32[]{:S(2)}, u32[]{:S(2)}) collective-permute-start(s32[48]{0:T(128)S(1)} %collective-permute-done), channel_id=1, source_target_pairs={{0,4},{1,5},{2,6},{3,7},{4,0},{5,1},{6,2},{7,3},{8,12},{9,13},{10,... | collective-permute-start | bytes 584 | tf_op jit(solution)/shard_map/ppermute | solution.py:233
  63.9 29.3 %collective-permute-start.5 = (s32[48]{0:T(128)S(1)}, s32[48]{0:T(128)S(1)}, u32[]{:S(2)}, u32[]{:S(2)}) collective-permute-start(s32[48]{0:T(128)S(1)} %collective-permute-done), channel_id=1, source_target_pairs={{0,5},{1,6},{2,7},{3,0},{4,1},{5,2},{6,3},{7,4},{8,13},{9,14},{10,... | collective-permute-start | bytes 584 | tf_op jit(solution)/shard_map/ppermute | solution.py:233
  88.4 6.8 %collective-permute-start.6 = (s32[48]{0:T(128)S(1)}, s32[48]{0:T(128)S(1)}, u32[]{:S(2)}, u32[]{:S(2)}) collective-permute-start(s32[48]{0:T(128)S(1)} %collective-permute-done), channel_id=1, source_target_pairs={{0,6},{1,7},{2,0},{3,1},{4,2},{5,3},{6,4},{7,5},{8,14},{9,15},{10,... | collective-permute-start | bytes 584 | tf_op jit(solution)/shard_map/ppermute | solution.py:233
  88.4 6.8 %collective-permute-start.7 = (s32[48]{0:T(128)S(1)}, s32[48]{0:T(128)S(1)}, u32[]{:S(2)}, u32[]{:S(2)}) collective-permute-start(s32[48]{0:T(128)S(1)} %collective-permute-done), channel_id=1, source_target_pairs={{0,7},{1,0},{2,1},{3,2},{4,3},{5,4},{6,5},{7,6},{8,15},{9,8},{10,9... | collective-permute-start | bytes 584 | tf_op jit(solution)/shard_map/ppermute | solution.py:233
  88.9 7.8 %collective-permute-start.9 = (s32[48]{0:T(128)S(1)}, s32[48]{0:T(128)S(1)}, u32[]{:S(2)}, u32[]{:S(2)}) collective-permute-start(s32[48]{0:T(128)S(1)} %collective-permute-done.8), channel_id=1, source_target_pairs={{0,1},{1,2},{2,3},{3,4},{4,5},{5,6},{6,7},{7,0},{8,9},{9,10},{10,1... | collective-permute-start | bytes 584 | tf_op jit(solution)/shard_map/ppermute | solution.py:233
  93.2 5.1 collective-permute-start.10
  95.1 4.6 collective-permute-start.11
  95.1 5.2 collective-permute-start.12
  96.8 5.4 collective-permute-start.13
  98.2 5.3 collective-permute-start.14
  99.7 6.2 %collective-permute-start.15 = (s32[48]{0:T(128)S(1)}, s32[48]{0:T(128)S(1)}, u32[]{:S(2)}, u32[]{:S(2)}) collective-permute-start(s32[48]{0:T(128)S(1)} %collective-permute-done.8), channel_id=1, source_target_pairs={{0,7},{1,0},{2,1},{3,2},{4,3},{5,4},{6,5},{7,6},{8,15},{9,8},{10,9... | collective-permute-start | bytes 584 | tf_op jit(solution)/shard_map/ppermute | solution.py:233
  113.3 18.7 %collective-permute-start.17 = (bf16[48,64,64]{2,1,0:T(8,128)(2,1)S(1)}, bf16[48,64,64]{2,1,0:T(8,128)(2,1)S(1)}, u32[]{:S(2)}, u32[]{:S(2)}) collective-permute-start(bf16[48,64,64]{2,1,0:T(8,128)(2,1)S(1)} %collective-permute-done.16), channel_id=1, source_target_pairs={{0,1},{1,2},{2,3},{3,4},{4,5},{5,6},{6,7},{7,0},{8,9},{9,10},{10,1... | collective-permute-start | bytes 1179656 | tf_op jit(solution)/shard_map/ppermute | solution.py:233
  117.4 31.5 %collective-permute-start.18 = (bf16[48,64,64]{2,1,0:T(8,128)(2,1)S(1)}, bf16[48,64,64]{2,1,0:T(8,128)(2,1)S(1)}, u32[]{:S(2)}, u32[]{:S(2)}) collective-permute-start(bf16[48,64,64]{2,1,0:T(8,128)(2,1)S(1)} %collective-permute-done.16), channel_id=1, source_target_pairs={{0,2},{1,3},{2,4},{3,5},{4,6},{5,7},{6,0},{7,1},{8,10},{9,11},{10,... | collective-permute-start | bytes 1179656 | tf_op jit(solution)/shard_map/ppermute | solution.py:233
  117.4 48.3 %collective-permute-start.19 = (bf16[48,64,64]{2,1,0:T(8,128)(2,1)S(1)}, bf16[48,64,64]{2,1,0:T(8,128)(2,1)S(1)}, u32[]{:S(2)}, u32[]{:S(2)}) collective-permute-start(bf16[48,64,64]{2,1,0:T(8,128)(2,1)S(1)} %collective-permute-done.16), channel_id=1, source_target_pairs={{0,3},{1,4},{2,5},{3,6},{4,7},{5,0},{6,1},{7,2},{8,11},{9,12},{10,... | collective-permute-start | bytes 1179656 | tf_op jit(solution)/shard_map/ppermute | solution.py:233
  120.0 126.2 %collective-permute-start.20 = (bf16[48,64,64]{2,1,0:T(8,128)(2,1)S(1)}, bf16[48,64,64]{2,1,0:T(8,128)(2,1)S(1)}, u32[]{:S(2)}, u32[]{:S(2)}) collective-permute-start(bf16[48,64,64]{2,1,0:T(8,128)(2,1)S(1)} %collective-permute-done.16), channel_id=1, source_target_pairs={{0,4},{1,5},{2,6},{3,7},{4,0},{5,1},{6,2},{7,3},{8,12},{9,13},{10,... | collective-permute-start | bytes 1179656 | tf_op jit(solution)/shard_map/ppermute | solution.py:233
  121.8 129.5 %collective-permute-start.21 = (bf16[48,64,64]{2,1,0:T(8,128)(2,1)S(1)}, bf16[48,64,64]{2,1,0:T(8,128)(2,1)S(1)}, u32[]{:S(2)}, u32[]{:S(2)}) collective-permute-start(bf16[48,64,64]{2,1,0:T(8,128)(2,1)S(1)} %collective-permute-done.16), channel_id=1, source_target_pairs={{0,5},{1,6},{2,7},{3,0},{4,1},{5,2},{6,3},{7,4},{8,13},{9,14},{10,... | collective-permute-start | bytes 1179656 | tf_op jit(solution)/shard_map/ppermute | solution.py:233
  132.0 119.4 %collective-permute-start.22 = (bf16[48,64,64]{2,1,0:T(8,128)(2,1)S(1)}, bf16[48,64,64]{2,1,0:T(8,128)(2,1)S(1)}, u32[]{:S(2)}, u32[]{:S(2)}) collective-permute-start(bf16[48,64,64]{2,1,0:T(8,128)(2,1)S(1)} %collective-permute-done.16), channel_id=1, source_target_pairs={{0,6},{1,7},{2,0},{3,1},{4,2},{5,3},{6,4},{7,5},{8,14},{9,15},{10,... | collective-permute-start | bytes 1179656 | tf_op jit(solution)/shard_map/ppermute | solution.py:233
  148.9 102.7 %collective-permute-start.23 = (bf16[48,64,64]{2,1,0:T(8,128)(2,1)S(1)}, bf16[48,64,64]{2,1,0:T(8,128)(2,1)S(1)}, u32[]{:S(2)}, u32[]{:S(2)}) collective-permute-start(bf16[48,64,64]{2,1,0:T(8,128)(2,1)S(1)} %collective-permute-done.16), channel_id=1, source_target_pairs={{0,7},{1,0},{2,1},{3,2},{4,3},{5,4},{6,5},{7,6},{8,15},{9,8},{10,9... | collective-permute-start | bytes 1179656 | tf_op jit(solution)/shard_map/ppermute | solution.py:233
  341.2 171.6 %collective-permute-start.24 = (bf16[512,3072]{1,0:T(8,128)(2,1)}, bf16[512,3072]{1,0:T(8,128)(2,1)S(1)}, u32[]{:S(2)}, u32[]{:S(2)}) collective-permute-start(bf16[512,3072]{1,0:T(8,128)(2,1)} %shard_map.47), channel_id=1, source_target_pairs={{0,4},{2,12},{4,20},{6,28},{8,0},{10,8},{12,16},{14,24},{16,6},{18... | collective-permute-start | bytes 9437192 | tf_op jit(solution)/shard_map/ppermute | solution.py:103
  401.4 145.0 %collective-permute-start.25 = (bf16[512,3072]{1,0:T(8,128)(2,1)}, bf16[512,3072]{1,0:T(8,128)(2,1)S(1)}, u32[]{:S(2)}, u32[]{:S(2)}) collective-permute-start(bf16[512,3072]{1,0:T(8,128)(2,1)} %shard_map.48), channel_id=1, source_target_pairs={{0,4},{2,12},{4,20},{6,28},{8,0},{10,8},{12,16},{14,24},{16,6},{18... | collective-permute-start | bytes 9437192 | tf_op jit(solution)/shard_map/ppermute | solution.py:103
Sparse Core Ops, SparseCore 0:
  13.9 96.1 all-gather.2
  111.7 84.9 all-gather.4

commit v13 on v12

--- a/solution.py
+++ b/solution.py
@@ -239,15 +239,43 @@
     entry_rows = entry_rows.reshape(-1)
     entry_cols = block_col.reshape(-1)
     entry_blocks = blocks.reshape(-1, BLK, BLK)
-    pieces = []
-    for start in range(0, ri_local * mu_local, ROW_CHUNK):
-        rows = lax.all_gather(own[start : start + ROW_CHUNK], "layer", axis=1, tiled=True)
-        (piece,) = block_sparse_product(
-            rows, entry_blocks, entry_rows, entry_cols, tile_cols * BLK, 1
-        )
-        pieces.append(product_to_owners(piece, row_count))
-    product = jnp.concatenate(pieces, axis=0)
+    if layer_count != 4:
+        pieces = []
+        for start in range(0, ri_local * mu_local, ROW_CHUNK):
+            rows = lax.all_gather(own[start : start + ROW_CHUNK], "layer", axis=1, tiled=True)
+            (piece,) = block_sparse_product(
+                rows, entry_blocks, entry_rows, entry_cols, tile_cols * BLK, 1
+            )
+            pieces.append(product_to_owners(piece, row_count))
+        product = jnp.concatenate(pieces, axis=0)
+        return product.reshape(ri_local, mu_local, tile_cols * BLK)
+    half = ri_local * mu_local // 2
+    halves = own.reshape(2, half, nu_local)
+    sent = jnp.stack([halves[0], halves[0], halves[1], halves[1]])
+    arrived = lax.all_to_all(sent, "layer", 0, 0)
+    rows = arrived.transpose(1, 0, 2).reshape(half, layer_count * nu_local)
+    across = [(i, i ^ 2) for i in range(4)]
+    other_blocks, other_rows, other_cols = (
+        lax.ppermute(part, "layer", across) for part in (entry_blocks, entry_rows, entry_cols)
+    )
+    (mine,) = block_sparse_product(rows, entry_blocks, entry_rows, entry_cols, tile_cols * BLK, 1)
+    mine = product_to_owners(mine, row_count)
+    (theirs,) = block_sparse_product(rows, other_blocks, other_rows, other_cols, tile_cols * BLK, 1)
+    quarter = spread(row_count)
+    theirs = lax.ppermute(
+        theirs,
+        ("layer", "row"),
+        [(a * 4 + b, b * 4 + quarter[a ^ 2]) for a in range(4) for b in range(4)],
+    )
+    inverse = [quarter.index(r) // 2 for r in range(4)]
+    first_half = jnp.array(inverse, jnp.int32)[lax.axis_index("row")]
+    product = jnp.where(
+        first_half == 0,
+        jnp.concatenate([mine, theirs], axis=0),
+        jnp.concatenate([theirs, mine], axis=0),
+    )
     return product.reshape(ri_local, mu_local, tile_cols * BLK)
+
 
 def solution(mesh):
     in_specs = (

time: 559 us -> 721 us (1.29)
  starting transfers between devices: 52.6 us -> 215 us
  waiting for transfers between devices: 284 us -> 198 us
  local copies, waits for them, and re-layouts: 27.1 us -> 82.7 us
  other arithmetic: 39.7 us -> 75.8 us
  between operations: 13.6 us -> 1.36 us
    ppermute x21, starting transfers between devices: 45.8 us -> 198 us  [per_device(): lax.ppermute(part, ('row', 'col'), pairs)]
    ppermute x2 -> x1, waiting for transfers between devices: 144 us -> 63.7 us  [product_to_owners(): lax.ppermute(value, ('layer', 'row'), [(a * size + b, b * size + quarter[...]
    ppermute x21, waiting for transfers between devices: 140 us -> 68.8 us  [per_device(): lax.ppermute(part, ('row', 'col'), pairs)]
    ppermute x0 -> x4, waiting for transfers between devices: none -> 65.4 us  [the longest x1 40 us: per_device(): lax.ppermute(theirs, ('layer', 'row'), [(a * 4 + b, b * 4 + quarter[a ^ 2...]
    reshape x0 -> x2, local copies, waits for them, and re-layouts: none -> 20 us  [the longest x1 10.9 us: per_device(): rows = arrived.transpose(1, 0, 2).reshape(half, layer_count * nu_local)]
    gather x1 -> x2, local copies, waits for them, and re-layouts: 15.9 us -> 32 us  [block_sparse_product(): padded = padded_blocks(blocks, block_rows, block_cols)[order]]
    ppermute x0 -> x1, local copies, waits for them, and re-layouts: none -> 9.44 us  [per_device(): lax.ppermute(part, 'layer', across)]
    all_to_all x0 -> x1, starting transfers between devices: none -> 9.13 us  [per_device(): arrived = lax.all_to_all(sent, 'layer', 0, 0)]
  transfers between devices with their start and end apart: 28 -> 30, of which waited for: 11 -> 11; matrix products, arithmetic and copies ran while one was open for 10% -> 18% of each run, Pallas kernels for 25% -> 11%
where the time goes in v13:
time: 721 us; the launch traced here: 712 us
  starting transfers between devices  215 us (30%)
  waiting for transfers between devices  198 us (27%)
  Pallas kernels  139 us (19%)
  local copies, waits for them, and re-layouts  82.7 us (11%)
  other arithmetic  75.8 us (11%)
    ppermute x21, starting transfers between devices, per_device(): lax.ppermute(part, ('row', 'col'), pairs)  198 us
    pallas_call x2, Pallas kernels, block_sparse_product(): pl.pallas_call(kernel, grid_spec=grid_spec, out_shape=jax.ShapeDtypeStruc...  121 us
    ppermute x21, waiting for transfers between devices, per_device(): lax.ppermute(part, ('row', 'col'), pairs)  68.8 us
    ppermute x1, waiting for transfers between devices, product_to_owners(): lax.ppermute(value, ('layer', 'row'), [(a * size + b, b * size + quarter[...  63.7 us
    ppermute x1, waiting for transfers between devices, per_device(): lax.ppermute(theirs, ('layer', 'row'), [(a * 4 + b, b * 4 + quarter[a ^ 2...  40 us
    gather x2, local copies, waits for them, and re-layouts, block_sparse_product(): padded = padded_blocks(blocks, block_rows, block_cols)[order]  32 us
    ppermute x3, waiting for transfers between devices, per_device(): lax.ppermute(part, 'layer', across)  25.4 us
    pallas_call x1, Pallas kernels, gathered_windows(): pl.pallas_call(kernel, grid_spec=grid_spec, out_shape=jax.ShapeDtypeStruc...  18.6 us
  transfers between devices with their start and end apart: 30, of which 11 were waited for; matrix products, arithmetic and copies ran while one was open for 18% of the time, Pallas kernels for 11%

profile of v13, /device:TPU:30, one launch (start us, length us, event | category | flops | bytes accessed | tf_op | source)
XLA Modules:
  0.0 712.1 jit_solution(7708365257855129317)
XLA Ops:
  2.8 9.2 %scatter_custom_fusion = s32[48]{0:T(128)S(1)} fusion(s32[1152]{0:T(1024)S(1)} %fusion.4, s32[1152]{0:T(1024)S(1)} %broadcast.344, s32[]{:T(128)} %constant.153.clone.1), kind=kCustom, calls=%fused_computation.116 | custom fusion | flops 1152 | bytes 196 | tf_op jit(solution)/shard_map/scatter-add | solution.py:133
  19.3 5.8 pad_maximum_fusion
  25.1 9.1 %all-to-all-start = ((bf16[4,512,3072]{2,1,0:T(8,128)(2,1)}), bf16[4,512,3072]{2,1,0:T(8,128)(2,1)}, u32[]{:S(2)}, u32[]{:S(2)}) async-start(bf16[4,512,3072]{2,1,0:T(8,128)(2,1)} %pad_maximum_fusion), calls=%async_computation | async-start | bytes 25165824 | tf_op jit(solution)/shard_map/all_to_all | solution.py:255
  36.3 18.6 %shard_map.55 = bf16[48,64,128]{2,1,0:T(8,128)(2,1)} custom-call(s32[48]{0:T(128)} %copy-done.1, s32[48]{0:T(128)} %and_select_fusion.cols_ref, bf16[1536,3072]{1,0:T(8,128)(2,1)} %green_ref.1), custom_call_target="tpu_custom_call" | custom-call | tf_op jit(solution)/shard_map/pallas_call | solution.py:122
  62.9 5.1 collective-permute-done.1
  68.0 25.5 %collective-permute-start.5 = (s32[48]{0:T(128)S(1)}, s32[48]{0:T(128)S(1)}, u32[]{:S(2)}, u32[]{:S(2)}) collective-permute-start(s32[48]{0:T(128)S(1)} %collective-permute-done), channel_id=1, source_target_pairs={{0,5},{1,6},{2,7},{3,0},{4,1},{5,2},{6,3},{7,4},{8,13},{9,14},{10,... | collective-permute-start | bytes 584 | tf_op jit(solution)/shard_map/ppermute | solution.py:233
  94.1 4.2 collective-permute-start.9
  111.3 3.8 sort.31
  124.0 68.3 %collective-permute-start.19 = (bf16[48,64,64]{2,1,0:T(8,128)(2,1)S(1)}, bf16[48,64,64]{2,1,0:T(8,128)(2,1)S(1)}, u32[]{:S(2)}, u32[]{:S(2)}) collective-permute-start(bf16[48,64,64]{2,1,0:T(8,128)(2,1)S(1)} %collective-permute-done.16), channel_id=1, source_target_pairs={{0,3},{1,4},{2,5},{3,6},{4,7},{5,0},{6,1},{7,2},{8,11},{9,12},{10,... | collective-permute-start | bytes 1179656 | tf_op jit(solution)/shard_map/ppermute | solution.py:233
  192.3 9.6 %collective-permute-start.20 = (bf16[48,64,64]{2,1,0:T(8,128)(2,1)S(1)}, bf16[48,64,64]{2,1,0:T(8,128)(2,1)S(1)}, u32[]{:S(2)}, u32[]{:S(2)}) collective-permute-start(bf16[48,64,64]{2,1,0:T(8,128)(2,1)S(1)} %collective-permute-done.16), channel_id=1, source_target_pairs={{0,4},{1,5},{2,6},{3,7},{4,0},{5,1},{6,2},{7,3},{8,12},{9,13},{10,... | collective-permute-start | bytes 1179656 | tf_op jit(solution)/shard_map/ppermute | solution.py:233
  203.3 5.7 collective-permute-start.21
  210.0 6.8 collective-permute-done.19
  216.7 71.4 %collective-permute-start.22 = (bf16[48,64,64]{2,1,0:T(8,128)(2,1)S(1)}, bf16[48,64,64]{2,1,0:T(8,128)(2,1)S(1)}, u32[]{:S(2)}, u32[]{:S(2)}) collective-permute-start(bf16[48,64,64]{2,1,0:T(8,128)(2,1)S(1)} %collective-permute-done.16), channel_id=1, source_target_pairs={{0,6},{1,7},{2,0},{3,1},{4,2},{5,3},{6,4},{7,5},{8,14},{9,15},{10,... | collective-permute-start | bytes 1179656 | tf_op jit(solution)/shard_map/ppermute | solution.py:233
  289.1 31.3 %collective-permute-done.20 = bf16[48,64,64]{2,1,0:T(8,128)(2,1)S(1)} collective-permute-done((bf16[48,64,64]{2,1,0:T(8,128)(2,1)S(1)}, bf16[48,64,64]{2,1,0:T(8,128)(2,1)S(1)}, u32[]{:S(2)}, u32[]{:S(2)}) %collective-permute-start.20) | collective-permute-done | bytes 393248 | tf_op jit(solution)/shard_map/ppermute | solution.py:233
  323.4 19.5 %collective-permute-done.23 = bf16[48,64,64]{2,1,0:T(8,128)(2,1)S(1)} collective-permute-done((bf16[48,64,64]{2,1,0:T(8,128)(2,1)S(1)}, bf16[48,64,64]{2,1,0:T(8,128)(2,1)S(1)}, u32[]{:S(2)}, u32[]{:S(2)}) %collective-permute-start.23) | collective-permute-done | bytes 393248 | tf_op jit(solution)/shard_map/ppermute | solution.py:233
  343.7 9.1 %copy.28 = bf16[384,64,64]{0,2,1:T(8,128)(2,1)} copy(bf16[384,64,64]{2,1,0:T(8,128)(2,1)} %bitcast.29) | data formatting | bytes 6291456 | tf_op jit(solution)/shard_map/reshape | solution.py:241
  366.5 4.2 broadcast_select_fusion.5
  370.8 6.4 broadcast_select_fusion.7
  377.2 5.2 pad_maximum_fusion.1
  382.4 16.0 %gather_fusion.3 = bf16[384,128,128]{2,1,0:T(8,128)(2,1)} fusion(bf16[384,128,128]{2,1,0:T(8,128)(2,1)} %pad_maximum_fusion.1, s32[1024]{0:T(1024)S(1)} %pad_clamp_fusion.2), kind=kCustom, calls=%fused_computation.3 | custom fusion | bytes 25167360 | tf_op jit(solution)/shard_map/gather | solution.py:164
  398.3 25.4 %collective-permute-done.27 = bf16[384,64,64]{0,2,1:T(8,128)(2,1)S(1)} collective-permute-done((bf16[384,64,64]{0,2,1:T(8,128)(2,1)}, bf16[384,64,64]{0,2,1:T(8,128)(2,1)S(1)}, u32[]{:S(2)}, u32[]{:S(2)}) %collective-permute-start.27) | collective-permute-done | bytes 3145760 | tf_op jit(solution)/shard_map/ppermute | solution.py:259
  423.7 9.4 %copy.29 = bf16[384,64,64]{2,1,0:T(8,128)(2,1)} copy(bf16[384,64,64]{0,2,1:T(8,128)(2,1)S(1)} %collective-permute-done.27) | data formatting | bytes 6291456 | tf_op jit(solution)/shard_map/ppermute | solution.py:259
  433.1 4.2 broadcast_select_fusion.1
  437.4 6.4 broadcast_select_fusion.3
  443.8 5.2 pad_maximum_fusion.2
  449.0 16.0 %gather_fusion.6 = bf16[384,128,128]{2,1,0:T(8,128)(2,1)} fusion(bf16[384,128,128]{2,1,0:T(8,128)(2,1)} %pad_maximum_fusion.2, s32[1024]{0:T(1024)S(1)} %pad_clamp_fusion), kind=kCustom, calls=%fused_computation.6 | custom fusion | bytes 25167360 | tf_op jit(solution)/shard_map/gather | solution.py:164
  465.0 10.9 %copy.31 = bf16[4,64,8,3072]{3,2,0,1:T(8,128)(2,1)} copy(bf16[4,64,8,3072]{3,2,1,0:T(8,128)(2,1)} %bitcast.31) | data formatting | bytes 25165824 | tf_op jit(solution)/shard_map/reshape | solution.py:256
  475.9 60.3 %shard_map.57 = bf16[512,3072]{1,0:T(8,128)(2,1)} custom-call(s32[25]{0:T(128)} %convert_reduce_fusion.starts_ref, s32[384]{0:T(512)} %add_select_fusion.3.k_ref, bf16[512,12288]{1,0:T(8,128)(2,1)} %bitcast.52, bf16[384,128,128]{2,1,0:T(8,128)(2,1)} %gather_fusion.6), custom_call_target="tpu_custom_call" | custom-call | tf_op jit(solution)/shard_map/pallas_call | solution.py:205
  538.2 60.3 %shard_map.56 = bf16[512,3072]{1,0:T(8,128)(2,1)} custom-call(s32[25]{0:T(128)} %convert_reduce_fusion.1.starts_ref, s32[384]{0:T(512)} %add_select_fusion.7.k_ref, bf16[512,12288]{1,0:T(8,128)(2,1)} %bitcast.53, bf16[384,128,128]{2,1,0:T(8,128)(2,1)} %gather_fusion.3), custom_call_target="tpu_custom_call" | custom-call | tf_op jit(solution)/shard_map/pallas_call | solution.py:205
  599.8 40.0 %collective-permute-done.28 = bf16[512,3072]{1,0:T(8,128)(2,1)S(1)} collective-permute-done((bf16[512,3072]{1,0:T(8,128)(2,1)}, bf16[512,3072]{1,0:T(8,128)(2,1)S(1)}, u32[]{:S(2)}, u32[]{:S(2)}) %collective-permute-start.28) | collective-permute-done | bytes 3145760 | tf_op jit(solution)/shard_map/ppermute | solution.py:265
  639.8 63.7 %collective-permute-done.24 = bf16[512,3072]{1,0:T(8,128)(2,1)} collective-permute-done((bf16[512,3072]{1,0:T(8,128)(2,1)}, bf16[512,3072]{1,0:T(8,128)(2,1)}, u32[]{:S(2)}, u32[]{:S(2)}) %collective-permute-start.24) | collective-permute-done | bytes 3145760 | tf_op jit(solution)/shard_map/ppermute | solution.py:103
  703.5 8.1 %fusion = bf16[128,8,3072]{2,1,0:T(8,128)(2,1)} fusion(bf16[512,3072]{1,0:T(8,128)(2,1)S(1)} %collective-permute-done.28, bf16[512,3072]{1,0:T(8,128)(2,1)} %collective-permute-done.24, pred[]{:T(512)} %bitcast), kind=kLoop, calls=%fused_computation.14 | loop fusion | flops 28311552 | bytes 12582913 | tf_op jit(solution)/shard_map/jit(_where)/select_n | solution.py:272
  (114 shorter events, 66.0 us)
Async XLA Ops:
  13.6 44.9 %collective-permute-start = (s32[48]{0:T(128)S(1)}, s32[48]{0:T(128)S(1)}, u32[]{:S(2)}, u32[]{:S(2)}) collective-permute-start(s32[48]{0:T(128)S(1)} %get-tuple-element.12), channel_id=1, source_target_pairs={{0,8},{2,24},{4,0},{6,16},{8,10},{10,26},{12,2},{14,18},{16,12},{1... | collective-permute-start | bytes 584 | tf_op jit(solution)/shard_map/ppermute | solution.py:94
  14.1 47.4 %collective-permute-start.8 = (s32[48]{0:T(128)S(1)}, s32[48]{0:T(128)S(1)}, u32[]{:S(2)}, u32[]{:S(2)}) collective-permute-start(s32[48]{0:T(128)S(1)} %and_select_fusion.2.rows_ref), channel_id=1, source_target_pairs={{0,8},{2,24},{4,0},{6,16},{8,10},{10,26},{12,2},{14,18},{16,12},{1... | collective-permute-start | bytes 584 | tf_op jit(solution)/shard_map/ppermute | solution.py:94
  25.1 9.6 %copy-start = (s32[24,48]{1,0:T(8,128)S(1)}, s32[24,48]{1,0:T(8,128)}, u32[]{:S(2)}) copy-start(s32[24,48]{1,0:T(8,128)} %param.8) | copy-start | bytes 13828
  25.1 439.9 %all-to-all-start = ((bf16[4,512,3072]{2,1,0:T(8,128)(2,1)}), bf16[4,512,3072]{2,1,0:T(8,128)(2,1)}, u32[]{:S(2)}, u32[]{:S(2)}) async-start(bf16[4,512,3072]{2,1,0:T(8,128)(2,1)} %pad_maximum_fusion), calls=%async_computation | async-start | bytes 25165824 | tf_op jit(solution)/shard_map/all_to_all | solution.py:255
  56.7 61.9 %collective-permute-start.16 = (bf16[48,64,64]{2,1,0:T(8,128)(2,1)S(1)}, bf16[48,64,64]{2,1,0:T(8,128)(2,1)S(1)}, u32[]{:S(2)}, u32[]{:S(2)}) collective-permute-start(bf16[48,64,64]{2,1,0:T(8,128)(2,1)S(1)} %fusion.1), channel_id=1, source_target_pairs={{0,8},{2,24},{4,0},{6,16},{8,10},{10,26},{12,2},{14,18},{16,12},{1... | collective-permute-start | bytes 1179656 | tf_op jit(solution)/shard_map/ppermute | solution.py:94
  58.4 9.6 %collective-permute-start.1 = (s32[48]{0:T(128)S(1)}, s32[48]{0:T(128)S(1)}, u32[]{:S(2)}, u32[]{:S(2)}) collective-permute-start(s32[48]{0:T(128)S(1)} %collective-permute-done), channel_id=1, source_target_pairs={{0,1},{1,2},{2,3},{3,4},{4,5},{5,6},{6,7},{7,0},{8,9},{9,10},{10,1... | collective-permute-start | bytes 584 | tf_op jit(solution)/shard_map/ppermute | solution.py:233
  58.5 35.0 %collective-permute-start.2 = (s32[48]{0:T(128)S(1)}, s32[48]{0:T(128)S(1)}, u32[]{:S(2)}, u32[]{:S(2)}) collective-permute-start(s32[48]{0:T(128)S(1)} %collective-permute-done), channel_id=1, source_target_pairs={{0,2},{1,3},{2,4},{3,5},{4,6},{5,7},{6,0},{7,1},{8,10},{9,11},{10,... | collective-permute-start | bytes 584 | tf_op jit(solution)/shard_map/ppermute | solution.py:233
  59.4 34.1 %collective-permute-start.3 = (s32[48]{0:T(128)S(1)}, s32[48]{0:T(128)S(1)}, u32[]{:S(2)}, u32[]{:S(2)}) collective-permute-start(s32[48]{0:T(128)S(1)} %collective-permute-done), channel_id=1, source_target_pairs={{0,3},{1,4},{2,5},{3,6},{4,7},{5,0},{6,1},{7,2},{8,11},{9,12},{10,... | collective-permute-start | bytes 584 | tf_op jit(solution)/shard_map/ppermute | solution.py:233
  61.4 32.6 %collective-permute-start.4 = (s32[48]{0:T(128)S(1)}, s32[48]{0:T(128)S(1)}, u32[]{:S(2)}, u32[]{:S(2)}) collective-permute-start(s32[48]{0:T(128)S(1)} %collective-permute-done), channel_id=1, source_target_pairs={{0,4},{1,5},{2,6},{3,7},{4,0},{5,1},{6,2},{7,3},{8,12},{9,13},{10,... | collective-permute-start | bytes 584 | tf_op jit(solution)/shard_map/ppermute | solution.py:233
  68.0 30.3 %collective-permute-start.5 = (s32[48]{0:T(128)S(1)}, s32[48]{0:T(128)S(1)}, u32[]{:S(2)}, u32[]{:S(2)}) collective-permute-start(s32[48]{0:T(128)S(1)} %collective-permute-done), channel_id=1, source_target_pairs={{0,5},{1,6},{2,7},{3,0},{4,1},{5,2},{6,3},{7,4},{8,13},{9,14},{10,... | collective-permute-start | bytes 584 | tf_op jit(solution)/shard_map/ppermute | solution.py:233
  93.5 6.8 collective-permute-start.6
  93.5 6.8 collective-permute-start.7
  94.1 7.8 %collective-permute-start.9 = (s32[48]{0:T(128)S(1)}, s32[48]{0:T(128)S(1)}, u32[]{:S(2)}, u32[]{:S(2)}) collective-permute-start(s32[48]{0:T(128)S(1)} %collective-permute-done.8), channel_id=1, source_target_pairs={{0,1},{1,2},{2,3},{3,4},{4,5},{5,6},{6,7},{7,0},{8,9},{9,10},{10,1... | collective-permute-start | bytes 584 | tf_op jit(solution)/shard_map/ppermute | solution.py:233
  98.3 5.1 collective-permute-start.10
  100.3 4.6 collective-permute-start.11
  100.3 5.2 collective-permute-start.12
  101.9 5.4 collective-permute-start.13
  103.4 5.3 collective-permute-start.14
  104.9 6.2 collective-permute-start.15
  105.4 250.4 %collective-permute-start.25 = (s32[384]{0:T(512)S(1)}, s32[384]{0:T(512)S(1)}, u32[]{:S(2)}, u32[]{:S(2)}) collective-permute-start(s32[384]{0:T(512)S(1)} %reshape.230), channel_id=1, source_target_pairs={{0,16},{8,24},{16,0},{24,8},{1,17},{9,25},{17,1},{25,9},{2,18},{10... | collective-permute-start | bytes 4616 | tf_op jit(solution)/shard_map/ppermute | solution.py:259
  111.3 251.1 %collective-permute-start.26 = (s32[384]{0:T(512)S(1)}, s32[384]{0:T(512)S(1)}, u32[]{:S(2)}, u32[]{:S(2)}) collective-permute-start(s32[384]{0:T(512)S(1)} %add.148), channel_id=1, source_target_pairs={{0,16},{8,24},{16,0},{24,8},{1,17},{9,25},{17,1},{25,9},{2,18},{10... | collective-permute-start | bytes 4616 | tf_op jit(solution)/shard_map/ppermute | solution.py:259
  118.5 73.8 %collective-permute-start.17 = (bf16[48,64,64]{2,1,0:T(8,128)(2,1)S(1)}, bf16[48,64,64]{2,1,0:T(8,128)(2,1)S(1)}, u32[]{:S(2)}, u32[]{:S(2)}) collective-permute-start(bf16[48,64,64]{2,1,0:T(8,128)(2,1)S(1)} %collective-permute-done.16), channel_id=1, source_target_pairs={{0,1},{1,2},{2,3},{3,4},{4,5},{5,6},{6,7},{7,0},{8,9},{9,10},{10,1... | collective-permute-start | bytes 1179656 | tf_op jit(solution)/shard_map/ppermute | solution.py:233
  122.6 80.7 %collective-permute-start.18 = (bf16[48,64,64]{2,1,0:T(8,128)(2,1)S(1)}, bf16[48,64,64]{2,1,0:T(8,128)(2,1)S(1)}, u32[]{:S(2)}, u32[]{:S(2)}) collective-permute-start(bf16[48,64,64]{2,1,0:T(8,128)(2,1)S(1)} %collective-permute-done.16), channel_id=1, source_target_pairs={{0,2},{1,3},{2,4},{3,5},{4,6},{5,7},{6,0},{7,1},{8,10},{9,11},{10,... | collective-permute-start | bytes 1179656 | tf_op jit(solution)/shard_map/ppermute | solution.py:233
  124.0 92.7 %collective-permute-start.19 = (bf16[48,64,64]{2,1,0:T(8,128)(2,1)S(1)}, bf16[48,64,64]{2,1,0:T(8,128)(2,1)S(1)}, u32[]{:S(2)}, u32[]{:S(2)}) collective-permute-start(bf16[48,64,64]{2,1,0:T(8,128)(2,1)S(1)} %collective-permute-done.16), channel_id=1, source_target_pairs={{0,3},{1,4},{2,5},{3,6},{4,7},{5,0},{6,1},{7,2},{8,11},{9,12},{10,... | collective-permute-start | bytes 1179656 | tf_op jit(solution)/shard_map/ppermute | solution.py:233
  192.3 128.1 %collective-permute-start.20 = (bf16[48,64,64]{2,1,0:T(8,128)(2,1)S(1)}, bf16[48,64,64]{2,1,0:T(8,128)(2,1)S(1)}, u32[]{:S(2)}, u32[]{:S(2)}) collective-permute-start(bf16[48,64,64]{2,1,0:T(8,128)(2,1)S(1)} %collective-permute-done.16), channel_id=1, source_target_pairs={{0,4},{1,5},{2,6},{3,7},{4,0},{5,1},{6,2},{7,3},{8,12},{9,13},{10,... | collective-permute-start | bytes 1179656 | tf_op jit(solution)/shard_map/ppermute | solution.py:233
  203.3 118.2 %collective-permute-start.21 = (bf16[48,64,64]{2,1,0:T(8,128)(2,1)S(1)}, bf16[48,64,64]{2,1,0:T(8,128)(2,1)S(1)}, u32[]{:S(2)}, u32[]{:S(2)}) collective-permute-start(bf16[48,64,64]{2,1,0:T(8,128)(2,1)S(1)} %collective-permute-done.16), channel_id=1, source_target_pairs={{0,5},{1,6},{2,7},{3,0},{4,1},{5,2},{6,3},{7,4},{8,13},{9,14},{10,... | collective-permute-start | bytes 1179656 | tf_op jit(solution)/shard_map/ppermute | solution.py:233
  216.7 105.7 %collective-permute-start.22 = (bf16[48,64,64]{2,1,0:T(8,128)(2,1)S(1)}, bf16[48,64,64]{2,1,0:T(8,128)(2,1)S(1)}, u32[]{:S(2)}, u32[]{:S(2)}) collective-permute-start(bf16[48,64,64]{2,1,0:T(8,128)(2,1)S(1)} %collective-permute-done.16), channel_id=1, source_target_pairs={{0,6},{1,7},{2,0},{3,1},{4,2},{5,3},{6,4},{7,5},{8,14},{9,15},{10,... | collective-permute-start | bytes 1179656 | tf_op jit(solution)/shard_map/ppermute | solution.py:233
  320.4 22.4 %collective-permute-start.23 = (bf16[48,64,64]{2,1,0:T(8,128)(2,1)S(1)}, bf16[48,64,64]{2,1,0:T(8,128)(2,1)S(1)}, u32[]{:S(2)}, u32[]{:S(2)}) collective-permute-start(bf16[48,64,64]{2,1,0:T(8,128)(2,1)S(1)} %collective-permute-done.16), channel_id=1, source_target_pairs={{0,7},{1,0},{2,1},{3,2},{4,3},{5,4},{6,5},{7,6},{8,15},{9,8},{10,9... | collective-permute-start | bytes 1179656 | tf_op jit(solution)/shard_map/ppermute | solution.py:233
  352.8 70.9 %collective-permute-start.27 = (bf16[384,64,64]{0,2,1:T(8,128)(2,1)}, bf16[384,64,64]{0,2,1:T(8,128)(2,1)S(1)}, u32[]{:S(2)}, u32[]{:S(2)}) collective-permute-start(bf16[384,64,64]{0,2,1:T(8,128)(2,1)} %copy.28), channel_id=1, source_target_pairs={{0,16},{8,24},{16,0},{24,8},{1,17},{9,25},{17,1},{25,9},{2,18},{10... | collective-permute-start | bytes 9437192 | tf_op jit(solution)/shard_map/ppermute | solution.py:259
  536.2 62.4 %copy-start.2 = (s32[4]{0:T(128)S(1)}, s32[4]{0:T(128)}, u32[]{:S(2)}) copy-start(s32[4]{0:T(128)} %constant.166.clone) | copy-start | bytes 52
  536.2 103.7 %collective-permute-start.28 = (bf16[512,3072]{1,0:T(8,128)(2,1)}, bf16[512,3072]{1,0:T(8,128)(2,1)S(1)}, u32[]{:S(2)}, u32[]{:S(2)}) collective-permute-start(bf16[512,3072]{1,0:T(8,128)(2,1)} %shard_map.57), channel_id=1, source_target_pairs={{0,6},{2,14},{4,22},{6,30},{8,2},{10,10},{12,18},{14,26},{16,4},{1... | collective-permute-start | bytes 9437192 | tf_op jit(solution)/shard_map/ppermute | solution.py:265
  598.5 105.0 %collective-permute-start.24 = (bf16[512,3072]{1,0:T(8,128)(2,1)}, bf16[512,3072]{1,0:T(8,128)(2,1)}, u32[]{:S(2)}, u32[]{:S(2)}) collective-permute-start(bf16[512,3072]{1,0:T(8,128)(2,1)} %shard_map.56), channel_id=1, source_target_pairs={{0,4},{2,12},{4,20},{6,28},{8,0},{10,8},{12,16},{14,24},{16,6},{18... | collective-permute-start | bytes 9437192 | tf_op jit(solution)/shard_map/ppermute | solution.py:103
  (1 other events, 4.8 us)

commit v14 on v12

--- a/solution.py
+++ b/solution.py
@@ -214,7 +214,7 @@
 def per_device(tensor, tensor_pattern, green, green_pattern):
     layer_count = lax.axis_size("layer")
     row_count = lax.axis_size("row")
-    if layer_count != row_count:
+    if layer_count != row_count or max(green_pattern.shape) > 256:
         return cannon_per_device(tensor, tensor_pattern, green, green_pattern)
     ri_local, mu_local, nu_local = tensor.shape
     tile_rows, tile_cols = green_pattern.shape
@@ -224,16 +224,20 @@
     layer_index = lax.axis_index("layer")
     col_count = lax.axis_size("col")
     blocks, block_row, block_col = compressed_tile(green, green_pattern)
-    parts = tuple(green_to_layers(part, row_count) for part in (blocks, block_row, block_col))
+    marks = jnp.zeros((blocks.shape[0], 16, BLK), jnp.bfloat16)
+    marks = marks.at[:, 0, 0].set(block_row.astype(jnp.bfloat16))
+    marks = marks.at[:, 0, 1].set(block_col.astype(jnp.bfloat16))
+    packed = green_to_layers(jnp.concatenate([blocks, marks], axis=1), row_count)
     group = row_count * col_count
     me = lax.axis_index("row") * col_count + lax.axis_index("col")
-    received = [parts]
+    received = [packed]
     for shift in range(1, group):
         pairs = [(i, (i + shift) % group) for i in range(group)]
-        received.append(tuple(lax.ppermute(part, ("row", "col"), pairs) for part in parts))
-    blocks, block_row, block_col = (
-        jnp.stack([got[k] for got in received]) for k in range(len(parts))
-    )
+        received.append(lax.ppermute(packed, ("row", "col"), pairs))
+    packed = jnp.stack(received)
+    blocks = packed[:, :, :BLK, :]
+    block_row = packed[:, :, BLK, 0].astype(jnp.int32)
+    block_col = packed[:, :, BLK, 1].astype(jnp.int32)
     band = ((me - jnp.arange(group)) % group)[:, None]
     entry_rows = band * tile_rows + block_row
     entry_rows = entry_rows.reshape(-1)

time: 559 us -> 587 us (1.050); the launches traced: 556 us -> 578 us
  local copies, waits for them, and re-layouts: 27.1 us -> 48.5 us
  other arithmetic: 39.7 us -> 59.9 us
  waiting for transfers between devices: 284 us -> 272 us
  starting transfers between devices: 52.6 us -> 45.2 us
    ppermute x21 -> x7, waiting for transfers between devices: 140 us -> 115 us  [per_device(): received.append(lax.ppermute(packed, ('row', 'col'), pairs))]
    convert_element_type x0 -> x3, other arithmetic: none -> 17.1 us  [the longest x1 16.1 us: per_device(): block_row = packed[:, :, BLK, 0].astype(jnp.int32)]
    ppermute x3 -> x1, waiting for transfers between devices: 0.01 us -> 9.51 us  [green_to_layers(): lax.ppermute(value, ('layer', 'row'), [(a * size + b, inverse[b] * size +...]
    slice x1, local copies, waits for them, and re-layouts: 0.08 us -> 8.71 us  [per_device(): blocks = packed[:, :, :BLK, :]]
    ppermute x21 -> x7, starting transfers between devices: 45.8 us -> 40.6 us  [per_device(): received.append(lax.ppermute(packed, ('row', 'col'), pairs))]
  transfers between devices with their start and end apart: 28 -> 12, of which waited for: 11 -> 6; matrix products, arithmetic and copies ran while one was open for 10% -> 17% of each run, Pallas kernels for 25% -> 24%
where the time goes in v14:
time: 587 us; the launch traced here: 578 us
  waiting for transfers between devices  272 us (46%)
  Pallas kernels  138 us (24%)
  other arithmetic  59.9 us (10%)
  local copies, waits for them, and re-layouts  48.5 us (8%)
  starting transfers between devices  45.2 us (8%)
  between operations  14 us (2%)
    ppermute x2, waiting for transfers between devices, product_to_owners(): lax.ppermute(value, ('layer', 'row'), [(a * size + b, b * size + quarter[...  146 us
    pallas_call x2, Pallas kernels, block_sparse_product(): pl.pallas_call(kernel, grid_spec=grid_spec, out_shape=jax.ShapeDtypeStruc...  120 us
    ppermute x7, waiting for transfers between devices, per_device(): received.append(lax.ppermute(packed, ('row', 'col'), pairs))  115 us
    ppermute x7, starting transfers between devices, per_device(): received.append(lax.ppermute(packed, ('row', 'col'), pairs))  40.6 us
    pallas_call x1, Pallas kernels, gathered_windows(): pl.pallas_call(kernel, grid_spec=grid_spec, out_shape=jax.ShapeDtypeStruc...  18.4 us
    convert_element_type x1, other arithmetic, per_device(): block_row = packed[:, :, BLK, 0].astype(jnp.int32)  16.1 us
    gather x1, local copies, waits for them, and re-layouts, block_sparse_product(): padded = padded_blocks(blocks, block_rows, block_cols)[order]  16 us
  transfers between devices with their start and end apart: 12, of which 6 were waited for; matrix products, arithmetic and copies ran while one was open for 17% of the time, Pallas kernels for 24%

profile of v14, /device:TPU:30, one launch (start us, length us, event | category | flops | bytes accessed | tf_op | source)
XLA Modules:
  0.0 577.9 jit_solution(8808790240783469442)
XLA Ops:
  7.5 3.2 broadcast_multiply_fusion
  10.7 3.0 slice_bitcast_fusion.1
  15.3 9.2 %scatter_custom_fusion = s32[48]{0:T(128)S(1)} fusion(s32[1152]{0:T(1024)S(1)} %fusion.7, s32[1152]{0:T(1024)S(1)} %broadcast.456, s32[]{:T(128)} %constant.189.clone.1), kind=kCustom, calls=%fused_computation.90 | custom fusion | flops 1152 | bytes 196 | tf_op jit(solution)/shard_map/scatter-add | solution.py:133
  29.0 18.4 %shard_map.46 = bf16[48,64,128]{2,1,0:T(8,128)(2,1)} custom-call(s32[48]{0:T(128)} %get-tuple-element.49.rows_ref, s32[48]{0:T(128)} %get-tuple-element.48.cols_ref, bf16[1536,3072]{1,0:T(8,128)(2,1)} %green_ref.1), custom_call_target="tpu_custom_call" | custom-call | tf_op jit(solution)/shard_map/pallas_call | solution.py:122
  48.0 4.8 scatter.9
  53.5 1.8 fusion
  56.1 4.5 collective-permute-start
  60.6 9.5 %collective-permute-done = bf16[48,80,64]{1,2,0:T(8,128)(2,1)S(1)} collective-permute-done((bf16[48,80,64]{1,2,0:T(8,128)(2,1)S(1)}, bf16[48,80,64]{1,2,0:T(8,128)(2,1)S(1)}, u32[]{:S(2)}, u32[]{:S(2)}) %collective-permute-start) | collective-permute-done | bytes 491552 | tf_op jit(solution)/shard_map/ppermute | solution.py:94
  70.1 8.3 %collective-permute-start.1 = (bf16[48,80,64]{1,2,0:T(8,128)(2,1)S(1)}, bf16[48,80,64]{1,2,0:T(8,128)(2,1)S(1)}, u32[]{:S(2)}, u32[]{:S(2)}) collective-permute-start(bf16[48,80,64]{1,2,0:T(8,128)(2,1)S(1)} %collective-permute-done), channel_id=1, source_target_pairs={{0,1},{1,2},{2,3},{3,4},{4,5},{5,6},{6,7},{7,0},{8,9},{9,10},{10,1... | collective-permute-start | bytes 1474568 | tf_op jit(solution)/shard_map/ppermute | solution.py:236
  78.6 14.6 %collective-permute-start.2 = (bf16[48,80,64]{1,2,0:T(8,128)(2,1)S(1)}, bf16[48,80,64]{1,2,0:T(8,128)(2,1)S(1)}, u32[]{:S(2)}, u32[]{:S(2)}) collective-permute-start(bf16[48,80,64]{1,2,0:T(8,128)(2,1)S(1)} %collective-permute-done), channel_id=1, source_target_pairs={{0,2},{1,3},{2,4},{3,5},{4,6},{5,7},{6,0},{7,1},{8,10},{9,11},{10,... | collective-permute-start | bytes 1474568 | tf_op jit(solution)/shard_map/ppermute | solution.py:236
  93.2 3.8 collective-permute-start.3
  97.0 1.5 collective-permute-start.5
  98.5 0.9 bitcast_dynamic-update-slice_fusion.7
  99.4 12.4 %collective-permute-start.6 = (bf16[48,80,64]{1,2,0:T(8,128)(2,1)S(1)}, bf16[48,80,64]{1,2,0:T(8,128)(2,1)S(1)}, u32[]{:S(2)}, u32[]{:S(2)}) collective-permute-start(bf16[48,80,64]{1,2,0:T(8,128)(2,1)S(1)} %collective-permute-done), channel_id=1, source_target_pairs={{0,6},{1,7},{2,0},{3,1},{4,2},{5,3},{6,4},{7,5},{8,14},{9,15},{10,... | collective-permute-start | bytes 1474568 | tf_op jit(solution)/shard_map/ppermute | solution.py:236
  112.8 15.4 %collective-permute-done.2 = bf16[48,80,64]{1,2,0:T(8,128)(2,1)S(1)} collective-permute-done((bf16[48,80,64]{1,2,0:T(8,128)(2,1)S(1)}, bf16[48,80,64]{1,2,0:T(8,128)(2,1)S(1)}, u32[]{:S(2)}, u32[]{:S(2)}) %collective-permute-start.2) | collective-permute-done | bytes 491552 | tf_op jit(solution)/shard_map/ppermute | solution.py:236
  128.2 0.9 bitcast_dynamic-update-slice_fusion.5
  129.2 0.9 bitcast_dynamic-update-slice_fusion.4
  130.1 99.5 %collective-permute-done.4 = bf16[48,80,64]{1,2,0:T(8,128)(2,1)S(1)} collective-permute-done((bf16[48,80,64]{1,2,0:T(8,128)(2,1)S(1)}, bf16[48,80,64]{1,2,0:T(8,128)(2,1)S(1)}, u32[]{:S(2)}, u32[]{:S(2)}) %collective-permute-start.4) | collective-permute-done | bytes 491552 | tf_op jit(solution)/shard_map/ppermute | solution.py:236
  233.8 8.7 %copy.34 = bf16[8,48,64,64]{3,2,1,0:T(8,128)(2,1)} copy(bf16[8,48,64,64]{2,3,1,0:T(8,128)(2,1)} %bitcast.35) | data formatting | bytes 6291456 | tf_op jit(solution)/shard_map/slice | solution.py:238
  242.6 16.1 %fusion.1 = (s32[8,48]{1,0:T(8,128)S(1)}, s32[8,48]{1,0:T(8,128)S(1)}) fusion(bf16[8,48,80,64]{2,3,1,0:T(8,128)(2,1)} %bitcast_dynamic-update-slice_fusion), kind=kLoop, calls=%fused_computation.27 | loop fusion | flops 768 | bytes 4608 | tf_op jit(solution)/shard_map/convert_element_type | solution.py:239
  258.9 3.8 sort.19
  262.7 2.8 gather_fusion.1
  265.5 4.3 bitcast_select_fusion.1
  269.8 6.4 %broadcast_select_fusion.1 = (bf16[384,64,128]{2,1,0:T(8,128)(2,1)S(1)}, bf16[384,64,128]{2,1,0:T(8,128)(2,1)S(1)}) fusion(pred[384]{0:T(512)(128)(4,1)S(1)} %get-tuple-element.35, bf16[384,64,64]{2,1,0:T(8,128)(2,1)S(1)} %get-tuple-element.44, bf16[384,64,64]{2,1,0:T(8,128)(2,1)S(1)} %get-tuple-element.43), kind=kLoop, calls=%fused_computation.11 | loop fusion | flops 18874368 | bytes 18874752 | tf_op jit(solution)/shard_map/jit(_where)/select_n | solution.py:151
  276.2 5.2 pad_maximum_fusion
  281.4 16.0 %gather_fusion.3 = bf16[384,128,128]{2,1,0:T(8,128)(2,1)} fusion(bf16[384,128,128]{2,1,0:T(8,128)(2,1)} %pad_maximum_fusion, s32[1024]{0:T(1024)S(1)} %pad_clamp_fusion), kind=kCustom, calls=%fused_computation.3 | custom fusion | bytes 25167360 | tf_op jit(solution)/shard_map/gather | solution.py:164
  297.3 2.8 gather_fusion.2
  301.3 60.1 %shard_map.47 = bf16[512,3072]{1,0:T(8,128)(2,1)} custom-call(s32[25]{0:T(128)} %convert_reduce_fusion.starts_ref, s32[384]{0:T(512)} %add_select_fusion.3.k_ref, bf16[512,12288]{1,0:T(8,128)(2,1)} %all-gather.3.cloned.1.call-done.t_ref, bf16[384,128,128]{2,1,0:T(8,128)(2,1)} %gather_fusion.3), custom_call_target="tpu_custom_call" | custom-call | tf_op jit(solution)/shard_map/pallas_call | solution.py:205
  361.4 59.9 %shard_map.48 = bf16[512,3072]{1,0:T(8,128)(2,1)} custom-call(s32[25]{0:T(128)} %convert_reduce_fusion.starts_ref, s32[384]{0:T(512)} %add_select_fusion.3.k_ref, bf16[512,12288]{1,0:T(8,128)(2,1)} %all-gather.5.cloned.1.call-done.t_ref, bf16[384,128,128]{2,1,0:T(8,128)(2,1)} %gather_fusion.3), custom_call_target="tpu_custom_call" | custom-call | tf_op jit(solution)/shard_map/pallas_call | solution.py:205
  421.3 112.4 %collective-permute-done.8 = bf16[512,3072]{1,0:T(8,128)(2,1)S(1)} collective-permute-done((bf16[512,3072]{1,0:T(8,128)(2,1)}, bf16[512,3072]{1,0:T(8,128)(2,1)S(1)}, u32[]{:S(2)}, u32[]{:S(2)}) %collective-permute-start.8) | collective-permute-done | bytes 3145760 | tf_op jit(solution)/shard_map/ppermute | solution.py:103
  533.7 33.7 %collective-permute-done.9 = bf16[512,3072]{1,0:T(8,128)(2,1)S(1)} collective-permute-done((bf16[512,3072]{1,0:T(8,128)(2,1)}, bf16[512,3072]{1,0:T(8,128)(2,1)S(1)}, u32[]{:S(2)}, u32[]{:S(2)}) %collective-permute-start.9) | collective-permute-done | bytes 3145760 | tf_op jit(solution)/shard_map/ppermute | solution.py:103
  567.4 3.1 maximum_bitcast_fusion
  (64 shorter events, 15.7 us)
Async XLA Ops:
  6.5 294.8 %all-gather.3.cloned.1.call-start = ((), (), s32[]{:S(2)}) async-start(), calls=%async_computation | async-start | bytes 15728640 | tf_op jit(solution)/shard_map/all_gather | solution.py:248
  13.7 0.8 copy-start
  13.7 347.7 %all-gather.5.cloned.1.call-start = ((), (), s32[]{:S(2)}) async-start(), calls=%async_computation.1 | async-start | bytes 15728640 | tf_op jit(solution)/shard_map/all_gather | solution.py:248
  56.1 14.0 %collective-permute-start = (bf16[48,80,64]{1,2,0:T(8,128)(2,1)S(1)}, bf16[48,80,64]{1,2,0:T(8,128)(2,1)S(1)}, u32[]{:S(2)}, u32[]{:S(2)}) collective-permute-start(bf16[48,80,64]{1,2,0:T(8,128)(2,1)S(1)} %copy.33), channel_id=1, source_target_pairs={{0,8},{2,24},{4,0},{6,16},{8,10},{10,26},{12,2},{14,18},{16,12},{1... | collective-permute-start | bytes 1474568 | tf_op jit(solution)/shard_map/ppermute | solution.py:94
  70.1 29.3 %collective-permute-start.1 = (bf16[48,80,64]{1,2,0:T(8,128)(2,1)S(1)}, bf16[48,80,64]{1,2,0:T(8,128)(2,1)S(1)}, u32[]{:S(2)}, u32[]{:S(2)}) collective-permute-start(bf16[48,80,64]{1,2,0:T(8,128)(2,1)S(1)} %collective-permute-done), channel_id=1, source_target_pairs={{0,1},{1,2},{2,3},{3,4},{4,5},{5,6},{6,7},{7,0},{8,9},{9,10},{10,1... | collective-permute-start | bytes 1474568 | tf_op jit(solution)/shard_map/ppermute | solution.py:236
  78.6 49.7 %collective-permute-start.2 = (bf16[48,80,64]{1,2,0:T(8,128)(2,1)S(1)}, bf16[48,80,64]{1,2,0:T(8,128)(2,1)S(1)}, u32[]{:S(2)}, u32[]{:S(2)}) collective-permute-start(bf16[48,80,64]{1,2,0:T(8,128)(2,1)S(1)} %collective-permute-done), channel_id=1, source_target_pairs={{0,2},{1,3},{2,4},{3,5},{4,6},{5,7},{6,0},{7,1},{8,10},{9,11},{10,... | collective-permute-start | bytes 1474568 | tf_op jit(solution)/shard_map/ppermute | solution.py:236
  93.2 36.0 %collective-permute-start.3 = (bf16[48,80,64]{1,2,0:T(8,128)(2,1)S(1)}, bf16[48,80,64]{1,2,0:T(8,128)(2,1)S(1)}, u32[]{:S(2)}, u32[]{:S(2)}) collective-permute-start(bf16[48,80,64]{1,2,0:T(8,128)(2,1)S(1)} %collective-permute-done), channel_id=1, source_target_pairs={{0,3},{1,4},{2,5},{3,6},{4,7},{5,0},{6,1},{7,2},{8,11},{9,12},{10,... | collective-permute-start | bytes 1474568 | tf_op jit(solution)/shard_map/ppermute | solution.py:236
  97.0 132.6 %collective-permute-start.4 = (bf16[48,80,64]{1,2,0:T(8,128)(2,1)S(1)}, bf16[48,80,64]{1,2,0:T(8,128)(2,1)S(1)}, u32[]{:S(2)}, u32[]{:S(2)}) collective-permute-start(bf16[48,80,64]{1,2,0:T(8,128)(2,1)S(1)} %collective-permute-done), channel_id=1, source_target_pairs={{0,4},{1,5},{2,6},{3,7},{4,0},{5,1},{6,2},{7,3},{8,12},{9,13},{10,... | collective-permute-start | bytes 1474568 | tf_op jit(solution)/shard_map/ppermute | solution.py:236
  97.0 134.0 %collective-permute-start.5 = (bf16[48,80,64]{1,2,0:T(8,128)(2,1)S(1)}, bf16[48,80,64]{1,2,0:T(8,128)(2,1)S(1)}, u32[]{:S(2)}, u32[]{:S(2)}) collective-permute-start(bf16[48,80,64]{1,2,0:T(8,128)(2,1)S(1)} %collective-permute-done), channel_id=1, source_target_pairs={{0,5},{1,6},{2,7},{3,0},{4,1},{5,2},{6,3},{7,4},{8,13},{9,14},{10,... | collective-permute-start | bytes 1474568 | tf_op jit(solution)/shard_map/ppermute | solution.py:236
  99.4 132.5 %collective-permute-start.6 = (bf16[48,80,64]{1,2,0:T(8,128)(2,1)S(1)}, bf16[48,80,64]{1,2,0:T(8,128)(2,1)S(1)}, u32[]{:S(2)}, u32[]{:S(2)}) collective-permute-start(bf16[48,80,64]{1,2,0:T(8,128)(2,1)S(1)} %collective-permute-done), channel_id=1, source_target_pairs={{0,6},{1,7},{2,0},{3,1},{4,2},{5,3},{6,4},{7,5},{8,14},{9,15},{10,... | collective-permute-start | bytes 1474568 | tf_op jit(solution)/shard_map/ppermute | solution.py:236
  128.2 104.7 %collective-permute-start.7 = (bf16[48,80,64]{1,2,0:T(8,128)(2,1)S(1)}, bf16[48,80,64]{1,2,0:T(8,128)(2,1)S(1)}, u32[]{:S(2)}, u32[]{:S(2)}) collective-permute-start(bf16[48,80,64]{1,2,0:T(8,128)(2,1)S(1)} %collective-permute-done), channel_id=1, source_target_pairs={{0,7},{1,0},{2,1},{3,2},{4,3},{5,4},{6,5},{7,6},{8,15},{9,8},{10,9... | collective-permute-start | bytes 1474568 | tf_op jit(solution)/shard_map/ppermute | solution.py:236
  361.4 172.3 %collective-permute-start.8 = (bf16[512,3072]{1,0:T(8,128)(2,1)}, bf16[512,3072]{1,0:T(8,128)(2,1)S(1)}, u32[]{:S(2)}, u32[]{:S(2)}) collective-permute-start(bf16[512,3072]{1,0:T(8,128)(2,1)} %shard_map.47), channel_id=1, source_target_pairs={{0,4},{2,12},{4,20},{6,28},{8,0},{10,8},{12,16},{14,24},{16,6},{18... | collective-permute-start | bytes 9437192 | tf_op jit(solution)/shard_map/ppermute | solution.py:103
  421.3 146.1 %collective-permute-start.9 = (bf16[512,3072]{1,0:T(8,128)(2,1)}, bf16[512,3072]{1,0:T(8,128)(2,1)S(1)}, u32[]{:S(2)}, u32[]{:S(2)}) collective-permute-start(bf16[512,3072]{1,0:T(8,128)(2,1)} %shard_map.48), channel_id=1, source_target_pairs={{0,4},{2,12},{4,20},{6,28},{8,0},{10,8},{12,16},{14,24},{16,6},{18... | collective-permute-start | bytes 9437192 | tf_op jit(solution)/shard_map/ppermute | solution.py:103
Sparse Core Ops, SparseCore 0:
  13.9 96.0 all-gather.2
  111.5 84.9 all-gather.4

commit v15 on v12

--- a/solution.py
+++ b/solution.py
@@ -8,7 +8,7 @@
 BLK = 64
 CAP = 48
 LANE = 128
-ROW_CHUNK = 512
+ROW_CHUNK = 256
 
 
 def passed_along(value, axis, by):

time: 559 us -> 545 us (0.975)
  waiting for transfers between devices: 284 us -> 213 us
  Pallas kernels: 139 us -> 193 us
    ppermute x2 -> x4, waiting for transfers between devices: 144 us -> 71.8 us  [product_to_owners(): lax.ppermute(value, ('layer', 'row'), [(a * size + b, b * size + quarter[...]
    pallas_call x2 -> x4, Pallas kernels: 121 us -> 176 us  [block_sparse_product(): pl.pallas_call(kernel, grid_spec=grid_spec, out_shape=jax.ShapeDtypeStruc...]
  transfers between devices with their start and end apart: 28 -> 32, of which waited for: 11 -> 12; matrix products, arithmetic and copies ran while one was open for 10% -> 10% of each run, Pallas kernels for 25% -> 35%
where the time goes in v15:
time: 545 us; the launch traced here: 543 us
  waiting for transfers between devices  213 us (39%)
  Pallas kernels  193 us (35%)
  starting transfers between devices  55.4 us (10%)
  other arithmetic  41 us (8%)
  local copies, waits for them, and re-layouts  26.8 us (5%)
  between operations  13.4 us (2%)
    pallas_call x4, Pallas kernels, block_sparse_product(): pl.pallas_call(kernel, grid_spec=grid_spec, out_shape=jax.ShapeDtypeStruc...  176 us
    ppermute x21, waiting for transfers between devices, per_device(): lax.ppermute(part, ('row', 'col'), pairs)  140 us
    ppermute x4, waiting for transfers between devices, product_to_owners(): lax.ppermute(value, ('layer', 'row'), [(a * size + b, b * size + quarter[...  71.8 us
    ppermute x21, starting transfers between devices, per_device(): lax.ppermute(part, ('row', 'col'), pairs)  46.7 us
    pallas_call x1, Pallas kernels, gathered_windows(): pl.pallas_call(kernel, grid_spec=grid_spec, out_shape=jax.ShapeDtypeStruc...  16.8 us
    gather x1, local copies, waits for them, and re-layouts, block_sparse_product(): padded = padded_blocks(blocks, block_rows, block_cols)[order]  15.9 us
  transfers between devices with their start and end apart: 32, of which 12 were waited for; matrix products, arithmetic and copies ran while one was open for 10% of the time, Pallas kernels for 35%

profile of v15, /device:TPU:30, one launch (start us, length us, event | category | flops | bytes accessed | tf_op | source)
XLA Modules:
  0.0 542.6 jit_solution(6807811904900526364)
XLA Ops:
  7.5 3.2 broadcast_multiply_fusion
  10.7 2.8 slice_bitcast_fusion.3
  16.4 9.2 %scatter_custom_fusion = s32[48]{0:T(128)S(1)} fusion(s32[1152]{0:T(1024)S(1)} %fusion.3, s32[1152]{0:T(1024)S(1)} %broadcast.328, s32[]{:T(128)} %constant.155.clone.1), kind=kCustom, calls=%fused_computation.82 | custom fusion | flops 1152 | bytes 196 | tf_op jit(solution)/shard_map/scatter-add | solution.py:133
  29.6 16.8 %shard_map.46 = bf16[48,64,128]{2,1,0:T(8,128)(2,1)} custom-call(s32[48]{0:T(128)} %copy-done.1, s32[48]{0:T(128)} %and_select_fusion.cols_ref, bf16[1536,3072]{1,0:T(8,128)(2,1)} %green_ref.1), custom_call_target="tpu_custom_call" | custom-call | tf_op jit(solution)/shard_map/pallas_call | solution.py:122
  49.5 6.1 %collective-permute-start.16 = (bf16[48,64,64]{2,1,0:T(8,128)(2,1)S(1)}, bf16[48,64,64]{2,1,0:T(8,128)(2,1)S(1)}, u32[]{:S(2)}, u32[]{:S(2)}) collective-permute-start(bf16[48,64,64]{2,1,0:T(8,128)(2,1)S(1)} %fusion), channel_id=1, source_target_pairs={{0,8},{2,24},{4,0},{6,16},{8,10},{10,26},{12,2},{14,18},{16,12},{1... | collective-permute-start | bytes 1179656 | tf_op jit(solution)/shard_map/ppermute | solution.py:94
  55.8 2.9 collective-permute-start.3
  60.1 5.1 collective-permute-done.1
  65.2 25.5 %collective-permute-start.5 = (s32[48]{0:T(128)S(1)}, s32[48]{0:T(128)S(1)}, u32[]{:S(2)}, u32[]{:S(2)}) collective-permute-start(s32[48]{0:T(128)S(1)} %collective-permute-done), channel_id=1, source_target_pairs={{0,5},{1,6},{2,7},{3,0},{4,1},{5,2},{6,3},{7,4},{8,13},{9,14},{10,... | collective-permute-start | bytes 584 | tf_op jit(solution)/shard_map/ppermute | solution.py:233
  91.3 4.2 collective-permute-start.9
  95.5 2.0 collective-permute-start.10
  102.6 1.8 collective-permute-done.13
  105.9 2.4 collective-permute-done.15
  108.5 3.8 sort.23
  112.3 2.8 gather_fusion.1
  116.3 2.8 gather_fusion
  119.8 2.6 collective-permute-start.19
  124.2 10.1 %collective-permute-done.17 = bf16[48,64,64]{2,1,0:T(8,128)(2,1)S(1)} collective-permute-done((bf16[48,64,64]{2,1,0:T(8,128)(2,1)S(1)}, bf16[48,64,64]{2,1,0:T(8,128)(2,1)S(1)}, u32[]{:S(2)}, u32[]{:S(2)}) %collective-permute-start.17) | collective-permute-done | bytes 393248 | tf_op jit(solution)/shard_map/ppermute | solution.py:233
  134.5 16.7 %collective-permute-done.18 = bf16[48,64,64]{2,1,0:T(8,128)(2,1)S(1)} collective-permute-done((bf16[48,64,64]{2,1,0:T(8,128)(2,1)S(1)}, bf16[48,64,64]{2,1,0:T(8,128)(2,1)S(1)}, u32[]{:S(2)}, u32[]{:S(2)}) %collective-permute-start.18) | collective-permute-done | bytes 393248 | tf_op jit(solution)/shard_map/ppermute | solution.py:233
  151.3 16.8 %collective-permute-done.19 = bf16[48,64,64]{2,1,0:T(8,128)(2,1)S(1)} collective-permute-done((bf16[48,64,64]{2,1,0:T(8,128)(2,1)S(1)}, bf16[48,64,64]{2,1,0:T(8,128)(2,1)S(1)}, u32[]{:S(2)}, u32[]{:S(2)}) %collective-permute-start.19) | collective-permute-done | bytes 393248 | tf_op jit(solution)/shard_map/ppermute | solution.py:233
  168.2 80.3 %collective-permute-done.20 = bf16[48,64,64]{2,1,0:T(8,128)(2,1)S(1)} collective-permute-done((bf16[48,64,64]{2,1,0:T(8,128)(2,1)S(1)}, bf16[48,64,64]{2,1,0:T(8,128)(2,1)S(1)}, u32[]{:S(2)}, u32[]{:S(2)}) %collective-permute-start.20) | collective-permute-done | bytes 393248 | tf_op jit(solution)/shard_map/ppermute | solution.py:233
  248.6 5.1 collective-permute-done.21
  255.6 6.3 %broadcast_select_fusion.1 = (bf16[384,64,128]{2,1,0:T(8,128)(2,1)S(1)}, bf16[384,64,128]{2,1,0:T(8,128)(2,1)S(1)}) fusion(pred[384]{0:T(512)(128)(4,1)S(1)} %fusion.6, bf16[384,64,64]{2,1,0:T(8,128)(2,1)S(1)} %get-tuple-element.15, bf16[384,64,64]{2,1,0:T(8,128)(2,1)S(1)} %get-tuple-element.14), kind=kLoop, calls=%fused_computation.11 | loop fusion | flops 18874368 | bytes 18874752 | tf_op jit(solution)/shard_map/jit(_where)/select_n | solution.py:151
  261.9 5.2 pad_maximum_fusion
  267.2 15.9 %gather_fusion.3 = bf16[384,128,128]{2,1,0:T(8,128)(2,1)} fusion(bf16[384,128,128]{2,1,0:T(8,128)(2,1)} %pad_maximum_fusion, s32[1024]{0:T(1024)S(1)} %pad_clamp_fusion.1), kind=kCustom, calls=%fused_computation.3 | custom fusion | bytes 25167360 | tf_op jit(solution)/shard_map/gather | solution.py:164
  283.1 43.9 %shard_map.47 = bf16[256,3072]{1,0:T(8,128)(2,1)} custom-call(s32[25]{0:T(128)} %convert_reduce_fusion.starts_ref, s32[384]{0:T(512)} %add_select_fusion.3.k_ref, bf16[256,12288]{1,0:T(8,128)(2,1)} %all-gather.5.cloned.1.call-done.t_ref, bf16[384,128,128]{2,1,0:T(8,128)(2,1)} %gather_fusion.3), custom_call_target="tpu_custom_call" | custom-call | tf_op jit(solution)/shard_map/pallas_call | solution.py:205
  327.0 44.1 %shard_map.48 = bf16[256,3072]{1,0:T(8,128)(2,1)} custom-call(s32[25]{0:T(128)} %convert_reduce_fusion.starts_ref, s32[384]{0:T(512)} %add_select_fusion.3.k_ref, bf16[256,12288]{1,0:T(8,128)(2,1)} %all-gather.7.cloned.1.call-done.t_ref, bf16[384,128,128]{2,1,0:T(8,128)(2,1)} %gather_fusion.3), custom_call_target="tpu_custom_call" | custom-call | tf_op jit(solution)/shard_map/pallas_call | solution.py:205
  372.4 43.9 %shard_map.49 = bf16[256,3072]{1,0:T(8,128)(2,1)} custom-call(s32[25]{0:T(128)} %convert_reduce_fusion.starts_ref, s32[384]{0:T(512)} %add_select_fusion.3.k_ref, bf16[256,12288]{1,0:T(8,128)(2,1)} %all-gather.9.cloned.1.call-done.t_ref, bf16[384,128,128]{2,1,0:T(8,128)(2,1)} %gather_fusion.3), custom_call_target="tpu_custom_call" | custom-call | tf_op jit(solution)/shard_map/pallas_call | solution.py:205
  416.3 43.9 %shard_map.50 = bf16[256,3072]{1,0:T(8,128)(2,1)} custom-call(s32[25]{0:T(128)} %convert_reduce_fusion.starts_ref, s32[384]{0:T(512)} %add_select_fusion.3.k_ref, bf16[256,12288]{1,0:T(8,128)(2,1)} %all-gather.11.cloned.1.call-done.t_ref, bf16[384,128,128]{2,1,0:T(8,128)(2,1)} %gather_fusion.3), custom_call_target="tpu_custom_call" | custom-call | tf_op jit(solution)/shard_map/pallas_call | solution.py:205
  460.2 38.0 %collective-permute-done.25 = bf16[256,3072]{1,0:T(8,128)(2,1)S(1)} collective-permute-done((bf16[256,3072]{1,0:T(8,128)(2,1)}, bf16[256,3072]{1,0:T(8,128)(2,1)S(1)}, u32[]{:S(2)}, u32[]{:S(2)}) %collective-permute-start.25) | collective-permute-done | bytes 1572896 | tf_op jit(solution)/shard_map/ppermute | solution.py:103
  498.2 17.0 %collective-permute-done.26 = bf16[256,3072]{1,0:T(8,128)(2,1)} collective-permute-done((bf16[256,3072]{1,0:T(8,128)(2,1)}, bf16[256,3072]{1,0:T(8,128)(2,1)}, u32[]{:S(2)}, u32[]{:S(2)}) %collective-permute-start.26) | collective-permute-done | bytes 1572896 | tf_op jit(solution)/shard_map/ppermute | solution.py:103
  515.2 16.7 %collective-permute-done.27 = bf16[256,3072]{1,0:T(8,128)(2,1)S(1)} collective-permute-done((bf16[256,3072]{1,0:T(8,128)(2,1)}, bf16[256,3072]{1,0:T(8,128)(2,1)S(1)}, u32[]{:S(2)}, u32[]{:S(2)}) %collective-permute-start.27) | collective-permute-done | bytes 1572896 | tf_op jit(solution)/shard_map/ppermute | solution.py:103
  531.9 4.1 maximum_bitcast_fusion
  (102 shorter events, 27.2 us)
Async XLA Ops:
  6.5 276.5 %all-gather.5.cloned.1.call-start = ((), (), s32[]{:S(2)}) async-start(), calls=%async_computation | async-start | bytes 7864320 | tf_op jit(solution)/shard_map/all_gather | solution.py:244
  13.6 313.4 %all-gather.7.cloned.1.call-start = ((), (), s32[]{:S(2)}) async-start(), calls=%async_computation.1 | async-start | bytes 7864320 | tf_op jit(solution)/shard_map/all_gather | solution.py:244
  14.3 358.0 %all-gather.9.cloned.1.call-start = ((), (), s32[]{:S(2)}) async-start(), calls=%async_computation.2 | async-start | bytes 7864320 | tf_op jit(solution)/shard_map/all_gather | solution.py:244
  15.1 401.3 %all-gather.11.cloned.1.call-start = ((), (), s32[]{:S(2)}) async-start(), calls=%async_computation.3 | async-start | bytes 7864320 | tf_op jit(solution)/shard_map/all_gather | solution.py:244
  27.8 27.8 %collective-permute-start = (s32[48]{0:T(128)S(1)}, s32[48]{0:T(128)S(1)}, u32[]{:S(2)}, u32[]{:S(2)}) collective-permute-start(s32[48]{0:T(128)S(1)} %get-tuple-element.10), channel_id=1, source_target_pairs={{0,8},{2,24},{4,0},{6,16},{8,10},{10,26},{12,2},{14,18},{16,12},{1... | collective-permute-start | bytes 584 | tf_op jit(solution)/shard_map/ppermute | solution.py:94
  28.3 30.3 %collective-permute-start.8 = (s32[48]{0:T(128)S(1)}, s32[48]{0:T(128)S(1)}, u32[]{:S(2)}, u32[]{:S(2)}) collective-permute-start(s32[48]{0:T(128)S(1)} %and_select_fusion.2.rows_ref), channel_id=1, source_target_pairs={{0,8},{2,24},{4,0},{6,16},{8,10},{10,26},{12,2},{14,18},{16,12},{1... | collective-permute-start | bytes 584 | tf_op jit(solution)/shard_map/ppermute | solution.py:94
  49.5 66.2 %collective-permute-start.16 = (bf16[48,64,64]{2,1,0:T(8,128)(2,1)S(1)}, bf16[48,64,64]{2,1,0:T(8,128)(2,1)S(1)}, u32[]{:S(2)}, u32[]{:S(2)}) collective-permute-start(bf16[48,64,64]{2,1,0:T(8,128)(2,1)S(1)} %fusion), channel_id=1, source_target_pairs={{0,8},{2,24},{4,0},{6,16},{8,10},{10,26},{12,2},{14,18},{16,12},{1... | collective-permute-start | bytes 1179656 | tf_op jit(solution)/shard_map/ppermute | solution.py:94
  55.6 9.5 %collective-permute-start.1 = (s32[48]{0:T(128)S(1)}, s32[48]{0:T(128)S(1)}, u32[]{:S(2)}, u32[]{:S(2)}) collective-permute-start(s32[48]{0:T(128)S(1)} %collective-permute-done), channel_id=1, source_target_pairs={{0,1},{1,2},{2,3},{3,4},{4,5},{5,6},{6,7},{7,0},{8,9},{9,10},{10,1... | collective-permute-start | bytes 584 | tf_op jit(solution)/shard_map/ppermute | solution.py:233
  55.7 35.0 %collective-permute-start.2 = (s32[48]{0:T(128)S(1)}, s32[48]{0:T(128)S(1)}, u32[]{:S(2)}, u32[]{:S(2)}) collective-permute-start(s32[48]{0:T(128)S(1)} %collective-permute-done), channel_id=1, source_target_pairs={{0,2},{1,3},{2,4},{3,5},{4,6},{5,7},{6,0},{7,1},{8,10},{9,11},{10,... | collective-permute-start | bytes 584 | tf_op jit(solution)/shard_map/ppermute | solution.py:233
  55.8 34.9 %collective-permute-start.3 = (s32[48]{0:T(128)S(1)}, s32[48]{0:T(128)S(1)}, u32[]{:S(2)}, u32[]{:S(2)}) collective-permute-start(s32[48]{0:T(128)S(1)} %collective-permute-done), channel_id=1, source_target_pairs={{0,3},{1,4},{2,5},{3,6},{4,7},{5,0},{6,1},{7,2},{8,11},{9,12},{10,... | collective-permute-start | bytes 584 | tf_op jit(solution)/shard_map/ppermute | solution.py:233
  58.7 32.6 %collective-permute-start.4 = (s32[48]{0:T(128)S(1)}, s32[48]{0:T(128)S(1)}, u32[]{:S(2)}, u32[]{:S(2)}) collective-permute-start(s32[48]{0:T(128)S(1)} %collective-permute-done), channel_id=1, source_target_pairs={{0,4},{1,5},{2,6},{3,7},{4,0},{5,1},{6,2},{7,3},{8,12},{9,13},{10,... | collective-permute-start | bytes 584 | tf_op jit(solution)/shard_map/ppermute | solution.py:233
  65.2 30.3 %collective-permute-start.5 = (s32[48]{0:T(128)S(1)}, s32[48]{0:T(128)S(1)}, u32[]{:S(2)}, u32[]{:S(2)}) collective-permute-start(s32[48]{0:T(128)S(1)} %collective-permute-done), channel_id=1, source_target_pairs={{0,5},{1,6},{2,7},{3,0},{4,1},{5,2},{6,3},{7,4},{8,13},{9,14},{10,... | collective-permute-start | bytes 584 | tf_op jit(solution)/shard_map/ppermute | solution.py:233
  90.7 6.8 %collective-permute-start.6 = (s32[48]{0:T(128)S(1)}, s32[48]{0:T(128)S(1)}, u32[]{:S(2)}, u32[]{:S(2)}) collective-permute-start(s32[48]{0:T(128)S(1)} %collective-permute-done), channel_id=1, source_target_pairs={{0,6},{1,7},{2,0},{3,1},{4,2},{5,3},{6,4},{7,5},{8,14},{9,15},{10,... | collective-permute-start | bytes 584 | tf_op jit(solution)/shard_map/ppermute | solution.py:233
  90.7 6.8 %collective-permute-start.7 = (s32[48]{0:T(128)S(1)}, s32[48]{0:T(128)S(1)}, u32[]{:S(2)}, u32[]{:S(2)}) collective-permute-start(s32[48]{0:T(128)S(1)} %collective-permute-done), channel_id=1, source_target_pairs={{0,7},{1,0},{2,1},{3,2},{4,3},{5,4},{6,5},{7,6},{8,15},{9,8},{10,9... | collective-permute-start | bytes 584 | tf_op jit(solution)/shard_map/ppermute | solution.py:233
  91.3 7.8 %collective-permute-start.9 = (s32[48]{0:T(128)S(1)}, s32[48]{0:T(128)S(1)}, u32[]{:S(2)}, u32[]{:S(2)}) collective-permute-start(s32[48]{0:T(128)S(1)} %collective-permute-done.8), channel_id=1, source_target_pairs={{0,1},{1,2},{2,3},{3,4},{4,5},{5,6},{6,7},{7,0},{8,9},{9,10},{10,1... | collective-permute-start | bytes 584 | tf_op jit(solution)/shard_map/ppermute | solution.py:233
  95.5 5.1 collective-permute-start.10
  97.4 4.6 collective-permute-start.11
  97.5 5.2 collective-permute-start.12
  99.1 5.4 collective-permute-start.13
  100.5 5.3 collective-permute-start.14
  102.1 6.2 %collective-permute-start.15 = (s32[48]{0:T(128)S(1)}, s32[48]{0:T(128)S(1)}, u32[]{:S(2)}, u32[]{:S(2)}) collective-permute-start(s32[48]{0:T(128)S(1)} %collective-permute-done.8), channel_id=1, source_target_pairs={{0,7},{1,0},{2,1},{3,2},{4,3},{5,4},{6,5},{7,6},{8,15},{9,8},{10,9... | collective-permute-start | bytes 584 | tf_op jit(solution)/shard_map/ppermute | solution.py:233
  115.7 18.7 %collective-permute-start.17 = (bf16[48,64,64]{2,1,0:T(8,128)(2,1)S(1)}, bf16[48,64,64]{2,1,0:T(8,128)(2,1)S(1)}, u32[]{:S(2)}, u32[]{:S(2)}) collective-permute-start(bf16[48,64,64]{2,1,0:T(8,128)(2,1)S(1)} %collective-permute-done.16), channel_id=1, source_target_pairs={{0,1},{1,2},{2,3},{3,4},{4,5},{5,6},{6,7},{7,0},{8,9},{9,10},{10,1... | collective-permute-start | bytes 1179656 | tf_op jit(solution)/shard_map/ppermute | solution.py:233
  119.7 31.5 %collective-permute-start.18 = (bf16[48,64,64]{2,1,0:T(8,128)(2,1)S(1)}, bf16[48,64,64]{2,1,0:T(8,128)(2,1)S(1)}, u32[]{:S(2)}, u32[]{:S(2)}) collective-permute-start(bf16[48,64,64]{2,1,0:T(8,128)(2,1)S(1)} %collective-permute-done.16), channel_id=1, source_target_pairs={{0,2},{1,3},{2,4},{3,5},{4,6},{5,7},{6,0},{7,1},{8,10},{9,11},{10,... | collective-permute-start | bytes 1179656 | tf_op jit(solution)/shard_map/ppermute | solution.py:233
  119.8 48.3 %collective-permute-start.19 = (bf16[48,64,64]{2,1,0:T(8,128)(2,1)S(1)}, bf16[48,64,64]{2,1,0:T(8,128)(2,1)S(1)}, u32[]{:S(2)}, u32[]{:S(2)}) collective-permute-start(bf16[48,64,64]{2,1,0:T(8,128)(2,1)S(1)} %collective-permute-done.16), channel_id=1, source_target_pairs={{0,3},{1,4},{2,5},{3,6},{4,7},{5,0},{6,1},{7,2},{8,11},{9,12},{10,... | collective-permute-start | bytes 1179656 | tf_op jit(solution)/shard_map/ppermute | solution.py:233
  122.4 126.1 %collective-permute-start.20 = (bf16[48,64,64]{2,1,0:T(8,128)(2,1)S(1)}, bf16[48,64,64]{2,1,0:T(8,128)(2,1)S(1)}, u32[]{:S(2)}, u32[]{:S(2)}) collective-permute-start(bf16[48,64,64]{2,1,0:T(8,128)(2,1)S(1)} %collective-permute-done.16), channel_id=1, source_target_pairs={{0,4},{1,5},{2,6},{3,7},{4,0},{5,1},{6,2},{7,3},{8,12},{9,13},{10,... | collective-permute-start | bytes 1179656 | tf_op jit(solution)/shard_map/ppermute | solution.py:233
  124.2 129.5 %collective-permute-start.21 = (bf16[48,64,64]{2,1,0:T(8,128)(2,1)S(1)}, bf16[48,64,64]{2,1,0:T(8,128)(2,1)S(1)}, u32[]{:S(2)}, u32[]{:S(2)}) collective-permute-start(bf16[48,64,64]{2,1,0:T(8,128)(2,1)S(1)} %collective-permute-done.16), channel_id=1, source_target_pairs={{0,5},{1,6},{2,7},{3,0},{4,1},{5,2},{6,3},{7,4},{8,13},{9,14},{10,... | collective-permute-start | bytes 1179656 | tf_op jit(solution)/shard_map/ppermute | solution.py:233
  134.4 119.4 %collective-permute-start.22 = (bf16[48,64,64]{2,1,0:T(8,128)(2,1)S(1)}, bf16[48,64,64]{2,1,0:T(8,128)(2,1)S(1)}, u32[]{:S(2)}, u32[]{:S(2)}) collective-permute-start(bf16[48,64,64]{2,1,0:T(8,128)(2,1)S(1)} %collective-permute-done.16), channel_id=1, source_target_pairs={{0,6},{1,7},{2,0},{3,1},{4,2},{5,3},{6,4},{7,5},{8,14},{9,15},{10,... | collective-permute-start | bytes 1179656 | tf_op jit(solution)/shard_map/ppermute | solution.py:233
  151.2 102.7 %collective-permute-start.23 = (bf16[48,64,64]{2,1,0:T(8,128)(2,1)S(1)}, bf16[48,64,64]{2,1,0:T(8,128)(2,1)S(1)}, u32[]{:S(2)}, u32[]{:S(2)}) collective-permute-start(bf16[48,64,64]{2,1,0:T(8,128)(2,1)S(1)} %collective-permute-done.16), channel_id=1, source_target_pairs={{0,7},{1,0},{2,1},{3,2},{4,3},{5,4},{6,5},{7,6},{8,15},{9,8},{10,9... | collective-permute-start | bytes 1179656 | tf_op jit(solution)/shard_map/ppermute | solution.py:233
  327.0 133.2 %collective-permute-start.24 = (bf16[256,3072]{1,0:T(8,128)(2,1)}, bf16[256,3072]{1,0:T(8,128)(2,1)S(1)}, u32[]{:S(2)}, u32[]{:S(2)}) collective-permute-start(bf16[256,3072]{1,0:T(8,128)(2,1)} %shard_map.47), channel_id=1, source_target_pairs={{0,4},{2,12},{4,20},{6,28},{8,0},{10,8},{12,16},{14,24},{16,6},{18... | collective-permute-start | bytes 4718600 | tf_op jit(solution)/shard_map/ppermute | solution.py:103
  371.0 127.2 %collective-permute-start.25 = (bf16[256,3072]{1,0:T(8,128)(2,1)}, bf16[256,3072]{1,0:T(8,128)(2,1)S(1)}, u32[]{:S(2)}, u32[]{:S(2)}) collective-permute-start(bf16[256,3072]{1,0:T(8,128)(2,1)} %shard_map.48), channel_id=1, source_target_pairs={{0,4},{2,12},{4,20},{6,28},{8,0},{10,8},{12,16},{14,24},{16,6},{18... | collective-permute-start | bytes 4718600 | tf_op jit(solution)/shard_map/ppermute | solution.py:103
  416.3 98.9 %collective-permute-start.26 = (bf16[256,3072]{1,0:T(8,128)(2,1)}, bf16[256,3072]{1,0:T(8,128)(2,1)}, u32[]{:S(2)}, u32[]{:S(2)}) collective-permute-start(bf16[256,3072]{1,0:T(8,128)(2,1)} %shard_map.49), channel_id=1, source_target_pairs={{0,4},{2,12},{4,20},{6,28},{8,0},{10,8},{12,16},{14,24},{16,6},{18... | collective-permute-start | bytes 4718600 | tf_op jit(solution)/shard_map/ppermute | solution.py:103
  460.2 71.8 %collective-permute-start.27 = (bf16[256,3072]{1,0:T(8,128)(2,1)}, bf16[256,3072]{1,0:T(8,128)(2,1)S(1)}, u32[]{:S(2)}, u32[]{:S(2)}) collective-permute-start(bf16[256,3072]{1,0:T(8,128)(2,1)} %shard_map.50), channel_id=1, source_target_pairs={{0,4},{2,12},{4,20},{6,28},{8,0},{10,8},{12,16},{14,24},{16,6},{18... | collective-permute-start | bytes 4718600 | tf_op jit(solution)/shard_map/ppermute | solution.py:103
  (2 other events, 3.4 us)
Sparse Core Ops, SparseCore 0:
  13.7 60.6 all-gather.4
  76.0 48.9 all-gather.6
  126.5 46.3 all-gather.8
  174.4 46.3 all-gather.10

commit v16 on v15

--- a/solution.py
+++ b/solution.py
@@ -234,6 +234,7 @@
     blocks, block_row, block_col = (
         jnp.stack([got[k] for got in received]) for k in range(len(parts))
     )
+    own, blocks = lax.optimization_barrier((own, blocks))
     band = ((me - jnp.arange(group)) % group)[:, None]
     entry_rows = band * tile_rows + block_row
     entry_rows = entry_rows.reshape(-1)

time: 545 us -> 628 us (1.15)
  the two profiles are of different devices: /device:TPU:30 before, /device:TPU:16 now
where the time goes in v16:
time: 628 us; the launch traced here: 626 us
  Pallas kernels  194 us (31%)
  waiting for transfers between devices  185 us (29%)
  starting transfers between devices  152 us (24%)
  other arithmetic  45.1 us (7%)
  local copies, waits for them, and re-layouts  35.7 us (6%)
  between operations  13.3 us (2%)
    pallas_call x4, Pallas kernels, block_sparse_product(): pl.pallas_call(kernel, grid_spec=grid_spec, out_shape=jax.ShapeDtypeStruc...  175 us
    ppermute x21, starting transfers between devices, per_device(): lax.ppermute(part, ('row', 'col'), pairs)  138 us
    all_gather x4, waiting for transfers between devices, per_device(): lax.all_gather(own[start:start + ROW_CHUNK], 'layer', axis=1, tiled=True)  69.3 us
    ppermute x3, waiting for transfers between devices, green_to_layers(): lax.ppermute(value, ('layer', 'row'), [(a * size + b, inverse[b] * size +...  43.3 us
    ppermute x21, waiting for transfers between devices, per_device(): lax.ppermute(part, ('row', 'col'), pairs)  35.5 us
    ppermute x4, waiting for transfers between devices, product_to_owners(): lax.ppermute(value, ('layer', 'row'), [(a * size + b, b * size + quarter[...  35.1 us
    pallas_call x1, Pallas kernels, gathered_windows(): pl.pallas_call(kernel, grid_spec=grid_spec, out_shape=jax.ShapeDtypeStruc...  18.7 us
    gather x1, local copies, waits for them, and re-layouts, block_sparse_product(): padded = padded_blocks(blocks, block_rows, block_cols)[order]  17.5 us
  transfers between devices with their start and end apart: 32, of which 10 were waited for; matrix products, arithmetic and copies ran while one was open for 9% of the time, Pallas kernels for 28%

profile of v16, /device:TPU:16, one launch (start us, length us, event | category | flops | bytes accessed | tf_op | source)
XLA Modules:
  0.0 625.6 jit_solution(1311836257077435822)
XLA Ops:
  10.1 9.2 %scatter_custom_fusion = s32[48]{0:T(128)S(1)} fusion(s32[1152]{0:T(1024)S(1)} %fusion.3, s32[1152]{0:T(1024)S(1)} %broadcast.328, s32[]{:T(128)} %constant.155.clone.1), kind=kCustom, calls=%fused_computation.78 | custom fusion | flops 1152 | bytes 196 | tf_op jit(solution)/shard_map/scatter-add | solution.py:133
  23.4 18.7 %shard_map.46 = bf16[48,64,128]{2,1,0:T(8,128)(2,1)} custom-call(s32[48]{0:T(128)} %and_select_fusion.2.rows_ref, s32[48]{0:T(128)} %and_select_fusion.cols_ref, bf16[1536,3072]{1,0:T(8,128)(2,1)} %green_ref.1), custom_call_target="tpu_custom_call" | custom-call | tf_op jit(solution)/shard_map/pallas_call | solution.py:122
  44.0 3.0 collective-permute-start.16
  47.2 39.9 %collective-permute-done.16 = bf16[48,64,64]{2,1,0:T(8,128)(2,1)S(1)} collective-permute-done((bf16[48,64,64]{2,1,0:T(8,128)(2,1)S(1)}, bf16[48,64,64]{2,1,0:T(8,128)(2,1)S(1)}, u32[]{:S(2)}, u32[]{:S(2)}) %collective-permute-start.16) | collective-permute-done | bytes 393248 | tf_op jit(solution)/shard_map/ppermute | solution.py:94
  87.0 18.4 %collective-permute-start.17 = (bf16[48,64,64]{2,1,0:T(8,128)(2,1)S(1)}, bf16[48,64,64]{2,1,0:T(8,128)(2,1)S(1)}, u32[]{:S(2)}, u32[]{:S(2)}) collective-permute-start(bf16[48,64,64]{2,1,0:T(8,128)(2,1)S(1)} %collective-permute-done.16), channel_id=1, source_target_pairs={{0,1},{1,2},{2,3},{3,4},{4,5},{5,6},{6,7},{7,0},{8,9},{9,10},{10,1... | collective-permute-start | bytes 1179656 | tf_op jit(solution)/shard_map/ppermute | solution.py:233
  105.4 3.2 multiply_bitcast_fusion
  109.6 4.3 collective-permute-start.19
  113.9 3.0 collective-permute-start.21
  116.9 16.1 %collective-permute-done.17 = bf16[48,64,64]{2,1,0:T(8,128)(2,1)S(1)} collective-permute-done((bf16[48,64,64]{2,1,0:T(8,128)(2,1)S(1)}, bf16[48,64,64]{2,1,0:T(8,128)(2,1)S(1)}, u32[]{:S(2)}, u32[]{:S(2)}) %collective-permute-start.17) | collective-permute-done | bytes 393248 | tf_op jit(solution)/shard_map/ppermute | solution.py:233
  133.9 73.1 %collective-permute-start.23 = (bf16[48,64,64]{2,1,0:T(8,128)(2,1)S(1)}, bf16[48,64,64]{2,1,0:T(8,128)(2,1)S(1)}, u32[]{:S(2)}, u32[]{:S(2)}) collective-permute-start(bf16[48,64,64]{2,1,0:T(8,128)(2,1)S(1)} %collective-permute-done.16), channel_id=1, source_target_pairs={{0,7},{1,0},{2,1},{3,2},{4,3},{5,4},{6,5},{7,6},{8,15},{9,8},{10,9... | collective-permute-start | bytes 1179656 | tf_op jit(solution)/shard_map/ppermute | solution.py:233
  214.0 15.8 %collective-permute-done.23 = bf16[48,64,64]{2,1,0:T(8,128)(2,1)S(1)} collective-permute-done((bf16[48,64,64]{2,1,0:T(8,128)(2,1)S(1)}, bf16[48,64,64]{2,1,0:T(8,128)(2,1)S(1)}, u32[]{:S(2)}, u32[]{:S(2)}) %collective-permute-start.23) | collective-permute-done | bytes 393248 | tf_op jit(solution)/shard_map/ppermute | solution.py:233
  235.7 3.4 collective-permute-done
  239.2 21.2 %collective-permute-start.2 = (s32[48]{0:T(128)S(1)}, s32[48]{0:T(128)S(1)}, u32[]{:S(2)}, u32[]{:S(2)}) collective-permute-start(s32[48]{0:T(128)S(1)} %collective-permute-done), channel_id=1, source_target_pairs={{0,2},{1,3},{2,4},{3,5},{4,6},{5,7},{6,0},{7,1},{8,10},{9,11},{10,... | collective-permute-start | bytes 584 | tf_op jit(solution)/shard_map/ppermute | solution.py:233
  260.4 3.8 collective-permute-start.5
  268.3 3.3 collective-permute-start.11
  271.6 3.4 collective-permute-start.13
  280.0 3.8 sort.23
  286.6 2.8 gather_fusion.1
  290.6 4.3 bitcast_select_fusion.1
  294.9 6.4 %broadcast_select_fusion.1 = (bf16[384,64,128]{2,1,0:T(8,128)(2,1)S(1)}, bf16[384,64,128]{2,1,0:T(8,128)(2,1)S(1)}) fusion(pred[384]{0:T(512)(128)(4,1)S(1)} %fusion.6, bf16[384,64,64]{2,1,0:T(8,128)(2,1)S(1)} %get-tuple-element.19, bf16[384,64,64]{2,1,0:T(8,128)(2,1)S(1)} %get-tuple-element.18), kind=kLoop, calls=%fused_computation.12 | loop fusion | flops 18874368 | bytes 18874752 | tf_op jit(solution)/shard_map/jit(_where)/select_n | solution.py:151
  301.4 5.2 pad_maximum_fusion
  306.6 17.5 %gather_fusion.3 = bf16[384,128,128]{2,1,0:T(8,128)(2,1)} fusion(bf16[384,128,128]{2,1,0:T(8,128)(2,1)} %pad_maximum_fusion, s32[1024]{0:T(1024)S(1)} %pad_clamp_fusion.1), kind=kCustom, calls=%fused_computation.3 | custom fusion | bytes 25167360 | tf_op jit(solution)/shard_map/gather | solution.py:164
  324.1 43.8 %shard_map.47 = bf16[256,3072]{1,0:T(8,128)(2,1)} custom-call(s32[25]{0:T(128)} %convert_reduce_fusion.starts_ref, s32[384]{0:T(512)} %add_select_fusion.3.k_ref, bf16[256,12288]{1,0:T(8,128)(2,1)} %all-gather.5.cloned.1.call-done.t_ref, bf16[384,128,128]{2,1,0:T(8,128)(2,1)} %gather_fusion.3), custom_call_target="tpu_custom_call" | custom-call | tf_op jit(solution)/shard_map/pallas_call | solution.py:205
  369.7 44.0 %shard_map.48 = bf16[256,3072]{1,0:T(8,128)(2,1)} custom-call(s32[25]{0:T(128)} %convert_reduce_fusion.starts_ref, s32[384]{0:T(512)} %add_select_fusion.3.k_ref, bf16[256,12288]{1,0:T(8,128)(2,1)} %all-gather.7.cloned.1.call-done.t_ref, bf16[384,128,128]{2,1,0:T(8,128)(2,1)} %gather_fusion.3), custom_call_target="tpu_custom_call" | custom-call | tf_op jit(solution)/shard_map/pallas_call | solution.py:205
  414.9 5.1 all-gather.9.cloned.1.call-done.t_ref
  420.0 43.8 %shard_map.49 = bf16[256,3072]{1,0:T(8,128)(2,1)} custom-call(s32[25]{0:T(128)} %convert_reduce_fusion.starts_ref, s32[384]{0:T(512)} %add_select_fusion.3.k_ref, bf16[256,12288]{1,0:T(8,128)(2,1)} %all-gather.9.cloned.1.call-done.t_ref, bf16[384,128,128]{2,1,0:T(8,128)(2,1)} %gather_fusion.3), custom_call_target="tpu_custom_call" | custom-call | tf_op jit(solution)/shard_map/pallas_call | solution.py:205
  463.8 4.2 collective-permute-start.26
  468.0 64.2 %all-gather.11.cloned.1.call-done.t_ref = bf16[256,12288]{1,0:T(8,128)(2,1)} async-done(((bf16[256,3072]{1,0:T(8,128)(2,1)}), bf16[256,12288]{1,0:T(8,128)(2,1)}) %all-gather.11.cloned.1.call-update) | async-done | bytes 6291472 | tf_op jit(solution)/shard_map/all_gather | solution.py:245
  532.2 43.7 %shard_map.50 = bf16[256,3072]{1,0:T(8,128)(2,1)} custom-call(s32[25]{0:T(128)} %convert_reduce_fusion.starts_ref, s32[384]{0:T(512)} %add_select_fusion.3.k_ref, bf16[256,12288]{1,0:T(8,128)(2,1)} %all-gather.11.cloned.1.call-done.t_ref, bf16[384,128,128]{2,1,0:T(8,128)(2,1)} %gather_fusion.3), custom_call_target="tpu_custom_call" | custom-call | tf_op jit(solution)/shard_map/pallas_call | solution.py:205
  576.0 3.9 collective-permute-start.27
  579.9 35.1 %collective-permute-done.27 = bf16[256,3072]{1,0:T(8,128)(2,1)S(1)} collective-permute-done((bf16[256,3072]{1,0:T(8,128)(2,1)}, bf16[256,3072]{1,0:T(8,128)(2,1)S(1)}, u32[]{:S(2)}, u32[]{:S(2)}) %collective-permute-start.27) | collective-permute-done | bytes 1572896 | tf_op jit(solution)/shard_map/ppermute | solution.py:103
  615.0 4.1 maximum_bitcast_fusion
  (102 shorter events, 40.4 us)
Async XLA Ops:
  6.5 317.6 %all-gather.5.cloned.1.call-start = ((), (), s32[]{:S(2)}) async-start(), calls=%async_computation | async-start | bytes 7864320 | tf_op jit(solution)/shard_map/all_gather | solution.py:245
  44.0 43.1 %collective-permute-start.16 = (bf16[48,64,64]{2,1,0:T(8,128)(2,1)S(1)}, bf16[48,64,64]{2,1,0:T(8,128)(2,1)S(1)}, u32[]{:S(2)}, u32[]{:S(2)}) collective-permute-start(bf16[48,64,64]{2,1,0:T(8,128)(2,1)S(1)} %fusion), channel_id=1, source_target_pairs={{0,8},{2,24},{4,0},{6,16},{8,10},{10,26},{12,2},{14,18},{16,12},{1... | collective-permute-start | bytes 1179656 | tf_op jit(solution)/shard_map/ppermute | solution.py:94
  87.0 45.9 %collective-permute-start.17 = (bf16[48,64,64]{2,1,0:T(8,128)(2,1)S(1)}, bf16[48,64,64]{2,1,0:T(8,128)(2,1)S(1)}, u32[]{:S(2)}, u32[]{:S(2)}) collective-permute-start(bf16[48,64,64]{2,1,0:T(8,128)(2,1)S(1)} %collective-permute-done.16), channel_id=1, source_target_pairs={{0,1},{1,2},{2,3},{3,4},{4,5},{5,6},{6,7},{7,0},{8,9},{9,10},{10,1... | collective-permute-start | bytes 1179656 | tf_op jit(solution)/shard_map/ppermute | solution.py:233
  108.6 25.3 %collective-permute-start.18 = (bf16[48,64,64]{2,1,0:T(8,128)(2,1)S(1)}, bf16[48,64,64]{2,1,0:T(8,128)(2,1)S(1)}, u32[]{:S(2)}, u32[]{:S(2)}) collective-permute-start(bf16[48,64,64]{2,1,0:T(8,128)(2,1)S(1)} %collective-permute-done.16), channel_id=1, source_target_pairs={{0,2},{1,3},{2,4},{3,5},{4,6},{5,7},{6,0},{7,1},{8,10},{9,11},{10,... | collective-permute-start | bytes 1179656 | tf_op jit(solution)/shard_map/ppermute | solution.py:233
  109.6 98.3 %collective-permute-start.19 = (bf16[48,64,64]{2,1,0:T(8,128)(2,1)S(1)}, bf16[48,64,64]{2,1,0:T(8,128)(2,1)S(1)}, u32[]{:S(2)}, u32[]{:S(2)}) collective-permute-start(bf16[48,64,64]{2,1,0:T(8,128)(2,1)S(1)} %collective-permute-done.16), channel_id=1, source_target_pairs={{0,3},{1,4},{2,5},{3,6},{4,7},{5,0},{6,1},{7,2},{8,11},{9,12},{10,... | collective-permute-start | bytes 1179656 | tf_op jit(solution)/shard_map/ppermute | solution.py:233
  113.9 95.0 %collective-permute-start.20 = (bf16[48,64,64]{2,1,0:T(8,128)(2,1)S(1)}, bf16[48,64,64]{2,1,0:T(8,128)(2,1)S(1)}, u32[]{:S(2)}, u32[]{:S(2)}) collective-permute-start(bf16[48,64,64]{2,1,0:T(8,128)(2,1)S(1)} %collective-permute-done.16), channel_id=1, source_target_pairs={{0,4},{1,5},{2,6},{3,7},{4,0},{5,1},{6,2},{7,3},{8,12},{9,13},{10,... | collective-permute-start | bytes 1179656 | tf_op jit(solution)/shard_map/ppermute | solution.py:233
  113.9 95.9 %collective-permute-start.21 = (bf16[48,64,64]{2,1,0:T(8,128)(2,1)S(1)}, bf16[48,64,64]{2,1,0:T(8,128)(2,1)S(1)}, u32[]{:S(2)}, u32[]{:S(2)}) collective-permute-start(bf16[48,64,64]{2,1,0:T(8,128)(2,1)S(1)} %collective-permute-done.16), channel_id=1, source_target_pairs={{0,5},{1,6},{2,7},{3,0},{4,1},{5,2},{6,3},{7,4},{8,13},{9,14},{10,... | collective-permute-start | bytes 1179656 | tf_op jit(solution)/shard_map/ppermute | solution.py:233
  133.0 80.0 %collective-permute-start.22 = (bf16[48,64,64]{2,1,0:T(8,128)(2,1)S(1)}, bf16[48,64,64]{2,1,0:T(8,128)(2,1)S(1)}, u32[]{:S(2)}, u32[]{:S(2)}) collective-permute-start(bf16[48,64,64]{2,1,0:T(8,128)(2,1)S(1)} %collective-permute-done.16), channel_id=1, source_target_pairs={{0,6},{1,7},{2,0},{3,1},{4,2},{5,3},{6,4},{7,5},{8,14},{9,15},{10,... | collective-permute-start | bytes 1179656 | tf_op jit(solution)/shard_map/ppermute | solution.py:233
  133.9 95.9 %collective-permute-start.23 = (bf16[48,64,64]{2,1,0:T(8,128)(2,1)S(1)}, bf16[48,64,64]{2,1,0:T(8,128)(2,1)S(1)}, u32[]{:S(2)}, u32[]{:S(2)}) collective-permute-start(bf16[48,64,64]{2,1,0:T(8,128)(2,1)S(1)} %collective-permute-done.16), channel_id=1, source_target_pairs={{0,7},{1,0},{2,1},{3,2},{4,3},{5,4},{6,5},{7,6},{8,15},{9,8},{10,9... | collective-permute-start | bytes 1179656 | tf_op jit(solution)/shard_map/ppermute | solution.py:233
  233.5 136.2 %all-gather.7.cloned.1.call-start = ((), (), s32[]{:S(2)}) async-start(), calls=%async_computation.1 | async-start | bytes 7864320 | tf_op jit(solution)/shard_map/all_gather | solution.py:245
  234.2 185.7 %all-gather.9.cloned.1.call-start = ((), (), s32[]{:S(2)}) async-start(), calls=%async_computation.2 | async-start | bytes 7864320 | tf_op jit(solution)/shard_map/all_gather | solution.py:245
  235.0 297.2 %all-gather.11.cloned.1.call-start = ((), (), s32[]{:S(2)}) async-start(), calls=%async_computation.3 | async-start | bytes 7864320 | tf_op jit(solution)/shard_map/all_gather | solution.py:245
  235.6 3.6 collective-permute-start
  235.6 24.8 %collective-permute-start.8 = (s32[48]{0:T(128)S(1)}, s32[48]{0:T(128)S(1)}, u32[]{:S(2)}, u32[]{:S(2)}) collective-permute-start(s32[48]{0:T(128)S(1)} %copy-done.1), channel_id=1, source_target_pairs={{0,8},{2,24},{4,0},{6,16},{8,10},{10,26},{12,2},{14,18},{16,12},{1... | collective-permute-start | bytes 584 | tf_op jit(solution)/shard_map/ppermute | solution.py:94
  239.2 25.1 %collective-permute-start.1 = (s32[48]{0:T(128)S(1)}, s32[48]{0:T(128)S(1)}, u32[]{:S(2)}, u32[]{:S(2)}) collective-permute-start(s32[48]{0:T(128)S(1)} %collective-permute-done), channel_id=1, source_target_pairs={{0,1},{1,2},{2,3},{3,4},{4,5},{5,6},{6,7},{7,0},{8,9},{9,10},{10,1... | collective-permute-start | bytes 584 | tf_op jit(solution)/shard_map/ppermute | solution.py:233
  239.2 26.5 %collective-permute-start.2 = (s32[48]{0:T(128)S(1)}, s32[48]{0:T(128)S(1)}, u32[]{:S(2)}, u32[]{:S(2)}) collective-permute-start(s32[48]{0:T(128)S(1)} %collective-permute-done), channel_id=1, source_target_pairs={{0,2},{1,3},{2,4},{3,5},{4,6},{5,7},{6,0},{7,1},{8,10},{9,11},{10,... | collective-permute-start | bytes 584 | tf_op jit(solution)/shard_map/ppermute | solution.py:233
  260.4 6.8 %collective-permute-start.3 = (s32[48]{0:T(128)S(1)}, s32[48]{0:T(128)S(1)}, u32[]{:S(2)}, u32[]{:S(2)}) collective-permute-start(s32[48]{0:T(128)S(1)} %collective-permute-done), channel_id=1, source_target_pairs={{0,3},{1,4},{2,5},{3,6},{4,7},{5,0},{6,1},{7,2},{8,11},{9,12},{10,... | collective-permute-start | bytes 584 | tf_op jit(solution)/shard_map/ppermute | solution.py:233
  260.4 7.3 %collective-permute-start.4 = (s32[48]{0:T(128)S(1)}, s32[48]{0:T(128)S(1)}, u32[]{:S(2)}, u32[]{:S(2)}) collective-permute-start(s32[48]{0:T(128)S(1)} %collective-permute-done), channel_id=1, source_target_pairs={{0,4},{1,5},{2,6},{3,7},{4,0},{5,1},{6,2},{7,3},{8,12},{9,13},{10,... | collective-permute-start | bytes 584 | tf_op jit(solution)/shard_map/ppermute | solution.py:233
  260.4 7.9 %collective-permute-start.5 = (s32[48]{0:T(128)S(1)}, s32[48]{0:T(128)S(1)}, u32[]{:S(2)}, u32[]{:S(2)}) collective-permute-start(s32[48]{0:T(128)S(1)} %collective-permute-done), channel_id=1, source_target_pairs={{0,5},{1,6},{2,7},{3,0},{4,1},{5,2},{6,3},{7,4},{8,13},{9,14},{10,... | collective-permute-start | bytes 584 | tf_op jit(solution)/shard_map/ppermute | solution.py:233
  264.2 7.4 %collective-permute-start.6 = (s32[48]{0:T(128)S(1)}, s32[48]{0:T(128)S(1)}, u32[]{:S(2)}, u32[]{:S(2)}) collective-permute-start(s32[48]{0:T(128)S(1)} %collective-permute-done), channel_id=1, source_target_pairs={{0,6},{1,7},{2,0},{3,1},{4,2},{5,3},{6,4},{7,5},{8,14},{9,15},{10,... | collective-permute-start | bytes 584 | tf_op jit(solution)/shard_map/ppermute | solution.py:233
  265.7 5.9 collective-permute-start.7
  267.2 8.0 %collective-permute-start.9 = (s32[48]{0:T(128)S(1)}, s32[48]{0:T(128)S(1)}, u32[]{:S(2)}, u32[]{:S(2)}) collective-permute-start(s32[48]{0:T(128)S(1)} %collective-permute-done.8), channel_id=1, source_target_pairs={{0,1},{1,2},{2,3},{3,4},{4,5},{5,6},{6,7},{7,0},{8,9},{9,10},{10,1... | collective-permute-start | bytes 584 | tf_op jit(solution)/shard_map/ppermute | solution.py:233
  267.7 8.4 %collective-permute-start.10 = (s32[48]{0:T(128)S(1)}, s32[48]{0:T(128)S(1)}, u32[]{:S(2)}, u32[]{:S(2)}) collective-permute-start(s32[48]{0:T(128)S(1)} %collective-permute-done.8), channel_id=1, source_target_pairs={{0,2},{1,3},{2,4},{3,5},{4,6},{5,7},{6,0},{7,1},{8,10},{9,11},{10,... | collective-permute-start | bytes 584 | tf_op jit(solution)/shard_map/ppermute | solution.py:233
  268.3 10.2 %collective-permute-start.11 = (s32[48]{0:T(128)S(1)}, s32[48]{0:T(128)S(1)}, u32[]{:S(2)}, u32[]{:S(2)}) collective-permute-start(s32[48]{0:T(128)S(1)} %collective-permute-done.8), channel_id=1, source_target_pairs={{0,3},{1,4},{2,5},{3,6},{4,7},{5,0},{6,1},{7,2},{8,11},{9,12},{10,... | collective-permute-start | bytes 584 | tf_op jit(solution)/shard_map/ppermute | solution.py:233
  271.6 6.9 %collective-permute-start.12 = (s32[48]{0:T(128)S(1)}, s32[48]{0:T(128)S(1)}, u32[]{:S(2)}, u32[]{:S(2)}) collective-permute-start(s32[48]{0:T(128)S(1)} %collective-permute-done.8), channel_id=1, source_target_pairs={{0,4},{1,5},{2,6},{3,7},{4,0},{5,1},{6,2},{7,3},{8,12},{9,13},{10,... | collective-permute-start | bytes 584 | tf_op jit(solution)/shard_map/ppermute | solution.py:233
  271.6 6.9 %collective-permute-start.13 = (s32[48]{0:T(128)S(1)}, s32[48]{0:T(128)S(1)}, u32[]{:S(2)}, u32[]{:S(2)}) collective-permute-start(s32[48]{0:T(128)S(1)} %collective-permute-done.8), channel_id=1, source_target_pairs={{0,5},{1,6},{2,7},{3,0},{4,1},{5,2},{6,3},{7,4},{8,13},{9,14},{10,... | collective-permute-start | bytes 584 | tf_op jit(solution)/shard_map/ppermute | solution.py:233
  275.2 3.6 collective-permute-start.14
  276.2 3.7 collective-permute-start.15
  367.9 211.9 %collective-permute-start.24 = (bf16[256,3072]{1,0:T(8,128)(2,1)}, bf16[256,3072]{1,0:T(8,128)(2,1)S(1)}, u32[]{:S(2)}, u32[]{:S(2)}) collective-permute-start(bf16[256,3072]{1,0:T(8,128)(2,1)} %shard_map.47), channel_id=1, source_target_pairs={{0,4},{2,12},{4,20},{6,28},{8,0},{10,8},{12,16},{14,24},{16,6},{18... | collective-permute-start | bytes 4718600 | tf_op jit(solution)/shard_map/ppermute | solution.py:103
  413.7 166.2 %collective-permute-start.25 = (bf16[256,3072]{1,0:T(8,128)(2,1)}, bf16[256,3072]{1,0:T(8,128)(2,1)S(1)}, u32[]{:S(2)}, u32[]{:S(2)}) collective-permute-start(bf16[256,3072]{1,0:T(8,128)(2,1)} %shard_map.48), channel_id=1, source_target_pairs={{0,4},{2,12},{4,20},{6,28},{8,0},{10,8},{12,16},{14,24},{16,6},{18... | collective-permute-start | bytes 4718600 | tf_op jit(solution)/shard_map/ppermute | solution.py:103
  463.8 116.1 %collective-permute-start.26 = (bf16[256,3072]{1,0:T(8,128)(2,1)}, bf16[256,3072]{1,0:T(8,128)(2,1)}, u32[]{:S(2)}, u32[]{:S(2)}) collective-permute-start(bf16[256,3072]{1,0:T(8,128)(2,1)} %shard_map.49), channel_id=1, source_target_pairs={{0,4},{2,12},{4,20},{6,28},{8,0},{10,8},{12,16},{14,24},{16,6},{18... | collective-permute-start | bytes 4718600 | tf_op jit(solution)/shard_map/ppermute | solution.py:103
  576.0 39.0 %collective-permute-start.27 = (bf16[256,3072]{1,0:T(8,128)(2,1)}, bf16[256,3072]{1,0:T(8,128)(2,1)S(1)}, u32[]{:S(2)}, u32[]{:S(2)}) collective-permute-start(bf16[256,3072]{1,0:T(8,128)(2,1)} %shard_map.50), channel_id=1, source_target_pairs={{0,4},{2,12},{4,20},{6,28},{8,0},{10,8},{12,16},{14,24},{16,6},{18... | collective-permute-start | bytes 4718600 | tf_op jit(solution)/shard_map/ppermute | solution.py:103
  (2 other events, 25.7 us)
Sparse Core Ops, SparseCore 0:
  233.6 64.3 all-gather.4
  299.5 46.5 all-gather.6
  347.7 72.2 all-gather.8
  421.4 110.7 all-gather.10

commit v17 on v15

--- a/solution.py
+++ b/solution.py
@@ -173,19 +173,24 @@
             def one(entry, acc):
                 return acc + jnp.dot(window(entry), g_ref[entry], preferred_element_type=jnp.float32)
 
+            def grouped(width, base):
+                def step(index, acc):
+                    entry = base + width * index
+                    lhs = jnp.concatenate([window(entry + j) for j in range(width)], axis=1)
+                    rhs = jnp.concatenate([g_ref[entry + j] for j in range(width)], axis=0)
+                    return acc + jnp.dot(lhs, rhs, preferred_element_type=jnp.float32)
+
+                return step
+
             for chunk in range(piece_chunks):
                 begin = starts_ref[first + chunk]
                 end = starts_ref[first + chunk + 1]
-                pairs = (end - begin) // 2
-
-                def two(pair, acc, begin=begin):
-                    entry = begin + 2 * pair
-                    lhs = jnp.concatenate([window(entry), window(entry + 1)], axis=1)
-                    rhs = jnp.concatenate([g_ref[entry], g_ref[entry + 1]], axis=0)
-                    return acc + jnp.dot(lhs, rhs, preferred_element_type=jnp.float32)
-
-                acc = lax.fori_loop(0, pairs, two, jnp.zeros((row_total, LANE), jnp.float32))
-                acc = lax.fori_loop(begin + 2 * pairs, end, one, acc)
+                acc = jnp.zeros((row_total, LANE), jnp.float32)
+                for width in (4, 2):
+                    count = (end - begin) // width
+                    acc = lax.fori_loop(0, count, grouped(width, begin), acc)
+                    begin = begin + width * count
+                acc = lax.fori_loop(begin, end, one, acc)
                 o_ref[:, chunk * LANE : (chunk + 1) * LANE] = acc.astype(o_ref.dtype)
 
         grid_spec = pltpu.PrefetchScalarGridSpec(

time: 545 us -> 539 us (0.989)
  Pallas kernels: 193 us -> 148 us
  waiting for transfers between devices: 213 us -> 248 us
    pallas_call x4, Pallas kernels: 176 us -> 131 us  [block_sparse_product(): pl.pallas_call(kernel, grid_spec=grid_spec, out_shape=jax.ShapeDtypeStruc...]
    ppermute x4, waiting for transfers between devices: 71.8 us -> 105 us  [product_to_owners(): lax.ppermute(value, ('layer', 'row'), [(a * size + b, b * size + quarter[...]
  transfers between devices with their start and end apart: 32 -> 32, of which waited for: 12 -> 13; matrix products, arithmetic and copies ran while one was open for 10% -> 11% of each run, Pallas kernels for 35% -> 28%
where the time goes in v17:
time: 539 us; the launch traced here: 532 us
  waiting for transfers between devices  248 us (46%)
  Pallas kernels  148 us (27%)
  starting transfers between devices  54.3 us (10%)
  other arithmetic  41 us (8%)
  local copies, waits for them, and re-layouts  26.8 us (5%)
  between operations  13.8 us (3%)
    ppermute x21, waiting for transfers between devices, per_device(): lax.ppermute(part, ('row', 'col'), pairs)  141 us
    pallas_call x4, Pallas kernels, block_sparse_product(): pl.pallas_call(kernel, grid_spec=grid_spec, out_shape=jax.ShapeDtypeStruc...  131 us
    ppermute x4, waiting for transfers between devices, product_to_owners(): lax.ppermute(value, ('layer', 'row'), [(a * size + b, b * size + quarter[...  105 us
    ppermute x21, starting transfers between devices, per_device(): lax.ppermute(part, ('row', 'col'), pairs)  45.8 us
    pallas_call x1, Pallas kernels, gathered_windows(): pl.pallas_call(kernel, grid_spec=grid_spec, out_shape=jax.ShapeDtypeStruc...  17.3 us
    gather x1, local copies, waits for them, and re-layouts, block_sparse_product(): padded = padded_blocks(blocks, block_rows, block_cols)[order]  15.9 us
  transfers between devices with their start and end apart: 32, of which 13 were waited for; matrix products, arithmetic and copies ran while one was open for 11% of the time, Pallas kernels for 28%

profile of v17, /device:TPU:30, one launch (start us, length us, event | category | flops | bytes accessed | tf_op | source)
XLA Modules:
  0.0 531.7 jit_solution(15979545016223743505)
XLA Ops:
  7.5 3.2 broadcast_multiply_fusion
  10.7 2.8 slice_bitcast_fusion.3
  16.4 9.2 %scatter_custom_fusion = s32[48]{0:T(128)S(1)} fusion(s32[1152]{0:T(1024)S(1)} %fusion.3, s32[1152]{0:T(1024)S(1)} %broadcast.328, s32[]{:T(128)} %constant.155.clone.1), kind=kCustom, calls=%fused_computation.82 | custom fusion | flops 1152 | bytes 196 | tf_op jit(solution)/shard_map/scatter-add | solution.py:133
  29.6 17.3 %shard_map.46 = bf16[48,64,128]{2,1,0:T(8,128)(2,1)} custom-call(s32[48]{0:T(128)} %copy-done.1, s32[48]{0:T(128)} %and_select_fusion.cols_ref, bf16[1536,3072]{1,0:T(8,128)(2,1)} %green_ref.1), custom_call_target="tpu_custom_call" | custom-call | tf_op jit(solution)/shard_map/pallas_call | solution.py:122
  50.1 5.5 %collective-permute-start.16 = (bf16[48,64,64]{2,1,0:T(8,128)(2,1)S(1)}, bf16[48,64,64]{2,1,0:T(8,128)(2,1)S(1)}, u32[]{:S(2)}, u32[]{:S(2)}) collective-permute-start(bf16[48,64,64]{2,1,0:T(8,128)(2,1)S(1)} %fusion), channel_id=1, source_target_pairs={{0,8},{2,24},{4,0},{6,16},{8,10},{10,26},{12,2},{14,18},{16,12},{1... | collective-permute-start | bytes 1179656 | tf_op jit(solution)/shard_map/ppermute | solution.py:94
  55.8 2.8 collective-permute-start.3
  60.1 5.1 collective-permute-done.1
  65.2 24.3 %collective-permute-start.5 = (s32[48]{0:T(128)S(1)}, s32[48]{0:T(128)S(1)}, u32[]{:S(2)}, u32[]{:S(2)}) collective-permute-start(s32[48]{0:T(128)S(1)} %collective-permute-done), channel_id=1, source_target_pairs={{0,5},{1,6},{2,7},{3,0},{4,1},{5,2},{6,3},{7,4},{8,13},{9,14},{10,... | collective-permute-start | bytes 584 | tf_op jit(solution)/shard_map/ppermute | solution.py:238
  90.1 4.2 collective-permute-start.9
  94.3 2.0 collective-permute-start.10
  104.7 2.4 collective-permute-done.15
  107.3 3.8 sort.23
  111.1 2.8 gather_fusion.1
  115.1 2.8 gather_fusion
  118.6 2.6 collective-permute-start.19
  123.1 10.1 %collective-permute-done.17 = bf16[48,64,64]{2,1,0:T(8,128)(2,1)S(1)} collective-permute-done((bf16[48,64,64]{2,1,0:T(8,128)(2,1)S(1)}, bf16[48,64,64]{2,1,0:T(8,128)(2,1)S(1)}, u32[]{:S(2)}, u32[]{:S(2)}) %collective-permute-start.17) | collective-permute-done | bytes 393248 | tf_op jit(solution)/shard_map/ppermute | solution.py:238
  133.3 16.7 %collective-permute-done.18 = bf16[48,64,64]{2,1,0:T(8,128)(2,1)S(1)} collective-permute-done((bf16[48,64,64]{2,1,0:T(8,128)(2,1)S(1)}, bf16[48,64,64]{2,1,0:T(8,128)(2,1)S(1)}, u32[]{:S(2)}, u32[]{:S(2)}) %collective-permute-start.18) | collective-permute-done | bytes 393248 | tf_op jit(solution)/shard_map/ppermute | solution.py:238
  150.3 16.6 %collective-permute-done.19 = bf16[48,64,64]{2,1,0:T(8,128)(2,1)S(1)} collective-permute-done((bf16[48,64,64]{2,1,0:T(8,128)(2,1)S(1)}, bf16[48,64,64]{2,1,0:T(8,128)(2,1)S(1)}, u32[]{:S(2)}, u32[]{:S(2)}) %collective-permute-start.19) | collective-permute-done | bytes 393248 | tf_op jit(solution)/shard_map/ppermute | solution.py:238
  167.0 81.2 %collective-permute-done.20 = bf16[48,64,64]{2,1,0:T(8,128)(2,1)S(1)} collective-permute-done((bf16[48,64,64]{2,1,0:T(8,128)(2,1)S(1)}, bf16[48,64,64]{2,1,0:T(8,128)(2,1)S(1)}, u32[]{:S(2)}, u32[]{:S(2)}) %collective-permute-start.20) | collective-permute-done | bytes 393248 | tf_op jit(solution)/shard_map/ppermute | solution.py:238
  248.3 5.1 collective-permute-done.21
  255.3 6.3 %broadcast_select_fusion.1 = (bf16[384,64,128]{2,1,0:T(8,128)(2,1)S(1)}, bf16[384,64,128]{2,1,0:T(8,128)(2,1)S(1)}) fusion(pred[384]{0:T(512)(128)(4,1)S(1)} %fusion.6, bf16[384,64,64]{2,1,0:T(8,128)(2,1)S(1)} %get-tuple-element.15, bf16[384,64,64]{2,1,0:T(8,128)(2,1)S(1)} %get-tuple-element.14), kind=kLoop, calls=%fused_computation.11 | loop fusion | flops 18874368 | bytes 18874752 | tf_op jit(solution)/shard_map/jit(_where)/select_n | solution.py:151
  261.7 5.2 pad_maximum_fusion
  266.9 15.9 %gather_fusion.3 = bf16[384,128,128]{2,1,0:T(8,128)(2,1)} fusion(bf16[384,128,128]{2,1,0:T(8,128)(2,1)} %pad_maximum_fusion, s32[1024]{0:T(1024)S(1)} %pad_clamp_fusion.1), kind=kCustom, calls=%fused_computation.3 | custom fusion | bytes 25167360 | tf_op jit(solution)/shard_map/gather | solution.py:164
  282.8 32.8 %shard_map.47 = bf16[256,3072]{1,0:T(8,128)(2,1)} custom-call(s32[25]{0:T(128)} %convert_reduce_fusion.starts_ref, s32[384]{0:T(512)} %add_select_fusion.3.k_ref, bf16[256,12288]{1,0:T(8,128)(2,1)} %all-gather.5.cloned.1.call-done.t_ref, bf16[384,128,128]{2,1,0:T(8,128)(2,1)} %gather_fusion.3), custom_call_target="tpu_custom_call" | custom-call | tf_op jit(solution)/shard_map/pallas_call | solution.py:210
  315.6 32.6 %shard_map.48 = bf16[256,3072]{1,0:T(8,128)(2,1)} custom-call(s32[25]{0:T(128)} %convert_reduce_fusion.starts_ref, s32[384]{0:T(512)} %add_select_fusion.3.k_ref, bf16[256,12288]{1,0:T(8,128)(2,1)} %all-gather.7.cloned.1.call-done.t_ref, bf16[384,128,128]{2,1,0:T(8,128)(2,1)} %gather_fusion.3), custom_call_target="tpu_custom_call" | custom-call | tf_op jit(solution)/shard_map/pallas_call | solution.py:210
  349.9 32.9 %shard_map.49 = bf16[256,3072]{1,0:T(8,128)(2,1)} custom-call(s32[25]{0:T(128)} %convert_reduce_fusion.starts_ref, s32[384]{0:T(512)} %add_select_fusion.3.k_ref, bf16[256,12288]{1,0:T(8,128)(2,1)} %all-gather.9.cloned.1.call-done.t_ref, bf16[384,128,128]{2,1,0:T(8,128)(2,1)} %gather_fusion.3), custom_call_target="tpu_custom_call" | custom-call | tf_op jit(solution)/shard_map/pallas_call | solution.py:210
  382.8 32.6 %shard_map.50 = bf16[256,3072]{1,0:T(8,128)(2,1)} custom-call(s32[25]{0:T(128)} %convert_reduce_fusion.starts_ref, s32[384]{0:T(512)} %add_select_fusion.3.k_ref, bf16[256,12288]{1,0:T(8,128)(2,1)} %all-gather.11.cloned.1.call-done.t_ref, bf16[384,128,128]{2,1,0:T(8,128)(2,1)} %gather_fusion.3), custom_call_target="tpu_custom_call" | custom-call | tf_op jit(solution)/shard_map/pallas_call | solution.py:210
  415.4 54.6 %collective-permute-done.24 = bf16[256,3072]{1,0:T(8,128)(2,1)S(1)} collective-permute-done((bf16[256,3072]{1,0:T(8,128)(2,1)}, bf16[256,3072]{1,0:T(8,128)(2,1)S(1)}, u32[]{:S(2)}, u32[]{:S(2)}) %collective-permute-start.24) | collective-permute-done | bytes 1572896 | tf_op jit(solution)/shard_map/ppermute | solution.py:103
  470.1 16.9 %collective-permute-done.25 = bf16[256,3072]{1,0:T(8,128)(2,1)S(1)} collective-permute-done((bf16[256,3072]{1,0:T(8,128)(2,1)}, bf16[256,3072]{1,0:T(8,128)(2,1)S(1)}, u32[]{:S(2)}, u32[]{:S(2)}) %collective-permute-start.25) | collective-permute-done | bytes 1572896 | tf_op jit(solution)/shard_map/ppermute | solution.py:103
  486.9 17.0 %collective-permute-done.26 = bf16[256,3072]{1,0:T(8,128)(2,1)} collective-permute-done((bf16[256,3072]{1,0:T(8,128)(2,1)}, bf16[256,3072]{1,0:T(8,128)(2,1)}, u32[]{:S(2)}, u32[]{:S(2)}) %collective-permute-start.26) | collective-permute-done | bytes 1572896 | tf_op jit(solution)/shard_map/ppermute | solution.py:103
  503.9 16.7 %collective-permute-done.27 = bf16[256,3072]{1,0:T(8,128)(2,1)S(1)} collective-permute-done((bf16[256,3072]{1,0:T(8,128)(2,1)}, bf16[256,3072]{1,0:T(8,128)(2,1)S(1)}, u32[]{:S(2)}, u32[]{:S(2)}) %collective-permute-start.27) | collective-permute-done | bytes 1572896 | tf_op jit(solution)/shard_map/ppermute | solution.py:103
  520.6 4.1 maximum_bitcast_fusion
  (102 shorter events, 29.7 us)
Async XLA Ops:
  6.5 276.3 %all-gather.5.cloned.1.call-start = ((), (), s32[]{:S(2)}) async-start(), calls=%async_computation | async-start | bytes 7864320 | tf_op jit(solution)/shard_map/all_gather | solution.py:249
  13.6 302.0 %all-gather.7.cloned.1.call-start = ((), (), s32[]{:S(2)}) async-start(), calls=%async_computation.1 | async-start | bytes 7864320 | tf_op jit(solution)/shard_map/all_gather | solution.py:249
  14.3 335.5 %all-gather.9.cloned.1.call-start = ((), (), s32[]{:S(2)}) async-start(), calls=%async_computation.2 | async-start | bytes 7864320 | tf_op jit(solution)/shard_map/all_gather | solution.py:249
  15.1 367.7 %all-gather.11.cloned.1.call-start = ((), (), s32[]{:S(2)}) async-start(), calls=%async_computation.3 | async-start | bytes 7864320 | tf_op jit(solution)/shard_map/all_gather | solution.py:249
  27.8 27.8 %collective-permute-start = (s32[48]{0:T(128)S(1)}, s32[48]{0:T(128)S(1)}, u32[]{:S(2)}, u32[]{:S(2)}) collective-permute-start(s32[48]{0:T(128)S(1)} %get-tuple-element.10), channel_id=1, source_target_pairs={{0,8},{2,24},{4,0},{6,16},{8,10},{10,26},{12,2},{14,18},{16,12},{1... | collective-permute-start | bytes 584 | tf_op jit(solution)/shard_map/ppermute | solution.py:94
  28.3 30.3 %collective-permute-start.8 = (s32[48]{0:T(128)S(1)}, s32[48]{0:T(128)S(1)}, u32[]{:S(2)}, u32[]{:S(2)}) collective-permute-start(s32[48]{0:T(128)S(1)} %and_select_fusion.2.rows_ref), channel_id=1, source_target_pairs={{0,8},{2,24},{4,0},{6,16},{8,10},{10,26},{12,2},{14,18},{16,12},{1... | collective-permute-start | bytes 584 | tf_op jit(solution)/shard_map/ppermute | solution.py:94
  50.1 64.5 %collective-permute-start.16 = (bf16[48,64,64]{2,1,0:T(8,128)(2,1)S(1)}, bf16[48,64,64]{2,1,0:T(8,128)(2,1)S(1)}, u32[]{:S(2)}, u32[]{:S(2)}) collective-permute-start(bf16[48,64,64]{2,1,0:T(8,128)(2,1)S(1)} %fusion), channel_id=1, source_target_pairs={{0,8},{2,24},{4,0},{6,16},{8,10},{10,26},{12,2},{14,18},{16,12},{1... | collective-permute-start | bytes 1179656 | tf_op jit(solution)/shard_map/ppermute | solution.py:94
  55.6 9.6 %collective-permute-start.1 = (s32[48]{0:T(128)S(1)}, s32[48]{0:T(128)S(1)}, u32[]{:S(2)}, u32[]{:S(2)}) collective-permute-start(s32[48]{0:T(128)S(1)} %collective-permute-done), channel_id=1, source_target_pairs={{0,1},{1,2},{2,3},{3,4},{4,5},{5,6},{6,7},{7,0},{8,9},{9,10},{10,1... | collective-permute-start | bytes 584 | tf_op jit(solution)/shard_map/ppermute | solution.py:238
  55.7 33.8 %collective-permute-start.2 = (s32[48]{0:T(128)S(1)}, s32[48]{0:T(128)S(1)}, u32[]{:S(2)}, u32[]{:S(2)}) collective-permute-start(s32[48]{0:T(128)S(1)} %collective-permute-done), channel_id=1, source_target_pairs={{0,2},{1,3},{2,4},{3,5},{4,6},{5,7},{6,0},{7,1},{8,10},{9,11},{10,... | collective-permute-start | bytes 584 | tf_op jit(solution)/shard_map/ppermute | solution.py:238
  55.8 33.7 %collective-permute-start.3 = (s32[48]{0:T(128)S(1)}, s32[48]{0:T(128)S(1)}, u32[]{:S(2)}, u32[]{:S(2)}) collective-permute-start(s32[48]{0:T(128)S(1)} %collective-permute-done), channel_id=1, source_target_pairs={{0,3},{1,4},{2,5},{3,6},{4,7},{5,0},{6,1},{7,2},{8,11},{9,12},{10,... | collective-permute-start | bytes 584 | tf_op jit(solution)/shard_map/ppermute | solution.py:238
  58.6 31.5 %collective-permute-start.4 = (s32[48]{0:T(128)S(1)}, s32[48]{0:T(128)S(1)}, u32[]{:S(2)}, u32[]{:S(2)}) collective-permute-start(s32[48]{0:T(128)S(1)} %collective-permute-done), channel_id=1, source_target_pairs={{0,4},{1,5},{2,6},{3,7},{4,0},{5,1},{6,2},{7,3},{8,12},{9,13},{10,... | collective-permute-start | bytes 584 | tf_op jit(solution)/shard_map/ppermute | solution.py:238
  65.2 29.1 %collective-permute-start.5 = (s32[48]{0:T(128)S(1)}, s32[48]{0:T(128)S(1)}, u32[]{:S(2)}, u32[]{:S(2)}) collective-permute-start(s32[48]{0:T(128)S(1)} %collective-permute-done), channel_id=1, source_target_pairs={{0,5},{1,6},{2,7},{3,0},{4,1},{5,2},{6,3},{7,4},{8,13},{9,14},{10,... | collective-permute-start | bytes 584 | tf_op jit(solution)/shard_map/ppermute | solution.py:238
  89.5 6.8 %collective-permute-start.6 = (s32[48]{0:T(128)S(1)}, s32[48]{0:T(128)S(1)}, u32[]{:S(2)}, u32[]{:S(2)}) collective-permute-start(s32[48]{0:T(128)S(1)} %collective-permute-done), channel_id=1, source_target_pairs={{0,6},{1,7},{2,0},{3,1},{4,2},{5,3},{6,4},{7,5},{8,14},{9,15},{10,... | collective-permute-start | bytes 584 | tf_op jit(solution)/shard_map/ppermute | solution.py:238
  89.5 6.8 %collective-permute-start.7 = (s32[48]{0:T(128)S(1)}, s32[48]{0:T(128)S(1)}, u32[]{:S(2)}, u32[]{:S(2)}) collective-permute-start(s32[48]{0:T(128)S(1)} %collective-permute-done), channel_id=1, source_target_pairs={{0,7},{1,0},{2,1},{3,2},{4,3},{5,4},{6,5},{7,6},{8,15},{9,8},{10,9... | collective-permute-start | bytes 584 | tf_op jit(solution)/shard_map/ppermute | solution.py:238
  90.1 7.8 %collective-permute-start.9 = (s32[48]{0:T(128)S(1)}, s32[48]{0:T(128)S(1)}, u32[]{:S(2)}, u32[]{:S(2)}) collective-permute-start(s32[48]{0:T(128)S(1)} %collective-permute-done.8), channel_id=1, source_target_pairs={{0,1},{1,2},{2,3},{3,4},{4,5},{5,6},{6,7},{7,0},{8,9},{9,10},{10,1... | collective-permute-start | bytes 584 | tf_op jit(solution)/shard_map/ppermute | solution.py:238
  94.3 5.1 collective-permute-start.10
  96.3 4.6 collective-permute-start.11
  96.3 5.2 collective-permute-start.12
  97.9 5.4 %collective-permute-start.13 = (s32[48]{0:T(128)S(1)}, s32[48]{0:T(128)S(1)}, u32[]{:S(2)}, u32[]{:S(2)}) collective-permute-start(s32[48]{0:T(128)S(1)} %collective-permute-done.8), channel_id=1, source_target_pairs={{0,5},{1,6},{2,7},{3,0},{4,1},{5,2},{6,3},{7,4},{8,13},{9,14},{10,... | collective-permute-start | bytes 584 | tf_op jit(solution)/shard_map/ppermute | solution.py:238
  99.4 5.3 %collective-permute-start.14 = (s32[48]{0:T(128)S(1)}, s32[48]{0:T(128)S(1)}, u32[]{:S(2)}, u32[]{:S(2)}) collective-permute-start(s32[48]{0:T(128)S(1)} %collective-permute-done.8), channel_id=1, source_target_pairs={{0,6},{1,7},{2,0},{3,1},{4,2},{5,3},{6,4},{7,5},{8,14},{9,15},{10,... | collective-permute-start | bytes 584 | tf_op jit(solution)/shard_map/ppermute | solution.py:238
  100.9 6.2 %collective-permute-start.15 = (s32[48]{0:T(128)S(1)}, s32[48]{0:T(128)S(1)}, u32[]{:S(2)}, u32[]{:S(2)}) collective-permute-start(s32[48]{0:T(128)S(1)} %collective-permute-done.8), channel_id=1, source_target_pairs={{0,7},{1,0},{2,1},{3,2},{4,3},{5,4},{6,5},{7,6},{8,15},{9,8},{10,9... | collective-permute-start | bytes 584 | tf_op jit(solution)/shard_map/ppermute | solution.py:238
  114.5 18.7 %collective-permute-start.17 = (bf16[48,64,64]{2,1,0:T(8,128)(2,1)S(1)}, bf16[48,64,64]{2,1,0:T(8,128)(2,1)S(1)}, u32[]{:S(2)}, u32[]{:S(2)}) collective-permute-start(bf16[48,64,64]{2,1,0:T(8,128)(2,1)S(1)} %collective-permute-done.16), channel_id=1, source_target_pairs={{0,1},{1,2},{2,3},{3,4},{4,5},{5,6},{6,7},{7,0},{8,9},{9,10},{10,1... | collective-permute-start | bytes 1179656 | tf_op jit(solution)/shard_map/ppermute | solution.py:238
  118.6 31.5 %collective-permute-start.18 = (bf16[48,64,64]{2,1,0:T(8,128)(2,1)S(1)}, bf16[48,64,64]{2,1,0:T(8,128)(2,1)S(1)}, u32[]{:S(2)}, u32[]{:S(2)}) collective-permute-start(bf16[48,64,64]{2,1,0:T(8,128)(2,1)S(1)} %collective-permute-done.16), channel_id=1, source_target_pairs={{0,2},{1,3},{2,4},{3,5},{4,6},{5,7},{6,0},{7,1},{8,10},{9,11},{10,... | collective-permute-start | bytes 1179656 | tf_op jit(solution)/shard_map/ppermute | solution.py:238
  118.6 48.3 %collective-permute-start.19 = (bf16[48,64,64]{2,1,0:T(8,128)(2,1)S(1)}, bf16[48,64,64]{2,1,0:T(8,128)(2,1)S(1)}, u32[]{:S(2)}, u32[]{:S(2)}) collective-permute-start(bf16[48,64,64]{2,1,0:T(8,128)(2,1)S(1)} %collective-permute-done.16), channel_id=1, source_target_pairs={{0,3},{1,4},{2,5},{3,6},{4,7},{5,0},{6,1},{7,2},{8,11},{9,12},{10,... | collective-permute-start | bytes 1179656 | tf_op jit(solution)/shard_map/ppermute | solution.py:238
  121.2 127.0 %collective-permute-start.20 = (bf16[48,64,64]{2,1,0:T(8,128)(2,1)S(1)}, bf16[48,64,64]{2,1,0:T(8,128)(2,1)S(1)}, u32[]{:S(2)}, u32[]{:S(2)}) collective-permute-start(bf16[48,64,64]{2,1,0:T(8,128)(2,1)S(1)} %collective-permute-done.16), channel_id=1, source_target_pairs={{0,4},{1,5},{2,6},{3,7},{4,0},{5,1},{6,2},{7,3},{8,12},{9,13},{10,... | collective-permute-start | bytes 1179656 | tf_op jit(solution)/shard_map/ppermute | solution.py:238
  123.0 130.4 %collective-permute-start.21 = (bf16[48,64,64]{2,1,0:T(8,128)(2,1)S(1)}, bf16[48,64,64]{2,1,0:T(8,128)(2,1)S(1)}, u32[]{:S(2)}, u32[]{:S(2)}) collective-permute-start(bf16[48,64,64]{2,1,0:T(8,128)(2,1)S(1)} %collective-permute-done.16), channel_id=1, source_target_pairs={{0,5},{1,6},{2,7},{3,0},{4,1},{5,2},{6,3},{7,4},{8,13},{9,14},{10,... | collective-permute-start | bytes 1179656 | tf_op jit(solution)/shard_map/ppermute | solution.py:238
  133.2 120.3 %collective-permute-start.22 = (bf16[48,64,64]{2,1,0:T(8,128)(2,1)S(1)}, bf16[48,64,64]{2,1,0:T(8,128)(2,1)S(1)}, u32[]{:S(2)}, u32[]{:S(2)}) collective-permute-start(bf16[48,64,64]{2,1,0:T(8,128)(2,1)S(1)} %collective-permute-done.16), channel_id=1, source_target_pairs={{0,6},{1,7},{2,0},{3,1},{4,2},{5,3},{6,4},{7,5},{8,14},{9,15},{10,... | collective-permute-start | bytes 1179656 | tf_op jit(solution)/shard_map/ppermute | solution.py:238
  150.0 103.6 %collective-permute-start.23 = (bf16[48,64,64]{2,1,0:T(8,128)(2,1)S(1)}, bf16[48,64,64]{2,1,0:T(8,128)(2,1)S(1)}, u32[]{:S(2)}, u32[]{:S(2)}) collective-permute-start(bf16[48,64,64]{2,1,0:T(8,128)(2,1)S(1)} %collective-permute-done.16), channel_id=1, source_target_pairs={{0,7},{1,0},{2,1},{3,2},{4,3},{5,4},{6,5},{7,6},{8,15},{9,8},{10,9... | collective-permute-start | bytes 1179656 | tf_op jit(solution)/shard_map/ppermute | solution.py:238
  315.6 154.5 %collective-permute-start.24 = (bf16[256,3072]{1,0:T(8,128)(2,1)}, bf16[256,3072]{1,0:T(8,128)(2,1)S(1)}, u32[]{:S(2)}, u32[]{:S(2)}) collective-permute-start(bf16[256,3072]{1,0:T(8,128)(2,1)} %shard_map.47), channel_id=1, source_target_pairs={{0,4},{2,12},{4,20},{6,28},{8,0},{10,8},{12,16},{14,24},{16,6},{18... | collective-permute-start | bytes 4718600 | tf_op jit(solution)/shard_map/ppermute | solution.py:103
  348.2 138.8 %collective-permute-start.25 = (bf16[256,3072]{1,0:T(8,128)(2,1)}, bf16[256,3072]{1,0:T(8,128)(2,1)S(1)}, u32[]{:S(2)}, u32[]{:S(2)}) collective-permute-start(bf16[256,3072]{1,0:T(8,128)(2,1)} %shard_map.48), channel_id=1, source_target_pairs={{0,4},{2,12},{4,20},{6,28},{8,0},{10,8},{12,16},{14,24},{16,6},{18... | collective-permute-start | bytes 4718600 | tf_op jit(solution)/shard_map/ppermute | solution.py:103
  382.8 121.1 %collective-permute-start.26 = (bf16[256,3072]{1,0:T(8,128)(2,1)}, bf16[256,3072]{1,0:T(8,128)(2,1)}, u32[]{:S(2)}, u32[]{:S(2)}) collective-permute-start(bf16[256,3072]{1,0:T(8,128)(2,1)} %shard_map.49), channel_id=1, source_target_pairs={{0,4},{2,12},{4,20},{6,28},{8,0},{10,8},{12,16},{14,24},{16,6},{18... | collective-permute-start | bytes 4718600 | tf_op jit(solution)/shard_map/ppermute | solution.py:103
  415.4 105.3 %collective-permute-start.27 = (bf16[256,3072]{1,0:T(8,128)(2,1)}, bf16[256,3072]{1,0:T(8,128)(2,1)S(1)}, u32[]{:S(2)}, u32[]{:S(2)}) collective-permute-start(bf16[256,3072]{1,0:T(8,128)(2,1)} %shard_map.50), channel_id=1, source_target_pairs={{0,4},{2,12},{4,20},{6,28},{8,0},{10,8},{12,16},{14,24},{16,6},{18... | collective-permute-start | bytes 4718600 | tf_op jit(solution)/shard_map/ppermute | solution.py:103
  (2 other events, 3.4 us)
Sparse Core Ops, SparseCore 0:
  13.7 60.6 all-gather.4
  76.0 48.9 all-gather.6
  126.5 46.3 all-gather.8
  174.4 46.3 all-gather.10

commit v18 on v17

--- a/solution.py
+++ b/solution.py
@@ -8,7 +8,7 @@
 BLK = 64
 CAP = 48
 LANE = 128
-ROW_CHUNK = 256
+ROW_CHUNK = 512
 
 
 def passed_along(value, axis, by):

time: 539 us -> 550 us (1.020)
  waiting for transfers between devices: 248 us -> 298 us
  Pallas kernels: 148 us -> 111 us
    ppermute x4 -> x2, waiting for transfers between devices: 105 us -> 156 us  [product_to_owners(): lax.ppermute(value, ('layer', 'row'), [(a * size + b, b * size + quarter[...]
    pallas_call x4 -> x2, Pallas kernels: 131 us -> 91.9 us  [block_sparse_product(): pl.pallas_call(kernel, grid_spec=grid_spec, out_shape=jax.ShapeDtypeStruc...]
  transfers between devices with their start and end apart: 32 -> 28, of which waited for: 13 -> 11; matrix products, arithmetic and copies ran while one was open for 11% -> 10% of each run, Pallas kernels for 28% -> 20%
where the time goes in v18:
time: 550 us; the launch traced here: 543 us
  waiting for transfers between devices  298 us (54%)
  Pallas kernels  111 us (20%)
  starting transfers between devices  53.3 us (10%)
  other arithmetic  39.7 us (7%)
  local copies, waits for them, and re-layouts  27.1 us (5%)
  between operations  13.8 us (3%)
    ppermute x2, waiting for transfers between devices, product_to_owners(): lax.ppermute(value, ('layer', 'row'), [(a * size + b, b * size + quarter[...  156 us
    ppermute x21, waiting for transfers between devices, per_device(): lax.ppermute(part, ('row', 'col'), pairs)  141 us
    pallas_call x2, Pallas kernels, block_sparse_product(): pl.pallas_call(kernel, grid_spec=grid_spec, out_shape=jax.ShapeDtypeStruc...  91.9 us
    ppermute x21, starting transfers between devices, per_device(): lax.ppermute(part, ('row', 'col'), pairs)  44.5 us
    pallas_call x1, Pallas kernels, gathered_windows(): pl.pallas_call(kernel, grid_spec=grid_spec, out_shape=jax.ShapeDtypeStruc...  19.1 us
    gather x1, local copies, waits for them, and re-layouts, block_sparse_product(): padded = padded_blocks(blocks, block_rows, block_cols)[order]  15.9 us
  transfers between devices with their start and end apart: 28, of which 11 were waited for; matrix products, arithmetic and copies ran while one was open for 10% of the time, Pallas kernels for 20%

profile of v18, /device:TPU:30, one launch (start us, length us, event | category | flops | bytes accessed | tf_op | source)
XLA Modules:
  0.0 542.7 jit_solution(5367151225143361419)
XLA Ops:
  7.5 3.2 broadcast_multiply_fusion
  10.7 3.1 slice_bitcast_fusion.1
  15.3 9.2 %scatter_custom_fusion = s32[48]{0:T(128)S(1)} fusion(s32[1152]{0:T(1024)S(1)} %fusion.3, s32[1152]{0:T(1024)S(1)} %broadcast.324, s32[]{:T(128)} %constant.133.clone.1), kind=kCustom, calls=%fused_computation.80 | custom fusion | flops 1152 | bytes 196 | tf_op jit(solution)/shard_map/scatter-add | solution.py:133
  28.3 19.1 %shard_map.46 = bf16[48,64,128]{2,1,0:T(8,128)(2,1)} custom-call(s32[48]{0:T(128)} %copy-done.1, s32[48]{0:T(128)} %and_select_fusion.cols_ref, bf16[1536,3072]{1,0:T(8,128)(2,1)} %green_ref.1), custom_call_target="tpu_custom_call" | custom-call | tf_op jit(solution)/shard_map/pallas_call | solution.py:122
  48.8 1.8 fusion
  50.5 3.8 collective-permute-start.16
  54.4 2.9 collective-permute-start.3
  58.8 5.1 collective-permute-done.1
  63.9 23.1 %collective-permute-start.5 = (s32[48]{0:T(128)S(1)}, s32[48]{0:T(128)S(1)}, u32[]{:S(2)}, u32[]{:S(2)}) collective-permute-start(s32[48]{0:T(128)S(1)} %collective-permute-done), channel_id=1, source_target_pairs={{0,5},{1,6},{2,7},{3,0},{4,1},{5,2},{6,3},{7,4},{8,13},{9,14},{10,... | collective-permute-start | bytes 584 | tf_op jit(solution)/shard_map/ppermute | solution.py:238
  87.8 3.9 collective-permute-start.9
  91.8 2.0 collective-permute-start.10
  98.9 1.8 collective-permute-done.13
  102.2 2.4 collective-permute-done.15
  104.8 3.8 sort.19
  108.6 2.8 gather_fusion.1
  112.6 2.8 gather_fusion
  116.1 2.6 collective-permute-start.19
  118.6 1.8 collective-permute-start.20
  120.5 10.1 %collective-permute-done.17 = bf16[48,64,64]{2,1,0:T(8,128)(2,1)S(1)} collective-permute-done((bf16[48,64,64]{2,1,0:T(8,128)(2,1)S(1)}, bf16[48,64,64]{2,1,0:T(8,128)(2,1)S(1)}, u32[]{:S(2)}, u32[]{:S(2)}) %collective-permute-start.17) | collective-permute-done | bytes 393248 | tf_op jit(solution)/shard_map/ppermute | solution.py:238
  130.7 16.7 %collective-permute-done.18 = bf16[48,64,64]{2,1,0:T(8,128)(2,1)S(1)} collective-permute-done((bf16[48,64,64]{2,1,0:T(8,128)(2,1)S(1)}, bf16[48,64,64]{2,1,0:T(8,128)(2,1)S(1)}, u32[]{:S(2)}, u32[]{:S(2)}) %collective-permute-start.18) | collective-permute-done | bytes 393248 | tf_op jit(solution)/shard_map/ppermute | solution.py:238
  147.8 16.6 %collective-permute-done.19 = bf16[48,64,64]{2,1,0:T(8,128)(2,1)S(1)} collective-permute-done((bf16[48,64,64]{2,1,0:T(8,128)(2,1)S(1)}, bf16[48,64,64]{2,1,0:T(8,128)(2,1)S(1)}, u32[]{:S(2)}, u32[]{:S(2)}) %collective-permute-start.19) | collective-permute-done | bytes 393248 | tf_op jit(solution)/shard_map/ppermute | solution.py:238
  164.5 81.5 %collective-permute-done.20 = bf16[48,64,64]{2,1,0:T(8,128)(2,1)S(1)} collective-permute-done((bf16[48,64,64]{2,1,0:T(8,128)(2,1)S(1)}, bf16[48,64,64]{2,1,0:T(8,128)(2,1)S(1)}, u32[]{:S(2)}, u32[]{:S(2)}) %collective-permute-start.20) | collective-permute-done | bytes 393248 | tf_op jit(solution)/shard_map/ppermute | solution.py:238
  246.1 5.0 collective-permute-done.21
  253.1 6.3 %broadcast_select_fusion.1 = (bf16[384,64,128]{2,1,0:T(8,128)(2,1)S(1)}, bf16[384,64,128]{2,1,0:T(8,128)(2,1)S(1)}) fusion(pred[384]{0:T(512)(128)(4,1)S(1)} %fusion.6, bf16[384,64,64]{2,1,0:T(8,128)(2,1)S(1)} %get-tuple-element.15, bf16[384,64,64]{2,1,0:T(8,128)(2,1)S(1)} %get-tuple-element.14), kind=kLoop, calls=%fused_computation.11 | loop fusion | flops 18874368 | bytes 18874752 | tf_op jit(solution)/shard_map/jit(_where)/select_n | solution.py:151
  259.4 5.2 pad_maximum_fusion
  264.6 15.9 %gather_fusion.3 = bf16[384,128,128]{2,1,0:T(8,128)(2,1)} fusion(bf16[384,128,128]{2,1,0:T(8,128)(2,1)} %pad_maximum_fusion, s32[1024]{0:T(1024)S(1)} %pad_clamp_fusion.1), kind=kCustom, calls=%fused_computation.3 | custom fusion | bytes 25167360 | tf_op jit(solution)/shard_map/gather | solution.py:164
  280.6 46.0 %shard_map.47 = bf16[512,3072]{1,0:T(8,128)(2,1)} custom-call(s32[25]{0:T(128)} %convert_reduce_fusion.starts_ref, s32[384]{0:T(512)} %add_select_fusion.3.k_ref, bf16[512,12288]{1,0:T(8,128)(2,1)} %all-gather.3.cloned.1.call-done.t_ref, bf16[384,128,128]{2,1,0:T(8,128)(2,1)} %gather_fusion.3), custom_call_target="tpu_custom_call" | custom-call | tf_op jit(solution)/shard_map/pallas_call | solution.py:210
  326.6 45.8 %shard_map.48 = bf16[512,3072]{1,0:T(8,128)(2,1)} custom-call(s32[25]{0:T(128)} %convert_reduce_fusion.starts_ref, s32[384]{0:T(512)} %add_select_fusion.3.k_ref, bf16[512,12288]{1,0:T(8,128)(2,1)} %all-gather.5.cloned.1.call-done.t_ref, bf16[384,128,128]{2,1,0:T(8,128)(2,1)} %gather_fusion.3), custom_call_target="tpu_custom_call" | custom-call | tf_op jit(solution)/shard_map/pallas_call | solution.py:210
  372.4 3.9 collective-permute-start.25
  376.3 122.5 %collective-permute-done.24 = bf16[512,3072]{1,0:T(8,128)(2,1)S(1)} collective-permute-done((bf16[512,3072]{1,0:T(8,128)(2,1)}, bf16[512,3072]{1,0:T(8,128)(2,1)S(1)}, u32[]{:S(2)}, u32[]{:S(2)}) %collective-permute-start.24) | collective-permute-done | bytes 3145760 | tf_op jit(solution)/shard_map/ppermute | solution.py:103
  498.8 33.7 %collective-permute-done.25 = bf16[512,3072]{1,0:T(8,128)(2,1)S(1)} collective-permute-done((bf16[512,3072]{1,0:T(8,128)(2,1)}, bf16[512,3072]{1,0:T(8,128)(2,1)S(1)}, u32[]{:S(2)}, u32[]{:S(2)}) %collective-permute-start.25) | collective-permute-done | bytes 3145760 | tf_op jit(solution)/shard_map/ppermute | solution.py:103
  532.5 3.1 maximum_bitcast_fusion
  (90 shorter events, 21.1 us)
Async XLA Ops:
  6.5 274.0 %all-gather.3.cloned.1.call-start = ((), (), s32[]{:S(2)}) async-start(), calls=%async_computation | async-start | bytes 15728640 | tf_op jit(solution)/shard_map/all_gather | solution.py:249
  13.8 0.8 copy-start
  13.8 312.8 %all-gather.5.cloned.1.call-start = ((), (), s32[]{:S(2)}) async-start(), calls=%async_computation.1 | async-start | bytes 15728640 | tf_op jit(solution)/shard_map/all_gather | solution.py:249
  26.6 27.8 %collective-permute-start = (s32[48]{0:T(128)S(1)}, s32[48]{0:T(128)S(1)}, u32[]{:S(2)}, u32[]{:S(2)}) collective-permute-start(s32[48]{0:T(128)S(1)} %get-tuple-element.10), channel_id=1, source_target_pairs={{0,8},{2,24},{4,0},{6,16},{8,10},{10,26},{12,2},{14,18},{16,12},{1... | collective-permute-start | bytes 584 | tf_op jit(solution)/shard_map/ppermute | solution.py:94
  27.1 1.2 copy-start.1
  27.1 30.2 %collective-permute-start.8 = (s32[48]{0:T(128)S(1)}, s32[48]{0:T(128)S(1)}, u32[]{:S(2)}, u32[]{:S(2)}) collective-permute-start(s32[48]{0:T(128)S(1)} %and_select_fusion.2.rows_ref), channel_id=1, source_target_pairs={{0,8},{2,24},{4,0},{6,16},{8,10},{10,26},{12,2},{14,18},{16,12},{1... | collective-permute-start | bytes 584 | tf_op jit(solution)/shard_map/ppermute | solution.py:94
  50.5 61.4 %collective-permute-start.16 = (bf16[48,64,64]{2,1,0:T(8,128)(2,1)S(1)}, bf16[48,64,64]{2,1,0:T(8,128)(2,1)S(1)}, u32[]{:S(2)}, u32[]{:S(2)}) collective-permute-start(bf16[48,64,64]{2,1,0:T(8,128)(2,1)S(1)} %fusion), channel_id=1, source_target_pairs={{0,8},{2,24},{4,0},{6,16},{8,10},{10,26},{12,2},{14,18},{16,12},{1... | collective-permute-start | bytes 1179656 | tf_op jit(solution)/shard_map/ppermute | solution.py:94
  54.3 9.5 %collective-permute-start.1 = (s32[48]{0:T(128)S(1)}, s32[48]{0:T(128)S(1)}, u32[]{:S(2)}, u32[]{:S(2)}) collective-permute-start(s32[48]{0:T(128)S(1)} %collective-permute-done), channel_id=1, source_target_pairs={{0,1},{1,2},{2,3},{3,4},{4,5},{5,6},{6,7},{7,0},{8,9},{9,10},{10,1... | collective-permute-start | bytes 584 | tf_op jit(solution)/shard_map/ppermute | solution.py:238
  54.4 32.6 %collective-permute-start.2 = (s32[48]{0:T(128)S(1)}, s32[48]{0:T(128)S(1)}, u32[]{:S(2)}, u32[]{:S(2)}) collective-permute-start(s32[48]{0:T(128)S(1)} %collective-permute-done), channel_id=1, source_target_pairs={{0,2},{1,3},{2,4},{3,5},{4,6},{5,7},{6,0},{7,1},{8,10},{9,11},{10,... | collective-permute-start | bytes 584 | tf_op jit(solution)/shard_map/ppermute | solution.py:238
  54.4 32.5 %collective-permute-start.3 = (s32[48]{0:T(128)S(1)}, s32[48]{0:T(128)S(1)}, u32[]{:S(2)}, u32[]{:S(2)}) collective-permute-start(s32[48]{0:T(128)S(1)} %collective-permute-done), channel_id=1, source_target_pairs={{0,3},{1,4},{2,5},{3,6},{4,7},{5,0},{6,1},{7,2},{8,11},{9,12},{10,... | collective-permute-start | bytes 584 | tf_op jit(solution)/shard_map/ppermute | solution.py:238
  57.3 30.5 %collective-permute-start.4 = (s32[48]{0:T(128)S(1)}, s32[48]{0:T(128)S(1)}, u32[]{:S(2)}, u32[]{:S(2)}) collective-permute-start(s32[48]{0:T(128)S(1)} %collective-permute-done), channel_id=1, source_target_pairs={{0,4},{1,5},{2,6},{3,7},{4,0},{5,1},{6,2},{7,3},{8,12},{9,13},{10,... | collective-permute-start | bytes 584 | tf_op jit(solution)/shard_map/ppermute | solution.py:238
  63.9 27.9 %collective-permute-start.5 = (s32[48]{0:T(128)S(1)}, s32[48]{0:T(128)S(1)}, u32[]{:S(2)}, u32[]{:S(2)}) collective-permute-start(s32[48]{0:T(128)S(1)} %collective-permute-done), channel_id=1, source_target_pairs={{0,5},{1,6},{2,7},{3,0},{4,1},{5,2},{6,3},{7,4},{8,13},{9,14},{10,... | collective-permute-start | bytes 584 | tf_op jit(solution)/shard_map/ppermute | solution.py:238
  87.0 6.8 %collective-permute-start.6 = (s32[48]{0:T(128)S(1)}, s32[48]{0:T(128)S(1)}, u32[]{:S(2)}, u32[]{:S(2)}) collective-permute-start(s32[48]{0:T(128)S(1)} %collective-permute-done), channel_id=1, source_target_pairs={{0,6},{1,7},{2,0},{3,1},{4,2},{5,3},{6,4},{7,5},{8,14},{9,15},{10,... | collective-permute-start | bytes 584 | tf_op jit(solution)/shard_map/ppermute | solution.py:238
  87.0 6.8 %collective-permute-start.7 = (s32[48]{0:T(128)S(1)}, s32[48]{0:T(128)S(1)}, u32[]{:S(2)}, u32[]{:S(2)}) collective-permute-start(s32[48]{0:T(128)S(1)} %collective-permute-done), channel_id=1, source_target_pairs={{0,7},{1,0},{2,1},{3,2},{4,3},{5,4},{6,5},{7,6},{8,15},{9,8},{10,9... | collective-permute-start | bytes 584 | tf_op jit(solution)/shard_map/ppermute | solution.py:238
  87.8 7.6 %collective-permute-start.9 = (s32[48]{0:T(128)S(1)}, s32[48]{0:T(128)S(1)}, u32[]{:S(2)}, u32[]{:S(2)}) collective-permute-start(s32[48]{0:T(128)S(1)} %collective-permute-done.8), channel_id=1, source_target_pairs={{0,1},{1,2},{2,3},{3,4},{4,5},{5,6},{6,7},{7,0},{8,9},{9,10},{10,1... | collective-permute-start | bytes 584 | tf_op jit(solution)/shard_map/ppermute | solution.py:238
  91.8 5.1 collective-permute-start.10
  93.8 4.6 collective-permute-start.11
  93.8 5.2 collective-permute-start.12
  95.4 5.4 collective-permute-start.13
  96.9 5.3 collective-permute-start.14
  98.4 6.2 %collective-permute-start.15 = (s32[48]{0:T(128)S(1)}, s32[48]{0:T(128)S(1)}, u32[]{:S(2)}, u32[]{:S(2)}) collective-permute-start(s32[48]{0:T(128)S(1)} %collective-permute-done.8), channel_id=1, source_target_pairs={{0,7},{1,0},{2,1},{3,2},{4,3},{5,4},{6,5},{7,6},{8,15},{9,8},{10,9... | collective-permute-start | bytes 584 | tf_op jit(solution)/shard_map/ppermute | solution.py:238
  112.0 18.7 %collective-permute-start.17 = (bf16[48,64,64]{2,1,0:T(8,128)(2,1)S(1)}, bf16[48,64,64]{2,1,0:T(8,128)(2,1)S(1)}, u32[]{:S(2)}, u32[]{:S(2)}) collective-permute-start(bf16[48,64,64]{2,1,0:T(8,128)(2,1)S(1)} %collective-permute-done.16), channel_id=1, source_target_pairs={{0,1},{1,2},{2,3},{3,4},{4,5},{5,6},{6,7},{7,0},{8,9},{9,10},{10,1... | collective-permute-start | bytes 1179656 | tf_op jit(solution)/shard_map/ppermute | solution.py:238
  116.0 31.5 %collective-permute-start.18 = (bf16[48,64,64]{2,1,0:T(8,128)(2,1)S(1)}, bf16[48,64,64]{2,1,0:T(8,128)(2,1)S(1)}, u32[]{:S(2)}, u32[]{:S(2)}) collective-permute-start(bf16[48,64,64]{2,1,0:T(8,128)(2,1)S(1)} %collective-permute-done.16), channel_id=1, source_target_pairs={{0,2},{1,3},{2,4},{3,5},{4,6},{5,7},{6,0},{7,1},{8,10},{9,11},{10,... | collective-permute-start | bytes 1179656 | tf_op jit(solution)/shard_map/ppermute | solution.py:238
  116.1 48.3 %collective-permute-start.19 = (bf16[48,64,64]{2,1,0:T(8,128)(2,1)S(1)}, bf16[48,64,64]{2,1,0:T(8,128)(2,1)S(1)}, u32[]{:S(2)}, u32[]{:S(2)}) collective-permute-start(bf16[48,64,64]{2,1,0:T(8,128)(2,1)S(1)} %collective-permute-done.16), channel_id=1, source_target_pairs={{0,3},{1,4},{2,5},{3,6},{4,7},{5,0},{6,1},{7,2},{8,11},{9,12},{10,... | collective-permute-start | bytes 1179656 | tf_op jit(solution)/shard_map/ppermute | solution.py:238
  118.6 127.4 %collective-permute-start.20 = (bf16[48,64,64]{2,1,0:T(8,128)(2,1)S(1)}, bf16[48,64,64]{2,1,0:T(8,128)(2,1)S(1)}, u32[]{:S(2)}, u32[]{:S(2)}) collective-permute-start(bf16[48,64,64]{2,1,0:T(8,128)(2,1)S(1)} %collective-permute-done.16), channel_id=1, source_target_pairs={{0,4},{1,5},{2,6},{3,7},{4,0},{5,1},{6,2},{7,3},{8,12},{9,13},{10,... | collective-permute-start | bytes 1179656 | tf_op jit(solution)/shard_map/ppermute | solution.py:238
  120.4 130.7 %collective-permute-start.21 = (bf16[48,64,64]{2,1,0:T(8,128)(2,1)S(1)}, bf16[48,64,64]{2,1,0:T(8,128)(2,1)S(1)}, u32[]{:S(2)}, u32[]{:S(2)}) collective-permute-start(bf16[48,64,64]{2,1,0:T(8,128)(2,1)S(1)} %collective-permute-done.16), channel_id=1, source_target_pairs={{0,5},{1,6},{2,7},{3,0},{4,1},{5,2},{6,3},{7,4},{8,13},{9,14},{10,... | collective-permute-start | bytes 1179656 | tf_op jit(solution)/shard_map/ppermute | solution.py:238
  130.6 120.6 %collective-permute-start.22 = (bf16[48,64,64]{2,1,0:T(8,128)(2,1)S(1)}, bf16[48,64,64]{2,1,0:T(8,128)(2,1)S(1)}, u32[]{:S(2)}, u32[]{:S(2)}) collective-permute-start(bf16[48,64,64]{2,1,0:T(8,128)(2,1)S(1)} %collective-permute-done.16), channel_id=1, source_target_pairs={{0,6},{1,7},{2,0},{3,1},{4,2},{5,3},{6,4},{7,5},{8,14},{9,15},{10,... | collective-permute-start | bytes 1179656 | tf_op jit(solution)/shard_map/ppermute | solution.py:238
  147.5 103.9 %collective-permute-start.23 = (bf16[48,64,64]{2,1,0:T(8,128)(2,1)S(1)}, bf16[48,64,64]{2,1,0:T(8,128)(2,1)S(1)}, u32[]{:S(2)}, u32[]{:S(2)}) collective-permute-start(bf16[48,64,64]{2,1,0:T(8,128)(2,1)S(1)} %collective-permute-done.16), channel_id=1, source_target_pairs={{0,7},{1,0},{2,1},{3,2},{4,3},{5,4},{6,5},{7,6},{8,15},{9,8},{10,9... | collective-permute-start | bytes 1179656 | tf_op jit(solution)/shard_map/ppermute | solution.py:238
  326.6 172.2 %collective-permute-start.24 = (bf16[512,3072]{1,0:T(8,128)(2,1)}, bf16[512,3072]{1,0:T(8,128)(2,1)S(1)}, u32[]{:S(2)}, u32[]{:S(2)}) collective-permute-start(bf16[512,3072]{1,0:T(8,128)(2,1)} %shard_map.47), channel_id=1, source_target_pairs={{0,4},{2,12},{4,20},{6,28},{8,0},{10,8},{12,16},{14,24},{16,6},{18... | collective-permute-start | bytes 9437192 | tf_op jit(solution)/shard_map/ppermute | solution.py:103
  372.4 160.0 %collective-permute-start.25 = (bf16[512,3072]{1,0:T(8,128)(2,1)}, bf16[512,3072]{1,0:T(8,128)(2,1)S(1)}, u32[]{:S(2)}, u32[]{:S(2)}) collective-permute-start(bf16[512,3072]{1,0:T(8,128)(2,1)} %shard_map.48), channel_id=1, source_target_pairs={{0,4},{2,12},{4,20},{6,28},{8,0},{10,8},{12,16},{14,24},{16,6},{18... | collective-permute-start | bytes 9437192 | tf_op jit(solution)/shard_map/ppermute | solution.py:103
Sparse Core Ops, SparseCore 0:
  13.9 96.1 all-gather.2
  111.7 84.9 all-gather.4

commit v19 on v18

--- a/solution.py
+++ b/solution.py
@@ -8,7 +8,7 @@
 BLK = 64
 CAP = 48
 LANE = 128
-ROW_CHUNK = 512
+ROW_CHUNK = 128
 
 
 def passed_along(value, axis, by):

time: 550 us -> 604 us (1.098)
  the two profiles are of different devices: /device:TPU:30 before, /device:TPU:5 now
where the time goes in v19:
time: 604 us; the launch traced here: 596 us
  Pallas kernels  236 us (39%)
  waiting for transfers between devices  189 us (31%)
  starting transfers between devices  85.2 us (14%)
  other arithmetic  37.4 us (6%)
  local copies, waits for them, and re-layouts  33.5 us (6%)
  between operations  14.3 us (2%)
    pallas_call x8, Pallas kernels, block_sparse_product(): pl.pallas_call(kernel, grid_spec=grid_spec, out_shape=jax.ShapeDtypeStruc...  217 us
    ppermute x21, waiting for transfers between devices, per_device(): lax.ppermute(part, ('row', 'col'), pairs)  112 us
    ppermute x8, waiting for transfers between devices, product_to_owners(): lax.ppermute(value, ('layer', 'row'), [(a * size + b, b * size + quarter[...  73.5 us
    ppermute x8, starting transfers between devices, product_to_owners(): lax.ppermute(value, ('layer', 'row'), [(a * size + b, b * size + quarter[...  39.2 us
    ppermute x21, starting transfers between devices, per_device(): lax.ppermute(part, ('row', 'col'), pairs)  37.5 us
    pallas_call x1, Pallas kernels, gathered_windows(): pl.pallas_call(kernel, grid_spec=grid_spec, out_shape=jax.ShapeDtypeStruc...  19.2 us
    gather x1, local copies, waits for them, and re-layouts, block_sparse_product(): padded = padded_blocks(blocks, block_rows, block_cols)[order]  16.3 us
  transfers between devices with their start and end apart: 40, of which 12 were waited for; matrix products, arithmetic and copies ran while one was open for 10% of the time, Pallas kernels for 40%

profile of v19, /device:TPU:5, one launch (start us, length us, event | category | flops | bytes accessed | tf_op | source)
XLA Modules:
  0.0 595.8 jit_solution(15394320257893979776)
XLA Ops:
  7.5 3.2 broadcast_multiply_fusion
  18.2 9.2 %scatter_custom_fusion = s32[48]{0:T(128)S(1)} fusion(s32[1152]{0:T(1024)S(1)} %fusion.3, s32[1152]{0:T(1024)S(1)} %broadcast.336, s32[]{:T(128)} %constant.199.clone.1), kind=kCustom, calls=%fused_computation.93 | custom fusion | flops 1152 | bytes 196 | tf_op jit(solution)/shard_map/scatter-add | solution.py:133
  33.1 19.2 %shard_map.46 = bf16[48,64,128]{2,1,0:T(8,128)(2,1)} custom-call(s32[48]{0:T(128)} %copy-done.4, s32[48]{0:T(128)} %and_select_fusion.cols_ref, bf16[1536,3072]{1,0:T(8,128)(2,1)} %green_ref.1), custom_call_target="tpu_custom_call" | custom-call | tf_op jit(solution)/shard_map/pallas_call | solution.py:122
  55.6 5.6 collective-permute-start.16
  61.7 3.2 collective-permute-start.4
  64.9 5.3 collective-permute-done.1
  70.2 7.6 %collective-permute-done.2 = s32[48]{0:T(128)S(1)} collective-permute-done((s32[48]{0:T(128)S(1)}, s32[48]{0:T(128)S(1)}, u32[]{:S(2)}, u32[]{:S(2)}) %collective-permute-start.2) | collective-permute-done | bytes 224 | tf_op jit(solution)/shard_map/ppermute | solution.py:238
  77.8 16.3 %collective-permute-start.7 = (s32[48]{0:T(128)S(1)}, s32[48]{0:T(128)S(1)}, u32[]{:S(2)}, u32[]{:S(2)}) collective-permute-start(s32[48]{0:T(128)S(1)} %collective-permute-done), channel_id=1, source_target_pairs={{0,7},{1,0},{2,1},{3,2},{4,3},{5,4},{6,5},{7,6},{8,15},{9,8},{10,9... | collective-permute-start | bytes 584 | tf_op jit(solution)/shard_map/ppermute | solution.py:238
  97.8 3.2 collective-permute-start.13
  104.7 3.8 sort.31
  122.6 3.8 collective-permute-done.17
  128.5 17.3 %collective-permute-done.18 = bf16[48,64,64]{2,1,0:T(8,128)(2,1)S(1)} collective-permute-done((bf16[48,64,64]{2,1,0:T(8,128)(2,1)S(1)}, bf16[48,64,64]{2,1,0:T(8,128)(2,1)S(1)}, u32[]{:S(2)}, u32[]{:S(2)}) %collective-permute-start.18) | collective-permute-done | bytes 393248 | tf_op jit(solution)/shard_map/ppermute | solution.py:238
  146.3 12.6 %collective-permute-done.19 = bf16[48,64,64]{2,1,0:T(8,128)(2,1)S(1)} collective-permute-done((bf16[48,64,64]{2,1,0:T(8,128)(2,1)S(1)}, bf16[48,64,64]{2,1,0:T(8,128)(2,1)S(1)}, u32[]{:S(2)}, u32[]{:S(2)}) %collective-permute-start.19) | collective-permute-done | bytes 393248 | tf_op jit(solution)/shard_map/ppermute | solution.py:238
  159.0 58.7 %collective-permute-done.20 = bf16[48,64,64]{2,1,0:T(8,128)(2,1)S(1)} collective-permute-done((bf16[48,64,64]{2,1,0:T(8,128)(2,1)S(1)}, bf16[48,64,64]{2,1,0:T(8,128)(2,1)S(1)}, u32[]{:S(2)}, u32[]{:S(2)}) %collective-permute-start.20) | collective-permute-done | bytes 393248 | tf_op jit(solution)/shard_map/ppermute | solution.py:238
  217.8 4.3 collective-permute-done.21
  224.1 6.3 %broadcast_select_fusion.1 = (bf16[384,64,128]{2,1,0:T(8,128)(2,1)S(1)}, bf16[384,64,128]{2,1,0:T(8,128)(2,1)S(1)}) fusion(pred[384]{0:T(512)(128)(4,1)S(1)} %fusion.6, bf16[384,64,64]{2,1,0:T(8,128)(2,1)S(1)} %get-tuple-element.15, bf16[384,64,64]{2,1,0:T(8,128)(2,1)S(1)} %get-tuple-element.14), kind=kLoop, calls=%fused_computation.10 | loop fusion | flops 18874368 | bytes 18874752 | tf_op jit(solution)/shard_map/jit(_where)/select_n | solution.py:151
  230.4 5.3 pad_maximum_fusion
  235.7 16.3 %gather_fusion.3 = bf16[384,128,128]{2,1,0:T(8,128)(2,1)} fusion(bf16[384,128,128]{2,1,0:T(8,128)(2,1)} %pad_maximum_fusion, s32[1024]{0:T(1024)S(1)} %pad_clamp_fusion.1), kind=kCustom, calls=%fused_computation.3 | custom fusion | bytes 25167360 | tf_op jit(solution)/shard_map/gather | solution.py:164
  251.9 27.2 %shard_map.47 = bf16[128,3072]{1,0:T(8,128)(2,1)} custom-call(s32[25]{0:T(128)} %convert_reduce_fusion.starts_ref, s32[384]{0:T(512)} %add_select_fusion.3.k_ref, bf16[128,12288]{1,0:T(8,128)(2,1)} %all-gather.9.cloned.1.call-done.t_ref, bf16[384,128,128]{2,1,0:T(8,128)(2,1)} %gather_fusion.3), custom_call_target="tpu_custom_call" | custom-call | tf_op jit(solution)/shard_map/pallas_call | solution.py:210
  279.5 27.2 %shard_map.48 = bf16[128,3072]{1,0:T(8,128)(2,1)} custom-call(s32[25]{0:T(128)} %convert_reduce_fusion.starts_ref, s32[384]{0:T(512)} %add_select_fusion.3.k_ref, bf16[128,12288]{1,0:T(8,128)(2,1)} %all-gather.11.cloned.1.call-done.t_ref, bf16[384,128,128]{2,1,0:T(8,128)(2,1)} %gather_fusion.3), custom_call_target="tpu_custom_call" | custom-call | tf_op jit(solution)/shard_map/pallas_call | solution.py:210
  306.7 28.2 %collective-permute-start.25 = (bf16[128,3072]{1,0:T(8,128)(2,1)}, bf16[128,3072]{1,0:T(8,128)(2,1)}, u32[]{:S(2)}, u32[]{:S(2)}) collective-permute-start(bf16[128,3072]{1,0:T(8,128)(2,1)} %shard_map.48), channel_id=1, source_target_pairs={{0,4},{2,12},{4,20},{6,28},{8,0},{10,8},{12,16},{14,24},{16,6},{18... | collective-permute-start | bytes 2359304 | tf_op jit(solution)/shard_map/ppermute | solution.py:103
  334.9 27.1 %shard_map.49 = bf16[128,3072]{1,0:T(8,128)(2,1)} custom-call(s32[25]{0:T(128)} %convert_reduce_fusion.starts_ref, s32[384]{0:T(512)} %add_select_fusion.3.k_ref, bf16[128,12288]{1,0:T(8,128)(2,1)} %all-gather.13.cloned.1.call-done.t_ref, bf16[384,128,128]{2,1,0:T(8,128)(2,1)} %gather_fusion.3), custom_call_target="tpu_custom_call" | custom-call | tf_op jit(solution)/shard_map/pallas_call | solution.py:210
  362.0 3.9 collective-permute-start.26
  365.9 27.0 %shard_map.50 = bf16[128,3072]{1,0:T(8,128)(2,1)} custom-call(s32[25]{0:T(128)} %convert_reduce_fusion.starts_ref, s32[384]{0:T(512)} %add_select_fusion.3.k_ref, bf16[128,12288]{1,0:T(8,128)(2,1)} %all-gather.15.cloned.1.call-done.t_ref, bf16[384,128,128]{2,1,0:T(8,128)(2,1)} %gather_fusion.3), custom_call_target="tpu_custom_call" | custom-call | tf_op jit(solution)/shard_map/pallas_call | solution.py:210
  392.9 5.8 collective-permute-start.27
  398.8 27.2 %shard_map.51 = bf16[128,3072]{1,0:T(8,128)(2,1)} custom-call(s32[25]{0:T(128)} %convert_reduce_fusion.starts_ref, s32[384]{0:T(512)} %add_select_fusion.3.k_ref, bf16[128,12288]{1,0:T(8,128)(2,1)} %all-gather.17.cloned.1.call-done.t_ref, bf16[384,128,128]{2,1,0:T(8,128)(2,1)} %gather_fusion.3), custom_call_target="tpu_custom_call" | custom-call | tf_op jit(solution)/shard_map/pallas_call | solution.py:210
  426.0 27.0 %shard_map.52 = bf16[128,3072]{1,0:T(8,128)(2,1)} custom-call(s32[25]{0:T(128)} %convert_reduce_fusion.starts_ref, s32[384]{0:T(512)} %add_select_fusion.3.k_ref, bf16[128,12288]{1,0:T(8,128)(2,1)} %all-gather.19.cloned.1.call-done.t_ref, bf16[384,128,128]{2,1,0:T(8,128)(2,1)} %gather_fusion.3), custom_call_target="tpu_custom_call" | custom-call | tf_op jit(solution)/shard_map/pallas_call | solution.py:210
  453.0 27.3 %shard_map.53 = bf16[128,3072]{1,0:T(8,128)(2,1)} custom-call(s32[25]{0:T(128)} %convert_reduce_fusion.starts_ref, s32[384]{0:T(512)} %add_select_fusion.3.k_ref, bf16[128,12288]{1,0:T(8,128)(2,1)} %all-gather.21.cloned.1.call-done.t_ref, bf16[384,128,128]{2,1,0:T(8,128)(2,1)} %gather_fusion.3), custom_call_target="tpu_custom_call" | custom-call | tf_op jit(solution)/shard_map/pallas_call | solution.py:210
  480.3 27.2 %shard_map.54 = bf16[128,3072]{1,0:T(8,128)(2,1)} custom-call(s32[25]{0:T(128)} %convert_reduce_fusion.starts_ref, s32[384]{0:T(512)} %add_select_fusion.3.k_ref, bf16[128,12288]{1,0:T(8,128)(2,1)} %all-gather.23.cloned.1.call-done.t_ref, bf16[384,128,128]{2,1,0:T(8,128)(2,1)} %gather_fusion.3), custom_call_target="tpu_custom_call" | custom-call | tf_op jit(solution)/shard_map/pallas_call | solution.py:210
  512.1 56.7 %collective-permute-done.29 = bf16[128,3072]{1,0:T(8,128)(2,1)S(1)} collective-permute-done((bf16[128,3072]{1,0:T(8,128)(2,1)S(1)}, bf16[128,3072]{1,0:T(8,128)(2,1)S(1)}, u32[]{:S(2)}, u32[]{:S(2)}) %collective-permute-start.29) | collective-permute-done | bytes 786464 | tf_op jit(solution)/shard_map/ppermute | solution.py:103
  568.9 8.4 %collective-permute-done.30 = bf16[128,3072]{1,0:T(8,128)(2,1)S(1)} collective-permute-done((bf16[128,3072]{1,0:T(8,128)(2,1)S(1)}, bf16[128,3072]{1,0:T(8,128)(2,1)S(1)}, u32[]{:S(2)}, u32[]{:S(2)}) %collective-permute-start.30) | collective-permute-done | bytes 786464 | tf_op jit(solution)/shard_map/ppermute | solution.py:103
  577.4 8.4 %collective-permute-done.31 = bf16[128,3072]{1,0:T(8,128)(2,1)S(1)} collective-permute-done((bf16[128,3072]{1,0:T(8,128)(2,1)}, bf16[128,3072]{1,0:T(8,128)(2,1)S(1)}, u32[]{:S(2)}, u32[]{:S(2)}) %collective-permute-start.31) | collective-permute-done | bytes 786464 | tf_op jit(solution)/shard_map/ppermute | solution.py:103
  (139 shorter events, 51.8 us)
Async XLA Ops:
  6.5 245.4 %all-gather.9.cloned.1.call-start = ((), (), s32[]{:S(2)}) async-start(), calls=%async_computation | async-start | bytes 3932160 | tf_op jit(solution)/shard_map/all_gather | solution.py:249
  13.5 266.0 %all-gather.11.cloned.1.call-start = ((), (), s32[]{:S(2)}) async-start(), calls=%async_computation.1 | async-start | bytes 3932160 | tf_op jit(solution)/shard_map/all_gather | solution.py:249
  14.2 320.7 %all-gather.13.cloned.1.call-start = ((), (), s32[]{:S(2)}) async-start(), calls=%async_computation.2 | async-start | bytes 3932160 | tf_op jit(solution)/shard_map/all_gather | solution.py:249
  14.9 350.9 %all-gather.15.cloned.1.call-start = ((), (), s32[]{:S(2)}) async-start(), calls=%async_computation.3 | async-start | bytes 3932160 | tf_op jit(solution)/shard_map/all_gather | solution.py:249
  15.5 383.2 %all-gather.17.cloned.1.call-start = ((), (), s32[]{:S(2)}) async-start(), calls=%async_computation.4 | async-start | bytes 3932160 | tf_op jit(solution)/shard_map/all_gather | solution.py:249
  16.1 409.9 %all-gather.19.cloned.1.call-start = ((), (), s32[]{:S(2)}) async-start(), calls=%async_computation.5 | async-start | bytes 3932160 | tf_op jit(solution)/shard_map/all_gather | solution.py:249
  16.7 436.3 %all-gather.21.cloned.1.call-start = ((), (), s32[]{:S(2)}) async-start(), calls=%async_computation.6 | async-start | bytes 3932160 | tf_op jit(solution)/shard_map/all_gather | solution.py:249
  17.4 462.9 %all-gather.23.cloned.1.call-start = ((), (), s32[]{:S(2)}) async-start(), calls=%async_computation.7 | async-start | bytes 3932160 | tf_op jit(solution)/shard_map/all_gather | solution.py:249
  29.8 31.5 %collective-permute-start = (s32[48]{0:T(128)S(1)}, s32[48]{0:T(128)S(1)}, u32[]{:S(2)}, u32[]{:S(2)}) collective-permute-start(s32[48]{0:T(128)S(1)} %get-tuple-element.10), channel_id=1, source_target_pairs={{0,8},{2,24},{4,0},{6,16},{8,10},{10,26},{12,2},{14,18},{16,12},{1... | collective-permute-start | bytes 584 | tf_op jit(solution)/shard_map/ppermute | solution.py:94
  31.2 30.5 %collective-permute-start.8 = (s32[48]{0:T(128)S(1)}, s32[48]{0:T(128)S(1)}, u32[]{:S(2)}, u32[]{:S(2)}) collective-permute-start(s32[48]{0:T(128)S(1)} %and_select_fusion.2.rows_ref), channel_id=1, source_target_pairs={{0,8},{2,24},{4,0},{6,16},{8,10},{10,26},{12,2},{14,18},{16,12},{1... | collective-permute-start | bytes 584 | tf_op jit(solution)/shard_map/ppermute | solution.py:94
  55.6 56.2 %collective-permute-start.16 = (bf16[48,64,64]{2,1,0:T(8,128)(2,1)S(1)}, bf16[48,64,64]{2,1,0:T(8,128)(2,1)S(1)}, u32[]{:S(2)}, u32[]{:S(2)}) collective-permute-start(bf16[48,64,64]{2,1,0:T(8,128)(2,1)S(1)} %fusion), channel_id=1, source_target_pairs={{0,8},{2,24},{4,0},{6,16},{8,10},{10,26},{12,2},{14,18},{16,12},{1... | collective-permute-start | bytes 1179656 | tf_op jit(solution)/shard_map/ppermute | solution.py:94
  61.4 16.4 %collective-permute-start.2 = (s32[48]{0:T(128)S(1)}, s32[48]{0:T(128)S(1)}, u32[]{:S(2)}, u32[]{:S(2)}) collective-permute-start(s32[48]{0:T(128)S(1)} %collective-permute-done), channel_id=1, source_target_pairs={{0,2},{1,3},{2,4},{3,5},{4,6},{5,7},{6,0},{7,1},{8,10},{9,11},{10,... | collective-permute-start | bytes 584 | tf_op jit(solution)/shard_map/ppermute | solution.py:238
  61.4 16.4 %collective-permute-start.3 = (s32[48]{0:T(128)S(1)}, s32[48]{0:T(128)S(1)}, u32[]{:S(2)}, u32[]{:S(2)}) collective-permute-start(s32[48]{0:T(128)S(1)} %collective-permute-done), channel_id=1, source_target_pairs={{0,3},{1,4},{2,5},{3,6},{4,7},{5,0},{6,1},{7,2},{8,11},{9,12},{10,... | collective-permute-start | bytes 584 | tf_op jit(solution)/shard_map/ppermute | solution.py:238
  61.7 32.4 %collective-permute-start.4 = (s32[48]{0:T(128)S(1)}, s32[48]{0:T(128)S(1)}, u32[]{:S(2)}, u32[]{:S(2)}) collective-permute-start(s32[48]{0:T(128)S(1)} %collective-permute-done), channel_id=1, source_target_pairs={{0,4},{1,5},{2,6},{3,7},{4,0},{5,1},{6,2},{7,3},{8,12},{9,13},{10,... | collective-permute-start | bytes 584 | tf_op jit(solution)/shard_map/ppermute | solution.py:238
  70.2 23.8 %collective-permute-start.5 = (s32[48]{0:T(128)S(1)}, s32[48]{0:T(128)S(1)}, u32[]{:S(2)}, u32[]{:S(2)}) collective-permute-start(s32[48]{0:T(128)S(1)} %collective-permute-done), channel_id=1, source_target_pairs={{0,5},{1,6},{2,7},{3,0},{4,1},{5,2},{6,3},{7,4},{8,13},{9,14},{10,... | collective-permute-start | bytes 584 | tf_op jit(solution)/shard_map/ppermute | solution.py:238
  77.8 16.3 %collective-permute-start.6 = (s32[48]{0:T(128)S(1)}, s32[48]{0:T(128)S(1)}, u32[]{:S(2)}, u32[]{:S(2)}) collective-permute-start(s32[48]{0:T(128)S(1)} %collective-permute-done), channel_id=1, source_target_pairs={{0,6},{1,7},{2,0},{3,1},{4,2},{5,3},{6,4},{7,5},{8,14},{9,15},{10,... | collective-permute-start | bytes 584 | tf_op jit(solution)/shard_map/ppermute | solution.py:238
  77.8 17.1 %collective-permute-start.7 = (s32[48]{0:T(128)S(1)}, s32[48]{0:T(128)S(1)}, u32[]{:S(2)}, u32[]{:S(2)}) collective-permute-start(s32[48]{0:T(128)S(1)} %collective-permute-done), channel_id=1, source_target_pairs={{0,7},{1,0},{2,1},{3,2},{4,3},{5,4},{6,5},{7,6},{8,15},{9,8},{10,9... | collective-permute-start | bytes 584 | tf_op jit(solution)/shard_map/ppermute | solution.py:238
  111.9 14.5 %collective-permute-start.17 = (bf16[48,64,64]{2,1,0:T(8,128)(2,1)S(1)}, bf16[48,64,64]{2,1,0:T(8,128)(2,1)S(1)}, u32[]{:S(2)}, u32[]{:S(2)}) collective-permute-start(bf16[48,64,64]{2,1,0:T(8,128)(2,1)S(1)} %collective-permute-done.16), channel_id=1, source_target_pairs={{0,1},{1,2},{2,3},{3,4},{4,5},{5,6},{6,7},{7,0},{8,9},{9,10},{10,1... | collective-permute-start | bytes 1179656 | tf_op jit(solution)/shard_map/ppermute | solution.py:238
  116.0 29.8 %collective-permute-start.18 = (bf16[48,64,64]{2,1,0:T(8,128)(2,1)S(1)}, bf16[48,64,64]{2,1,0:T(8,128)(2,1)S(1)}, u32[]{:S(2)}, u32[]{:S(2)}) collective-permute-start(bf16[48,64,64]{2,1,0:T(8,128)(2,1)S(1)} %collective-permute-done.16), channel_id=1, source_target_pairs={{0,2},{1,3},{2,4},{3,5},{4,6},{5,7},{6,0},{7,1},{8,10},{9,11},{10,... | collective-permute-start | bytes 1179656 | tf_op jit(solution)/shard_map/ppermute | solution.py:238
  117.5 41.5 %collective-permute-start.19 = (bf16[48,64,64]{2,1,0:T(8,128)(2,1)S(1)}, bf16[48,64,64]{2,1,0:T(8,128)(2,1)S(1)}, u32[]{:S(2)}, u32[]{:S(2)}) collective-permute-start(bf16[48,64,64]{2,1,0:T(8,128)(2,1)S(1)} %collective-permute-done.16), channel_id=1, source_target_pairs={{0,3},{1,4},{2,5},{3,6},{4,7},{5,0},{6,1},{7,2},{8,11},{9,12},{10,... | collective-permute-start | bytes 1179656 | tf_op jit(solution)/shard_map/ppermute | solution.py:238
  119.0 98.7 %collective-permute-start.20 = (bf16[48,64,64]{2,1,0:T(8,128)(2,1)S(1)}, bf16[48,64,64]{2,1,0:T(8,128)(2,1)S(1)}, u32[]{:S(2)}, u32[]{:S(2)}) collective-permute-start(bf16[48,64,64]{2,1,0:T(8,128)(2,1)S(1)} %collective-permute-done.16), channel_id=1, source_target_pairs={{0,4},{1,5},{2,6},{3,7},{4,0},{5,1},{6,2},{7,3},{8,12},{9,13},{10,... | collective-permute-start | bytes 1179656 | tf_op jit(solution)/shard_map/ppermute | solution.py:238
  120.3 101.8 %collective-permute-start.21 = (bf16[48,64,64]{2,1,0:T(8,128)(2,1)S(1)}, bf16[48,64,64]{2,1,0:T(8,128)(2,1)S(1)}, u32[]{:S(2)}, u32[]{:S(2)}) collective-permute-start(bf16[48,64,64]{2,1,0:T(8,128)(2,1)S(1)} %collective-permute-done.16), channel_id=1, source_target_pairs={{0,5},{1,6},{2,7},{3,0},{4,1},{5,2},{6,3},{7,4},{8,13},{9,14},{10,... | collective-permute-start | bytes 1179656 | tf_op jit(solution)/shard_map/ppermute | solution.py:238
  126.4 95.9 %collective-permute-start.22 = (bf16[48,64,64]{2,1,0:T(8,128)(2,1)S(1)}, bf16[48,64,64]{2,1,0:T(8,128)(2,1)S(1)}, u32[]{:S(2)}, u32[]{:S(2)}) collective-permute-start(bf16[48,64,64]{2,1,0:T(8,128)(2,1)S(1)} %collective-permute-done.16), channel_id=1, source_target_pairs={{0,6},{1,7},{2,0},{3,1},{4,2},{5,3},{6,4},{7,5},{8,14},{9,15},{10,... | collective-permute-start | bytes 1179656 | tf_op jit(solution)/shard_map/ppermute | solution.py:238
  145.8 76.6 %collective-permute-start.23 = (bf16[48,64,64]{2,1,0:T(8,128)(2,1)S(1)}, bf16[48,64,64]{2,1,0:T(8,128)(2,1)S(1)}, u32[]{:S(2)}, u32[]{:S(2)}) collective-permute-start(bf16[48,64,64]{2,1,0:T(8,128)(2,1)S(1)} %collective-permute-done.16), channel_id=1, source_target_pairs={{0,7},{1,0},{2,1},{3,2},{4,3},{5,4},{6,5},{7,6},{8,15},{9,8},{10,9... | collective-permute-start | bytes 1179656 | tf_op jit(solution)/shard_map/ppermute | solution.py:238
  279.1 228.4 %collective-permute-start.24 = (bf16[128,3072]{1,0:T(8,128)(2,1)}, bf16[128,3072]{1,0:T(8,128)(2,1)S(1)}, u32[]{:S(2)}, u32[]{:S(2)}) collective-permute-start(bf16[128,3072]{1,0:T(8,128)(2,1)} %shard_map.47), channel_id=1, source_target_pairs={{0,4},{2,12},{4,20},{6,28},{8,0},{10,8},{12,16},{14,24},{16,6},{18... | collective-permute-start | bytes 2359304 | tf_op jit(solution)/shard_map/ppermute | solution.py:103
  306.7 201.6 %collective-permute-start.25 = (bf16[128,3072]{1,0:T(8,128)(2,1)}, bf16[128,3072]{1,0:T(8,128)(2,1)}, u32[]{:S(2)}, u32[]{:S(2)}) collective-permute-start(bf16[128,3072]{1,0:T(8,128)(2,1)} %shard_map.48), channel_id=1, source_target_pairs={{0,4},{2,12},{4,20},{6,28},{8,0},{10,8},{12,16},{14,24},{16,6},{18... | collective-permute-start | bytes 2359304 | tf_op jit(solution)/shard_map/ppermute | solution.py:103
  362.0 147.6 %collective-permute-start.26 = (bf16[128,3072]{1,0:T(8,128)(2,1)}, bf16[128,3072]{1,0:T(8,128)(2,1)S(1)}, u32[]{:S(2)}, u32[]{:S(2)}) collective-permute-start(bf16[128,3072]{1,0:T(8,128)(2,1)} %shard_map.49), channel_id=1, source_target_pairs={{0,4},{2,12},{4,20},{6,28},{8,0},{10,8},{12,16},{14,24},{16,6},{18... | collective-permute-start | bytes 2359304 | tf_op jit(solution)/shard_map/ppermute | solution.py:103
  392.9 116.8 %collective-permute-start.27 = (bf16[128,3072]{1,0:T(8,128)(2,1)}, bf16[128,3072]{1,0:T(8,128)(2,1)}, u32[]{:S(2)}, u32[]{:S(2)}) collective-permute-start(bf16[128,3072]{1,0:T(8,128)(2,1)} %shard_map.50), channel_id=1, source_target_pairs={{0,4},{2,12},{4,20},{6,28},{8,0},{10,8},{12,16},{14,24},{16,6},{18... | collective-permute-start | bytes 2359304 | tf_op jit(solution)/shard_map/ppermute | solution.py:103
  426.0 84.9 %collective-permute-start.28 = (bf16[128,3072]{1,0:T(8,128)(2,1)}, bf16[128,3072]{1,0:T(8,128)(2,1)}, u32[]{:S(2)}, u32[]{:S(2)}) collective-permute-start(bf16[128,3072]{1,0:T(8,128)(2,1)} %shard_map.51), channel_id=1, source_target_pairs={{0,4},{2,12},{4,20},{6,28},{8,0},{10,8},{12,16},{14,24},{16,6},{18... | collective-permute-start | bytes 2359304 | tf_op jit(solution)/shard_map/ppermute | solution.py:103
  507.5 61.4 %collective-permute-start.29 = (bf16[128,3072]{1,0:T(8,128)(2,1)S(1)}, bf16[128,3072]{1,0:T(8,128)(2,1)S(1)}, u32[]{:S(2)}, u32[]{:S(2)}) collective-permute-start(bf16[128,3072]{1,0:T(8,128)(2,1)S(1)} %copy-done.1), channel_id=1, source_target_pairs={{0,4},{2,12},{4,20},{6,28},{8,0},{10,8},{12,16},{14,24},{16,6},{18... | collective-permute-start | bytes 2359304 | tf_op jit(solution)/shard_map/ppermute | solution.py:103
  508.3 69.0 %collective-permute-start.30 = (bf16[128,3072]{1,0:T(8,128)(2,1)S(1)}, bf16[128,3072]{1,0:T(8,128)(2,1)S(1)}, u32[]{:S(2)}, u32[]{:S(2)}) collective-permute-start(bf16[128,3072]{1,0:T(8,128)(2,1)S(1)} %copy-done), channel_id=1, source_target_pairs={{0,4},{2,12},{4,20},{6,28},{8,0},{10,8},{12,16},{14,24},{16,6},{18... | collective-permute-start | bytes 2359304 | tf_op jit(solution)/shard_map/ppermute | solution.py:103
  509.6 76.1 %collective-permute-start.31 = (bf16[128,3072]{1,0:T(8,128)(2,1)}, bf16[128,3072]{1,0:T(8,128)(2,1)S(1)}, u32[]{:S(2)}, u32[]{:S(2)}) collective-permute-start(bf16[128,3072]{1,0:T(8,128)(2,1)} %shard_map.54), channel_id=1, source_target_pairs={{0,4},{2,12},{4,20},{6,28},{8,0},{10,8},{12,16},{14,24},{16,6},{18... | collective-permute-start | bytes 2359304 | tf_op jit(solution)/shard_map/ppermute | solution.py:103
  (13 other events, 111.0 us)
Sparse Core Ops, SparseCore 0:
  13.6 30.1 all-gather.8
  45.3 41.6 all-gather.10
  88.6 32.2 all-gather.12
  122.3 28.5 all-gather.14
  152.3 28.5 all-gather.16
  182.3 28.5 all-gather.18
  212.4 28.5 all-gather.20
  242.6 28.7 all-gather.22

commit v20 on v17

--- a/solution.py
+++ b/solution.py
@@ -245,8 +245,13 @@
     entry_cols = block_col.reshape(-1)
     entry_blocks = blocks.reshape(-1, BLK, BLK)
     pieces = []
-    for start in range(0, ri_local * mu_local, ROW_CHUNK):
-        rows = lax.all_gather(own[start : start + ROW_CHUNK], "layer", axis=1, tiled=True)
+    total_rows = ri_local * mu_local
+    bounds = [0]
+    while bounds[-1] < total_rows:
+        size = ROW_CHUNK if bounds[-1] < total_rows // 2 else 2 * ROW_CHUNK
+        bounds.append(min(total_rows, bounds[-1] + size))
+    for start, stop in zip(bounds[:-1], bounds[1:]):
+        rows = lax.all_gather(own[start:stop], "layer", axis=1, tiled=True)
         (piece,) = block_sparse_product(
             rows, entry_blocks, entry_rows, entry_cols, tile_cols * BLK, 1
         )

time: 539 us -> 557 us (1.033)
  waiting for transfers between devices: 248 us -> 277 us
  Pallas kernels: 148 us -> 130 us
    ppermute x4 -> x3, waiting for transfers between devices: 105 us -> 137 us  [product_to_owners(): lax.ppermute(value, ('layer', 'row'), [(a * size + b, b * size + quarter[...]
    pallas_call x4 -> x3, Pallas kernels: 131 us -> 112 us  [block_sparse_product(): pl.pallas_call(kernel, grid_spec=grid_spec, out_shape=jax.ShapeDtypeStruc...]
  transfers between devices with their start and end apart: 32 -> 30, of which waited for: 13 -> 11; matrix products, arithmetic and copies ran while one was open for 11% -> 11% of each run, Pallas kernels for 28% -> 24%
where the time goes in v20:
time: 557 us; the launch traced here: 548 us
  waiting for transfers between devices  277 us (50%)
  Pallas kernels  130 us (23%)
  starting transfers between devices  54 us (10%)
  other arithmetic  41.3 us (7%)
  local copies, waits for them, and re-layouts  32.1 us (6%)
  between operations  13.6 us (2%)
    ppermute x21, waiting for transfers between devices, per_device(): lax.ppermute(part, ('row', 'col'), pairs)  140 us
    ppermute x3, waiting for transfers between devices, product_to_owners(): lax.ppermute(value, ('layer', 'row'), [(a * size + b, b * size + quarter[...  137 us
    pallas_call x3, Pallas kernels, block_sparse_product(): pl.pallas_call(kernel, grid_spec=grid_spec, out_shape=jax.ShapeDtypeStruc...  112 us
    ppermute x21, starting transfers between devices, per_device(): lax.ppermute(part, ('row', 'col'), pairs)  45.8 us
    pallas_call x1, Pallas kernels, gathered_windows(): pl.pallas_call(kernel, grid_spec=grid_spec, out_shape=jax.ShapeDtypeStruc...  18.4 us
    gather x1, local copies, waits for them, and re-layouts, block_sparse_product(): padded = padded_blocks(blocks, block_rows, block_cols)[order]  15.8 us
  transfers between devices with their start and end apart: 30, of which 11 were waited for; matrix products, arithmetic and copies ran while one was open for 11% of the time, Pallas kernels for 24%

profile of v20, /device:TPU:30, one launch (start us, length us, event | category | flops | bytes accessed | tf_op | source)
XLA Modules:
  0.0 548.1 jit_solution(12729015350688171158)
XLA Ops:
  7.5 3.2 broadcast_multiply_fusion
  10.7 2.7 copy-done
  15.3 3.7 slice_bitcast_fusion.2
  20.5 9.2 %scatter_custom_fusion = s32[48]{0:T(128)S(1)} fusion(s32[1152]{0:T(1024)S(1)} %fusion.3, s32[1152]{0:T(1024)S(1)} %broadcast.326, s32[]{:T(128)} %constant.144.clone.1), kind=kCustom, calls=%fused_computation.81 | custom fusion | flops 1152 | bytes 196 | tf_op jit(solution)/shard_map/scatter-add | solution.py:133
  33.8 18.4 %shard_map.46 = bf16[48,64,128]{2,1,0:T(8,128)(2,1)} custom-call(s32[48]{0:T(128)} %copy-done.2, s32[48]{0:T(128)} %and_select_fusion.cols_ref, bf16[1536,3072]{1,0:T(8,128)(2,1)} %green_ref.1), custom_call_target="tpu_custom_call" | custom-call | tf_op jit(solution)/shard_map/pallas_call | solution.py:122
  55.5 4.5 collective-permute-start.16
  60.2 2.9 collective-permute-start.3
  64.5 5.1 collective-permute-done.1
  69.6 24.4 %collective-permute-start.5 = (s32[48]{0:T(128)S(1)}, s32[48]{0:T(128)S(1)}, u32[]{:S(2)}, u32[]{:S(2)}) collective-permute-start(s32[48]{0:T(128)S(1)} %collective-permute-done), channel_id=1, source_target_pairs={{0,5},{1,6},{2,7},{3,0},{4,1},{5,2},{6,3},{7,4},{8,13},{9,14},{10,... | collective-permute-start | bytes 584 | tf_op jit(solution)/shard_map/ppermute | solution.py:238
  94.6 4.2 collective-permute-start.9
  98.8 2.0 collective-permute-start.10
  106.0 1.8 collective-permute-done.13
  109.2 2.4 collective-permute-done.15
  111.8 3.8 sort.21
  115.6 2.8 gather_fusion.1
  119.6 2.8 gather_fusion
  123.1 2.6 collective-permute-start.19
  127.6 10.1 %collective-permute-done.17 = bf16[48,64,64]{2,1,0:T(8,128)(2,1)S(1)} collective-permute-done((bf16[48,64,64]{2,1,0:T(8,128)(2,1)S(1)}, bf16[48,64,64]{2,1,0:T(8,128)(2,1)S(1)}, u32[]{:S(2)}, u32[]{:S(2)}) %collective-permute-start.17) | collective-permute-done | bytes 393248 | tf_op jit(solution)/shard_map/ppermute | solution.py:238
  137.8 16.7 %collective-permute-done.18 = bf16[48,64,64]{2,1,0:T(8,128)(2,1)S(1)} collective-permute-done((bf16[48,64,64]{2,1,0:T(8,128)(2,1)S(1)}, bf16[48,64,64]{2,1,0:T(8,128)(2,1)S(1)}, u32[]{:S(2)}, u32[]{:S(2)}) %collective-permute-start.18) | collective-permute-done | bytes 393248 | tf_op jit(solution)/shard_map/ppermute | solution.py:238
  154.9 16.6 %collective-permute-done.19 = bf16[48,64,64]{2,1,0:T(8,128)(2,1)S(1)} collective-permute-done((bf16[48,64,64]{2,1,0:T(8,128)(2,1)S(1)}, bf16[48,64,64]{2,1,0:T(8,128)(2,1)S(1)}, u32[]{:S(2)}, u32[]{:S(2)}) %collective-permute-start.19) | collective-permute-done | bytes 393248 | tf_op jit(solution)/shard_map/ppermute | solution.py:238
  171.6 80.3 %collective-permute-done.20 = bf16[48,64,64]{2,1,0:T(8,128)(2,1)S(1)} collective-permute-done((bf16[48,64,64]{2,1,0:T(8,128)(2,1)S(1)}, bf16[48,64,64]{2,1,0:T(8,128)(2,1)S(1)}, u32[]{:S(2)}, u32[]{:S(2)}) %collective-permute-start.20) | collective-permute-done | bytes 393248 | tf_op jit(solution)/shard_map/ppermute | solution.py:238
  252.0 5.0 collective-permute-done.21
  259.0 6.3 %broadcast_select_fusion.1 = (bf16[384,64,128]{2,1,0:T(8,128)(2,1)S(1)}, bf16[384,64,128]{2,1,0:T(8,128)(2,1)S(1)}) fusion(pred[384]{0:T(512)(128)(4,1)S(1)} %fusion.6, bf16[384,64,64]{2,1,0:T(8,128)(2,1)S(1)} %get-tuple-element.15, bf16[384,64,64]{2,1,0:T(8,128)(2,1)S(1)} %get-tuple-element.14), kind=kLoop, calls=%fused_computation.11 | loop fusion | flops 18874368 | bytes 18874752 | tf_op jit(solution)/shard_map/jit(_where)/select_n | solution.py:151
  265.3 5.3 pad_maximum_fusion
  270.6 15.8 %gather_fusion.3 = bf16[384,128,128]{2,1,0:T(8,128)(2,1)} fusion(bf16[384,128,128]{2,1,0:T(8,128)(2,1)} %pad_maximum_fusion, s32[1024]{0:T(1024)S(1)} %pad_clamp_fusion.1), kind=kCustom, calls=%fused_computation.3 | custom fusion | bytes 25167360 | tf_op jit(solution)/shard_map/gather | solution.py:164
  286.5 46.2 %shard_map.49 = bf16[512,3072]{1,0:T(8,128)(2,1)} custom-call(s32[25]{0:T(128)} %convert_reduce_fusion.starts_ref, s32[384]{0:T(512)} %add_select_fusion.3.k_ref, bf16[512,12288]{1,0:T(8,128)(2,1)} %all-gather.8.cloned.1.call-done.t_ref, bf16[384,128,128]{2,1,0:T(8,128)(2,1)} %gather_fusion.3), custom_call_target="tpu_custom_call" | custom-call | tf_op jit(solution)/shard_map/pallas_call | solution.py:210
  332.7 32.8 %shard_map.47 = bf16[256,3072]{1,0:T(8,128)(2,1)} custom-call(s32[25]{0:T(128)} %convert_reduce_fusion.starts_ref, s32[384]{0:T(512)} %add_select_fusion.3.k_ref, bf16[256,12288]{1,0:T(8,128)(2,1)} %all-gather.4.cloned.1.call-done.t_ref, bf16[384,128,128]{2,1,0:T(8,128)(2,1)} %gather_fusion.3), custom_call_target="tpu_custom_call" | custom-call | tf_op jit(solution)/shard_map/pallas_call | solution.py:210
  365.4 2.2 collective-permute-start.24
  367.6 32.6 %shard_map.48 = bf16[256,3072]{1,0:T(8,128)(2,1)} custom-call(s32[25]{0:T(128)} %convert_reduce_fusion.starts_ref, s32[384]{0:T(512)} %add_select_fusion.3.k_ref, bf16[256,12288]{1,0:T(8,128)(2,1)} %all-gather.6.cloned.1.call-done.t_ref, bf16[384,128,128]{2,1,0:T(8,128)(2,1)} %gather_fusion.3), custom_call_target="tpu_custom_call" | custom-call | tf_op jit(solution)/shard_map/pallas_call | solution.py:210
  400.4 120.1 %collective-permute-done.24 = bf16[256,3072]{1,0:T(8,128)(2,1)} collective-permute-done((bf16[256,3072]{1,0:T(8,128)(2,1)}, bf16[256,3072]{1,0:T(8,128)(2,1)}, u32[]{:S(2)}, u32[]{:S(2)}) %collective-permute-start.24) | collective-permute-done | bytes 1572896 | tf_op jit(solution)/shard_map/ppermute | solution.py:103
  520.5 16.7 %collective-permute-done.25 = bf16[256,3072]{1,0:T(8,128)(2,1)S(1)} collective-permute-done((bf16[256,3072]{1,0:T(8,128)(2,1)}, bf16[256,3072]{1,0:T(8,128)(2,1)S(1)}, u32[]{:S(2)}, u32[]{:S(2)}) %collective-permute-start.25) | collective-permute-done | bytes 1572896 | tf_op jit(solution)/shard_map/ppermute | solution.py:103
  537.3 4.1 maximum_bitcast_fusion
  (99 shorter events, 27.0 us)
Async XLA Ops:
  6.5 279.9 %all-gather.8.cloned.1.call-start = ((), (), s32[]{:S(2)}) async-start(), calls=%async_computation.2 | async-start | bytes 15728640 | tf_op jit(solution)/shard_map/all_gather | solution.py:254
  10.7 2.7 copy-start
  15.2 4.6 copy-start.1
  15.3 317.4 %all-gather.4.cloned.1.call-start = ((), (), s32[]{:S(2)}) async-start(), calls=%async_computation | async-start | bytes 7864320 | tf_op jit(solution)/shard_map/all_gather | solution.py:254
  19.1 348.5 %all-gather.6.cloned.1.call-start = ((), (), s32[]{:S(2)}) async-start(), calls=%async_computation.1 | async-start | bytes 7864320 | tf_op jit(solution)/shard_map/all_gather | solution.py:254
  32.1 27.9 %collective-permute-start = (s32[48]{0:T(128)S(1)}, s32[48]{0:T(128)S(1)}, u32[]{:S(2)}, u32[]{:S(2)}) collective-permute-start(s32[48]{0:T(128)S(1)} %get-tuple-element.10), channel_id=1, source_target_pairs={{0,8},{2,24},{4,0},{6,16},{8,10},{10,26},{12,2},{14,18},{16,12},{1... | collective-permute-start | bytes 584 | tf_op jit(solution)/shard_map/ppermute | solution.py:94
  32.6 30.4 %collective-permute-start.8 = (s32[48]{0:T(128)S(1)}, s32[48]{0:T(128)S(1)}, u32[]{:S(2)}, u32[]{:S(2)}) collective-permute-start(s32[48]{0:T(128)S(1)} %and_select_fusion.2.rows_ref), channel_id=1, source_target_pairs={{0,8},{2,24},{4,0},{6,16},{8,10},{10,26},{12,2},{14,18},{16,12},{1... | collective-permute-start | bytes 584 | tf_op jit(solution)/shard_map/ppermute | solution.py:94
  55.5 63.6 %collective-permute-start.16 = (bf16[48,64,64]{2,1,0:T(8,128)(2,1)S(1)}, bf16[48,64,64]{2,1,0:T(8,128)(2,1)S(1)}, u32[]{:S(2)}, u32[]{:S(2)}) collective-permute-start(bf16[48,64,64]{2,1,0:T(8,128)(2,1)S(1)} %fusion), channel_id=1, source_target_pairs={{0,8},{2,24},{4,0},{6,16},{8,10},{10,26},{12,2},{14,18},{16,12},{1... | collective-permute-start | bytes 1179656 | tf_op jit(solution)/shard_map/ppermute | solution.py:94
  60.0 9.5 %collective-permute-start.1 = (s32[48]{0:T(128)S(1)}, s32[48]{0:T(128)S(1)}, u32[]{:S(2)}, u32[]{:S(2)}) collective-permute-start(s32[48]{0:T(128)S(1)} %collective-permute-done), channel_id=1, source_target_pairs={{0,1},{1,2},{2,3},{3,4},{4,5},{5,6},{6,7},{7,0},{8,9},{9,10},{10,1... | collective-permute-start | bytes 584 | tf_op jit(solution)/shard_map/ppermute | solution.py:238
  60.1 33.9 %collective-permute-start.2 = (s32[48]{0:T(128)S(1)}, s32[48]{0:T(128)S(1)}, u32[]{:S(2)}, u32[]{:S(2)}) collective-permute-start(s32[48]{0:T(128)S(1)} %collective-permute-done), channel_id=1, source_target_pairs={{0,2},{1,3},{2,4},{3,5},{4,6},{5,7},{6,0},{7,1},{8,10},{9,11},{10,... | collective-permute-start | bytes 584 | tf_op jit(solution)/shard_map/ppermute | solution.py:238
  60.2 33.9 %collective-permute-start.3 = (s32[48]{0:T(128)S(1)}, s32[48]{0:T(128)S(1)}, u32[]{:S(2)}, u32[]{:S(2)}) collective-permute-start(s32[48]{0:T(128)S(1)} %collective-permute-done), channel_id=1, source_target_pairs={{0,3},{1,4},{2,5},{3,6},{4,7},{5,0},{6,1},{7,2},{8,11},{9,12},{10,... | collective-permute-start | bytes 584 | tf_op jit(solution)/shard_map/ppermute | solution.py:238
  63.1 31.5 %collective-permute-start.4 = (s32[48]{0:T(128)S(1)}, s32[48]{0:T(128)S(1)}, u32[]{:S(2)}, u32[]{:S(2)}) collective-permute-start(s32[48]{0:T(128)S(1)} %collective-permute-done), channel_id=1, source_target_pairs={{0,4},{1,5},{2,6},{3,7},{4,0},{5,1},{6,2},{7,3},{8,12},{9,13},{10,... | collective-permute-start | bytes 584 | tf_op jit(solution)/shard_map/ppermute | solution.py:238
  69.6 29.2 %collective-permute-start.5 = (s32[48]{0:T(128)S(1)}, s32[48]{0:T(128)S(1)}, u32[]{:S(2)}, u32[]{:S(2)}) collective-permute-start(s32[48]{0:T(128)S(1)} %collective-permute-done), channel_id=1, source_target_pairs={{0,5},{1,6},{2,7},{3,0},{4,1},{5,2},{6,3},{7,4},{8,13},{9,14},{10,... | collective-permute-start | bytes 584 | tf_op jit(solution)/shard_map/ppermute | solution.py:238
  94.0 6.8 %collective-permute-start.6 = (s32[48]{0:T(128)S(1)}, s32[48]{0:T(128)S(1)}, u32[]{:S(2)}, u32[]{:S(2)}) collective-permute-start(s32[48]{0:T(128)S(1)} %collective-permute-done), channel_id=1, source_target_pairs={{0,6},{1,7},{2,0},{3,1},{4,2},{5,3},{6,4},{7,5},{8,14},{9,15},{10,... | collective-permute-start | bytes 584 | tf_op jit(solution)/shard_map/ppermute | solution.py:238
  94.0 6.8 %collective-permute-start.7 = (s32[48]{0:T(128)S(1)}, s32[48]{0:T(128)S(1)}, u32[]{:S(2)}, u32[]{:S(2)}) collective-permute-start(s32[48]{0:T(128)S(1)} %collective-permute-done), channel_id=1, source_target_pairs={{0,7},{1,0},{2,1},{3,2},{4,3},{5,4},{6,5},{7,6},{8,15},{9,8},{10,9... | collective-permute-start | bytes 584 | tf_op jit(solution)/shard_map/ppermute | solution.py:238
  94.6 7.8 %collective-permute-start.9 = (s32[48]{0:T(128)S(1)}, s32[48]{0:T(128)S(1)}, u32[]{:S(2)}, u32[]{:S(2)}) collective-permute-start(s32[48]{0:T(128)S(1)} %collective-permute-done.8), channel_id=1, source_target_pairs={{0,1},{1,2},{2,3},{3,4},{4,5},{5,6},{6,7},{7,0},{8,9},{9,10},{10,1... | collective-permute-start | bytes 584 | tf_op jit(solution)/shard_map/ppermute | solution.py:238
  98.8 5.1 collective-permute-start.10
  100.8 4.6 collective-permute-start.11
  100.8 5.2 collective-permute-start.12
  102.4 5.4 collective-permute-start.13
  103.9 5.3 collective-permute-start.14
  105.4 6.2 %collective-permute-start.15 = (s32[48]{0:T(128)S(1)}, s32[48]{0:T(128)S(1)}, u32[]{:S(2)}, u32[]{:S(2)}) collective-permute-start(s32[48]{0:T(128)S(1)} %collective-permute-done.8), channel_id=1, source_target_pairs={{0,7},{1,0},{2,1},{3,2},{4,3},{5,4},{6,5},{7,6},{8,15},{9,8},{10,9... | collective-permute-start | bytes 584 | tf_op jit(solution)/shard_map/ppermute | solution.py:238
  119.1 18.7 %collective-permute-start.17 = (bf16[48,64,64]{2,1,0:T(8,128)(2,1)S(1)}, bf16[48,64,64]{2,1,0:T(8,128)(2,1)S(1)}, u32[]{:S(2)}, u32[]{:S(2)}) collective-permute-start(bf16[48,64,64]{2,1,0:T(8,128)(2,1)S(1)} %collective-permute-done.16), channel_id=1, source_target_pairs={{0,1},{1,2},{2,3},{3,4},{4,5},{5,6},{6,7},{7,0},{8,9},{9,10},{10,1... | collective-permute-start | bytes 1179656 | tf_op jit(solution)/shard_map/ppermute | solution.py:238
  123.1 31.5 %collective-permute-start.18 = (bf16[48,64,64]{2,1,0:T(8,128)(2,1)S(1)}, bf16[48,64,64]{2,1,0:T(8,128)(2,1)S(1)}, u32[]{:S(2)}, u32[]{:S(2)}) collective-permute-start(bf16[48,64,64]{2,1,0:T(8,128)(2,1)S(1)} %collective-permute-done.16), channel_id=1, source_target_pairs={{0,2},{1,3},{2,4},{3,5},{4,6},{5,7},{6,0},{7,1},{8,10},{9,11},{10,... | collective-permute-start | bytes 1179656 | tf_op jit(solution)/shard_map/ppermute | solution.py:238
  123.1 48.3 %collective-permute-start.19 = (bf16[48,64,64]{2,1,0:T(8,128)(2,1)S(1)}, bf16[48,64,64]{2,1,0:T(8,128)(2,1)S(1)}, u32[]{:S(2)}, u32[]{:S(2)}) collective-permute-start(bf16[48,64,64]{2,1,0:T(8,128)(2,1)S(1)} %collective-permute-done.16), channel_id=1, source_target_pairs={{0,3},{1,4},{2,5},{3,6},{4,7},{5,0},{6,1},{7,2},{8,11},{9,12},{10,... | collective-permute-start | bytes 1179656 | tf_op jit(solution)/shard_map/ppermute | solution.py:238
  125.7 126.2 %collective-permute-start.20 = (bf16[48,64,64]{2,1,0:T(8,128)(2,1)S(1)}, bf16[48,64,64]{2,1,0:T(8,128)(2,1)S(1)}, u32[]{:S(2)}, u32[]{:S(2)}) collective-permute-start(bf16[48,64,64]{2,1,0:T(8,128)(2,1)S(1)} %collective-permute-done.16), channel_id=1, source_target_pairs={{0,4},{1,5},{2,6},{3,7},{4,0},{5,1},{6,2},{7,3},{8,12},{9,13},{10,... | collective-permute-start | bytes 1179656 | tf_op jit(solution)/shard_map/ppermute | solution.py:238
  127.5 129.5 %collective-permute-start.21 = (bf16[48,64,64]{2,1,0:T(8,128)(2,1)S(1)}, bf16[48,64,64]{2,1,0:T(8,128)(2,1)S(1)}, u32[]{:S(2)}, u32[]{:S(2)}) collective-permute-start(bf16[48,64,64]{2,1,0:T(8,128)(2,1)S(1)} %collective-permute-done.16), channel_id=1, source_target_pairs={{0,5},{1,6},{2,7},{3,0},{4,1},{5,2},{6,3},{7,4},{8,13},{9,14},{10,... | collective-permute-start | bytes 1179656 | tf_op jit(solution)/shard_map/ppermute | solution.py:238
  137.7 119.4 %collective-permute-start.22 = (bf16[48,64,64]{2,1,0:T(8,128)(2,1)S(1)}, bf16[48,64,64]{2,1,0:T(8,128)(2,1)S(1)}, u32[]{:S(2)}, u32[]{:S(2)}) collective-permute-start(bf16[48,64,64]{2,1,0:T(8,128)(2,1)S(1)} %collective-permute-done.16), channel_id=1, source_target_pairs={{0,6},{1,7},{2,0},{3,1},{4,2},{5,3},{6,4},{7,5},{8,14},{9,15},{10,... | collective-permute-start | bytes 1179656 | tf_op jit(solution)/shard_map/ppermute | solution.py:238
  154.6 102.7 %collective-permute-start.23 = (bf16[48,64,64]{2,1,0:T(8,128)(2,1)S(1)}, bf16[48,64,64]{2,1,0:T(8,128)(2,1)S(1)}, u32[]{:S(2)}, u32[]{:S(2)}) collective-permute-start(bf16[48,64,64]{2,1,0:T(8,128)(2,1)S(1)} %collective-permute-done.16), channel_id=1, source_target_pairs={{0,7},{1,0},{2,1},{3,2},{4,3},{5,4},{6,5},{7,6},{8,15},{9,8},{10,9... | collective-permute-start | bytes 1179656 | tf_op jit(solution)/shard_map/ppermute | solution.py:238
  332.7 204.6 %collective-permute-start.26 = (bf16[512,3072]{1,0:T(8,128)(2,1)}, bf16[512,3072]{1,0:T(8,128)(2,1)S(1)}, u32[]{:S(2)}, u32[]{:S(2)}) collective-permute-start(bf16[512,3072]{1,0:T(8,128)(2,1)} %shard_map.49), channel_id=1, source_target_pairs={{0,4},{2,12},{4,20},{6,28},{8,0},{10,8},{12,16},{14,24},{16,6},{18... | collective-permute-start | bytes 9437192 | tf_op jit(solution)/shard_map/ppermute | solution.py:103
  365.4 155.1 %collective-permute-start.24 = (bf16[256,3072]{1,0:T(8,128)(2,1)}, bf16[256,3072]{1,0:T(8,128)(2,1)}, u32[]{:S(2)}, u32[]{:S(2)}) collective-permute-start(bf16[256,3072]{1,0:T(8,128)(2,1)} %shard_map.47), channel_id=1, source_target_pairs={{0,4},{2,12},{4,20},{6,28},{8,0},{10,8},{12,16},{14,24},{16,6},{18... | collective-permute-start | bytes 4718600 | tf_op jit(solution)/shard_map/ppermute | solution.py:103
  400.2 137.1 %collective-permute-start.25 = (bf16[256,3072]{1,0:T(8,128)(2,1)}, bf16[256,3072]{1,0:T(8,128)(2,1)S(1)}, u32[]{:S(2)}, u32[]{:S(2)}) collective-permute-start(bf16[256,3072]{1,0:T(8,128)(2,1)} %shard_map.48), channel_id=1, source_target_pairs={{0,4},{2,12},{4,20},{6,28},{8,0},{10,8},{12,16},{14,24},{16,6},{18... | collective-permute-start | bytes 4718600 | tf_op jit(solution)/shard_map/ppermute | solution.py:103
  (1 other events, 1.2 us)
Sparse Core Ops, SparseCore 0:
  15.4 96.1 all-gather.7
  113.1 49.2 all-gather.3
  163.9 46.3 all-gather.5

commit v21 on v17

--- a/solution.py
+++ b/solution.py
@@ -186,7 +186,7 @@
                 begin = starts_ref[first + chunk]
                 end = starts_ref[first + chunk + 1]
                 acc = jnp.zeros((row_total, LANE), jnp.float32)
-                for width in (4, 2):
+                for width in (8, 4, 2):
                     count = (end - begin) // width
                     acc = lax.fori_loop(0, count, grouped(width, begin), acc)
                     begin = begin + width * count

time: 539 us -> 535 us (level)
  Pallas kernels: 148 us -> 130 us
  waiting for transfers between devices: 248 us -> 263 us
    pallas_call x4, Pallas kernels: 131 us -> 112 us  [block_sparse_product(): pl.pallas_call(kernel, grid_spec=grid_spec, out_shape=jax.ShapeDtypeStruc...]
    ppermute x4, waiting for transfers between devices: 105 us -> 121 us  [product_to_owners(): lax.ppermute(value, ('layer', 'row'), [(a * size + b, b * size + quarter[...]
  transfers between devices with their start and end apart: 32 -> 32, of which waited for: 13 -> 13; matrix products, arithmetic and copies ran while one was open for 11% -> 11% of each run, Pallas kernels for 28% -> 25%
where the time goes in v21:
time: 535 us; the launch traced here: 527 us
  waiting for transfers between devices  263 us (49%)
  Pallas kernels  130 us (24%)
  starting transfers between devices  52.1 us (10%)
  other arithmetic  41 us (8%)
  local copies, waits for them, and re-layouts  26.8 us (5%)
  between operations  13.6 us (3%)
    ppermute x21, waiting for transfers between devices, per_device(): lax.ppermute(part, ('row', 'col'), pairs)  140 us
    ppermute x4, waiting for transfers between devices, product_to_owners(): lax.ppermute(value, ('layer', 'row'), [(a * size + b, b * size + quarter[...  121 us
    pallas_call x4, Pallas kernels, block_sparse_product(): pl.pallas_call(kernel, grid_spec=grid_spec, out_shape=jax.ShapeDtypeStruc...  112 us
    ppermute x21, starting transfers between devices, per_device(): lax.ppermute(part, ('row', 'col'), pairs)  46.3 us
    pallas_call x1, Pallas kernels, gathered_windows(): pl.pallas_call(kernel, grid_spec=grid_spec, out_shape=jax.ShapeDtypeStruc...  18.3 us
    gather x1, local copies, waits for them, and re-layouts, block_sparse_product(): padded = padded_blocks(blocks, block_rows, block_cols)[order]  15.9 us
  transfers between devices with their start and end apart: 32, of which 13 were waited for; matrix products, arithmetic and copies ran while one was open for 11% of the time, Pallas kernels for 25%

profile of v21, /device:TPU:30, one launch (start us, length us, event | category | flops | bytes accessed | tf_op | source)
XLA Modules:
  0.0 526.9 jit_solution(5330423577882997071)
XLA Ops:
  7.5 3.2 broadcast_multiply_fusion
  10.7 2.8 slice_bitcast_fusion.3
  16.4 9.2 %scatter_custom_fusion = s32[48]{0:T(128)S(1)} fusion(s32[1152]{0:T(1024)S(1)} %fusion.3, s32[1152]{0:T(1024)S(1)} %broadcast.328, s32[]{:T(128)} %constant.155.clone.1), kind=kCustom, calls=%fused_computation.82 | custom fusion | flops 1152 | bytes 196 | tf_op jit(solution)/shard_map/scatter-add | solution.py:133
  29.6 18.3 %shard_map.46 = bf16[48,64,128]{2,1,0:T(8,128)(2,1)} custom-call(s32[48]{0:T(128)} %copy-done.1, s32[48]{0:T(128)} %and_select_fusion.cols_ref, bf16[1536,3072]{1,0:T(8,128)(2,1)} %green_ref.1), custom_call_target="tpu_custom_call" | custom-call | tf_op jit(solution)/shard_map/pallas_call | solution.py:122
  51.0 4.0 collective-permute-start.16
  55.2 2.9 collective-permute-start.3
  59.5 5.1 collective-permute-done.1
  64.6 24.7 %collective-permute-start.5 = (s32[48]{0:T(128)S(1)}, s32[48]{0:T(128)S(1)}, u32[]{:S(2)}, u32[]{:S(2)}) collective-permute-start(s32[48]{0:T(128)S(1)} %collective-permute-done), channel_id=1, source_target_pairs={{0,5},{1,6},{2,7},{3,0},{4,1},{5,2},{6,3},{7,4},{8,13},{9,14},{10,... | collective-permute-start | bytes 584 | tf_op jit(solution)/shard_map/ppermute | solution.py:238
  90.0 4.2 collective-permute-start.9
  94.2 2.0 collective-permute-start.10
  104.6 2.4 collective-permute-done.15
  107.2 3.8 sort.23
  111.0 2.8 gather_fusion.1
  115.0 2.8 gather_fusion
  118.5 2.6 collective-permute-start.19
  122.9 10.1 %collective-permute-done.17 = bf16[48,64,64]{2,1,0:T(8,128)(2,1)S(1)} collective-permute-done((bf16[48,64,64]{2,1,0:T(8,128)(2,1)S(1)}, bf16[48,64,64]{2,1,0:T(8,128)(2,1)S(1)}, u32[]{:S(2)}, u32[]{:S(2)}) %collective-permute-start.17) | collective-permute-done | bytes 393248 | tf_op jit(solution)/shard_map/ppermute | solution.py:238
  133.2 16.7 %collective-permute-done.18 = bf16[48,64,64]{2,1,0:T(8,128)(2,1)S(1)} collective-permute-done((bf16[48,64,64]{2,1,0:T(8,128)(2,1)S(1)}, bf16[48,64,64]{2,1,0:T(8,128)(2,1)S(1)}, u32[]{:S(2)}, u32[]{:S(2)}) %collective-permute-start.18) | collective-permute-done | bytes 393248 | tf_op jit(solution)/shard_map/ppermute | solution.py:238
  150.3 16.5 %collective-permute-done.19 = bf16[48,64,64]{2,1,0:T(8,128)(2,1)S(1)} collective-permute-done((bf16[48,64,64]{2,1,0:T(8,128)(2,1)S(1)}, bf16[48,64,64]{2,1,0:T(8,128)(2,1)S(1)}, u32[]{:S(2)}, u32[]{:S(2)}) %collective-permute-start.19) | collective-permute-done | bytes 393248 | tf_op jit(solution)/shard_map/ppermute | solution.py:238
  166.9 80.4 %collective-permute-done.20 = bf16[48,64,64]{2,1,0:T(8,128)(2,1)S(1)} collective-permute-done((bf16[48,64,64]{2,1,0:T(8,128)(2,1)S(1)}, bf16[48,64,64]{2,1,0:T(8,128)(2,1)S(1)}, u32[]{:S(2)}, u32[]{:S(2)}) %collective-permute-start.20) | collective-permute-done | bytes 393248 | tf_op jit(solution)/shard_map/ppermute | solution.py:238
  247.5 5.1 collective-permute-done.21
  254.5 6.3 %broadcast_select_fusion.1 = (bf16[384,64,128]{2,1,0:T(8,128)(2,1)S(1)}, bf16[384,64,128]{2,1,0:T(8,128)(2,1)S(1)}) fusion(pred[384]{0:T(512)(128)(4,1)S(1)} %fusion.6, bf16[384,64,64]{2,1,0:T(8,128)(2,1)S(1)} %get-tuple-element.15, bf16[384,64,64]{2,1,0:T(8,128)(2,1)S(1)} %get-tuple-element.14), kind=kLoop, calls=%fused_computation.11 | loop fusion | flops 18874368 | bytes 18874752 | tf_op jit(solution)/shard_map/jit(_where)/select_n | solution.py:151
  260.8 5.2 pad_maximum_fusion
  266.0 15.9 %gather_fusion.3 = bf16[384,128,128]{2,1,0:T(8,128)(2,1)} fusion(bf16[384,128,128]{2,1,0:T(8,128)(2,1)} %pad_maximum_fusion, s32[1024]{0:T(1024)S(1)} %pad_clamp_fusion.1), kind=kCustom, calls=%fused_computation.3 | custom fusion | bytes 25167360 | tf_op jit(solution)/shard_map/gather | solution.py:164
  281.9 28.1 %shard_map.47 = bf16[256,3072]{1,0:T(8,128)(2,1)} custom-call(s32[25]{0:T(128)} %convert_reduce_fusion.starts_ref, s32[384]{0:T(512)} %add_select_fusion.3.k_ref, bf16[256,12288]{1,0:T(8,128)(2,1)} %all-gather.5.cloned.1.call-done.t_ref, bf16[384,128,128]{2,1,0:T(8,128)(2,1)} %gather_fusion.3), custom_call_target="tpu_custom_call" | custom-call | tf_op jit(solution)/shard_map/pallas_call | solution.py:210
  310.1 27.8 %shard_map.48 = bf16[256,3072]{1,0:T(8,128)(2,1)} custom-call(s32[25]{0:T(128)} %convert_reduce_fusion.starts_ref, s32[384]{0:T(512)} %add_select_fusion.3.k_ref, bf16[256,12288]{1,0:T(8,128)(2,1)} %all-gather.7.cloned.1.call-done.t_ref, bf16[384,128,128]{2,1,0:T(8,128)(2,1)} %gather_fusion.3), custom_call_target="tpu_custom_call" | custom-call | tf_op jit(solution)/shard_map/pallas_call | solution.py:210
  338.5 28.3 %shard_map.49 = bf16[256,3072]{1,0:T(8,128)(2,1)} custom-call(s32[25]{0:T(128)} %convert_reduce_fusion.starts_ref, s32[384]{0:T(512)} %add_select_fusion.3.k_ref, bf16[256,12288]{1,0:T(8,128)(2,1)} %all-gather.9.cloned.1.call-done.t_ref, bf16[384,128,128]{2,1,0:T(8,128)(2,1)} %gather_fusion.3), custom_call_target="tpu_custom_call" | custom-call | tf_op jit(solution)/shard_map/pallas_call | solution.py:210
  366.8 27.8 %shard_map.50 = bf16[256,3072]{1,0:T(8,128)(2,1)} custom-call(s32[25]{0:T(128)} %convert_reduce_fusion.starts_ref, s32[384]{0:T(512)} %add_select_fusion.3.k_ref, bf16[256,12288]{1,0:T(8,128)(2,1)} %all-gather.11.cloned.1.call-done.t_ref, bf16[384,128,128]{2,1,0:T(8,128)(2,1)} %gather_fusion.3), custom_call_target="tpu_custom_call" | custom-call | tf_op jit(solution)/shard_map/pallas_call | solution.py:210
  394.6 70.9 %collective-permute-done.24 = bf16[256,3072]{1,0:T(8,128)(2,1)S(1)} collective-permute-done((bf16[256,3072]{1,0:T(8,128)(2,1)}, bf16[256,3072]{1,0:T(8,128)(2,1)S(1)}, u32[]{:S(2)}, u32[]{:S(2)}) %collective-permute-start.24) | collective-permute-done | bytes 1572896 | tf_op jit(solution)/shard_map/ppermute | solution.py:103
  465.4 16.9 %collective-permute-done.25 = bf16[256,3072]{1,0:T(8,128)(2,1)S(1)} collective-permute-done((bf16[256,3072]{1,0:T(8,128)(2,1)}, bf16[256,3072]{1,0:T(8,128)(2,1)S(1)}, u32[]{:S(2)}, u32[]{:S(2)}) %collective-permute-start.25) | collective-permute-done | bytes 1572896 | tf_op jit(solution)/shard_map/ppermute | solution.py:103
  482.3 17.0 %collective-permute-done.26 = bf16[256,3072]{1,0:T(8,128)(2,1)} collective-permute-done((bf16[256,3072]{1,0:T(8,128)(2,1)}, bf16[256,3072]{1,0:T(8,128)(2,1)}, u32[]{:S(2)}, u32[]{:S(2)}) %collective-permute-start.26) | collective-permute-done | bytes 1572896 | tf_op jit(solution)/shard_map/ppermute | solution.py:103
  499.3 16.7 %collective-permute-done.27 = bf16[256,3072]{1,0:T(8,128)(2,1)S(1)} collective-permute-done((bf16[256,3072]{1,0:T(8,128)(2,1)}, bf16[256,3072]{1,0:T(8,128)(2,1)S(1)}, u32[]{:S(2)}, u32[]{:S(2)}) %collective-permute-start.27) | collective-permute-done | bytes 1572896 | tf_op jit(solution)/shard_map/ppermute | solution.py:103
  516.0 4.1 maximum_bitcast_fusion
  (102 shorter events, 28.6 us)
Async XLA Ops:
  6.5 275.4 %all-gather.5.cloned.1.call-start = ((), (), s32[]{:S(2)}) async-start(), calls=%async_computation | async-start | bytes 7864320 | tf_op jit(solution)/shard_map/all_gather | solution.py:249
  13.6 296.5 %all-gather.7.cloned.1.call-start = ((), (), s32[]{:S(2)}) async-start(), calls=%async_computation.1 | async-start | bytes 7864320 | tf_op jit(solution)/shard_map/all_gather | solution.py:249
  14.3 324.1 %all-gather.9.cloned.1.call-start = ((), (), s32[]{:S(2)}) async-start(), calls=%async_computation.2 | async-start | bytes 7864320 | tf_op jit(solution)/shard_map/all_gather | solution.py:249
  15.1 351.7 %all-gather.11.cloned.1.call-start = ((), (), s32[]{:S(2)}) async-start(), calls=%async_computation.3 | async-start | bytes 7864320 | tf_op jit(solution)/shard_map/all_gather | solution.py:249
  27.8 27.3 %collective-permute-start = (s32[48]{0:T(128)S(1)}, s32[48]{0:T(128)S(1)}, u32[]{:S(2)}, u32[]{:S(2)}) collective-permute-start(s32[48]{0:T(128)S(1)} %get-tuple-element.10), channel_id=1, source_target_pairs={{0,8},{2,24},{4,0},{6,16},{8,10},{10,26},{12,2},{14,18},{16,12},{1... | collective-permute-start | bytes 584 | tf_op jit(solution)/shard_map/ppermute | solution.py:94
  28.3 29.8 %collective-permute-start.8 = (s32[48]{0:T(128)S(1)}, s32[48]{0:T(128)S(1)}, u32[]{:S(2)}, u32[]{:S(2)}) collective-permute-start(s32[48]{0:T(128)S(1)} %and_select_fusion.2.rows_ref), channel_id=1, source_target_pairs={{0,8},{2,24},{4,0},{6,16},{8,10},{10,26},{12,2},{14,18},{16,12},{1... | collective-permute-start | bytes 584 | tf_op jit(solution)/shard_map/ppermute | solution.py:94
  51.0 63.4 %collective-permute-start.16 = (bf16[48,64,64]{2,1,0:T(8,128)(2,1)S(1)}, bf16[48,64,64]{2,1,0:T(8,128)(2,1)S(1)}, u32[]{:S(2)}, u32[]{:S(2)}) collective-permute-start(bf16[48,64,64]{2,1,0:T(8,128)(2,1)S(1)} %fusion), channel_id=1, source_target_pairs={{0,8},{2,24},{4,0},{6,16},{8,10},{10,26},{12,2},{14,18},{16,12},{1... | collective-permute-start | bytes 1179656 | tf_op jit(solution)/shard_map/ppermute | solution.py:94
  55.1 9.5 %collective-permute-start.1 = (s32[48]{0:T(128)S(1)}, s32[48]{0:T(128)S(1)}, u32[]{:S(2)}, u32[]{:S(2)}) collective-permute-start(s32[48]{0:T(128)S(1)} %collective-permute-done), channel_id=1, source_target_pairs={{0,1},{1,2},{2,3},{3,4},{4,5},{5,6},{6,7},{7,0},{8,9},{9,10},{10,1... | collective-permute-start | bytes 584 | tf_op jit(solution)/shard_map/ppermute | solution.py:238
  55.2 34.2 %collective-permute-start.2 = (s32[48]{0:T(128)S(1)}, s32[48]{0:T(128)S(1)}, u32[]{:S(2)}, u32[]{:S(2)}) collective-permute-start(s32[48]{0:T(128)S(1)} %collective-permute-done), channel_id=1, source_target_pairs={{0,2},{1,3},{2,4},{3,5},{4,6},{5,7},{6,0},{7,1},{8,10},{9,11},{10,... | collective-permute-start | bytes 584 | tf_op jit(solution)/shard_map/ppermute | solution.py:238
  55.2 34.2 %collective-permute-start.3 = (s32[48]{0:T(128)S(1)}, s32[48]{0:T(128)S(1)}, u32[]{:S(2)}, u32[]{:S(2)}) collective-permute-start(s32[48]{0:T(128)S(1)} %collective-permute-done), channel_id=1, source_target_pairs={{0,3},{1,4},{2,5},{3,6},{4,7},{5,0},{6,1},{7,2},{8,11},{9,12},{10,... | collective-permute-start | bytes 584 | tf_op jit(solution)/shard_map/ppermute | solution.py:238
  58.1 31.9 %collective-permute-start.4 = (s32[48]{0:T(128)S(1)}, s32[48]{0:T(128)S(1)}, u32[]{:S(2)}, u32[]{:S(2)}) collective-permute-start(s32[48]{0:T(128)S(1)} %collective-permute-done), channel_id=1, source_target_pairs={{0,4},{1,5},{2,6},{3,7},{4,0},{5,1},{6,2},{7,3},{8,12},{9,13},{10,... | collective-permute-start | bytes 584 | tf_op jit(solution)/shard_map/ppermute | solution.py:238
  64.6 29.5 %collective-permute-start.5 = (s32[48]{0:T(128)S(1)}, s32[48]{0:T(128)S(1)}, u32[]{:S(2)}, u32[]{:S(2)}) collective-permute-start(s32[48]{0:T(128)S(1)} %collective-permute-done), channel_id=1, source_target_pairs={{0,5},{1,6},{2,7},{3,0},{4,1},{5,2},{6,3},{7,4},{8,13},{9,14},{10,... | collective-permute-start | bytes 584 | tf_op jit(solution)/shard_map/ppermute | solution.py:238
  89.4 6.8 %collective-permute-start.6 = (s32[48]{0:T(128)S(1)}, s32[48]{0:T(128)S(1)}, u32[]{:S(2)}, u32[]{:S(2)}) collective-permute-start(s32[48]{0:T(128)S(1)} %collective-permute-done), channel_id=1, source_target_pairs={{0,6},{1,7},{2,0},{3,1},{4,2},{5,3},{6,4},{7,5},{8,14},{9,15},{10,... | collective-permute-start | bytes 584 | tf_op jit(solution)/shard_map/ppermute | solution.py:238
  89.4 6.8 %collective-permute-start.7 = (s32[48]{0:T(128)S(1)}, s32[48]{0:T(128)S(1)}, u32[]{:S(2)}, u32[]{:S(2)}) collective-permute-start(s32[48]{0:T(128)S(1)} %collective-permute-done), channel_id=1, source_target_pairs={{0,7},{1,0},{2,1},{3,2},{4,3},{5,4},{6,5},{7,6},{8,15},{9,8},{10,9... | collective-permute-start | bytes 584 | tf_op jit(solution)/shard_map/ppermute | solution.py:238
  90.0 7.8 %collective-permute-start.9 = (s32[48]{0:T(128)S(1)}, s32[48]{0:T(128)S(1)}, u32[]{:S(2)}, u32[]{:S(2)}) collective-permute-start(s32[48]{0:T(128)S(1)} %collective-permute-done.8), channel_id=1, source_target_pairs={{0,1},{1,2},{2,3},{3,4},{4,5},{5,6},{6,7},{7,0},{8,9},{9,10},{10,1... | collective-permute-start | bytes 584 | tf_op jit(solution)/shard_map/ppermute | solution.py:238
  94.2 5.1 collective-permute-start.10
  96.2 4.6 collective-permute-start.11
  96.2 5.2 collective-permute-start.12
  97.8 5.4 %collective-permute-start.13 = (s32[48]{0:T(128)S(1)}, s32[48]{0:T(128)S(1)}, u32[]{:S(2)}, u32[]{:S(2)}) collective-permute-start(s32[48]{0:T(128)S(1)} %collective-permute-done.8), channel_id=1, source_target_pairs={{0,5},{1,6},{2,7},{3,0},{4,1},{5,2},{6,3},{7,4},{8,13},{9,14},{10,... | collective-permute-start | bytes 584 | tf_op jit(solution)/shard_map/ppermute | solution.py:238
  99.3 5.3 %collective-permute-start.14 = (s32[48]{0:T(128)S(1)}, s32[48]{0:T(128)S(1)}, u32[]{:S(2)}, u32[]{:S(2)}) collective-permute-start(s32[48]{0:T(128)S(1)} %collective-permute-done.8), channel_id=1, source_target_pairs={{0,6},{1,7},{2,0},{3,1},{4,2},{5,3},{6,4},{7,5},{8,14},{9,15},{10,... | collective-permute-start | bytes 584 | tf_op jit(solution)/shard_map/ppermute | solution.py:238
  100.8 6.2 %collective-permute-start.15 = (s32[48]{0:T(128)S(1)}, s32[48]{0:T(128)S(1)}, u32[]{:S(2)}, u32[]{:S(2)}) collective-permute-start(s32[48]{0:T(128)S(1)} %collective-permute-done.8), channel_id=1, source_target_pairs={{0,7},{1,0},{2,1},{3,2},{4,3},{5,4},{6,5},{7,6},{8,15},{9,8},{10,9... | collective-permute-start | bytes 584 | tf_op jit(solution)/shard_map/ppermute | solution.py:238
  114.4 18.7 %collective-permute-start.17 = (bf16[48,64,64]{2,1,0:T(8,128)(2,1)S(1)}, bf16[48,64,64]{2,1,0:T(8,128)(2,1)S(1)}, u32[]{:S(2)}, u32[]{:S(2)}) collective-permute-start(bf16[48,64,64]{2,1,0:T(8,128)(2,1)S(1)} %collective-permute-done.16), channel_id=1, source_target_pairs={{0,1},{1,2},{2,3},{3,4},{4,5},{5,6},{6,7},{7,0},{8,9},{9,10},{10,1... | collective-permute-start | bytes 1179656 | tf_op jit(solution)/shard_map/ppermute | solution.py:238
  118.4 31.5 %collective-permute-start.18 = (bf16[48,64,64]{2,1,0:T(8,128)(2,1)S(1)}, bf16[48,64,64]{2,1,0:T(8,128)(2,1)S(1)}, u32[]{:S(2)}, u32[]{:S(2)}) collective-permute-start(bf16[48,64,64]{2,1,0:T(8,128)(2,1)S(1)} %collective-permute-done.16), channel_id=1, source_target_pairs={{0,2},{1,3},{2,4},{3,5},{4,6},{5,7},{6,0},{7,1},{8,10},{9,11},{10,... | collective-permute-start | bytes 1179656 | tf_op jit(solution)/shard_map/ppermute | solution.py:238
  118.5 48.3 %collective-permute-start.19 = (bf16[48,64,64]{2,1,0:T(8,128)(2,1)S(1)}, bf16[48,64,64]{2,1,0:T(8,128)(2,1)S(1)}, u32[]{:S(2)}, u32[]{:S(2)}) collective-permute-start(bf16[48,64,64]{2,1,0:T(8,128)(2,1)S(1)} %collective-permute-done.16), channel_id=1, source_target_pairs={{0,3},{1,4},{2,5},{3,6},{4,7},{5,0},{6,1},{7,2},{8,11},{9,12},{10,... | collective-permute-start | bytes 1179656 | tf_op jit(solution)/shard_map/ppermute | solution.py:238
  121.1 126.3 %collective-permute-start.20 = (bf16[48,64,64]{2,1,0:T(8,128)(2,1)S(1)}, bf16[48,64,64]{2,1,0:T(8,128)(2,1)S(1)}, u32[]{:S(2)}, u32[]{:S(2)}) collective-permute-start(bf16[48,64,64]{2,1,0:T(8,128)(2,1)S(1)} %collective-permute-done.16), channel_id=1, source_target_pairs={{0,4},{1,5},{2,6},{3,7},{4,0},{5,1},{6,2},{7,3},{8,12},{9,13},{10,... | collective-permute-start | bytes 1179656 | tf_op jit(solution)/shard_map/ppermute | solution.py:238
  122.9 129.6 %collective-permute-start.21 = (bf16[48,64,64]{2,1,0:T(8,128)(2,1)S(1)}, bf16[48,64,64]{2,1,0:T(8,128)(2,1)S(1)}, u32[]{:S(2)}, u32[]{:S(2)}) collective-permute-start(bf16[48,64,64]{2,1,0:T(8,128)(2,1)S(1)} %collective-permute-done.16), channel_id=1, source_target_pairs={{0,5},{1,6},{2,7},{3,0},{4,1},{5,2},{6,3},{7,4},{8,13},{9,14},{10,... | collective-permute-start | bytes 1179656 | tf_op jit(solution)/shard_map/ppermute | solution.py:238
  133.1 119.6 %collective-permute-start.22 = (bf16[48,64,64]{2,1,0:T(8,128)(2,1)S(1)}, bf16[48,64,64]{2,1,0:T(8,128)(2,1)S(1)}, u32[]{:S(2)}, u32[]{:S(2)}) collective-permute-start(bf16[48,64,64]{2,1,0:T(8,128)(2,1)S(1)} %collective-permute-done.16), channel_id=1, source_target_pairs={{0,6},{1,7},{2,0},{3,1},{4,2},{5,3},{6,4},{7,5},{8,14},{9,15},{10,... | collective-permute-start | bytes 1179656 | tf_op jit(solution)/shard_map/ppermute | solution.py:238
  149.9 102.8 %collective-permute-start.23 = (bf16[48,64,64]{2,1,0:T(8,128)(2,1)S(1)}, bf16[48,64,64]{2,1,0:T(8,128)(2,1)S(1)}, u32[]{:S(2)}, u32[]{:S(2)}) collective-permute-start(bf16[48,64,64]{2,1,0:T(8,128)(2,1)S(1)} %collective-permute-done.16), channel_id=1, source_target_pairs={{0,7},{1,0},{2,1},{3,2},{4,3},{5,4},{6,5},{7,6},{8,15},{9,8},{10,9... | collective-permute-start | bytes 1179656 | tf_op jit(solution)/shard_map/ppermute | solution.py:238
  310.1 155.4 %collective-permute-start.24 = (bf16[256,3072]{1,0:T(8,128)(2,1)}, bf16[256,3072]{1,0:T(8,128)(2,1)S(1)}, u32[]{:S(2)}, u32[]{:S(2)}) collective-permute-start(bf16[256,3072]{1,0:T(8,128)(2,1)} %shard_map.47), channel_id=1, source_target_pairs={{0,4},{2,12},{4,20},{6,28},{8,0},{10,8},{12,16},{14,24},{16,6},{18... | collective-permute-start | bytes 4718600 | tf_op jit(solution)/shard_map/ppermute | solution.py:103
  337.8 144.5 %collective-permute-start.25 = (bf16[256,3072]{1,0:T(8,128)(2,1)}, bf16[256,3072]{1,0:T(8,128)(2,1)S(1)}, u32[]{:S(2)}, u32[]{:S(2)}) collective-permute-start(bf16[256,3072]{1,0:T(8,128)(2,1)} %shard_map.48), channel_id=1, source_target_pairs={{0,4},{2,12},{4,20},{6,28},{8,0},{10,8},{12,16},{14,24},{16,6},{18... | collective-permute-start | bytes 4718600 | tf_op jit(solution)/shard_map/ppermute | solution.py:103
  366.8 132.5 %collective-permute-start.26 = (bf16[256,3072]{1,0:T(8,128)(2,1)}, bf16[256,3072]{1,0:T(8,128)(2,1)}, u32[]{:S(2)}, u32[]{:S(2)}) collective-permute-start(bf16[256,3072]{1,0:T(8,128)(2,1)} %shard_map.49), channel_id=1, source_target_pairs={{0,4},{2,12},{4,20},{6,28},{8,0},{10,8},{12,16},{14,24},{16,6},{18... | collective-permute-start | bytes 4718600 | tf_op jit(solution)/shard_map/ppermute | solution.py:103
  394.6 121.4 %collective-permute-start.27 = (bf16[256,3072]{1,0:T(8,128)(2,1)}, bf16[256,3072]{1,0:T(8,128)(2,1)S(1)}, u32[]{:S(2)}, u32[]{:S(2)}) collective-permute-start(bf16[256,3072]{1,0:T(8,128)(2,1)} %shard_map.50), channel_id=1, source_target_pairs={{0,4},{2,12},{4,20},{6,28},{8,0},{10,8},{12,16},{14,24},{16,6},{18... | collective-permute-start | bytes 4718600 | tf_op jit(solution)/shard_map/ppermute | solution.py:103
  (2 other events, 3.4 us)
Sparse Core Ops, SparseCore 0:
  13.7 60.6 all-gather.4
  76.0 48.9 all-gather.6
  126.5 46.3 all-gather.8
  174.4 46.3 all-gather.10
